TPU v7x, 32 devices: a whole 2x2x4 slice. The times are simulated.
32 devices in a mesh: batch: 8 (over z, y), width: 4 (over x, core).
Axes of the slice: x: 2, y: 2, z: 4, core: 2. Of those that a mesh axis runs over, the one named last changes fastest.
Arguments:
- teacher: bfloat16 [2048, 4096], P('batch', 'width'), may hold values from -48 to 48, as said below
- student: bfloat16 [2048, 1024], P('batch', 'width'), may hold values from -48 to 48, as said below
Outputs:
- grad: float32 [2048, 1024], P('batch', 'width')
Inputs may be any that keep to these rules, and one draw needn't show every extreme that they name: `teacher`: Real-valued embeddings. `student`: Real-valued embeddings.
All inputs are finite; a program needn't handle non-finite values.
Results may differ from a plain program's by a relative error of at most 0.00075.
Values may be sent and summed in bfloat16 or wider, within the bound.
No kernel may reach another device: no remote copies, remote signals or barrier semaphores. Data moves between devices by JAX's collectives and lax.ppermute only.
A program may use at most 64 MiB of HBM per device.

v0:
```python
import jax
import jax.numpy as jnp
import numpy as np
from jax import lax
from jax.sharding import PartitionSpec as P

DT = 4096
DS = 1024
REACH = 4


def passed_along(block, axis, distance):
    devices = range(lax.axis_size(axis))
    route = [(i - distance, i) for i in devices if i - distance in devices]
    return lax.ppermute(block, axis, route)


def body(teacher, student):
    group = lax.axis_size("batch")
    owner = lax.axis_index("batch")
    rows_dev = teacher.shape[0]
    teacher_list = [teacher]
    student_list = [student]
    moving = (teacher, student)
    for offset in range(REACH):
        moving = passed_along((moving[0], moving[1]), "batch", -1)
        teacher_list.append(moving[0])
        student_list.append(moving[1])
    offset_list = list(range(REACH + 1))
    moving = (teacher, student)
    for offset in range(REACH):
        moving = passed_along((moving[0], moving[1]), "batch", 1)
        teacher_list.insert(0, moving[0])
        student_list.insert(0, moving[1])
        offset_list.insert(0, -(offset + 1))
    band_teacher = jnp.stack(teacher_list, axis=0)
    band_student = jnp.stack(student_list, axis=0)
    own_tsq = jnp.sum(jnp.square(teacher.astype(jnp.float32)), axis=1) / DT
    own_ssq = jnp.sum(jnp.square(student.astype(jnp.float32)), axis=1) / DS
    band_tsq = jnp.sum(jnp.square(band_teacher.astype(jnp.float32)), axis=2) / DT
    band_ssq = jnp.sum(jnp.square(band_student.astype(jnp.float32)), axis=2) / DS
    tgram = jnp.einsum("rk,wck->wrc", teacher, band_teacher, preferred_element_type=jnp.float32)
    sgram = jnp.einsum("rk,wck->wrc", student, band_student, preferred_element_type=jnp.float32)
    student_part = own_ssq[None, :, None] + band_ssq[:, None, :] - 2.0 * sgram / DS
    teacher_part = own_tsq[None, :, None] + band_tsq[:, None, :] - 2.0 * tgram / DT
    shard_terms = student_part - teacher_part
    partner = owner + jnp.asarray(np.array(offset_list, dtype=np.int32))
    valid = jnp.logical_and(partner >= 0, partner < group)
    residual = lax.psum(shard_terms, "width")
    residual = jnp.where(valid[:, None, None], residual, jnp.zeros_like(residual))
    residual_low = residual.astype(jnp.bfloat16)
    row_total = jnp.sum(residual, axis=(0, 2))
    pulled = jnp.einsum(
        "wrc,wck->rk", residual_low, band_student, preferred_element_type=jnp.float32
    )
    near_count = (2 * REACH + 1) * rows_dev
    grad = (student.astype(jnp.float32) * row_total[:, None] - pulled) / near_count
    return grad


def solution(mesh):
    in_specs = (P("batch", "width"), P("batch", "width"))
    out_specs = P("batch", "width")
    return jax.shard_map(body, mesh=mesh, in_specs=in_specs, out_specs=out_specs, check_vma=False)
```

profile of v0, /device:TPU:24, one launch (start us, length us, event | category | flops | bytes accessed | tf_op | source)
XLA Modules:
  0.0 209.2 jit_solution(6608622640676647879)
XLA Ops:
  6.5 0.0 copy-start.1
  6.5 0.0 all-reduce.2.cloned.1.call-start
  6.5 3.5 %collective-permute-start = (bf16[256,256]{1,0:T(8,128)(2,1)}, bf16[256,256]{1,0:T(8,128)(2,1)S(1)}, u32[]{:S(2)}, u32[]{:S(2)}) collective-permute-start(bf16[256,256]{1,0:T(8,128)(2,1)} %param.4), channel_id=1, source_target_pairs={{0,4},{4,8},{8,12},{12,16},{16,20},{20,24},{24,28},{1,5},{5,9},{9,... | collective-permute-start | bytes 393224 | tf_op jit(solution)/shard_map/ppermute | solution.py:15
  10.1 3.3 %collective-permute-start.4 = (bf16[256,256]{1,0:T(8,128)(2,1)}, bf16[256,256]{1,0:T(8,128)(2,1)S(1)}, u32[]{:S(2)}, u32[]{:S(2)}) collective-permute-start(bf16[256,256]{1,0:T(8,128)(2,1)} %param.4), channel_id=1, source_target_pairs={{4,0},{8,4},{12,8},{16,12},{20,16},{24,20},{28,24},{5,1},{9,5},{13... | collective-permute-start | bytes 393224 | tf_op jit(solution)/shard_map/ppermute | solution.py:15
  13.4 2.5 %collective-permute-start.8 = (bf16[256,1024]{1,0:T(8,128)(2,1)}, bf16[256,1024]{1,0:T(8,128)(2,1)S(1)}, u32[]{:S(2)}, u32[]{:S(2)}) collective-permute-start(bf16[256,1024]{1,0:T(8,128)(2,1)} %param.3), channel_id=1, source_target_pairs={{0,4},{4,8},{8,12},{12,16},{16,20},{20,24},{24,28},{1,5},{5,9},{9,... | collective-permute-start | bytes 1572872 | tf_op jit(solution)/shard_map/ppermute | solution.py:15
  16.0 4.2 %collective-permute-start.12 = (bf16[256,1024]{1,0:T(8,128)(2,1)}, bf16[256,1024]{1,0:T(8,128)(2,1)S(1)}, u32[]{:S(2)}, u32[]{:S(2)}) collective-permute-start(bf16[256,1024]{1,0:T(8,128)(2,1)} %param.3), channel_id=1, source_target_pairs={{4,0},{8,4},{12,8},{16,12},{20,16},{24,20},{28,24},{5,1},{9,5},{13... | collective-permute-start | bytes 1572872 | tf_op jit(solution)/shard_map/ppermute | solution.py:15
  20.2 0.0 collective-permute-done
  20.2 1.9 collective-permute-start.1
  22.1 1.2 multiply_reduce_fusion.2
  23.3 0.0 collective-permute-done.4
  23.4 4.8 %collective-permute-start.5 = (bf16[256,256]{1,0:T(8,128)(2,1)S(1)}, bf16[256,256]{1,0:T(8,128)(2,1)S(1)}, u32[]{:S(2)}, u32[]{:S(2)}) collective-permute-start(bf16[256,256]{1,0:T(8,128)(2,1)S(1)} %collective-permute-done.4), channel_id=1, source_target_pairs={{4,0},{8,4},{12,8},{16,12},{20,16},{24,20},{28,24},{5,1},{9,5},{13... | collective-permute-start | bytes 393224 | tf_op jit(solution)/shard_map/ppermute | solution.py:15
  28.2 4.3 %collective-permute-done.1 = bf16[256,256]{1,0:T(8,128)(2,1)S(1)} collective-permute-done((bf16[256,256]{1,0:T(8,128)(2,1)S(1)}, bf16[256,256]{1,0:T(8,128)(2,1)S(1)}, u32[]{:S(2)}, u32[]{:S(2)}) %collective-permute-start.1) | collective-permute-done | bytes 131104 | tf_op jit(solution)/shard_map/ppermute | solution.py:15
  32.4 1.9 collective-permute-start.2
  34.4 1.0 fusion.8
  35.4 11.0 %collective-permute-done.5 = bf16[256,256]{1,0:T(8,128)(2,1)S(1)} collective-permute-done((bf16[256,256]{1,0:T(8,128)(2,1)S(1)}, bf16[256,256]{1,0:T(8,128)(2,1)S(1)}, u32[]{:S(2)}, u32[]{:S(2)}) %collective-permute-start.5) | collective-permute-done | bytes 131104 | tf_op jit(solution)/shard_map/ppermute | solution.py:15
  46.4 6.0 %collective-permute-start.6 = (bf16[256,256]{1,0:T(8,128)(2,1)S(1)}, bf16[256,256]{1,0:T(8,128)(2,1)S(1)}, u32[]{:S(2)}, u32[]{:S(2)}) collective-permute-start(bf16[256,256]{1,0:T(8,128)(2,1)S(1)} %collective-permute-done.5), channel_id=1, source_target_pairs={{4,0},{8,4},{12,8},{16,12},{20,16},{24,20},{28,24},{5,1},{9,5},{13... | collective-permute-start | bytes 393224 | tf_op jit(solution)/shard_map/ppermute | solution.py:15
  52.4 0.8 collective-permute-done.2
  53.2 1.9 collective-permute-start.3
  55.1 0.8 collective-permute-done.6
  55.9 4.7 %collective-permute-start.7 = (bf16[256,256]{1,0:T(8,128)(2,1)S(1)}, bf16[256,256]{1,0:T(8,128)(2,1)S(1)}, u32[]{:S(2)}, u32[]{:S(2)}) collective-permute-start(bf16[256,256]{1,0:T(8,128)(2,1)S(1)} %collective-permute-done.6), channel_id=1, source_target_pairs={{4,0},{8,4},{12,8},{16,12},{20,16},{24,20},{28,24},{5,1},{9,5},{13... | collective-permute-start | bytes 393224 | tf_op jit(solution)/shard_map/ppermute | solution.py:15
  60.6 0.4 collective-permute-done.3
  61.0 0.0 collective-permute-done.8
  61.0 1.9 collective-permute-start.9
  63.0 0.9 bitcast_dynamic-update-slice_fusion.13
  63.9 0.0 collective-permute-done.12
  63.9 4.8 %collective-permute-start.13 = (bf16[256,1024]{1,0:T(8,128)(2,1)S(1)}, bf16[256,1024]{1,0:T(8,128)(2,1)S(1)}, u32[]{:S(2)}, u32[]{:S(2)}) collective-permute-start(bf16[256,1024]{1,0:T(8,128)(2,1)S(1)} %collective-permute-done.12), channel_id=1, source_target_pairs={{4,0},{8,4},{12,8},{16,12},{20,16},{24,20},{28,24},{5,1},{9,5},{13... | collective-permute-start | bytes 1572872 | tf_op jit(solution)/shard_map/ppermute | solution.py:15
  68.8 7.4 %collective-permute-done.9 = bf16[256,1024]{1,0:T(8,128)(2,1)S(1)} collective-permute-done((bf16[256,1024]{1,0:T(8,128)(2,1)S(1)}, bf16[256,1024]{1,0:T(8,128)(2,1)S(1)}, u32[]{:S(2)}, u32[]{:S(2)}) %collective-permute-start.9) | collective-permute-done | bytes 524320 | tf_op jit(solution)/shard_map/ppermute | solution.py:15
  76.2 1.9 collective-permute-start.10
  78.2 0.0 collective-permute-done.7
  78.2 0.4 multiply_reduce_fusion.1
  78.6 8.8 %collective-permute-done.13 = bf16[256,1024]{1,0:T(8,128)(2,1)S(1)} collective-permute-done((bf16[256,1024]{1,0:T(8,128)(2,1)S(1)}, bf16[256,1024]{1,0:T(8,128)(2,1)S(1)}, u32[]{:S(2)}, u32[]{:S(2)}) %collective-permute-start.13) | collective-permute-done | bytes 524320 | tf_op jit(solution)/shard_map/ppermute | solution.py:15
  87.4 5.4 %collective-permute-start.14 = (bf16[256,1024]{1,0:T(8,128)(2,1)S(1)}, bf16[256,1024]{1,0:T(8,128)(2,1)S(1)}, u32[]{:S(2)}, u32[]{:S(2)}) collective-permute-start(bf16[256,1024]{1,0:T(8,128)(2,1)S(1)} %collective-permute-done.13), channel_id=1, source_target_pairs={{4,0},{8,4},{12,8},{16,12},{20,16},{24,20},{28,24},{5,1},{9,5},{13... | collective-permute-start | bytes 1572872 | tf_op jit(solution)/shard_map/ppermute | solution.py:15
  92.7 8.7 %collective-permute-done.10 = bf16[256,1024]{1,0:T(8,128)(2,1)S(1)} collective-permute-done((bf16[256,1024]{1,0:T(8,128)(2,1)S(1)}, bf16[256,1024]{1,0:T(8,128)(2,1)S(1)}, u32[]{:S(2)}, u32[]{:S(2)}) %collective-permute-start.10) | collective-permute-done | bytes 524320 | tf_op jit(solution)/shard_map/ppermute | solution.py:15
  101.5 1.9 collective-permute-start.11
  103.4 0.0 copy-done.1
  103.4 0.5 fusion.9
  103.9 0.0 copy-start.2
  103.9 8.7 %collective-permute-done.14 = bf16[256,1024]{1,0:T(8,128)(2,1)S(1)} collective-permute-done((bf16[256,1024]{1,0:T(8,128)(2,1)S(1)}, bf16[256,1024]{1,0:T(8,128)(2,1)S(1)}, u32[]{:S(2)}, u32[]{:S(2)}) %collective-permute-start.14) | collective-permute-done | bytes 524320 | tf_op jit(solution)/shard_map/ppermute | solution.py:15
  112.6 6.2 %collective-permute-start.15 = (bf16[256,1024]{1,0:T(8,128)(2,1)S(1)}, bf16[256,1024]{1,0:T(8,128)(2,1)S(1)}, u32[]{:S(2)}, u32[]{:S(2)}) collective-permute-start(bf16[256,1024]{1,0:T(8,128)(2,1)S(1)} %collective-permute-done.14), channel_id=1, source_target_pairs={{4,0},{8,4},{12,8},{16,12},{20,16},{24,20},{28,24},{5,1},{9,5},{13... | collective-permute-start | bytes 1572872 | tf_op jit(solution)/shard_map/ppermute | solution.py:15
  118.8 7.6 %collective-permute-done.11 = bf16[256,1024]{1,0:T(8,128)(2,1)S(1)} collective-permute-done((bf16[256,1024]{1,0:T(8,128)(2,1)S(1)}, bf16[256,1024]{1,0:T(8,128)(2,1)S(1)}, u32[]{:S(2)}, u32[]{:S(2)}) %collective-permute-start.11) | collective-permute-done | bytes 524320 | tf_op jit(solution)/shard_map/ppermute | solution.py:15
  126.6 0.0 copy-done.2
  126.8 10.8 %collective-permute-done.15 = bf16[256,1024]{1,0:T(8,128)(2,1)S(1)} collective-permute-done((bf16[256,1024]{1,0:T(8,128)(2,1)S(1)}, bf16[256,1024]{1,0:T(8,128)(2,1)S(1)}, u32[]{:S(2)}, u32[]{:S(2)}) %collective-permute-start.15) | collective-permute-done | bytes 524320 | tf_op jit(solution)/shard_map/ppermute | solution.py:15
  137.6 1.0 multiply_reduce_fusion
  138.6 3.0 %fusion = f32[9,256,256]{1,2,0:T(8,128)} fusion(f32[9,256,256]{2,1,0:T(8,128)S(1)} %fusion.9, bf16[9,256,1024]{2,1,0:T(8,128)(2,1)S(1)} %bitcast_dynamic-update-slice_fusion, f32[9,256]{1,0:T(8,128)S(1)} %broadcast_multiply_fusion, f32[256]{0:T(256)S(1)} %broadcast_multiply_fusion.2, f32[9,256]{1,0:T(8,128)S(1)} %broadcast_multiply_fusion.1, ...), kind=kOutput, calls=%fused_computation.2 | convolution fusion | flops 1212088320 | bytes 9981952 | tf_op jit(solution)/shard_map/rk,wck->wrc/dot_general | solution.py:42
  141.7 0.0 copy-start.3
  141.7 0.0 all-reduce.2.cloned.1.call-update
  141.7 0.6 copy-done.3
  142.3 56.2 %all-reduce.2.cloned.1.call-done = f32[9,256,256]{1,2,0:T(8,128)} async-done(((f32[9,256,256]{1,2,0:T(8,128)}), f32[9,256,256]{1,2,0:T(8,128)}) %all-reduce.2.cloned.1.call-update) | async-done | bytes 2359312 | tf_op jit(solution)/shard_map/psum | solution.py:49
  198.5 0.0 copy-start
  198.5 2.2 %select_reduce_fusion = f32[256]{0:T(256)S(1)} fusion(f32[9,256,256]{1,2,0:T(8,128)} %all-reduce.2.cloned.1.call-done, pred[9]{0:T(512)(128)(4,1)S(1)} %compare_and_fusion), kind=kLoop, calls=%fused_computation.6 | loop fusion | flops 1179392 | bytes 2360329 | tf_op jit(solution)/shard_map/reduce_sum | solution.py:52
  200.8 0.1 copy-done
  200.9 1.4 fusion.6
  (22 shorter events, 0.4 us)
Async XLA Ops:
  6.5 96.9 %copy-start.1 = (bf16[256,256]{1,0:T(8,128)(2,1)S(1)}, bf16[256,256]{1,0:T(8,128)(2,1)}, u32[]{:S(2)}) copy-start(bf16[256,256]{1,0:T(8,128)(2,1)} %param.4) | copy-start | bytes 393220
  6.5 192.0 %all-reduce.2.cloned.1.call-start = ((), (), s32[]{:S(2)}) async-start(), calls=%async_computation | async-start | bytes 4718592 | tf_op jit(solution)/shard_map/psum | solution.py:49
  6.5 13.6 %collective-permute-start = (bf16[256,256]{1,0:T(8,128)(2,1)}, bf16[256,256]{1,0:T(8,128)(2,1)S(1)}, u32[]{:S(2)}, u32[]{:S(2)}) collective-permute-start(bf16[256,256]{1,0:T(8,128)(2,1)} %param.4), channel_id=1, source_target_pairs={{0,4},{4,8},{8,12},{12,16},{16,20},{20,24},{24,28},{1,5},{5,9},{9,... | collective-permute-start | bytes 393224 | tf_op jit(solution)/shard_map/ppermute | solution.py:15
  10.1 13.3 %collective-permute-start.4 = (bf16[256,256]{1,0:T(8,128)(2,1)}, bf16[256,256]{1,0:T(8,128)(2,1)S(1)}, u32[]{:S(2)}, u32[]{:S(2)}) collective-permute-start(bf16[256,256]{1,0:T(8,128)(2,1)} %param.4), channel_id=1, source_target_pairs={{4,0},{8,4},{12,8},{16,12},{20,16},{24,20},{28,24},{5,1},{9,5},{13... | collective-permute-start | bytes 393224 | tf_op jit(solution)/shard_map/ppermute | solution.py:15
  13.4 47.6 %collective-permute-start.8 = (bf16[256,1024]{1,0:T(8,128)(2,1)}, bf16[256,1024]{1,0:T(8,128)(2,1)S(1)}, u32[]{:S(2)}, u32[]{:S(2)}) collective-permute-start(bf16[256,1024]{1,0:T(8,128)(2,1)} %param.3), channel_id=1, source_target_pairs={{0,4},{4,8},{8,12},{12,16},{16,20},{20,24},{24,28},{1,5},{5,9},{9,... | collective-permute-start | bytes 1572872 | tf_op jit(solution)/shard_map/ppermute | solution.py:15
  16.0 48.0 %collective-permute-start.12 = (bf16[256,1024]{1,0:T(8,128)(2,1)}, bf16[256,1024]{1,0:T(8,128)(2,1)S(1)}, u32[]{:S(2)}, u32[]{:S(2)}) collective-permute-start(bf16[256,1024]{1,0:T(8,128)(2,1)} %param.3), channel_id=1, source_target_pairs={{4,0},{8,4},{12,8},{16,12},{20,16},{24,20},{28,24},{5,1},{9,5},{13... | collective-permute-start | bytes 1572872 | tf_op jit(solution)/shard_map/ppermute | solution.py:15
  20.2 12.2 %collective-permute-start.1 = (bf16[256,256]{1,0:T(8,128)(2,1)S(1)}, bf16[256,256]{1,0:T(8,128)(2,1)S(1)}, u32[]{:S(2)}, u32[]{:S(2)}) collective-permute-start(bf16[256,256]{1,0:T(8,128)(2,1)S(1)} %collective-permute-done), channel_id=1, source_target_pairs={{0,4},{4,8},{8,12},{12,16},{16,20},{20,24},{24,28},{1,5},{5,9},{9,... | collective-permute-start | bytes 393224 | tf_op jit(solution)/shard_map/ppermute | solution.py:15
  23.4 23.0 %collective-permute-start.5 = (bf16[256,256]{1,0:T(8,128)(2,1)S(1)}, bf16[256,256]{1,0:T(8,128)(2,1)S(1)}, u32[]{:S(2)}, u32[]{:S(2)}) collective-permute-start(bf16[256,256]{1,0:T(8,128)(2,1)S(1)} %collective-permute-done.4), channel_id=1, source_target_pairs={{4,0},{8,4},{12,8},{16,12},{20,16},{24,20},{28,24},{5,1},{9,5},{13... | collective-permute-start | bytes 393224 | tf_op jit(solution)/shard_map/ppermute | solution.py:15
  32.4 20.7 %collective-permute-start.2 = (bf16[256,256]{1,0:T(8,128)(2,1)S(1)}, bf16[256,256]{1,0:T(8,128)(2,1)S(1)}, u32[]{:S(2)}, u32[]{:S(2)}) collective-permute-start(bf16[256,256]{1,0:T(8,128)(2,1)S(1)} %collective-permute-done.1), channel_id=1, source_target_pairs={{0,4},{4,8},{8,12},{12,16},{16,20},{20,24},{24,28},{1,5},{5,9},{9,... | collective-permute-start | bytes 393224 | tf_op jit(solution)/shard_map/ppermute | solution.py:15
  46.4 9.5 %collective-permute-start.6 = (bf16[256,256]{1,0:T(8,128)(2,1)S(1)}, bf16[256,256]{1,0:T(8,128)(2,1)S(1)}, u32[]{:S(2)}, u32[]{:S(2)}) collective-permute-start(bf16[256,256]{1,0:T(8,128)(2,1)S(1)} %collective-permute-done.5), channel_id=1, source_target_pairs={{4,0},{8,4},{12,8},{16,12},{20,16},{24,20},{28,24},{5,1},{9,5},{13... | collective-permute-start | bytes 393224 | tf_op jit(solution)/shard_map/ppermute | solution.py:15
  53.2 7.8 %collective-permute-start.3 = (bf16[256,256]{1,0:T(8,128)(2,1)S(1)}, bf16[256,256]{1,0:T(8,128)(2,1)S(1)}, u32[]{:S(2)}, u32[]{:S(2)}) collective-permute-start(bf16[256,256]{1,0:T(8,128)(2,1)S(1)} %collective-permute-done.2), channel_id=1, source_target_pairs={{0,4},{4,8},{8,12},{12,16},{16,20},{20,24},{24,28},{1,5},{5,9},{9,... | collective-permute-start | bytes 393224 | tf_op jit(solution)/shard_map/ppermute | solution.py:15
  55.9 22.3 %collective-permute-start.7 = (bf16[256,256]{1,0:T(8,128)(2,1)S(1)}, bf16[256,256]{1,0:T(8,128)(2,1)S(1)}, u32[]{:S(2)}, u32[]{:S(2)}) collective-permute-start(bf16[256,256]{1,0:T(8,128)(2,1)S(1)} %collective-permute-done.6), channel_id=1, source_target_pairs={{4,0},{8,4},{12,8},{16,12},{20,16},{24,20},{28,24},{5,1},{9,5},{13... | collective-permute-start | bytes 393224 | tf_op jit(solution)/shard_map/ppermute | solution.py:15
  61.0 15.2 %collective-permute-start.9 = (bf16[256,1024]{1,0:T(8,128)(2,1)S(1)}, bf16[256,1024]{1,0:T(8,128)(2,1)S(1)}, u32[]{:S(2)}, u32[]{:S(2)}) collective-permute-start(bf16[256,1024]{1,0:T(8,128)(2,1)S(1)} %collective-permute-done.8), channel_id=1, source_target_pairs={{0,4},{4,8},{8,12},{12,16},{16,20},{20,24},{24,28},{1,5},{5,9},{9,... | collective-permute-start | bytes 1572872 | tf_op jit(solution)/shard_map/ppermute | solution.py:15
  63.9 23.4 %collective-permute-start.13 = (bf16[256,1024]{1,0:T(8,128)(2,1)S(1)}, bf16[256,1024]{1,0:T(8,128)(2,1)S(1)}, u32[]{:S(2)}, u32[]{:S(2)}) collective-permute-start(bf16[256,1024]{1,0:T(8,128)(2,1)S(1)} %collective-permute-done.12), channel_id=1, source_target_pairs={{4,0},{8,4},{12,8},{16,12},{20,16},{24,20},{28,24},{5,1},{9,5},{13... | collective-permute-start | bytes 1572872 | tf_op jit(solution)/shard_map/ppermute | solution.py:15
  76.2 25.2 %collective-permute-start.10 = (bf16[256,1024]{1,0:T(8,128)(2,1)S(1)}, bf16[256,1024]{1,0:T(8,128)(2,1)S(1)}, u32[]{:S(2)}, u32[]{:S(2)}) collective-permute-start(bf16[256,1024]{1,0:T(8,128)(2,1)S(1)} %collective-permute-done.9), channel_id=1, source_target_pairs={{0,4},{4,8},{8,12},{12,16},{16,20},{20,24},{24,28},{1,5},{5,9},{9,... | collective-permute-start | bytes 1572872 | tf_op jit(solution)/shard_map/ppermute | solution.py:15
  87.4 25.2 %collective-permute-start.14 = (bf16[256,1024]{1,0:T(8,128)(2,1)S(1)}, bf16[256,1024]{1,0:T(8,128)(2,1)S(1)}, u32[]{:S(2)}, u32[]{:S(2)}) collective-permute-start(bf16[256,1024]{1,0:T(8,128)(2,1)S(1)} %collective-permute-done.13), channel_id=1, source_target_pairs={{4,0},{8,4},{12,8},{16,12},{20,16},{24,20},{28,24},{5,1},{9,5},{13... | collective-permute-start | bytes 1572872 | tf_op jit(solution)/shard_map/ppermute | solution.py:15
  101.5 25.0 %collective-permute-start.11 = (bf16[256,1024]{1,0:T(8,128)(2,1)S(1)}, bf16[256,1024]{1,0:T(8,128)(2,1)S(1)}, u32[]{:S(2)}, u32[]{:S(2)}) collective-permute-start(bf16[256,1024]{1,0:T(8,128)(2,1)S(1)} %collective-permute-done.10), channel_id=1, source_target_pairs={{0,4},{4,8},{8,12},{12,16},{16,20},{20,24},{24,28},{1,5},{5,9},{9,... | collective-permute-start | bytes 1572872 | tf_op jit(solution)/shard_map/ppermute | solution.py:15
  103.9 22.7 %copy-start.2 = (bf16[256,1024]{1,0:T(8,128)(2,1)S(1)}, bf16[256,1024]{1,0:T(8,128)(2,1)}, u32[]{:S(2)}) copy-start(bf16[256,1024]{1,0:T(8,128)(2,1)} %param.3) | copy-start | bytes 1572868
  112.6 25.0 %collective-permute-start.15 = (bf16[256,1024]{1,0:T(8,128)(2,1)S(1)}, bf16[256,1024]{1,0:T(8,128)(2,1)S(1)}, u32[]{:S(2)}, u32[]{:S(2)}) collective-permute-start(bf16[256,1024]{1,0:T(8,128)(2,1)S(1)} %collective-permute-done.14), channel_id=1, source_target_pairs={{4,0},{8,4},{12,8},{16,12},{20,16},{24,20},{28,24},{5,1},{9,5},{13... | collective-permute-start | bytes 1572872 | tf_op jit(solution)/shard_map/ppermute | solution.py:15
  141.7 0.7 copy-start.3
  198.5 2.4 %copy-start = (f32[9,256,256]{1,2,0:T(8,128)S(1)}, f32[9,256,256]{1,2,0:T(8,128)}, u32[]{:S(2)}) copy-start(f32[9,256,256]{1,2,0:T(8,128)} %all-reduce.2.cloned.1.call-done) | copy-start | bytes 7077892
Sparse Core Ops, SparseCore 0:
  141.8 56.6 all-reduce.1
where the time goes:
time: 212 us; the launch traced here: 209 us
  waiting for transfers between devices  125 us (59%)
  starting transfers between devices  57.1 us (27%)
  between operations  13.8 us (7%)
  other arithmetic  5.87 us (3%)
  matrix products  4.91 us (2%)
    ppermute x16, waiting for transfers between devices, passed_along(): return lax.ppermute(block, axis, route)  69.2 us
    ppermute x16, starting transfers between devices, passed_along(): return lax.ppermute(block, axis, route)  57.1 us
    psum x1, waiting for transfers between devices, body(): residual = lax.psum(shard_terms, 'width')  56.2 us
  transfers between devices with their start and end apart: 17, of which 12 were waited for; matrix products, arithmetic and copies ran while one was open for 2% of the time, Pallas kernels for 0%

commit v1 on v0

v1 whole, which is shorter than its diff:
```python
import jax
import jax.numpy as jnp
from jax import lax
from jax.sharding import PartitionSpec as P

REACH = 4


def shifted(block, axis, distance):
    size = lax.axis_size(axis)
    route = [(i + distance, i) for i in range(size) if 0 <= i + distance < size]
    return lax.ppermute(block, axis, route)


def body(teacher, student):
    group = lax.axis_size("batch")
    owner = lax.axis_index("batch")
    width = lax.axis_size("width")
    rows_dev = teacher.shape[0]
    dt = teacher.shape[1] * width
    ds = student.shape[1] * width
    reach = min(REACH, group - 1)
    near_count = (2 * REACH + 1) * rows_dev

    teacher_band = [teacher]
    student_band = [student]
    for d in range(1, reach + 1):
        t_d, s_d = shifted((teacher, student), "batch", d)
        teacher_band.append(t_d)
        student_band.append(s_d)

    def sq(x):
        xf = x.astype(jnp.float32)
        return jnp.sum(xf * xf, axis=1)

    gram_parts = []
    q_parts = []
    for t_d, s_d in zip(teacher_band, student_band):
        tg = lax.dot_general(teacher, t_d, (((1,), (1,)), ((), ())), preferred_element_type=jnp.float32)
        sg = lax.dot_general(student, s_d, (((1,), (1,)), ((), ())), preferred_element_type=jnp.float32)
        gram_parts.append(sg * (2.0 / ds) - tg * (2.0 / dt))
        q_parts.append(sq(s_d) / ds - sq(t_d) / dt)
    gram = lax.psum(jnp.stack(gram_parts), "width")
    q = lax.psum(jnp.stack(q_parts), "width")

    own_q = q[0]
    student_f = student.astype(jnp.float32)
    row_total = jnp.zeros((rows_dev,), jnp.float32)
    pulled = jnp.zeros(student.shape, jnp.float32)
    for d in range(reach + 1):
        resid = own_q[:, None] + q[d][None, :] - gram[d]
        if d > 0:
            valid = owner + d < group
            resid = jnp.where(valid, resid, jnp.zeros_like(resid))
        low = resid.astype(jnp.bfloat16)
        row_total = row_total + jnp.sum(resid, axis=1)
        pulled = pulled + jnp.dot(low, student_band[d], preferred_element_type=jnp.float32)
        if d > 0:
            back = lax.dot_general(low, student, (((0,), (0,)), ((), ())), preferred_element_type=jnp.float32)
            col = jnp.sum(resid, axis=0)
            back_r, col_r = shifted((back, col), "batch", -d)
            pulled = pulled + back_r
            row_total = row_total + col_r
    grad = (student_f * row_total[:, None] - pulled) / near_count
    return grad


def solution(mesh):
    in_specs = (P("batch", "width"), P("batch", "width"))
    out_specs = P("batch", "width")
    return jax.shard_map(body, mesh=mesh, in_specs=in_specs, out_specs=out_specs, check_vma=False)
```

time: 212 us -> 196 us (0.925); the launches traced: 209 us -> 196 us
  starting transfers between devices: 57.1 us -> 37.5 us
  blocking collectives: 0 us -> 6.36 us
  matrix products: 4.91 us -> 10.7 us
  waiting for transfers between devices: 125 us -> 122 us
    ppermute x16, starting transfers between devices: 57.1 us -> 37.5 us  [shifted(): return lax.ppermute(block, axis, route)]
    ppermute x16, waiting for transfers between devices: 69.2 us -> 60.9 us  [shifted(): return lax.ppermute(block, axis, route)]
    psum x0 -> x1, blocking collectives: none -> 6.36 us  [body(): q = lax.psum(jnp.stack(q_parts), 'width')]
    dot_general x3 -> x19, matrix products: 4.91 us -> 10.7 us  [the longest x5 4.68 us: body(): lax.dot_general(student, s_d, (((1,), (1,)), ((), ())), preferred_element...]
    psum x1, waiting for transfers between devices: 56.2 us -> 61.1 us  [body(): gram = lax.psum(jnp.stack(gram_parts), 'width')]
    reduce_sum x5 -> x11, other arithmetic: 5.84 us -> 5.17 us  [the longest x10 3.45 us: sq(): return jnp.sum(xf * xf, axis=1)]
  transfers between devices with their start and end apart: 17 -> 17, of which waited for: 12 -> 8; matrix products, arithmetic and copies ran while one was open for 2% -> 5% of each run, Pallas kernels for 0% -> 0%
where the time goes in v1:
time: 196 us
  waiting for transfers between devices  122 us (62%)
  starting transfers between devices  37.5 us (19%)
  between operations  13.8 us (7%)
  matrix products  10.7 us (5%)
  blocking collectives  6.36 us (3%)
  other arithmetic  5.22 us (3%)
    psum x1, waiting for transfers between devices, body(): gram = lax.psum(jnp.stack(gram_parts), 'width')  61.1 us
    ppermute x16, waiting for transfers between devices, shifted(): return lax.ppermute(block, axis, route)  60.9 us
    ppermute x16, starting transfers between devices, shifted(): return lax.ppermute(block, axis, route)  37.5 us
    psum x1, blocking collectives, body(): q = lax.psum(jnp.stack(q_parts), 'width')  6.36 us
    dot_general x5, matrix products, body(): lax.dot_general(student, s_d, (((1,), (1,)), ((), ())), preferred_element...  4.68 us
  transfers between devices with their start and end apart: 17, of which 8 were waited for; matrix products, arithmetic and copies ran while one was open for 5% of the time, Pallas kernels for 0%

profile of v1, /device:TPU:24, one launch (start us, length us, event | category | flops | bytes accessed | tf_op | source)
XLA Modules:
  0.0 195.6 jit_solution(8529367265711799001)
XLA Ops:
  6.5 2.4 %collective-permute-start.6 = (bf16[256,256]{1,0:T(8,128)(2,1)}, bf16[256,256]{1,0:T(8,128)(2,1)S(1)}, u32[]{:S(2)}, u32[]{:S(2)}) collective-permute-start(bf16[256,256]{1,0:T(8,128)(2,1)} %param.3), channel_id=1, source_target_pairs={{16,0},{20,4},{24,8},{28,12},{17,1},{21,5},{25,9},{29,13},{18,2},{... | collective-permute-start | bytes 393224 | tf_op jit(solution)/shard_map/ppermute | solution.py:12
  8.9 2.2 %collective-permute-start.4 = (bf16[256,256]{1,0:T(8,128)(2,1)}, bf16[256,256]{1,0:T(8,128)(2,1)S(1)}, u32[]{:S(2)}, u32[]{:S(2)}) collective-permute-start(bf16[256,256]{1,0:T(8,128)(2,1)} %param.3), channel_id=1, source_target_pairs={{12,0},{16,4},{20,8},{24,12},{28,16},{13,1},{17,5},{21,9},{25,13},... | collective-permute-start | bytes 393224 | tf_op jit(solution)/shard_map/ppermute | solution.py:12
  11.2 2.4 %collective-permute-start.2 = (bf16[256,256]{1,0:T(8,128)(2,1)}, bf16[256,256]{1,0:T(8,128)(2,1)S(1)}, u32[]{:S(2)}, u32[]{:S(2)}) collective-permute-start(bf16[256,256]{1,0:T(8,128)(2,1)} %param.3), channel_id=1, source_target_pairs={{8,0},{12,4},{16,8},{20,12},{24,16},{28,20},{9,1},{13,5},{17,9},{2... | collective-permute-start | bytes 393224 | tf_op jit(solution)/shard_map/ppermute | solution.py:12
  13.5 2.0 %collective-permute-start = (bf16[256,256]{1,0:T(8,128)(2,1)}, bf16[256,256]{1,0:T(8,128)(2,1)S(1)}, u32[]{:S(2)}, u32[]{:S(2)}) collective-permute-start(bf16[256,256]{1,0:T(8,128)(2,1)} %param.3), channel_id=1, source_target_pairs={{4,0},{8,4},{12,8},{16,12},{20,16},{24,20},{28,24},{5,1},{9,5},{13... | collective-permute-start | bytes 393224 | tf_op jit(solution)/shard_map/ppermute | solution.py:12
  15.6 1.3 collective-permute-start.7
  16.9 1.2 multiply_reduce_fusion.4
  18.2 1.0 fusion.22
  19.2 1.5 convolution_multiply_fusion.9
  20.7 0.9 fusion.16
  21.7 0.0 collective-permute-done.6
  21.7 1.3 collective-permute-start.5
  23.1 0.1 multiply_reduce_fusion.5
  23.2 0.0 collective-permute-done.4
  23.2 2.5 %collective-permute-start.3 = (bf16[256,1024]{1,0:T(8,128)(2,1)S(1)}, bf16[256,1024]{1,0:T(8,128)(2,1)S(1)}, u32[]{:S(2)}, u32[]{:S(2)}) collective-permute-start(bf16[256,1024]{1,0:T(8,128)(2,1)S(1)} %copy-done), channel_id=1, source_target_pairs={{8,0},{12,4},{16,8},{20,12},{24,16},{28,20},{9,1},{13,5},{17,9},{2... | collective-permute-start | bytes 1572872 | tf_op jit(solution)/shard_map/ppermute | solution.py:12
  25.7 0.1 multiply_reduce_fusion.6
  25.8 0.0 collective-permute-done.2
  25.8 10.2 %collective-permute-start.1 = (bf16[256,1024]{1,0:T(8,128)(2,1)S(1)}, bf16[256,1024]{1,0:T(8,128)(2,1)S(1)}, u32[]{:S(2)}, u32[]{:S(2)}) collective-permute-start(bf16[256,1024]{1,0:T(8,128)(2,1)S(1)} %copy-done), channel_id=1, source_target_pairs={{4,0},{8,4},{12,8},{16,12},{20,16},{24,20},{28,24},{5,1},{9,5},{13... | collective-permute-start | bytes 1572872 | tf_op jit(solution)/shard_map/ppermute | solution.py:12
  36.0 0.1 multiply_reduce_fusion.7
  36.2 0.0 collective-permute-done
  36.2 0.1 multiply_reduce_fusion.8
  36.3 0.0 collective-permute-done.7
  36.3 0.3 convolution_multiply_fusion.5
  36.6 6.8 %collective-permute-done.5 = bf16[256,1024]{1,0:T(8,128)(2,1)S(1)} collective-permute-done((bf16[256,1024]{1,0:T(8,128)(2,1)S(1)}, bf16[256,1024]{1,0:T(8,128)(2,1)S(1)}, u32[]{:S(2)}, u32[]{:S(2)}) %collective-permute-start.5) | collective-permute-done | bytes 524320 | tf_op jit(solution)/shard_map/ppermute | solution.py:12
  43.4 0.3 convolution_multiply_fusion.6
  43.8 10.9 %collective-permute-done.3 = bf16[256,1024]{1,0:T(8,128)(2,1)S(1)} collective-permute-done((bf16[256,1024]{1,0:T(8,128)(2,1)S(1)}, bf16[256,1024]{1,0:T(8,128)(2,1)S(1)}, u32[]{:S(2)}, u32[]{:S(2)}) %collective-permute-start.3) | collective-permute-done | bytes 524320 | tf_op jit(solution)/shard_map/ppermute | solution.py:12
  54.7 0.3 convolution_multiply_fusion.7
  55.0 10.3 %collective-permute-done.1 = bf16[256,1024]{1,0:T(8,128)(2,1)S(1)} collective-permute-done((bf16[256,1024]{1,0:T(8,128)(2,1)S(1)}, bf16[256,1024]{1,0:T(8,128)(2,1)S(1)}, u32[]{:S(2)}, u32[]{:S(2)}) %collective-permute-start.1) | collective-permute-done | bytes 524320 | tf_op jit(solution)/shard_map/ppermute | solution.py:12
  65.3 0.3 convolution_multiply_fusion.8
  65.7 0.9 fusion.13
  66.6 0.9 fusion.10
  67.5 0.9 fusion.7
  68.5 0.9 fusion.4
  69.4 0.0 all-reduce.2.cloned.1.call-update
  69.4 0.2 multiply_reduce_fusion
  69.6 0.2 multiply_reduce_fusion.1
  69.8 0.2 multiply_reduce_fusion.2
  70.0 0.2 multiply_reduce_fusion.3
  70.2 6.4 %psum.14 = f32[5,256]{1,0:T(8,128)S(1)} all-reduce(f32[5,256]{1,0:T(8,128)S(1)} %stack.26), channel_id=1, replica_groups=mesh['batch'=8,'width'=4] {'width'}, use_global_device_ids=true, to_apply=%region_10.0 | all-reduce | flops 1280 | bytes 10240 | tf_op jit(solution)/shard_map/psum | solution.py:44
  76.6 61.1 %all-reduce.2.cloned.1.call-done = f32[5,256,256]{2,1,0:T(8,128)} async-done(((f32[5,256,256]{2,1,0:T(8,128)}), f32[5,256,256]{2,1,0:T(8,128)}) %all-reduce.2.cloned.1.call-update) | async-done | bytes 1310736 | tf_op jit(solution)/shard_map/psum | solution.py:43
  137.7 1.7 fusion.38
  139.4 3.4 %collective-permute-start.8 = (f32[256]{0:T(256)S(1)}, f32[256]{0:T(256)S(1)}, u32[]{:S(2)}, u32[]{:S(2)}) collective-permute-start(f32[256]{0:T(256)S(1)} %get-tuple-element.6), channel_id=1, source_target_pairs={{0,4},{4,8},{8,12},{12,16},{16,20},{20,24},{24,28},{1,5},{5,9},{9,... | collective-permute-start | bytes 3080 | tf_op jit(solution)/shard_map/ppermute | solution.py:12
  142.8 1.3 collective-permute-start.11
  144.1 1.3 collective-permute-start.10
  145.4 1.3 collective-permute-start.9
  146.7 0.3 fusion.64
  147.0 1.9 collective-permute-start.12
  149.0 0.2 fusion.62
  149.2 0.2 fusion.54
  149.4 0.2 fusion.58
  149.7 0.3 fusion.56
  150.0 0.3 fusion.52
  150.3 0.3 fusion.60
  150.6 0.0 collective-permute-done.8
  150.6 1.3 collective-permute-start.13
  151.9 0.0 collective-permute-done.11
  151.9 1.3 collective-permute-start.15
  153.2 1.3 collective-permute-start.14
  154.5 0.2 fusion.48
  154.8 0.0 collective-permute-done.9
  154.8 4.2 %collective-permute-done.12 = f32[256,256]{1,0:T(8,128)S(1)} collective-permute-done((f32[256,256]{1,0:T(8,128)S(1)}, f32[256,256]{1,0:T(8,128)S(1)}, u32[]{:S(2)}, u32[]{:S(2)}) %collective-permute-start.12) | collective-permute-done | bytes 262176 | tf_op jit(solution)/shard_map/ppermute | solution.py:12
  159.0 3.8 %collective-permute-done.13 = f32[256,256]{1,0:T(8,128)S(1)} collective-permute-done((f32[256,256]{1,0:T(8,128)S(1)}, f32[256,256]{1,0:T(8,128)S(1)}, u32[]{:S(2)}, u32[]{:S(2)}) %collective-permute-start.13) | collective-permute-done | bytes 262176 | tf_op jit(solution)/shard_map/ppermute | solution.py:12
  162.9 13.7 %collective-permute-done.15 = f32[256,256]{1,0:T(8,128)S(1)} collective-permute-done((f32[256,256]{1,0:T(8,128)S(1)}, f32[256,256]{1,0:T(8,128)S(1)}, u32[]{:S(2)}, u32[]{:S(2)}) %collective-permute-start.15) | collective-permute-done | bytes 262176 | tf_op jit(solution)/shard_map/ppermute | solution.py:12
  176.5 11.2 %collective-permute-done.14 = f32[256,256]{1,0:T(8,128)S(1)} collective-permute-done((f32[256,256]{1,0:T(8,128)S(1)}, f32[256,256]{1,0:T(8,128)S(1)}, u32[]{:S(2)}, u32[]{:S(2)}) %collective-permute-start.14) | collective-permute-done | bytes 262176 | tf_op jit(solution)/shard_map/ppermute | solution.py:12
  187.7 1.0 fusion.24
  (16 shorter events, 0.1 us)
Async XLA Ops:
  6.5 14.2 %copy-start.1 = (bf16[256,256]{1,0:T(8,128)(2,1)S(1)}, bf16[256,256]{1,0:T(8,128)(2,1)}, u32[]{:S(2)}) copy-start(bf16[256,256]{1,0:T(8,128)(2,1)} %param.3) | copy-start | bytes 393220
  6.5 15.2 %copy-start = (bf16[256,1024]{1,0:T(8,128)(2,1)S(1)}, bf16[256,1024]{1,0:T(8,128)(2,1)}, u32[]{:S(2)}) copy-start(bf16[256,1024]{1,0:T(8,128)(2,1)} %param.2) | copy-start | bytes 1572868
  6.5 131.2 %all-reduce.2.cloned.1.call-start = ((), (), s32[]{:S(2)}) async-start(), calls=%async_computation | async-start | bytes 2621440 | tf_op jit(solution)/shard_map/psum | solution.py:43
  6.5 15.2 %collective-permute-start.6 = (bf16[256,256]{1,0:T(8,128)(2,1)}, bf16[256,256]{1,0:T(8,128)(2,1)S(1)}, u32[]{:S(2)}, u32[]{:S(2)}) collective-permute-start(bf16[256,256]{1,0:T(8,128)(2,1)} %param.3), channel_id=1, source_target_pairs={{16,0},{20,4},{24,8},{28,12},{17,1},{21,5},{25,9},{29,13},{18,2},{... | collective-permute-start | bytes 393224 | tf_op jit(solution)/shard_map/ppermute | solution.py:12
  8.9 14.3 %collective-permute-start.4 = (bf16[256,256]{1,0:T(8,128)(2,1)}, bf16[256,256]{1,0:T(8,128)(2,1)S(1)}, u32[]{:S(2)}, u32[]{:S(2)}) collective-permute-start(bf16[256,256]{1,0:T(8,128)(2,1)} %param.3), channel_id=1, source_target_pairs={{12,0},{16,4},{20,8},{24,12},{28,16},{13,1},{17,5},{21,9},{25,13},... | collective-permute-start | bytes 393224 | tf_op jit(solution)/shard_map/ppermute | solution.py:12
  11.2 14.7 %collective-permute-start.2 = (bf16[256,256]{1,0:T(8,128)(2,1)}, bf16[256,256]{1,0:T(8,128)(2,1)S(1)}, u32[]{:S(2)}, u32[]{:S(2)}) collective-permute-start(bf16[256,256]{1,0:T(8,128)(2,1)} %param.3), channel_id=1, source_target_pairs={{8,0},{12,4},{16,8},{20,12},{24,16},{28,20},{9,1},{13,5},{17,9},{2... | collective-permute-start | bytes 393224 | tf_op jit(solution)/shard_map/ppermute | solution.py:12
  13.5 22.6 %collective-permute-start = (bf16[256,256]{1,0:T(8,128)(2,1)}, bf16[256,256]{1,0:T(8,128)(2,1)S(1)}, u32[]{:S(2)}, u32[]{:S(2)}) collective-permute-start(bf16[256,256]{1,0:T(8,128)(2,1)} %param.3), channel_id=1, source_target_pairs={{4,0},{8,4},{12,8},{16,12},{20,16},{24,20},{28,24},{5,1},{9,5},{13... | collective-permute-start | bytes 393224 | tf_op jit(solution)/shard_map/ppermute | solution.py:12
  15.6 20.7 %collective-permute-start.7 = (bf16[256,1024]{1,0:T(8,128)(2,1)}, bf16[256,1024]{1,0:T(8,128)(2,1)S(1)}, u32[]{:S(2)}, u32[]{:S(2)}) collective-permute-start(bf16[256,1024]{1,0:T(8,128)(2,1)} %param.2), channel_id=1, source_target_pairs={{16,0},{20,4},{24,8},{28,12},{17,1},{21,5},{25,9},{29,13},{18,2},{... | collective-permute-start | bytes 1572872 | tf_op jit(solution)/shard_map/ppermute | solution.py:12
  21.7 21.7 %collective-permute-start.5 = (bf16[256,1024]{1,0:T(8,128)(2,1)S(1)}, bf16[256,1024]{1,0:T(8,128)(2,1)S(1)}, u32[]{:S(2)}, u32[]{:S(2)}) collective-permute-start(bf16[256,1024]{1,0:T(8,128)(2,1)S(1)} %copy-done), channel_id=1, source_target_pairs={{12,0},{16,4},{20,8},{24,12},{28,16},{13,1},{17,5},{21,9},{25,13},... | collective-permute-start | bytes 1572872 | tf_op jit(solution)/shard_map/ppermute | solution.py:12
  23.2 31.5 %collective-permute-start.3 = (bf16[256,1024]{1,0:T(8,128)(2,1)S(1)}, bf16[256,1024]{1,0:T(8,128)(2,1)S(1)}, u32[]{:S(2)}, u32[]{:S(2)}) collective-permute-start(bf16[256,1024]{1,0:T(8,128)(2,1)S(1)} %copy-done), channel_id=1, source_target_pairs={{8,0},{12,4},{16,8},{20,12},{24,16},{28,20},{9,1},{13,5},{17,9},{2... | collective-permute-start | bytes 1572872 | tf_op jit(solution)/shard_map/ppermute | solution.py:12
  25.8 39.5 %collective-permute-start.1 = (bf16[256,1024]{1,0:T(8,128)(2,1)S(1)}, bf16[256,1024]{1,0:T(8,128)(2,1)S(1)}, u32[]{:S(2)}, u32[]{:S(2)}) collective-permute-start(bf16[256,1024]{1,0:T(8,128)(2,1)S(1)} %copy-done), channel_id=1, source_target_pairs={{4,0},{8,4},{12,8},{16,12},{20,16},{24,20},{28,24},{5,1},{9,5},{13... | collective-permute-start | bytes 1572872 | tf_op jit(solution)/shard_map/ppermute | solution.py:12
  137.7 9.0 %copy-start.2 = (f32[5,256,256]{2,1,0:T(8,128)S(1)}, f32[5,256,256]{2,1,0:T(8,128)}, u32[]{:S(2)}) copy-start(f32[5,256,256]{2,1,0:T(8,128)} %all-reduce.2.cloned.1.call-done) | copy-start | bytes 3932164
  139.4 11.2 %collective-permute-start.8 = (f32[256]{0:T(256)S(1)}, f32[256]{0:T(256)S(1)}, u32[]{:S(2)}, u32[]{:S(2)}) collective-permute-start(f32[256]{0:T(256)S(1)} %get-tuple-element.6), channel_id=1, source_target_pairs={{0,4},{4,8},{8,12},{12,16},{16,20},{20,24},{24,28},{1,5},{5,9},{9,... | collective-permute-start | bytes 3080 | tf_op jit(solution)/shard_map/ppermute | solution.py:12
  142.8 9.1 %collective-permute-start.11 = (f32[256]{0:T(256)S(1)}, f32[256]{0:T(256)S(1)}, u32[]{:S(2)}, u32[]{:S(2)}) collective-permute-start(f32[256]{0:T(256)S(1)} %get-tuple-element.13), channel_id=1, source_target_pairs={{0,16},{4,20},{8,24},{12,28},{1,17},{5,21},{9,25},{13,29},{2,18},{... | collective-permute-start | bytes 3080 | tf_op jit(solution)/shard_map/ppermute | solution.py:12
  144.1 9.1 %collective-permute-start.10 = (f32[256]{0:T(256)S(1)}, f32[256]{0:T(256)S(1)}, u32[]{:S(2)}, u32[]{:S(2)}) collective-permute-start(f32[256]{0:T(256)S(1)} %get-tuple-element.15), channel_id=1, source_target_pairs={{0,12},{4,16},{8,20},{12,24},{16,28},{1,13},{5,17},{9,21},{13,25},... | collective-permute-start | bytes 3080 | tf_op jit(solution)/shard_map/ppermute | solution.py:12
  145.4 9.4 %collective-permute-start.9 = (f32[256]{0:T(256)S(1)}, f32[256]{0:T(256)S(1)}, u32[]{:S(2)}, u32[]{:S(2)}) collective-permute-start(f32[256]{0:T(256)S(1)} %get-tuple-element.17), channel_id=1, source_target_pairs={{0,8},{4,12},{8,16},{12,20},{16,24},{20,28},{1,9},{5,13},{9,17},{1... | collective-permute-start | bytes 3080 | tf_op jit(solution)/shard_map/ppermute | solution.py:12
  147.0 12.0 %collective-permute-start.12 = (f32[256,256]{1,0:T(8,128)S(1)}, f32[256,256]{1,0:T(8,128)S(1)}, u32[]{:S(2)}, u32[]{:S(2)}) collective-permute-start(f32[256,256]{1,0:T(8,128)S(1)} %fusion.64), channel_id=1, source_target_pairs={{0,4},{4,8},{8,12},{12,16},{16,20},{20,24},{24,28},{1,5},{5,9},{9,... | collective-permute-start | bytes 786440 | tf_op jit(solution)/shard_map/ppermute | solution.py:12
  150.6 12.2 %collective-permute-start.13 = (f32[256,256]{1,0:T(8,128)S(1)}, f32[256,256]{1,0:T(8,128)S(1)}, u32[]{:S(2)}, u32[]{:S(2)}) collective-permute-start(f32[256,256]{1,0:T(8,128)S(1)} %fusion.60), channel_id=1, source_target_pairs={{0,8},{4,12},{8,16},{12,20},{16,24},{20,28},{1,9},{5,13},{9,17},{1... | collective-permute-start | bytes 786440 | tf_op jit(solution)/shard_map/ppermute | solution.py:12
  151.9 24.6 %collective-permute-start.15 = (f32[256,256]{1,0:T(8,128)S(1)}, f32[256,256]{1,0:T(8,128)S(1)}, u32[]{:S(2)}, u32[]{:S(2)}) collective-permute-start(f32[256,256]{1,0:T(8,128)S(1)} %fusion.52), channel_id=1, source_target_pairs={{0,16},{4,20},{8,24},{12,28},{1,17},{5,21},{9,25},{13,29},{2,18},{... | collective-permute-start | bytes 786440 | tf_op jit(solution)/shard_map/ppermute | solution.py:12
  153.2 34.5 %collective-permute-start.14 = (f32[256,256]{1,0:T(8,128)S(1)}, f32[256,256]{1,0:T(8,128)S(1)}, u32[]{:S(2)}, u32[]{:S(2)}) collective-permute-start(f32[256,256]{1,0:T(8,128)S(1)} %fusion.56), channel_id=1, source_target_pairs={{0,12},{4,16},{8,20},{12,24},{16,28},{1,13},{5,17},{9,21},{13,25},... | collective-permute-start | bytes 786440 | tf_op jit(solution)/shard_map/ppermute | solution.py:12
Sparse Core Ops, SparseCore 0:
  69.6 68.0 all-reduce.1

commit v2 on v1

--- a/solution.py
+++ b/solution.py
@@ -12,36 +12,72 @@
     return lax.ppermute(block, axis, route)
 
 
+def swapped(block, axis, mask):
+    size = lax.axis_size(axis)
+    return lax.ppermute(block, axis, [(i, i ^ mask) for i in range(size)])
+
+
+def halves(x, axis, bit):
+    half = x.shape[axis] // 2
+    mine = (lax.axis_index("width") // bit) % 2
+    keep = lax.dynamic_slice_in_dim(x, mine * half, half, axis)
+    send = lax.dynamic_slice_in_dim(x, (1 - mine) * half, half, axis)
+    return keep, send, mine
+
+
+def joined(keep, got, axis, mine):
+    first = jnp.where(mine == 0, keep, got)
+    second = jnp.where(mine == 0, got, keep)
+    return jnp.concatenate([first, second], axis=axis)
+
+
+def width_sum(x):
+    width = lax.axis_size("width")
+    if width != 4:
+        return lax.psum(x, "width")
+    keep, send, core = halves(x, 2, 1)
+    part = keep + swapped(send, "width", 1)
+    keep, send, chip = halves(part, 1, 2)
+    part = keep + swapped(send, "width", 2)
+    part = joined(part, swapped(part, "width", 2), 1, chip)
+    return joined(part, swapped(part, "width", 1), 2, core)
+
+
 def body(teacher, student):
     group = lax.axis_size("batch")
     owner = lax.axis_index("batch")
     width = lax.axis_size("width")
     rows_dev = teacher.shape[0]
-    dt = teacher.shape[1] * width
-    ds = student.shape[1] * width
+    ft = teacher.shape[1]
+    fs = student.shape[1]
+    dt = ft * width
+    ds = fs * width
     reach = min(REACH, group - 1)
     near_count = (2 * REACH + 1) * rows_dev
 
+    both = jnp.concatenate([teacher, student], axis=1)
     teacher_band = [teacher]
     student_band = [student]
     for d in range(1, reach + 1):
-        t_d, s_d = shifted((teacher, student), "batch", d)
-        teacher_band.append(t_d)
-        student_band.append(s_d)
+        got = shifted(both, "batch", d)
+        teacher_band.append(got[:, :ft])
+        student_band.append(got[:, ft:])
 
     def sq(x):
         xf = x.astype(jnp.float32)
         return jnp.sum(xf * xf, axis=1)
 
-    gram_parts = []
-    q_parts = []
+    pad = (-(rows_dev + 1)) % 8
+    parts = []
     for t_d, s_d in zip(teacher_band, student_band):
         tg = lax.dot_general(teacher, t_d, (((1,), (1,)), ((), ())), preferred_element_type=jnp.float32)
         sg = lax.dot_general(student, s_d, (((1,), (1,)), ((), ())), preferred_element_type=jnp.float32)
-        gram_parts.append(sg * (2.0 / ds) - tg * (2.0 / dt))
-        q_parts.append(sq(s_d) / ds - sq(t_d) / dt)
-    gram = lax.psum(jnp.stack(gram_parts), "width")
-    q = lax.psum(jnp.stack(q_parts), "width")
+        q_d = sq(s_d) / ds - sq(t_d) / dt
+        parts.append(jnp.concatenate(
+            [sg * (2.0 / ds) - tg * (2.0 / dt), q_d[None, :], jnp.zeros((pad, rows_dev), jnp.float32)], axis=0))
+    total = width_sum(jnp.stack(parts))
+    gram = total[:, :rows_dev, :]
+    q = total[:, rows_dev, :]
 
     own_q = q[0]
     student_f = student.astype(jnp.float32)
@@ -58,9 +94,14 @@
         if d > 0:
             back = lax.dot_general(low, student, (((0,), (0,)), ((), ())), preferred_element_type=jnp.float32)
             col = jnp.sum(resid, axis=0)
-            back_r, col_r = shifted((back, col), "batch", -d)
-            pulled = pulled + back_r
-            row_total = row_total + col_r
+            if fs == rows_dev:
+                got = shifted(jnp.concatenate([back, col[None, :]], axis=0), "batch", -d)
+                pulled = pulled + got[:rows_dev]
+                row_total = row_total + got[rows_dev]
+            else:
+                back_r, col_r = shifted((back, col), "batch", -d)
+                pulled = pulled + back_r
+                row_total = row_total + col_r
     grad = (student_f * row_total[:, None] - pulled) / near_count
     return grad
 

time: 196 us -> 155 us (0.79)
  the two profiles are of different devices: /device:TPU:24 before, /device:TPU:8 now
where the time goes in v2:
time: 155 us
  waiting for transfers between devices  88.3 us (57%)
  starting transfers between devices  41.9 us (27%)
  matrix products  11.1 us (7%)
  other arithmetic  8.91 us (6%)
  local copies, waits for them, and re-layouts  3.85 us (2%)
    ppermute x8, waiting for transfers between devices, shifted(): return lax.ppermute(block, axis, route)  67.2 us
    ppermute x8, starting transfers between devices, shifted(): return lax.ppermute(block, axis, route)  38.7 us
    ppermute x4, waiting for transfers between devices, swapped(): return lax.ppermute(block, axis, [(i, i ^ mask) for i in range(size)])  21.1 us
    reduce_sum x10, other arithmetic, sq(): return jnp.sum(xf * xf, axis=1)  5.37 us
    dot_general x5, matrix products, body(): lax.dot_general(teacher, t_d, (((1,), (1,)), ((), ())), preferred_element...  3.77 us
    dot_general x5, matrix products, body(): jnp.dot(low, student_band[d], preferred_element_type=jnp.float32)  3.56 us
    ppermute x4, starting transfers between devices, swapped(): return lax.ppermute(block, axis, [(i, i ^ mask) for i in range(size)])  3.19 us
  transfers between devices with their start and end apart: 12, of which 8 were waited for; matrix products, arithmetic and copies ran while one was open for 5% of the time, Pallas kernels for 0%

profile of v2, /device:TPU:8, one launch (start us, length us, event | category | flops | bytes accessed | tf_op | source)
XLA Modules:
  0.0 154.5 jit_solution(18026091178171585926)
XLA Ops:
  0.0 1.9 %constant_dynamic-update-slice_fusion.1 = bf16[256,1280]{1,0:T(8,128)(2,1)} fusion(bf16[256,1024]{1,0:T(8,128)(2,1)} %param.2), kind=kLoop, calls=%fused_computation.127 | loop fusion | bytes 1048576
  1.9 1.6 %constant_dynamic-update-slice_fusion = bf16[256,1280]{1,0:T(8,128)(2,1)} fusion(bf16[256,1280]{1,0:T(8,128)(2,1)} %constant_dynamic-update-slice_fusion.1, bf16[256,256]{1,0:T(8,128)(2,1)} %param.3), kind=kLoop, calls=%fused_computation.126 | loop fusion | bytes 262144 | tf_op jit(solution)/shard_map/concatenate | solution.py:58
  3.5 3.3 %collective-permute-start = (bf16[256,1280]{1,0:T(8,128)(2,1)}, bf16[256,1280]{1,0:T(8,128)(2,1)S(1)}, u32[]{:S(2)}, u32[]{:S(2)}) collective-permute-start(bf16[256,1280]{1,0:T(8,128)(2,1)} %constant_dynamic-update-slice_fusion), channel_id=1, source_target_pairs={{4,0},{8,4},{12,8},{16,12},{20,16},{24,20},{28,24},{5,1},{9,5},{13... | collective-permute-start | bytes 1966088 | tf_op jit(solution)/shard_map/ppermute | solution.py:12
  6.9 1.9 %collective-permute-start.1 = (bf16[256,1280]{1,0:T(8,128)(2,1)}, bf16[256,1280]{1,0:T(8,128)(2,1)S(1)}, u32[]{:S(2)}, u32[]{:S(2)}) collective-permute-start(bf16[256,1280]{1,0:T(8,128)(2,1)} %constant_dynamic-update-slice_fusion), channel_id=1, source_target_pairs={{8,0},{12,4},{16,8},{20,12},{24,16},{28,20},{9,1},{13,5},{17,9},{2... | collective-permute-start | bytes 1966088 | tf_op jit(solution)/shard_map/ppermute | solution.py:12
  8.8 1.3 collective-permute-start.2
  10.1 1.3 collective-permute-start.3
  11.4 0.2 multiply_reduce_fusion.4
  11.6 0.1 fusion.25
  11.7 0.3 convolution_multiply_fusion.9
  12.1 0.1 copy.5
  12.2 0.1 pad.26.clone
  12.3 0.2 fusion.10
  12.5 0.1 fusion.20
  12.6 9.6 %collective-permute-done = bf16[256,1280]{1,0:T(8,128)(2,1)S(1)} collective-permute-done((bf16[256,1280]{1,0:T(8,128)(2,1)}, bf16[256,1280]{1,0:T(8,128)(2,1)S(1)}, u32[]{:S(2)}, u32[]{:S(2)}) %collective-permute-start) | collective-permute-done | bytes 655392 | tf_op jit(solution)/shard_map/ppermute | solution.py:12
  22.3 0.1 multiply_reduce_fusion.8
  22.4 43.9 %collective-permute-done.1 = bf16[256,1280]{1,0:T(8,128)(2,1)S(1)} collective-permute-done((bf16[256,1280]{1,0:T(8,128)(2,1)}, bf16[256,1280]{1,0:T(8,128)(2,1)S(1)}, u32[]{:S(2)}, u32[]{:S(2)}) %collective-permute-start.1) | collective-permute-done | bytes 655392 | tf_op jit(solution)/shard_map/ppermute | solution.py:12
  66.3 0.1 multiply_reduce_fusion.7
  66.4 0.2 multiply_reduce_fusion.3
  66.6 0.2 multiply_reduce_fusion.2
  66.8 1.2 multiply_reduce_fusion.1
  68.0 1.0 multiply_reduce_fusion.6
  69.1 1.2 multiply_reduce_fusion
  70.3 1.0 multiply_reduce_fusion.5
  71.4 0.3 convolution_multiply_fusion.8
  71.7 0.2 fusion.9
  72.0 0.1 fusion.21
  72.1 0.3 convolution_multiply_fusion.7
  72.4 0.2 fusion.7
  72.6 0.1 fusion.22
  72.7 1.4 convolution_multiply_fusion.6
  74.1 1.1 fusion.5
  75.3 0.1 fusion.23
  75.4 1.4 convolution_multiply_fusion.5
  76.8 1.1 fusion.3
  77.9 0.1 fusion.24
  78.0 0.1 constant_dynamic-slice_fusion.1
  78.1 0.1 collective-permute-start.4
  78.2 2.2 %collective-permute-done.4 = f32[5,264,128]{2,1,0:T(8,128)} collective-permute-done((f32[5,264,128]{2,1,0:T(8,128)S(1)}, f32[5,264,128]{2,1,0:T(8,128)}, u32[]{:S(2)}, u32[]{:S(2)}) %collective-permute-start.4) | collective-permute-done | bytes 675872 | tf_op jit(solution)/shard_map/ppermute | solution.py:17
  80.4 1.2 dynamic-slice_add_fusion
  81.6 1.6 %collective-permute-start.5 = (f32[5,132,128]{2,1,0:T(8,128)S(1)}, f32[5,132,128]{2,1,0:T(8,128)S(1)}, u32[]{:S(2)}, u32[]{:S(2)}) collective-permute-start(f32[5,132,128]{2,1,0:T(8,128)S(1)} %constant_dynamic-slice_fusion), channel_id=1, source_target_pairs={{0,2},{1,3},{2,0},{3,1},{4,6},{5,7},{6,4},{7,5},{8,10},{9,11},{10,... | collective-permute-start | bytes 1013768 | tf_op jit(solution)/shard_map/ppermute | solution.py:17
  83.2 8.7 %collective-permute-done.5 = f32[5,132,128]{2,1,0:T(8,128)S(1)} collective-permute-done((f32[5,132,128]{2,1,0:T(8,128)S(1)}, f32[5,132,128]{2,1,0:T(8,128)S(1)}, u32[]{:S(2)}, u32[]{:S(2)}) %collective-permute-start.5) | collective-permute-done | bytes 337952 | tf_op jit(solution)/shard_map/ppermute | solution.py:17
  91.9 1.6 %collective-permute-start.6 = (f32[5,132,128]{2,1,0:T(8,128)S(1)}, f32[5,132,128]{2,1,0:T(8,128)S(1)}, u32[]{:S(2)}, u32[]{:S(2)}) collective-permute-start(f32[5,132,128]{2,1,0:T(8,128)S(1)} %dynamic-slice_add_fusion.1), channel_id=1, source_target_pairs={{0,2},{1,3},{2,0},{3,1},{4,6},{5,7},{6,4},{7,5},{8,10},{9,11},{10,... | collective-permute-start | bytes 1013768 | tf_op jit(solution)/shard_map/ppermute | solution.py:17
  93.5 7.8 %collective-permute-done.6 = f32[5,132,128]{2,1,0:T(8,128)S(1)} collective-permute-done((f32[5,132,128]{2,1,0:T(8,128)S(1)}, f32[5,132,128]{2,1,0:T(8,128)S(1)}, u32[]{:S(2)}, u32[]{:S(2)}) %collective-permute-start.6) | collective-permute-done | bytes 337952 | tf_op jit(solution)/shard_map/ppermute | solution.py:17
  101.3 0.1 broadcast_select_fusion.3
  101.4 0.9 pad_maximum_fusion
  102.3 2.3 %collective-permute-done.7 = f32[5,264,128]{2,1,0:T(8,128)S(1)} collective-permute-done((f32[5,264,128]{2,1,0:T(8,128)}, f32[5,264,128]{2,1,0:T(8,128)S(1)}, u32[]{:S(2)}, u32[]{:S(2)}) %collective-permute-start.7) | collective-permute-done | bytes 675872 | tf_op jit(solution)/shard_map/ppermute | solution.py:17
  104.7 0.1 broadcast_select_fusion.1
  104.8 0.2 fusion.78
  105.0 0.2 fusion.60
  105.3 1.3 collective-permute-start.11
  106.6 0.3 fusion.75
  106.9 0.2 fusion.46
  107.1 0.2 fusion.63
  107.4 1.3 collective-permute-start.10
  108.7 0.2 fusion.66
  108.9 26.3 %collective-permute-start.9 = (f32[257,256]{1,0:T(8,128)S(1)}, f32[257,256]{1,0:T(8,128)S(1)}, u32[]{:S(2)}, u32[]{:S(2)}) collective-permute-start(f32[257,256]{1,0:T(8,128)S(1)} %pad_maximum_fusion.2), channel_id=1, source_target_pairs={{0,8},{4,12},{8,16},{12,20},{16,24},{20,28},{1,9},{5,13},{9,17},{1... | collective-permute-start | bytes 789512 | tf_op jit(solution)/shard_map/ppermute | solution.py:12
  135.3 0.2 fusion.69
  135.5 1.9 %collective-permute-start.8 = (f32[257,256]{1,0:T(8,128)S(1)}, f32[257,256]{1,0:T(8,128)S(1)}, u32[]{:S(2)}, u32[]{:S(2)}) collective-permute-start(f32[257,256]{1,0:T(8,128)S(1)} %pad_maximum_fusion.1), channel_id=1, source_target_pairs={{0,4},{4,8},{8,12},{12,16},{16,20},{20,24},{24,28},{1,5},{5,9},{9,... | collective-permute-start | bytes 789512 | tf_op jit(solution)/shard_map/ppermute | solution.py:12
  137.4 1.1 fusion.48
  138.5 1.1 fusion.51
  139.6 0.2 fusion.54
  139.9 10.9 %collective-permute-done.9 = f32[257,256]{1,0:T(8,128)S(1)} collective-permute-done((f32[257,256]{1,0:T(8,128)S(1)}, f32[257,256]{1,0:T(8,128)S(1)}, u32[]{:S(2)}, u32[]{:S(2)}) %collective-permute-start.9) | collective-permute-done | bytes 263200 | tf_op jit(solution)/shard_map/ppermute | solution.py:12
  150.7 2.8 %collective-permute-done.8 = f32[257,256]{1,0:T(8,128)S(1)} collective-permute-done((f32[257,256]{1,0:T(8,128)S(1)}, f32[257,256]{1,0:T(8,128)S(1)}, u32[]{:S(2)}, u32[]{:S(2)}) %collective-permute-start.8) | collective-permute-done | bytes 263200 | tf_op jit(solution)/shard_map/ppermute | solution.py:12
  153.5 1.0 fusion.27
  (27 shorter events, 0.2 us)
Async XLA Ops:
  0.0 11.4 %copy-start.1 = (bf16[256,1024]{1,0:T(8,128)(2,1)S(1)}, bf16[256,1024]{1,0:T(8,128)(2,1)}, u32[]{:S(2)}) copy-start(bf16[256,1024]{1,0:T(8,128)(2,1)} %param.2) | copy-start | bytes 1572868
  0.0 11.6 %copy-start = (bf16[256,256]{1,0:T(8,128)(2,1)S(1)}, bf16[256,256]{1,0:T(8,128)(2,1)}, u32[]{:S(2)}) copy-start(bf16[256,256]{1,0:T(8,128)(2,1)} %param.3) | copy-start | bytes 393220
  3.5 18.7 %collective-permute-start = (bf16[256,1280]{1,0:T(8,128)(2,1)}, bf16[256,1280]{1,0:T(8,128)(2,1)S(1)}, u32[]{:S(2)}, u32[]{:S(2)}) collective-permute-start(bf16[256,1280]{1,0:T(8,128)(2,1)} %constant_dynamic-update-slice_fusion), channel_id=1, source_target_pairs={{4,0},{8,4},{12,8},{16,12},{20,16},{24,20},{28,24},{5,1},{9,5},{13... | collective-permute-start | bytes 1966088 | tf_op jit(solution)/shard_map/ppermute | solution.py:12
  6.9 59.5 %collective-permute-start.1 = (bf16[256,1280]{1,0:T(8,128)(2,1)}, bf16[256,1280]{1,0:T(8,128)(2,1)S(1)}, u32[]{:S(2)}, u32[]{:S(2)}) collective-permute-start(bf16[256,1280]{1,0:T(8,128)(2,1)} %constant_dynamic-update-slice_fusion), channel_id=1, source_target_pairs={{8,0},{12,4},{16,8},{20,12},{24,16},{28,20},{9,1},{13,5},{17,9},{2... | collective-permute-start | bytes 1966088 | tf_op jit(solution)/shard_map/ppermute | solution.py:12
  8.8 58.0 %collective-permute-start.2 = (bf16[256,1280]{1,0:T(8,128)(2,1)}, bf16[256,1280]{1,0:T(8,128)(2,1)}, u32[]{:S(2)}, u32[]{:S(2)}) collective-permute-start(bf16[256,1280]{1,0:T(8,128)(2,1)} %constant_dynamic-update-slice_fusion), channel_id=1, source_target_pairs={{12,0},{16,4},{20,8},{24,12},{28,16},{13,1},{17,5},{21,9},{25,13},... | collective-permute-start | bytes 1966088 | tf_op jit(solution)/shard_map/ppermute | solution.py:12
  10.1 59.0 %collective-permute-start.3 = (bf16[256,1280]{1,0:T(8,128)(2,1)}, bf16[256,1280]{1,0:T(8,128)(2,1)}, u32[]{:S(2)}, u32[]{:S(2)}) collective-permute-start(bf16[256,1280]{1,0:T(8,128)(2,1)} %constant_dynamic-update-slice_fusion), channel_id=1, source_target_pairs={{16,0},{20,4},{24,8},{28,12},{17,1},{21,5},{25,9},{29,13},{18,2},{... | collective-permute-start | bytes 1966088 | tf_op jit(solution)/shard_map/ppermute | solution.py:12
  78.1 2.3 %collective-permute-start.4 = (f32[5,264,128]{2,1,0:T(8,128)S(1)}, f32[5,264,128]{2,1,0:T(8,128)}, u32[]{:S(2)}, u32[]{:S(2)}) collective-permute-start(f32[5,264,128]{2,1,0:T(8,128)S(1)} %constant_dynamic-slice_fusion.1), channel_id=1, source_target_pairs={{0,1},{1,0},{2,3},{3,2},{4,5},{5,4},{6,7},{7,6},{8,9},{9,8},{10,11... | collective-permute-start | bytes 2027528 | tf_op jit(solution)/shard_map/ppermute | solution.py:17
  81.6 10.3 %collective-permute-start.5 = (f32[5,132,128]{2,1,0:T(8,128)S(1)}, f32[5,132,128]{2,1,0:T(8,128)S(1)}, u32[]{:S(2)}, u32[]{:S(2)}) collective-permute-start(f32[5,132,128]{2,1,0:T(8,128)S(1)} %constant_dynamic-slice_fusion), channel_id=1, source_target_pairs={{0,2},{1,3},{2,0},{3,1},{4,6},{5,7},{6,4},{7,5},{8,10},{9,11},{10,... | collective-permute-start | bytes 1013768 | tf_op jit(solution)/shard_map/ppermute | solution.py:17
  91.9 9.4 %collective-permute-start.6 = (f32[5,132,128]{2,1,0:T(8,128)S(1)}, f32[5,132,128]{2,1,0:T(8,128)S(1)}, u32[]{:S(2)}, u32[]{:S(2)}) collective-permute-start(f32[5,132,128]{2,1,0:T(8,128)S(1)} %dynamic-slice_add_fusion.1), channel_id=1, source_target_pairs={{0,2},{1,3},{2,0},{3,1},{4,6},{5,7},{6,4},{7,5},{8,10},{9,11},{10,... | collective-permute-start | bytes 1013768 | tf_op jit(solution)/shard_map/ppermute | solution.py:17
  102.3 2.3 %collective-permute-start.7 = (f32[5,264,128]{2,1,0:T(8,128)}, f32[5,264,128]{2,1,0:T(8,128)S(1)}, u32[]{:S(2)}, u32[]{:S(2)}) collective-permute-start(f32[5,264,128]{2,1,0:T(8,128)} %pad_maximum_fusion), channel_id=1, source_target_pairs={{0,1},{1,0},{2,3},{3,2},{4,5},{5,4},{6,7},{7,6},{8,9},{9,8},{10,11... | collective-permute-start | bytes 2027528 | tf_op jit(solution)/shard_map/ppermute | solution.py:17
  105.3 34.6 %collective-permute-start.11 = (f32[257,256]{1,0:T(8,128)S(1)}, f32[257,256]{1,0:T(8,128)S(1)}, u32[]{:S(2)}, u32[]{:S(2)}) collective-permute-start(f32[257,256]{1,0:T(8,128)S(1)} %pad_maximum_fusion.4), channel_id=1, source_target_pairs={{0,16},{4,20},{8,24},{12,28},{1,17},{5,21},{9,25},{13,29},{2,18},{... | collective-permute-start | bytes 789512 | tf_op jit(solution)/shard_map/ppermute | solution.py:12
  107.4 32.5 %collective-permute-start.10 = (f32[257,256]{1,0:T(8,128)S(1)}, f32[257,256]{1,0:T(8,128)S(1)}, u32[]{:S(2)}, u32[]{:S(2)}) collective-permute-start(f32[257,256]{1,0:T(8,128)S(1)} %pad_maximum_fusion.3), channel_id=1, source_target_pairs={{0,12},{4,16},{8,20},{12,24},{16,28},{1,13},{5,17},{9,21},{13,25},... | collective-permute-start | bytes 789512 | tf_op jit(solution)/shard_map/ppermute | solution.py:12
  108.9 41.8 %collective-permute-start.9 = (f32[257,256]{1,0:T(8,128)S(1)}, f32[257,256]{1,0:T(8,128)S(1)}, u32[]{:S(2)}, u32[]{:S(2)}) collective-permute-start(f32[257,256]{1,0:T(8,128)S(1)} %pad_maximum_fusion.2), channel_id=1, source_target_pairs={{0,8},{4,12},{8,16},{12,20},{16,24},{20,28},{1,9},{5,13},{9,17},{1... | collective-permute-start | bytes 789512 | tf_op jit(solution)/shard_map/ppermute | solution.py:12
  135.5 18.0 %collective-permute-start.8 = (f32[257,256]{1,0:T(8,128)S(1)}, f32[257,256]{1,0:T(8,128)S(1)}, u32[]{:S(2)}, u32[]{:S(2)}) collective-permute-start(f32[257,256]{1,0:T(8,128)S(1)} %pad_maximum_fusion.1), channel_id=1, source_target_pairs={{0,4},{4,8},{8,12},{12,16},{16,20},{20,24},{24,28},{1,5},{5,9},{9,... | collective-permute-start | bytes 789512 | tf_op jit(solution)/shard_map/ppermute | solution.py:12

commit v3 on v2

--- a/solution.py
+++ b/solution.py
@@ -55,11 +55,12 @@
     reach = min(REACH, group - 1)
     near_count = (2 * REACH + 1) * rows_dev
 
+    offsets = [0] + [d if d % 2 else -d for d in range(1, reach + 1)]
     both = jnp.concatenate([teacher, student], axis=1)
     teacher_band = [teacher]
     student_band = [student]
-    for d in range(1, reach + 1):
-        got = shifted(both, "batch", d)
+    for e in offsets[1:]:
+        got = shifted(both, "batch", e)
         teacher_band.append(got[:, :ft])
         student_band.append(got[:, ft:])
 
@@ -83,10 +84,10 @@
     student_f = student.astype(jnp.float32)
     row_total = jnp.zeros((rows_dev,), jnp.float32)
     pulled = jnp.zeros(student.shape, jnp.float32)
-    for d in range(reach + 1):
+    for d, e in enumerate(offsets):
         resid = own_q[:, None] + q[d][None, :] - gram[d]
         if d > 0:
-            valid = owner + d < group
+            valid = jnp.logical_and(owner + e >= 0, owner + e < group)
             resid = jnp.where(valid, resid, jnp.zeros_like(resid))
         low = resid.astype(jnp.bfloat16)
         row_total = row_total + jnp.sum(resid, axis=1)
@@ -95,11 +96,11 @@
             back = lax.dot_general(low, student, (((0,), (0,)), ((), ())), preferred_element_type=jnp.float32)
             col = jnp.sum(resid, axis=0)
             if fs == rows_dev:
-                got = shifted(jnp.concatenate([back, col[None, :]], axis=0), "batch", -d)
+                got = shifted(jnp.concatenate([back, col[None, :]], axis=0), "batch", -e)
                 pulled = pulled + got[:rows_dev]
                 row_total = row_total + got[rows_dev]
             else:
-                back_r, col_r = shifted((back, col), "batch", -d)
+                back_r, col_r = shifted((back, col), "batch", -e)
                 pulled = pulled + back_r
                 row_total = row_total + col_r
     grad = (student_f * row_total[:, None] - pulled) / near_count

time: 155 us -> 116 us (0.75)
  the two profiles are of different devices: /device:TPU:8 before, /device:TPU:24 now
where the time goes in v3:
time: 116 us; the launch traced here: 115 us
  waiting for transfers between devices  65.2 us (56%)
  starting transfers between devices  25 us (22%)
  matrix products  11.1 us (10%)
  other arithmetic  8.9 us (8%)
  local copies, waits for them, and re-layouts  3.85 us (3%)
    ppermute x8, waiting for transfers between devices, shifted(): return lax.ppermute(block, axis, route)  44.1 us
    ppermute x8, starting transfers between devices, shifted(): return lax.ppermute(block, axis, route)  21.8 us
    ppermute x4, waiting for transfers between devices, swapped(): return lax.ppermute(block, axis, [(i, i ^ mask) for i in range(size)])  21.1 us
    reduce_sum x10, other arithmetic, sq(): return jnp.sum(xf * xf, axis=1)  5.37 us
    dot_general x5, matrix products, body(): lax.dot_general(teacher, t_d, (((1,), (1,)), ((), ())), preferred_element...  3.77 us
    dot_general x5, matrix products, body(): jnp.dot(low, student_band[d], preferred_element_type=jnp.float32)  3.56 us
    ppermute x4, starting transfers between devices, swapped(): return lax.ppermute(block, axis, [(i, i ^ mask) for i in range(size)])  3.19 us
    dot_general x5, matrix products, body(): lax.dot_general(student, s_d, (((1,), (1,)), ((), ())), preferred_element...  2.92 us
  transfers between devices with their start and end apart: 12, of which 10 were waited for; matrix products, arithmetic and copies ran while one was open for 7% of the time, Pallas kernels for 0%

profile of v3, /device:TPU:24, one launch (start us, length us, event | category | flops | bytes accessed | tf_op | source)
XLA Modules:
  0.0 114.6 jit_solution(4818133236403075959)
XLA Ops:
  0.0 1.9 %constant_dynamic-update-slice_fusion.1 = bf16[256,1280]{1,0:T(8,128)(2,1)} fusion(bf16[256,1024]{1,0:T(8,128)(2,1)} %param.2), kind=kLoop, calls=%fused_computation.127 | loop fusion | bytes 1048576
  1.9 1.6 %constant_dynamic-update-slice_fusion = bf16[256,1280]{1,0:T(8,128)(2,1)} fusion(bf16[256,1280]{1,0:T(8,128)(2,1)} %constant_dynamic-update-slice_fusion.1, bf16[256,256]{1,0:T(8,128)(2,1)} %param.3), kind=kLoop, calls=%fused_computation.126 | loop fusion | bytes 262144 | tf_op jit(solution)/shard_map/concatenate | solution.py:59
  3.5 3.3 %collective-permute-start = (bf16[256,1280]{1,0:T(8,128)(2,1)}, bf16[256,1280]{1,0:T(8,128)(2,1)S(1)}, u32[]{:S(2)}, u32[]{:S(2)}) collective-permute-start(bf16[256,1280]{1,0:T(8,128)(2,1)} %constant_dynamic-update-slice_fusion), channel_id=1, source_target_pairs={{4,0},{8,4},{12,8},{16,12},{20,16},{24,20},{28,24},{5,1},{9,5},{13... | collective-permute-start | bytes 1966088 | tf_op jit(solution)/shard_map/ppermute | solution.py:12
  6.9 1.3 %collective-permute-start.1 = (bf16[256,1280]{1,0:T(8,128)(2,1)}, bf16[256,1280]{1,0:T(8,128)(2,1)S(1)}, u32[]{:S(2)}, u32[]{:S(2)}) collective-permute-start(bf16[256,1280]{1,0:T(8,128)(2,1)} %constant_dynamic-update-slice_fusion), channel_id=1, source_target_pairs={{0,8},{4,12},{8,16},{12,20},{16,24},{20,28},{1,9},{5,13},{9,17},{1... | collective-permute-start | bytes 1966088 | tf_op jit(solution)/shard_map/ppermute | solution.py:12
  8.2 5.3 %collective-permute-start.2 = (bf16[256,1280]{1,0:T(8,128)(2,1)}, bf16[256,1280]{1,0:T(8,128)(2,1)}, u32[]{:S(2)}, u32[]{:S(2)}) collective-permute-start(bf16[256,1280]{1,0:T(8,128)(2,1)} %constant_dynamic-update-slice_fusion), channel_id=1, source_target_pairs={{12,0},{16,4},{20,8},{24,12},{28,16},{13,1},{17,5},{21,9},{25,13},... | collective-permute-start | bytes 1966088 | tf_op jit(solution)/shard_map/ppermute | solution.py:12
  13.5 1.3 %collective-permute-start.3 = (bf16[256,1280]{1,0:T(8,128)(2,1)}, bf16[256,1280]{1,0:T(8,128)(2,1)}, u32[]{:S(2)}, u32[]{:S(2)}) collective-permute-start(bf16[256,1280]{1,0:T(8,128)(2,1)} %constant_dynamic-update-slice_fusion), channel_id=1, source_target_pairs={{0,16},{4,20},{8,24},{12,28},{1,17},{5,21},{9,25},{13,29},{2,18},{... | collective-permute-start | bytes 1966088 | tf_op jit(solution)/shard_map/ppermute | solution.py:12
  14.8 0.2 multiply_reduce_fusion.4
  15.0 0.1 fusion.25
  15.1 0.3 convolution_multiply_fusion.9
  15.4 0.1 copy.5
  15.6 0.1 pad.26.clone
  15.7 0.2 fusion.10
  15.9 0.1 fusion.20
  16.0 6.2 %collective-permute-done = bf16[256,1280]{1,0:T(8,128)(2,1)S(1)} collective-permute-done((bf16[256,1280]{1,0:T(8,128)(2,1)}, bf16[256,1280]{1,0:T(8,128)(2,1)S(1)}, u32[]{:S(2)}, u32[]{:S(2)}) %collective-permute-start) | collective-permute-done | bytes 655392 | tf_op jit(solution)/shard_map/ppermute | solution.py:12
  22.3 0.1 multiply_reduce_fusion.8
  22.4 3.2 %collective-permute-done.1 = bf16[256,1280]{1,0:T(8,128)(2,1)S(1)} collective-permute-done((bf16[256,1280]{1,0:T(8,128)(2,1)}, bf16[256,1280]{1,0:T(8,128)(2,1)S(1)}, u32[]{:S(2)}, u32[]{:S(2)}) %collective-permute-start.1) | collective-permute-done | bytes 655392 | tf_op jit(solution)/shard_map/ppermute | solution.py:12
  25.6 0.1 multiply_reduce_fusion.7
  25.7 0.2 multiply_reduce_fusion.3
  25.9 0.2 multiply_reduce_fusion.2
  26.1 9.1 %collective-permute-done.2 = bf16[256,1280]{1,0:T(8,128)(2,1)} collective-permute-done((bf16[256,1280]{1,0:T(8,128)(2,1)}, bf16[256,1280]{1,0:T(8,128)(2,1)}, u32[]{:S(2)}, u32[]{:S(2)}) %collective-permute-start.2) | collective-permute-done | bytes 655392 | tf_op jit(solution)/shard_map/ppermute | solution.py:12
  35.2 1.2 %multiply_reduce_fusion.1 = f32[256]{0:T(256)S(1)} fusion(bf16[256,1280]{1,0:T(8,128)(2,1)} %collective-permute-done.2), kind=kLoop, calls=%fused_computation.44 | loop fusion | flops 786176 | bytes 525312 | tf_op jit(solution)/shard_map/reduce_sum | solution.py:69
  36.4 1.0 multiply_reduce_fusion.6
  37.5 15.7 %collective-permute-done.3 = bf16[256,1280]{1,0:T(8,128)(2,1)} collective-permute-done((bf16[256,1280]{1,0:T(8,128)(2,1)}, bf16[256,1280]{1,0:T(8,128)(2,1)}, u32[]{:S(2)}, u32[]{:S(2)}) %collective-permute-start.3) | collective-permute-done | bytes 655392 | tf_op jit(solution)/shard_map/ppermute | solution.py:12
  53.2 1.2 %multiply_reduce_fusion = f32[256]{0:T(256)S(1)} fusion(bf16[256,1280]{1,0:T(8,128)(2,1)} %collective-permute-done.3), kind=kLoop, calls=%fused_computation.43 | loop fusion | flops 786176 | bytes 525312 | tf_op jit(solution)/shard_map/reduce_sum | solution.py:69
  54.5 1.0 multiply_reduce_fusion.5
  55.5 0.3 convolution_multiply_fusion.8
  55.8 0.2 fusion.9
  56.1 0.1 fusion.21
  56.2 0.3 convolution_multiply_fusion.7
  56.5 0.2 fusion.7
  56.7 0.1 fusion.22
  56.9 1.4 %convolution_multiply_fusion.6 = f32[256,256]{0,1:T(8,128)S(1)} fusion(bf16[256,1024]{1,0:T(8,128)(2,1)S(1)} %copy-done.1, bf16[256,1280]{1,0:T(8,128)(2,1)} %collective-permute-done.2), kind=kOutput, calls=%fused_computation.35 | convolution fusion | flops 134283264 | bytes 1310720 | tf_op jit(solution)/shard_map/dot_general | solution.py:74
  58.2 1.1 fusion.5
  59.4 0.1 fusion.23
  59.5 1.4 %convolution_multiply_fusion.5 = f32[256,256]{0,1:T(8,128)S(1)} fusion(bf16[256,1024]{1,0:T(8,128)(2,1)S(1)} %copy-done.1, bf16[256,1280]{1,0:T(8,128)(2,1)} %collective-permute-done.3), kind=kOutput, calls=%fused_computation.34 | convolution fusion | flops 134283264 | bytes 1310720 | tf_op jit(solution)/shard_map/dot_general | solution.py:74
  60.9 1.1 fusion.3
  62.0 0.1 fusion.24
  62.3 2.2 %collective-permute-done.4 = f32[5,264,128]{2,1,0:T(8,128)} collective-permute-done((f32[5,264,128]{2,1,0:T(8,128)S(1)}, f32[5,264,128]{2,1,0:T(8,128)}, u32[]{:S(2)}, u32[]{:S(2)}) %collective-permute-start.4) | collective-permute-done | bytes 675872 | tf_op jit(solution)/shard_map/ppermute | solution.py:17
  64.5 1.2 %dynamic-slice_add_fusion = f32[5,264,128]{2,1,0:T(8,128)S(1)} fusion(f32[5,264,128]{2,1,0:T(8,128)} %collective-permute-done.4, f32[5,264,256]{2,1,0:T(8,128)S(1)} %fusion.24, s32[]{:T(128)S(6)} %select_n.83), kind=kLoop, calls=%fused_computation.49 | loop fusion | flops 168960 | bytes 2027524 | tf_op jit(solution)/shard_map/add | solution.py:39
  65.7 1.6 %collective-permute-start.5 = (f32[5,132,128]{2,1,0:T(8,128)S(1)}, f32[5,132,128]{2,1,0:T(8,128)S(1)}, u32[]{:S(2)}, u32[]{:S(2)}) collective-permute-start(f32[5,132,128]{2,1,0:T(8,128)S(1)} %constant_dynamic-slice_fusion), channel_id=1, source_target_pairs={{0,2},{1,3},{2,0},{3,1},{4,6},{5,7},{6,4},{7,5},{8,10},{9,11},{10,... | collective-permute-start | bytes 1013768 | tf_op jit(solution)/shard_map/ppermute | solution.py:17
  67.3 8.7 %collective-permute-done.5 = f32[5,132,128]{2,1,0:T(8,128)S(1)} collective-permute-done((f32[5,132,128]{2,1,0:T(8,128)S(1)}, f32[5,132,128]{2,1,0:T(8,128)S(1)}, u32[]{:S(2)}, u32[]{:S(2)}) %collective-permute-start.5) | collective-permute-done | bytes 337952 | tf_op jit(solution)/shard_map/ppermute | solution.py:17
  76.0 1.6 %collective-permute-start.6 = (f32[5,132,128]{2,1,0:T(8,128)S(1)}, f32[5,132,128]{2,1,0:T(8,128)S(1)}, u32[]{:S(2)}, u32[]{:S(2)}) collective-permute-start(f32[5,132,128]{2,1,0:T(8,128)S(1)} %dynamic-slice_add_fusion.1), channel_id=1, source_target_pairs={{0,2},{1,3},{2,0},{3,1},{4,6},{5,7},{6,4},{7,5},{8,10},{9,11},{10,... | collective-permute-start | bytes 1013768 | tf_op jit(solution)/shard_map/ppermute | solution.py:17
  77.6 7.8 %collective-permute-done.6 = f32[5,132,128]{2,1,0:T(8,128)S(1)} collective-permute-done((f32[5,132,128]{2,1,0:T(8,128)S(1)}, f32[5,132,128]{2,1,0:T(8,128)S(1)}, u32[]{:S(2)}, u32[]{:S(2)}) %collective-permute-start.6) | collective-permute-done | bytes 337952 | tf_op jit(solution)/shard_map/ppermute | solution.py:17
  85.4 0.1 broadcast_select_fusion.3
  85.5 0.9 pad_maximum_fusion
  86.5 2.3 %collective-permute-done.7 = f32[5,264,128]{2,1,0:T(8,128)S(1)} collective-permute-done((f32[5,264,128]{2,1,0:T(8,128)}, f32[5,264,128]{2,1,0:T(8,128)S(1)}, u32[]{:S(2)}, u32[]{:S(2)}) %collective-permute-start.7) | collective-permute-done | bytes 675872 | tf_op jit(solution)/shard_map/ppermute | solution.py:17
  88.8 0.1 broadcast_select_fusion.1
  88.9 0.2 fusion.78
  89.1 0.2 fusion.60
  89.4 1.5 %collective-permute-start.11 = (f32[257,256]{1,0:T(8,128)S(1)}, f32[257,256]{1,0:T(8,128)S(1)}, u32[]{:S(2)}, u32[]{:S(2)}) collective-permute-start(f32[257,256]{1,0:T(8,128)S(1)} %pad_maximum_fusion.4), channel_id=1, source_target_pairs={{16,0},{20,4},{24,8},{28,12},{17,1},{21,5},{25,9},{29,13},{18,2},{... | collective-permute-start | bytes 789512 | tf_op jit(solution)/shard_map/ppermute | solution.py:12
  90.8 0.3 fusion.75
  91.2 0.2 fusion.46
  91.4 0.2 fusion.63
  91.6 1.3 %collective-permute-start.10 = (f32[257,256]{1,0:T(8,128)S(1)}, f32[257,256]{1,0:T(8,128)S(1)}, u32[]{:S(2)}, u32[]{:S(2)}) collective-permute-start(f32[257,256]{1,0:T(8,128)S(1)} %pad_maximum_fusion.3), channel_id=1, source_target_pairs={{0,12},{4,16},{8,20},{12,24},{16,28},{1,13},{5,17},{9,21},{13,25},... | collective-permute-start | bytes 789512 | tf_op jit(solution)/shard_map/ppermute | solution.py:12
  92.9 0.2 fusion.66
  93.2 4.6 %collective-permute-start.9 = (f32[257,256]{1,0:T(8,128)S(1)}, f32[257,256]{1,0:T(8,128)S(1)}, u32[]{:S(2)}, u32[]{:S(2)}) collective-permute-start(f32[257,256]{1,0:T(8,128)S(1)} %pad_maximum_fusion.2), channel_id=1, source_target_pairs={{8,0},{12,4},{16,8},{20,12},{24,16},{28,20},{9,1},{13,5},{17,9},{2... | collective-permute-start | bytes 789512 | tf_op jit(solution)/shard_map/ppermute | solution.py:12
  97.8 0.2 fusion.69
  98.1 3.2 %collective-permute-start.8 = (f32[257,256]{1,0:T(8,128)S(1)}, f32[257,256]{1,0:T(8,128)S(1)}, u32[]{:S(2)}, u32[]{:S(2)}) collective-permute-start(f32[257,256]{1,0:T(8,128)S(1)} %pad_maximum_fusion.1), channel_id=1, source_target_pairs={{0,4},{4,8},{8,12},{12,16},{16,20},{20,24},{24,28},{1,5},{5,9},{9,... | collective-permute-start | bytes 789512 | tf_op jit(solution)/shard_map/ppermute | solution.py:12
  101.3 1.1 fusion.48
  102.4 1.1 fusion.51
  103.5 0.2 fusion.54
  103.7 4.2 %collective-permute-done.10 = f32[257,256]{1,0:T(8,128)S(1)} collective-permute-done((f32[257,256]{1,0:T(8,128)S(1)}, f32[257,256]{1,0:T(8,128)S(1)}, u32[]{:S(2)}, u32[]{:S(2)}) %collective-permute-start.10) | collective-permute-done | bytes 263200 | tf_op jit(solution)/shard_map/ppermute | solution.py:12
  107.9 5.7 %collective-permute-done.8 = f32[257,256]{1,0:T(8,128)S(1)} collective-permute-done((f32[257,256]{1,0:T(8,128)S(1)}, f32[257,256]{1,0:T(8,128)S(1)}, u32[]{:S(2)}, u32[]{:S(2)}) %collective-permute-start.8) | collective-permute-done | bytes 263200 | tf_op jit(solution)/shard_map/ppermute | solution.py:12
  113.6 1.0 fusion.27
  (27 shorter events, 0.4 us)
Async XLA Ops:
  0.0 14.8 %copy-start.1 = (bf16[256,1024]{1,0:T(8,128)(2,1)S(1)}, bf16[256,1024]{1,0:T(8,128)(2,1)}, u32[]{:S(2)}) copy-start(bf16[256,1024]{1,0:T(8,128)(2,1)} %param.2) | copy-start | bytes 1572868
  0.0 15.0 %copy-start = (bf16[256,256]{1,0:T(8,128)(2,1)S(1)}, bf16[256,256]{1,0:T(8,128)(2,1)}, u32[]{:S(2)}) copy-start(bf16[256,256]{1,0:T(8,128)(2,1)} %param.3) | copy-start | bytes 393220
  3.5 18.7 %collective-permute-start = (bf16[256,1280]{1,0:T(8,128)(2,1)}, bf16[256,1280]{1,0:T(8,128)(2,1)S(1)}, u32[]{:S(2)}, u32[]{:S(2)}) collective-permute-start(bf16[256,1280]{1,0:T(8,128)(2,1)} %constant_dynamic-update-slice_fusion), channel_id=1, source_target_pairs={{4,0},{8,4},{12,8},{16,12},{20,16},{24,20},{28,24},{5,1},{9,5},{13... | collective-permute-start | bytes 1966088 | tf_op jit(solution)/shard_map/ppermute | solution.py:12
  6.9 18.8 %collective-permute-start.1 = (bf16[256,1280]{1,0:T(8,128)(2,1)}, bf16[256,1280]{1,0:T(8,128)(2,1)S(1)}, u32[]{:S(2)}, u32[]{:S(2)}) collective-permute-start(bf16[256,1280]{1,0:T(8,128)(2,1)} %constant_dynamic-update-slice_fusion), channel_id=1, source_target_pairs={{0,8},{4,12},{8,16},{12,20},{16,24},{20,28},{1,9},{5,13},{9,17},{1... | collective-permute-start | bytes 1966088 | tf_op jit(solution)/shard_map/ppermute | solution.py:12
  8.2 27.1 %collective-permute-start.2 = (bf16[256,1280]{1,0:T(8,128)(2,1)}, bf16[256,1280]{1,0:T(8,128)(2,1)}, u32[]{:S(2)}, u32[]{:S(2)}) collective-permute-start(bf16[256,1280]{1,0:T(8,128)(2,1)} %constant_dynamic-update-slice_fusion), channel_id=1, source_target_pairs={{12,0},{16,4},{20,8},{24,12},{28,16},{13,1},{17,5},{21,9},{25,13},... | collective-permute-start | bytes 1966088 | tf_op jit(solution)/shard_map/ppermute | solution.py:12
  13.5 39.7 %collective-permute-start.3 = (bf16[256,1280]{1,0:T(8,128)(2,1)}, bf16[256,1280]{1,0:T(8,128)(2,1)}, u32[]{:S(2)}, u32[]{:S(2)}) collective-permute-start(bf16[256,1280]{1,0:T(8,128)(2,1)} %constant_dynamic-update-slice_fusion), channel_id=1, source_target_pairs={{0,16},{4,20},{8,24},{12,28},{1,17},{5,21},{9,25},{13,29},{2,18},{... | collective-permute-start | bytes 1966088 | tf_op jit(solution)/shard_map/ppermute | solution.py:12
  62.2 2.3 %collective-permute-start.4 = (f32[5,264,128]{2,1,0:T(8,128)S(1)}, f32[5,264,128]{2,1,0:T(8,128)}, u32[]{:S(2)}, u32[]{:S(2)}) collective-permute-start(f32[5,264,128]{2,1,0:T(8,128)S(1)} %constant_dynamic-slice_fusion.1), channel_id=1, source_target_pairs={{0,1},{1,0},{2,3},{3,2},{4,5},{5,4},{6,7},{7,6},{8,9},{9,8},{10,11... | collective-permute-start | bytes 2027528 | tf_op jit(solution)/shard_map/ppermute | solution.py:17
  65.7 10.3 %collective-permute-start.5 = (f32[5,132,128]{2,1,0:T(8,128)S(1)}, f32[5,132,128]{2,1,0:T(8,128)S(1)}, u32[]{:S(2)}, u32[]{:S(2)}) collective-permute-start(f32[5,132,128]{2,1,0:T(8,128)S(1)} %constant_dynamic-slice_fusion), channel_id=1, source_target_pairs={{0,2},{1,3},{2,0},{3,1},{4,6},{5,7},{6,4},{7,5},{8,10},{9,11},{10,... | collective-permute-start | bytes 1013768 | tf_op jit(solution)/shard_map/ppermute | solution.py:17
  76.0 9.4 %collective-permute-start.6 = (f32[5,132,128]{2,1,0:T(8,128)S(1)}, f32[5,132,128]{2,1,0:T(8,128)S(1)}, u32[]{:S(2)}, u32[]{:S(2)}) collective-permute-start(f32[5,132,128]{2,1,0:T(8,128)S(1)} %dynamic-slice_add_fusion.1), channel_id=1, source_target_pairs={{0,2},{1,3},{2,0},{3,1},{4,6},{5,7},{6,4},{7,5},{8,10},{9,11},{10,... | collective-permute-start | bytes 1013768 | tf_op jit(solution)/shard_map/ppermute | solution.py:17
  86.4 2.3 %collective-permute-start.7 = (f32[5,264,128]{2,1,0:T(8,128)}, f32[5,264,128]{2,1,0:T(8,128)S(1)}, u32[]{:S(2)}, u32[]{:S(2)}) collective-permute-start(f32[5,264,128]{2,1,0:T(8,128)} %pad_maximum_fusion), channel_id=1, source_target_pairs={{0,1},{1,0},{2,3},{3,2},{4,5},{5,4},{6,7},{7,6},{8,9},{9,8},{10,11... | collective-permute-start | bytes 2027528 | tf_op jit(solution)/shard_map/ppermute | solution.py:17
  89.4 14.3 %collective-permute-start.11 = (f32[257,256]{1,0:T(8,128)S(1)}, f32[257,256]{1,0:T(8,128)S(1)}, u32[]{:S(2)}, u32[]{:S(2)}) collective-permute-start(f32[257,256]{1,0:T(8,128)S(1)} %pad_maximum_fusion.4), channel_id=1, source_target_pairs={{16,0},{20,4},{24,8},{28,12},{17,1},{21,5},{25,9},{29,13},{18,2},{... | collective-permute-start | bytes 789512 | tf_op jit(solution)/shard_map/ppermute | solution.py:12
  91.6 16.3 %collective-permute-start.10 = (f32[257,256]{1,0:T(8,128)S(1)}, f32[257,256]{1,0:T(8,128)S(1)}, u32[]{:S(2)}, u32[]{:S(2)}) collective-permute-start(f32[257,256]{1,0:T(8,128)S(1)} %pad_maximum_fusion.3), channel_id=1, source_target_pairs={{0,12},{4,16},{8,20},{12,24},{16,28},{1,13},{5,17},{9,21},{13,25},... | collective-permute-start | bytes 789512 | tf_op jit(solution)/shard_map/ppermute | solution.py:12
  93.2 14.7 %collective-permute-start.9 = (f32[257,256]{1,0:T(8,128)S(1)}, f32[257,256]{1,0:T(8,128)S(1)}, u32[]{:S(2)}, u32[]{:S(2)}) collective-permute-start(f32[257,256]{1,0:T(8,128)S(1)} %pad_maximum_fusion.2), channel_id=1, source_target_pairs={{8,0},{12,4},{16,8},{20,12},{24,16},{28,20},{9,1},{13,5},{17,9},{2... | collective-permute-start | bytes 789512 | tf_op jit(solution)/shard_map/ppermute | solution.py:12
  98.1 15.5 %collective-permute-start.8 = (f32[257,256]{1,0:T(8,128)S(1)}, f32[257,256]{1,0:T(8,128)S(1)}, u32[]{:S(2)}, u32[]{:S(2)}) collective-permute-start(f32[257,256]{1,0:T(8,128)S(1)} %pad_maximum_fusion.1), channel_id=1, source_target_pairs={{0,4},{4,8},{8,12},{12,16},{16,20},{20,24},{24,28},{1,5},{5,9},{9,... | collective-permute-start | bytes 789512 | tf_op jit(solution)/shard_map/ppermute | solution.py:12

commit v4 on v3

--- a/solution.py
+++ b/solution.py
@@ -69,40 +69,45 @@
         return jnp.sum(xf * xf, axis=1)
 
     pad = (-(rows_dev + 1)) % 8
-    parts = []
-    for t_d, s_d in zip(teacher_band, student_band):
+
+    def tile_part(t_d, s_d):
         tg = lax.dot_general(teacher, t_d, (((1,), (1,)), ((), ())), preferred_element_type=jnp.float32)
         sg = lax.dot_general(student, s_d, (((1,), (1,)), ((), ())), preferred_element_type=jnp.float32)
         q_d = sq(s_d) / ds - sq(t_d) / dt
-        parts.append(jnp.concatenate(
-            [sg * (2.0 / ds) - tg * (2.0 / dt), q_d[None, :], jnp.zeros((pad, rows_dev), jnp.float32)], axis=0))
-    total = width_sum(jnp.stack(parts))
-    gram = total[:, :rows_dev, :]
-    q = total[:, rows_dev, :]
+        return jnp.concatenate(
+            [sg * (2.0 / ds) - tg * (2.0 / dt), q_d[None, :], jnp.zeros((pad, rows_dev), jnp.float32)], axis=0)
 
-    own_q = q[0]
     student_f = student.astype(jnp.float32)
     row_total = jnp.zeros((rows_dev,), jnp.float32)
     pulled = jnp.zeros(student.shape, jnp.float32)
-    for d, e in enumerate(offsets):
-        resid = own_q[:, None] + q[d][None, :] - gram[d]
-        if d > 0:
-            valid = jnp.logical_and(owner + e >= 0, owner + e < group)
-            resid = jnp.where(valid, resid, jnp.zeros_like(resid))
-        low = resid.astype(jnp.bfloat16)
-        row_total = row_total + jnp.sum(resid, axis=1)
-        pulled = pulled + jnp.dot(low, student_band[d], preferred_element_type=jnp.float32)
-        if d > 0:
-            back = lax.dot_general(low, student, (((0,), (0,)), ((), ())), preferred_element_type=jnp.float32)
-            col = jnp.sum(resid, axis=0)
-            if fs == rows_dev:
-                got = shifted(jnp.concatenate([back, col[None, :]], axis=0), "batch", -e)
-                pulled = pulled + got[:rows_dev]
-                row_total = row_total + got[rows_dev]
-            else:
-                back_r, col_r = shifted((back, col), "batch", -e)
-                pulled = pulled + back_r
-                row_total = row_total + col_r
+    own_q = None
+    split = min(3, len(offsets))
+    for group_idx in ([list(range(split)), list(range(split, len(offsets)))]):
+        if not group_idx:
+            continue
+        total = width_sum(jnp.stack([tile_part(teacher_band[d], student_band[d]) for d in group_idx]))
+        if own_q is None:
+            own_q = total[0, rows_dev, :]
+        for k, d in enumerate(group_idx):
+            e = offsets[d]
+            resid = own_q[:, None] + total[k, rows_dev, :][None, :] - total[k, :rows_dev, :]
+            if d > 0:
+                valid = jnp.logical_and(owner + e >= 0, owner + e < group)
+                resid = jnp.where(valid, resid, jnp.zeros_like(resid))
+            low = resid.astype(jnp.bfloat16)
+            row_total = row_total + jnp.sum(resid, axis=1)
+            pulled = pulled + jnp.dot(low, student_band[d], preferred_element_type=jnp.float32)
+            if d > 0:
+                back = lax.dot_general(low, student, (((0,), (0,)), ((), ())), preferred_element_type=jnp.float32)
+                col = jnp.sum(resid, axis=0)
+                if fs == rows_dev:
+                    got = shifted(jnp.concatenate([back, col[None, :]], axis=0), "batch", -e)
+                    pulled = pulled + got[:rows_dev]
+                    row_total = row_total + got[rows_dev]
+                else:
+                    back_r, col_r = shifted((back, col), "batch", -e)
+                    pulled = pulled + back_r
+                    row_total = row_total + col_r
     grad = (student_f * row_total[:, None] - pulled) / near_count
     return grad
 

time: 116 us -> 104 us (0.90)
  waiting for transfers between devices: 65.2 us -> 56.4 us
  matrix products: 11.1 us -> 7.8 us
  other arithmetic: 8.9 us -> 7.12 us
  local copies, waits for them, and re-layouts: 3.85 us -> 5.32 us
  starting transfers between devices: 25 us -> 26.2 us
    ppermute x4 -> x8, waiting for transfers between devices: 21.1 us -> 12.1 us  [swapped(): return lax.ppermute(block, axis, [(i, i ^ mask) for i in range(size)])]
    reduce_sum x10, other arithmetic: 5.37 us -> 1.48 us  [sq(): return jnp.sum(xf * xf, axis=1)]
    ppermute x4 -> x8, starting transfers between devices: 3.19 us -> 6.35 us  [swapped(): return lax.ppermute(block, axis, [(i, i ^ mask) for i in range(size)])]
    dot_general x10, matrix products: 6.69 us -> 4.2 us  [the longest x5 2.38 us: tile_part(): lax.dot_general(teacher, t_d, (((1,), (1,)), ((), ())), preferred_element...]
    ppermute x8, starting transfers between devices: 21.8 us -> 19.8 us  [shifted(): return lax.ppermute(block, axis, route)]
    unnamed x5 -> x9, local copies, waits for them, and re-layouts: 1.94 us -> 2.65 us
  transfers between devices with their start and end apart: 12 -> 16, of which waited for: 10 -> 12; matrix products, arithmetic and copies ran while one was open for 7% -> 12% of each run, Pallas kernels for 0% -> 0%
where the time goes in v4:
time: 104 us; the launch traced here: 103 us
  waiting for transfers between devices  56.4 us (54%)
  starting transfers between devices  26.2 us (25%)
  matrix products  7.8 us (8%)
  other arithmetic  7.12 us (7%)
  local copies, waits for them, and re-layouts  5.32 us (5%)
    ppermute x8, waiting for transfers between devices, shifted(): return lax.ppermute(block, axis, route)  44.2 us
    ppermute x8, starting transfers between devices, shifted(): return lax.ppermute(block, axis, route)  19.8 us
    ppermute x8, waiting for transfers between devices, swapped(): return lax.ppermute(block, axis, [(i, i ^ mask) for i in range(size)])  12.1 us
    ppermute x8, starting transfers between devices, swapped(): return lax.ppermute(block, axis, [(i, i ^ mask) for i in range(size)])  6.35 us
    dot_general x5, matrix products, body(): jnp.dot(low, student_band[d], preferred_element_type=jnp.float32)  2.7 us
    unnamed x9, local copies, waits for them, and re-layouts  2.65 us
    dot_general x5, matrix products, tile_part(): lax.dot_general(teacher, t_d, (((1,), (1,)), ((), ())), preferred_element...  2.38 us
  transfers between devices with their start and end apart: 16, of which 12 were waited for; matrix products, arithmetic and copies ran while one was open for 12% of the time, Pallas kernels for 0%

profile of v4, /device:TPU:24, one launch (start us, length us, event | category | flops | bytes accessed | tf_op | source)
XLA Modules:
  0.0 103.2 jit_solution(1269518517146841039)
XLA Ops:
  0.0 1.9 %constant_dynamic-update-slice_fusion.1 = bf16[256,1280]{1,0:T(8,128)(2,1)} fusion(bf16[256,1024]{1,0:T(8,128)(2,1)} %param.2), kind=kLoop, calls=%fused_computation.132 | loop fusion | bytes 1048576
  1.9 0.7 constant_dynamic-update-slice_fusion
  2.6 3.3 %collective-permute-start = (bf16[256,1280]{1,0:T(8,128)(2,1)}, bf16[256,1280]{1,0:T(8,128)(2,1)S(1)}, u32[]{:S(2)}, u32[]{:S(2)}) collective-permute-start(bf16[256,1280]{1,0:T(8,128)(2,1)} %constant_dynamic-update-slice_fusion), channel_id=1, source_target_pairs={{4,0},{8,4},{12,8},{16,12},{20,16},{24,20},{28,24},{5,1},{9,5},{13... | collective-permute-start | bytes 1966088 | tf_op jit(solution)/shard_map/ppermute | solution.py:12
  5.9 1.3 %collective-permute-start.1 = (bf16[256,1280]{1,0:T(8,128)(2,1)}, bf16[256,1280]{1,0:T(8,128)(2,1)S(1)}, u32[]{:S(2)}, u32[]{:S(2)}) collective-permute-start(bf16[256,1280]{1,0:T(8,128)(2,1)} %constant_dynamic-update-slice_fusion), channel_id=1, source_target_pairs={{0,8},{4,12},{8,16},{12,20},{16,24},{20,28},{1,9},{5,13},{9,17},{1... | collective-permute-start | bytes 1966088 | tf_op jit(solution)/shard_map/ppermute | solution.py:12
  7.2 4.5 %collective-permute-start.8 = (bf16[256,1280]{1,0:T(8,128)(2,1)}, bf16[256,1280]{1,0:T(8,128)(2,1)S(1)}, u32[]{:S(2)}, u32[]{:S(2)}) collective-permute-start(bf16[256,1280]{1,0:T(8,128)(2,1)} %constant_dynamic-update-slice_fusion), channel_id=1, source_target_pairs={{12,0},{16,4},{20,8},{24,12},{28,16},{13,1},{17,5},{21,9},{25,13},... | collective-permute-start | bytes 1966088 | tf_op jit(solution)/shard_map/ppermute | solution.py:12
  11.7 1.3 %collective-permute-start.9 = (bf16[256,1280]{1,0:T(8,128)(2,1)}, bf16[256,1280]{1,0:T(8,128)(2,1)S(1)}, u32[]{:S(2)}, u32[]{:S(2)}) collective-permute-start(bf16[256,1280]{1,0:T(8,128)(2,1)} %constant_dynamic-update-slice_fusion), channel_id=1, source_target_pairs={{0,16},{4,20},{8,24},{12,28},{1,17},{5,21},{9,25},{13,29},{2,18},{... | collective-permute-start | bytes 1966088 | tf_op jit(solution)/shard_map/ppermute | solution.py:12
  13.1 1.0 %convolution_multiply_fusion.9 = f32[256,256]{0,1:T(8,128)} fusion(bf16[256,1024]{1,0:T(8,128)(2,1)S(1)} %copy-done.1), kind=kOutput, calls=%fused_computation.30 | convolution fusion | flops 134283264 | bytes 786432 | tf_op jit(solution)/shard_map/dot_general | solution.py:74
  14.1 0.2 multiply_reduce_fusion.4
  14.3 1.1 %copy.5 = f32[256,256]{1,0:T(8,128)S(1)} copy(f32[256,256]{0,1:T(8,128)} %convolution_multiply_fusion.9) | data formatting | bytes 524288 | tf_op jit(solution)/shard_map/mul | solution.py:78
  15.5 0.9 fusion.10
  16.5 4.8 %collective-permute-done = bf16[256,1280]{1,0:T(8,128)(2,1)S(1)} collective-permute-done((bf16[256,1280]{1,0:T(8,128)(2,1)}, bf16[256,1280]{1,0:T(8,128)(2,1)S(1)}, u32[]{:S(2)}, u32[]{:S(2)}) %collective-permute-start) | collective-permute-done | bytes 655392 | tf_op jit(solution)/shard_map/ppermute | solution.py:12
  21.4 3.2 %collective-permute-done.1 = bf16[256,1280]{1,0:T(8,128)(2,1)S(1)} collective-permute-done((bf16[256,1280]{1,0:T(8,128)(2,1)}, bf16[256,1280]{1,0:T(8,128)(2,1)S(1)}, u32[]{:S(2)}, u32[]{:S(2)}) %collective-permute-start.1) | collective-permute-done | bytes 655392 | tf_op jit(solution)/shard_map/ppermute | solution.py:12
  24.8 0.2 multiply_reduce_fusion.3
  25.0 0.2 multiply_reduce_fusion.2
  25.2 9.1 %collective-permute-done.8 = bf16[256,1280]{1,0:T(8,128)(2,1)S(1)} collective-permute-done((bf16[256,1280]{1,0:T(8,128)(2,1)}, bf16[256,1280]{1,0:T(8,128)(2,1)S(1)}, u32[]{:S(2)}, u32[]{:S(2)}) %collective-permute-start.8) | collective-permute-done | bytes 655392 | tf_op jit(solution)/shard_map/ppermute | solution.py:12
  34.3 0.2 multiply_reduce_fusion.1
  34.5 0.1 multiply_reduce_fusion.6
  34.6 17.6 %collective-permute-done.9 = bf16[256,1280]{1,0:T(8,128)(2,1)S(1)} collective-permute-done((bf16[256,1280]{1,0:T(8,128)(2,1)}, bf16[256,1280]{1,0:T(8,128)(2,1)S(1)}, u32[]{:S(2)}, u32[]{:S(2)}) %collective-permute-start.9) | collective-permute-done | bytes 655392 | tf_op jit(solution)/shard_map/ppermute | solution.py:12
  52.2 0.2 multiply_reduce_fusion
  52.4 0.1 multiply_reduce_fusion.5
  52.5 0.3 convolution_multiply_fusion.8
  52.8 0.3 convolution_multiply_fusion.7
  53.2 0.3 convolution_multiply_fusion.6
  53.5 0.3 convolution_multiply_fusion.5
  53.9 0.2 fusion.9
  54.1 0.2 fusion.7
  54.3 0.2 fusion.5
  54.6 0.2 fusion.3
  54.8 0.7 copy-done.3
  55.5 0.2 maximum_bitcast_fusion
  55.7 0.7 fusion.20
  56.5 0.8 constant_dynamic-slice_fusion.2
  57.3 0.5 collective-permute-start.2
  57.8 0.5 collective-permute-done.10
  58.3 1.0 fusion.22
  59.3 1.6 %collective-permute-start.11 = (f32[2,132,128]{2,1,0:T(8,128)S(1)}, f32[2,132,128]{2,1,0:T(8,128)S(1)}, u32[]{:S(2)}, u32[]{:S(2)}) collective-permute-start(f32[2,132,128]{2,1,0:T(8,128)S(1)} %constant_dynamic-slice_fusion), channel_id=1, source_target_pairs={{0,2},{1,3},{2,0},{3,1},{4,6},{5,7},{6,4},{7,5},{8,10},{9,11},{10,... | collective-permute-start | bytes 405512 | tf_op jit(solution)/shard_map/ppermute | solution.py:17
  60.9 1.0 %dynamic-slice_add_fusion = f32[3,264,128]{2,1,0:T(8,128)S(1)} fusion(f32[3,264,128]{2,1,0:T(8,128)} %collective-permute-done.2, f32[3,264,256]{2,1,0:T(8,128)S(1)} %pad_maximum_fusion, s32[]{:T(128)S(6)} %select_n.117), kind=kLoop, calls=%fused_computation.54 | loop fusion | flops 101376 | bytes 1216516 | tf_op jit(solution)/shard_map/add | solution.py:39
  62.0 0.6 collective-permute-start.3
  62.6 3.1 %collective-permute-done.11 = f32[2,132,128]{2,1,0:T(8,128)S(1)} collective-permute-done((f32[2,132,128]{2,1,0:T(8,128)S(1)}, f32[2,132,128]{2,1,0:T(8,128)S(1)}, u32[]{:S(2)}, u32[]{:S(2)}) %collective-permute-start.11) | collective-permute-done | bytes 135200 | tf_op jit(solution)/shard_map/ppermute | solution.py:17
  65.7 1.8 %collective-permute-start.12 = (f32[2,132,128]{2,1,0:T(8,128)S(1)}, f32[2,132,128]{2,1,0:T(8,128)S(1)}, u32[]{:S(2)}, u32[]{:S(2)}) collective-permute-start(f32[2,132,128]{2,1,0:T(8,128)S(1)} %dynamic-slice_add_fusion.2), channel_id=1, source_target_pairs={{0,2},{1,3},{2,0},{3,1},{4,6},{5,7},{6,4},{7,5},{8,10},{9,11},{10,... | collective-permute-start | bytes 405512 | tf_op jit(solution)/shard_map/ppermute | solution.py:17
  67.5 2.6 %collective-permute-done.3 = f32[3,132,128]{2,1,0:T(8,128)S(1)} collective-permute-done((f32[3,132,128]{2,1,0:T(8,128)S(1)}, f32[3,132,128]{2,1,0:T(8,128)S(1)}, u32[]{:S(2)}, u32[]{:S(2)}) %collective-permute-start.3) | collective-permute-done | bytes 202784 | tf_op jit(solution)/shard_map/ppermute | solution.py:17
  70.2 1.8 %collective-permute-start.4 = (f32[3,132,128]{2,1,0:T(8,128)S(1)}, f32[3,132,128]{2,1,0:T(8,128)S(1)}, u32[]{:S(2)}, u32[]{:S(2)}) collective-permute-start(f32[3,132,128]{2,1,0:T(8,128)S(1)} %dynamic-slice_add_fusion.1), channel_id=1, source_target_pairs={{0,2},{1,3},{2,0},{3,1},{4,6},{5,7},{6,4},{7,5},{8,10},{9,11},{10,... | collective-permute-start | bytes 608264 | tf_op jit(solution)/shard_map/ppermute | solution.py:17
  72.0 1.1 %collective-permute-done.12 = f32[2,132,128]{2,1,0:T(8,128)S(1)} collective-permute-done((f32[2,132,128]{2,1,0:T(8,128)S(1)}, f32[2,132,128]{2,1,0:T(8,128)S(1)}, u32[]{:S(2)}, u32[]{:S(2)}) %collective-permute-start.12) | collective-permute-done | bytes 135200 | tf_op jit(solution)/shard_map/ppermute | solution.py:17
  73.3 3.7 %collective-permute-done.4 = f32[3,132,128]{2,1,0:T(8,128)S(1)} collective-permute-done((f32[3,132,128]{2,1,0:T(8,128)S(1)}, f32[3,132,128]{2,1,0:T(8,128)S(1)}, u32[]{:S(2)}, u32[]{:S(2)}) %collective-permute-start.4) | collective-permute-done | bytes 202784 | tf_op jit(solution)/shard_map/ppermute | solution.py:17
  77.1 0.8 pad_maximum_fusion.1
  77.9 1.0 broadcast_select_fusion.3
  78.9 0.9 collective-permute-done.5
  79.9 0.3 fusion.75
  80.2 0.2 fusion.57
  80.4 1.6 %collective-permute-start.15 = (f32[257,256]{1,0:T(8,128)S(1)}, f32[257,256]{1,0:T(8,128)S(1)}, u32[]{:S(2)}, u32[]{:S(2)}) collective-permute-start(f32[257,256]{1,0:T(8,128)S(1)} %pad_maximum_fusion.6), channel_id=1, source_target_pairs={{16,0},{20,4},{24,8},{28,12},{17,1},{21,5},{25,9},{29,13},{18,2},{... | collective-permute-start | bytes 789512 | tf_op jit(solution)/shard_map/ppermute | solution.py:12
  82.0 0.2 fusion.60
  82.3 1.3 %collective-permute-start.14 = (f32[257,256]{1,0:T(8,128)S(1)}, f32[257,256]{1,0:T(8,128)S(1)}, u32[]{:S(2)}, u32[]{:S(2)}) collective-permute-start(f32[257,256]{1,0:T(8,128)S(1)} %pad_maximum_fusion.5), channel_id=1, source_target_pairs={{0,12},{4,16},{8,20},{12,24},{16,28},{1,13},{5,17},{9,21},{13,25},... | collective-permute-start | bytes 789512 | tf_op jit(solution)/shard_map/ppermute | solution.py:12
  83.6 0.3 fusion.73
  83.8 0.2 fusion.63
  84.1 4.6 %collective-permute-start.7 = (f32[257,256]{1,0:T(8,128)S(1)}, f32[257,256]{1,0:T(8,128)S(1)}, u32[]{:S(2)}, u32[]{:S(2)}) collective-permute-start(f32[257,256]{1,0:T(8,128)S(1)} %pad_maximum_fusion.3), channel_id=1, source_target_pairs={{8,0},{12,4},{16,8},{20,12},{24,16},{28,20},{9,1},{13,5},{17,9},{2... | collective-permute-start | bytes 789512 | tf_op jit(solution)/shard_map/ppermute | solution.py:12
  88.7 0.2 fusion.66
  89.0 1.9 %collective-permute-start.6 = (f32[257,256]{1,0:T(8,128)S(1)}, f32[257,256]{1,0:T(8,128)S(1)}, u32[]{:S(2)}, u32[]{:S(2)}) collective-permute-start(f32[257,256]{1,0:T(8,128)S(1)} %pad_maximum_fusion.2), channel_id=1, source_target_pairs={{0,4},{4,8},{8,12},{12,16},{16,20},{20,24},{24,28},{1,5},{5,9},{9,... | collective-permute-start | bytes 789512 | tf_op jit(solution)/shard_map/ppermute | solution.py:12
  90.9 1.1 %fusion.45 = f32[256,256]{1,0:T(8,128)S(1)} fusion(bf16[256,1280]{1,0:T(8,128)(2,1)} %copy-done.2, bf16[256,256]{1,0:T(8,128)(2,1)S(1)} %get-tuple-element.28), kind=kOutput, calls=%fused_computation.106 | convolution fusion | flops 33554432 | bytes 524288 | tf_op jit(solution)/shard_map/dot_general | solution.py:99
  92.0 0.2 fusion.48
  92.2 0.2 fusion.43
  92.4 0.2 fusion.51
  92.7 3.8 %collective-permute-done.14 = f32[257,256]{1,0:T(8,128)S(1)} collective-permute-done((f32[257,256]{1,0:T(8,128)S(1)}, f32[257,256]{1,0:T(8,128)S(1)}, u32[]{:S(2)}, u32[]{:S(2)}) %collective-permute-start.14) | collective-permute-done | bytes 263200 | tf_op jit(solution)/shard_map/ppermute | solution.py:12
  96.5 5.6 %collective-permute-done.6 = f32[257,256]{1,0:T(8,128)S(1)} collective-permute-done((f32[257,256]{1,0:T(8,128)S(1)}, f32[257,256]{1,0:T(8,128)S(1)}, u32[]{:S(2)}, u32[]{:S(2)}) %collective-permute-start.6) | collective-permute-done | bytes 263200 | tf_op jit(solution)/shard_map/ppermute | solution.py:12
  102.2 1.0 fusion.25
  (44 shorter events, 1.0 us)
Async XLA Ops:
  0.0 13.0 %copy-start.1 = (bf16[256,1024]{1,0:T(8,128)(2,1)S(1)}, bf16[256,1024]{1,0:T(8,128)(2,1)}, u32[]{:S(2)}) copy-start(bf16[256,1024]{1,0:T(8,128)(2,1)} %param.2) | copy-start | bytes 1572868
  0.0 1.9 %copy-start = (bf16[256,256]{1,0:T(8,128)(2,1)S(1)}, bf16[256,256]{1,0:T(8,128)(2,1)}, u32[]{:S(2)}) copy-start(bf16[256,256]{1,0:T(8,128)(2,1)} %param.3) | copy-start | bytes 393220
  2.6 18.7 %collective-permute-start = (bf16[256,1280]{1,0:T(8,128)(2,1)}, bf16[256,1280]{1,0:T(8,128)(2,1)S(1)}, u32[]{:S(2)}, u32[]{:S(2)}) collective-permute-start(bf16[256,1280]{1,0:T(8,128)(2,1)} %constant_dynamic-update-slice_fusion), channel_id=1, source_target_pairs={{4,0},{8,4},{12,8},{16,12},{20,16},{24,20},{28,24},{5,1},{9,5},{13... | collective-permute-start | bytes 1966088 | tf_op jit(solution)/shard_map/ppermute | solution.py:12
  5.9 18.8 %collective-permute-start.1 = (bf16[256,1280]{1,0:T(8,128)(2,1)}, bf16[256,1280]{1,0:T(8,128)(2,1)S(1)}, u32[]{:S(2)}, u32[]{:S(2)}) collective-permute-start(bf16[256,1280]{1,0:T(8,128)(2,1)} %constant_dynamic-update-slice_fusion), channel_id=1, source_target_pairs={{0,8},{4,12},{8,16},{12,20},{16,24},{20,28},{1,9},{5,13},{9,17},{1... | collective-permute-start | bytes 1966088 | tf_op jit(solution)/shard_map/ppermute | solution.py:12
  7.2 27.1 %collective-permute-start.8 = (bf16[256,1280]{1,0:T(8,128)(2,1)}, bf16[256,1280]{1,0:T(8,128)(2,1)S(1)}, u32[]{:S(2)}, u32[]{:S(2)}) collective-permute-start(bf16[256,1280]{1,0:T(8,128)(2,1)} %constant_dynamic-update-slice_fusion), channel_id=1, source_target_pairs={{12,0},{16,4},{20,8},{24,12},{28,16},{13,1},{17,5},{21,9},{25,13},... | collective-permute-start | bytes 1966088 | tf_op jit(solution)/shard_map/ppermute | solution.py:12
  11.7 40.4 %collective-permute-start.9 = (bf16[256,1280]{1,0:T(8,128)(2,1)}, bf16[256,1280]{1,0:T(8,128)(2,1)S(1)}, u32[]{:S(2)}, u32[]{:S(2)}) collective-permute-start(bf16[256,1280]{1,0:T(8,128)(2,1)} %constant_dynamic-update-slice_fusion), channel_id=1, source_target_pairs={{0,16},{4,20},{8,24},{12,28},{1,17},{5,21},{9,25},{13,29},{2,18},{... | collective-permute-start | bytes 1966088 | tf_op jit(solution)/shard_map/ppermute | solution.py:12
  52.2 2.4 %copy-start.2 = (bf16[256,1280]{1,0:T(8,128)(2,1)}, bf16[256,1280]{1,0:T(8,128)(2,1)S(1)}, u32[]{:S(2)}) copy-start(bf16[256,1280]{1,0:T(8,128)(2,1)S(1)} %collective-permute-done.9) | copy-start | bytes 1966084
  54.6 1.0 copy-start.3
  56.4 1.9 %collective-permute-start.10 = (f32[2,264,128]{2,1,0:T(8,128)}, f32[2,264,128]{2,1,0:T(8,128)}, u32[]{:S(2)}, u32[]{:S(2)}) collective-permute-start(f32[2,264,128]{2,1,0:T(8,128)} %fusion.20), channel_id=1, source_target_pairs={{0,1},{1,0},{2,3},{3,2},{4,5},{5,4},{6,7},{7,6},{8,9},{9,8},{10,11... | collective-permute-start | bytes 811016 | tf_op jit(solution)/shard_map/ppermute | solution.py:17
  57.3 3.6 %collective-permute-start.2 = (f32[3,264,128]{2,1,0:T(8,128)}, f32[3,264,128]{2,1,0:T(8,128)}, u32[]{:S(2)}, u32[]{:S(2)}) collective-permute-start(f32[3,264,128]{2,1,0:T(8,128)} %constant_dynamic-slice_fusion.2), channel_id=1, source_target_pairs={{0,1},{1,0},{2,3},{3,2},{4,5},{5,4},{6,7},{7,6},{8,9},{9,8},{10,11... | collective-permute-start | bytes 1216520 | tf_op jit(solution)/shard_map/ppermute | solution.py:17
  59.3 6.4 %collective-permute-start.11 = (f32[2,132,128]{2,1,0:T(8,128)S(1)}, f32[2,132,128]{2,1,0:T(8,128)S(1)}, u32[]{:S(2)}, u32[]{:S(2)}) collective-permute-start(f32[2,132,128]{2,1,0:T(8,128)S(1)} %constant_dynamic-slice_fusion), channel_id=1, source_target_pairs={{0,2},{1,3},{2,0},{3,1},{4,6},{5,7},{6,4},{7,5},{8,10},{9,11},{10,... | collective-permute-start | bytes 405512 | tf_op jit(solution)/shard_map/ppermute | solution.py:17
  62.0 8.2 %collective-permute-start.3 = (f32[3,132,128]{2,1,0:T(8,128)S(1)}, f32[3,132,128]{2,1,0:T(8,128)S(1)}, u32[]{:S(2)}, u32[]{:S(2)}) collective-permute-start(f32[3,132,128]{2,1,0:T(8,128)S(1)} %constant_dynamic-slice_fusion.1), channel_id=1, source_target_pairs={{0,2},{1,3},{2,0},{3,1},{4,6},{5,7},{6,4},{7,5},{8,10},{9,11},{10,... | collective-permute-start | bytes 608264 | tf_op jit(solution)/shard_map/ppermute | solution.py:17
  65.7 7.4 %collective-permute-start.12 = (f32[2,132,128]{2,1,0:T(8,128)S(1)}, f32[2,132,128]{2,1,0:T(8,128)S(1)}, u32[]{:S(2)}, u32[]{:S(2)}) collective-permute-start(f32[2,132,128]{2,1,0:T(8,128)S(1)} %dynamic-slice_add_fusion.2), channel_id=1, source_target_pairs={{0,2},{1,3},{2,0},{3,1},{4,6},{5,7},{6,4},{7,5},{8,10},{9,11},{10,... | collective-permute-start | bytes 405512 | tf_op jit(solution)/shard_map/ppermute | solution.py:17
  70.2 6.8 %collective-permute-start.4 = (f32[3,132,128]{2,1,0:T(8,128)S(1)}, f32[3,132,128]{2,1,0:T(8,128)S(1)}, u32[]{:S(2)}, u32[]{:S(2)}) collective-permute-start(f32[3,132,128]{2,1,0:T(8,128)S(1)} %dynamic-slice_add_fusion.1), channel_id=1, source_target_pairs={{0,2},{1,3},{2,0},{3,1},{4,6},{5,7},{6,4},{7,5},{8,10},{9,11},{10,... | collective-permute-start | bytes 608264 | tf_op jit(solution)/shard_map/ppermute | solution.py:17
  73.2 4.7 %collective-permute-start.13 = (f32[2,264,128]{2,1,0:T(8,128)S(1)}, f32[2,264,128]{2,1,0:T(8,128)}, u32[]{:S(2)}, u32[]{:S(2)}) collective-permute-start(f32[2,264,128]{2,1,0:T(8,128)S(1)} %pad_maximum_fusion.4), channel_id=1, source_target_pairs={{0,1},{1,0},{2,3},{3,2},{4,5},{5,4},{6,7},{7,6},{8,9},{9,8},{10,11... | collective-permute-start | bytes 811016 | tf_op jit(solution)/shard_map/ppermute | solution.py:17
  77.9 2.0 %collective-permute-start.5 = (f32[3,264,128]{2,1,0:T(8,128)}, f32[3,264,128]{2,1,0:T(8,128)S(1)}, u32[]{:S(2)}, u32[]{:S(2)}) collective-permute-start(f32[3,264,128]{2,1,0:T(8,128)} %pad_maximum_fusion.1), channel_id=1, source_target_pairs={{0,1},{1,0},{2,3},{3,2},{4,5},{5,4},{6,7},{7,6},{8,9},{9,8},{10,11... | collective-permute-start | bytes 1216520 | tf_op jit(solution)/shard_map/ppermute | solution.py:17
  80.4 12.2 %collective-permute-start.15 = (f32[257,256]{1,0:T(8,128)S(1)}, f32[257,256]{1,0:T(8,128)S(1)}, u32[]{:S(2)}, u32[]{:S(2)}) collective-permute-start(f32[257,256]{1,0:T(8,128)S(1)} %pad_maximum_fusion.6), channel_id=1, source_target_pairs={{16,0},{20,4},{24,8},{28,12},{17,1},{21,5},{25,9},{29,13},{18,2},{... | collective-permute-start | bytes 789512 | tf_op jit(solution)/shard_map/ppermute | solution.py:12
  82.3 14.2 %collective-permute-start.14 = (f32[257,256]{1,0:T(8,128)S(1)}, f32[257,256]{1,0:T(8,128)S(1)}, u32[]{:S(2)}, u32[]{:S(2)}) collective-permute-start(f32[257,256]{1,0:T(8,128)S(1)} %pad_maximum_fusion.5), channel_id=1, source_target_pairs={{0,12},{4,16},{8,20},{12,24},{16,28},{1,13},{5,17},{9,21},{13,25},... | collective-permute-start | bytes 789512 | tf_op jit(solution)/shard_map/ppermute | solution.py:12
  84.1 12.4 %collective-permute-start.7 = (f32[257,256]{1,0:T(8,128)S(1)}, f32[257,256]{1,0:T(8,128)S(1)}, u32[]{:S(2)}, u32[]{:S(2)}) collective-permute-start(f32[257,256]{1,0:T(8,128)S(1)} %pad_maximum_fusion.3), channel_id=1, source_target_pairs={{8,0},{12,4},{16,8},{20,12},{24,16},{28,20},{9,1},{13,5},{17,9},{2... | collective-permute-start | bytes 789512 | tf_op jit(solution)/shard_map/ppermute | solution.py:12
  89.0 13.2 %collective-permute-start.6 = (f32[257,256]{1,0:T(8,128)S(1)}, f32[257,256]{1,0:T(8,128)S(1)}, u32[]{:S(2)}, u32[]{:S(2)}) collective-permute-start(f32[257,256]{1,0:T(8,128)S(1)} %pad_maximum_fusion.2), channel_id=1, source_target_pairs={{0,4},{4,8},{8,12},{12,16},{16,20},{20,24},{24,28},{1,5},{5,9},{9,... | collective-permute-start | bytes 789512 | tf_op jit(solution)/shard_map/ppermute | solution.py:12

commit v5 on v1

v5 whole, which is shorter than its diff:
```python
import jax
import jax.numpy as jnp
from jax import lax
from jax.sharding import PartitionSpec as P

REACH = 4


def shifted(block, axis, distance):
    size = lax.axis_size(axis)
    route = [(i + distance, i) for i in range(size) if 0 <= i + distance < size]
    return lax.ppermute(block, axis, route)


def swapped(block, axis, mask):
    size = lax.axis_size(axis)
    return lax.ppermute(block, axis, [(i, i ^ mask) for i in range(size)])


def split_sum(x, axis, mask, bit):
    keep = lax.dynamic_index_in_dim(x, bit, axis, keepdims=False)
    send = lax.dynamic_index_in_dim(x, 1 - bit, axis, keepdims=False)
    return keep + swapped(send, "width", mask)


def gathered(x, axis, mask, bit):
    got = swapped(x, "width", mask)
    first = jnp.where(bit == 0, x, got)
    second = jnp.where(bit == 0, got, x)
    return jnp.stack([first, second], axis=axis)


def body(teacher, student):
    group = lax.axis_size("batch")
    owner = lax.axis_index("batch")
    width = lax.axis_size("width")
    widx = lax.axis_index("width")
    core_bit = widx % 2
    chip_bit = (widx // 2) % 2
    n = teacher.shape[0]
    ft = teacher.shape[1]
    fs = student.shape[1]
    dt = ft * width
    ds = fs * width
    m = n // 4
    reach = min(REACH, group - 1)
    near_count = (2 * REACH + 1) * n

    offsets = [d if d % 2 else -d for d in range(1, reach + 1)]
    both = jnp.concatenate([teacher, student], axis=1)
    blocks = [shifted(both, "batch", e) for e in offsets]
    givers = [shifted(student, "batch", -e) for e in offsets]
    t_band = [teacher] + [b[:, :ft] for b in blocks]
    s_band = [student] + [b[:, ft:] for b in blocks]
    tiles = len(t_band)

    def sq(x):
        xf = x.astype(jnp.float32)
        return jnp.sum(xf * xf, axis=1)

    own_q = sq(student) / ds - sq(teacher) / dt
    zero = jnp.zeros((n,), jnp.float32)
    parts = []
    for k in range(tiles):
        tg = lax.dot_general(teacher, t_band[k], (((1,), (1,)), ((), ())), preferred_element_type=jnp.float32)
        sg = lax.dot_general(student, s_band[k], (((1,), (1,)), ((), ())), preferred_element_type=jnp.float32)
        g = sg * (2.0 / ds) - tg * (2.0 / dt)
        q_p = own_q if k == 0 else sq(s_band[k]) / ds - sq(t_band[k]) / dt
        extra = jnp.stack([q_p, own_q if k == 0 else zero, jnp.sum(g, axis=0), jnp.sum(g, axis=1)]
                          + [zero] * 4)
        chunks = jnp.concatenate([g.reshape(4, m, n), jnp.broadcast_to(extra, (4, 8, n))], axis=1)
        parts.append(chunks.reshape(2, 2, m + 8, n))
    mine = split_sum(jnp.stack(parts), 2, 1, core_bit)
    mine = split_sum(mine, 1, 2, chip_bit)

    q_p = mine[:, m, :]
    own_q = mine[0, m + 1, :]
    g_col = mine[:, m + 2, :]
    g_row = mine[:, m + 3, :]
    partner = owner + jnp.array([0] + offsets, jnp.int32)
    valid = jnp.logical_and(partner >= 0, partner < group)
    q_rows = lax.dynamic_slice_in_dim(own_q, widx * m, m)
    resid = q_rows[None, :, None] + q_p[:, None, :] - mine[:, :m, :]
    resid = jnp.where(valid[:, None, None], resid, jnp.zeros_like(resid))
    row_sums = n * own_q[None, :] + jnp.sum(q_p, axis=1, keepdims=True) - g_row
    col_sums = jnp.sum(own_q) + n * q_p - g_col
    row_total = jnp.sum(jnp.where(valid[:, None], row_sums, jnp.zeros_like(row_sums)), axis=0)

    received = []
    for k, e in enumerate(offsets):
        pack = jnp.concatenate([resid[k + 1], col_sums[k + 1][None, :], jnp.zeros((7, n), jnp.float32)], axis=0)
        got = shifted(pack, "batch", -e)
        received.append(got[:m])
        row_total = row_total + got[m]

    low = jnp.concatenate([resid, jnp.stack(received)], axis=0).astype(jnp.bfloat16)
    low = gathered(low, 1, 2, chip_bit)
    low = gathered(low, 2, 1, core_bit)
    low = low.reshape(low.shape[0], n, n)

    pulled = jnp.zeros(student.shape, jnp.float32)
    for k in range(tiles):
        pulled = pulled + jnp.dot(low[k], s_band[k], preferred_element_type=jnp.float32)
    for k in range(len(offsets)):
        pulled = pulled + lax.dot_general(low[tiles + k], givers[k], (((0,), (0,)), ((), ())),
                                          preferred_element_type=jnp.float32)
    grad = (student.astype(jnp.float32) * row_total[:, None] - pulled) / near_count
    return grad


def solution(mesh):
    in_specs = (P("batch", "width"), P("batch", "width"))
    out_specs = P("batch", "width")
    return jax.shard_map(body, mesh=mesh, in_specs=in_specs, out_specs=out_specs, check_vma=False)
```

time: 196 us -> 128 us (0.65)
  the two profiles are of different devices: /device:TPU:24 before, /device:TPU:0 now
where the time goes in v5:
time: 128 us; the launch traced here: 127 us
  starting transfers between devices  51 us (40%)
  waiting for transfers between devices  44.1 us (34%)
  matrix products  14.3 us (11%)
  other arithmetic  10.8 us (8%)
  local copies, waits for them, and re-layouts  6.01 us (5%)
    ppermute x12, starting transfers between devices, shifted(): return lax.ppermute(block, axis, route)  47.6 us
    ppermute x12, waiting for transfers between devices, shifted(): return lax.ppermute(block, axis, route)  27.7 us
    ppermute x4, waiting for transfers between devices, swapped(): return lax.ppermute(block, axis, [(i, i ^ mask) for i in range(size)])  16.4 us
    reduce_sum x10, other arithmetic, sq(): return jnp.sum(xf * xf, axis=1)  7.36 us
    dot_general x5, matrix products, body(): lax.dot_general(teacher, t_band[k], (((1,), (1,)), ((), ())), preferred_e...  4.82 us
    dot_general x5, matrix products, body(): jnp.dot(low[k], s_band[k], preferred_element_type=jnp.float32)  4.4 us
    dot_general x5, matrix products, body(): lax.dot_general(student, s_band[k], (((1,), (1,)), ((), ())), preferred_e...  4.23 us
    ppermute x4, starting transfers between devices, swapped(): return lax.ppermute(block, axis, [(i, i ^ mask) for i in range(size)])  3.41 us
  transfers between devices with their start and end apart: 16, of which 7 were waited for; matrix products, arithmetic and copies ran while one was open for 10% of the time, Pallas kernels for 0%

profile of v5, /device:TPU:0, one launch (start us, length us, event | category | flops | bytes accessed | tf_op | source)
XLA Modules:
  0.0 127.0 jit_solution(3010867032403639700)
XLA Ops:
  0.0 1.9 %constant_dynamic-update-slice_fusion.1 = bf16[256,1280]{1,0:T(8,128)(2,1)} fusion(bf16[256,1024]{1,0:T(8,128)(2,1)} %param.3), kind=kLoop, calls=%fused_computation.114 | loop fusion | bytes 1048576
  1.9 1.6 %constant_dynamic-update-slice_fusion = bf16[256,1280]{1,0:T(8,128)(2,1)} fusion(bf16[256,1280]{1,0:T(8,128)(2,1)} %constant_dynamic-update-slice_fusion.1, bf16[256,256]{1,0:T(8,128)(2,1)} %param.4), kind=kLoop, calls=%fused_computation.113 | loop fusion | bytes 262144 | tf_op jit(solution)/shard_map/concatenate | solution.py:50
  3.5 1.3 %collective-permute-start = (bf16[256,1280]{1,0:T(8,128)(2,1)}, bf16[256,1280]{1,0:T(8,128)(2,1)}, u32[]{:S(2)}, u32[]{:S(2)}) collective-permute-start(bf16[256,1280]{1,0:T(8,128)(2,1)} %constant_dynamic-update-slice_fusion), channel_id=1, source_target_pairs={{4,0},{8,4},{12,8},{16,12},{20,16},{24,20},{28,24},{5,1},{9,5},{13... | collective-permute-start | bytes 1966088 | tf_op jit(solution)/shard_map/ppermute | solution.py:12
  4.8 7.0 %collective-permute-start.1 = (bf16[256,1280]{1,0:T(8,128)(2,1)}, bf16[256,1280]{1,0:T(8,128)(2,1)S(1)}, u32[]{:S(2)}, u32[]{:S(2)}) collective-permute-start(bf16[256,1280]{1,0:T(8,128)(2,1)} %constant_dynamic-update-slice_fusion), channel_id=1, source_target_pairs={{0,8},{4,12},{8,16},{12,20},{16,24},{20,28},{1,9},{5,13},{9,17},{1... | collective-permute-start | bytes 1966088 | tf_op jit(solution)/shard_map/ppermute | solution.py:12
  11.8 1.3 %collective-permute-start.2 = (bf16[256,1280]{1,0:T(8,128)(2,1)}, bf16[256,1280]{1,0:T(8,128)(2,1)}, u32[]{:S(2)}, u32[]{:S(2)}) collective-permute-start(bf16[256,1280]{1,0:T(8,128)(2,1)} %constant_dynamic-update-slice_fusion), channel_id=1, source_target_pairs={{12,0},{16,4},{20,8},{24,12},{28,16},{13,1},{17,5},{21,9},{25,13},... | collective-permute-start | bytes 1966088 | tf_op jit(solution)/shard_map/ppermute | solution.py:12
  13.1 6.3 %collective-permute-start.3 = (bf16[256,1280]{1,0:T(8,128)(2,1)}, bf16[256,1280]{1,0:T(8,128)(2,1)}, u32[]{:S(2)}, u32[]{:S(2)}) collective-permute-start(bf16[256,1280]{1,0:T(8,128)(2,1)} %constant_dynamic-update-slice_fusion), channel_id=1, source_target_pairs={{0,16},{4,20},{8,24},{12,28},{1,17},{5,21},{9,25},{13,29},{2,18},{... | collective-permute-start | bytes 1966088 | tf_op jit(solution)/shard_map/ppermute | solution.py:12
  19.5 0.3 convolution_multiply_fusion.9
  19.8 0.2 multiply_reduce_fusion.4
  20.0 0.1 fusion.16
  20.1 0.3 fusion.54
  20.5 16.9 %collective-permute-done = bf16[256,1280]{1,0:T(8,128)(2,1)} collective-permute-done((bf16[256,1280]{1,0:T(8,128)(2,1)}, bf16[256,1280]{1,0:T(8,128)(2,1)}, u32[]{:S(2)}, u32[]{:S(2)}) %collective-permute-start) | collective-permute-done | bytes 655392 | tf_op jit(solution)/shard_map/ppermute | solution.py:12
  37.5 1.4 %convolution_multiply_fusion.8 = f32[256,256]{1,0:T(8,128)S(1)} fusion(bf16[256,1024]{1,0:T(8,128)(2,1)S(1)} %copy-done.1, bf16[256,1280]{1,0:T(8,128)(2,1)} %collective-permute-done), kind=kOutput, calls=%fused_computation.34 | convolution fusion | flops 134283264 | bytes 1310720 | tf_op jit(solution)/shard_map/dot_general | solution.py:65
  38.9 1.2 fusion.53
  40.1 0.1 copy.34
  40.2 0.3 convolution_multiply_fusion.7
  40.6 0.3 fusion.52
  40.9 0.8 copy.37
  41.7 1.4 %convolution_multiply_fusion.6 = f32[256,256]{1,0:T(8,128)S(1)} fusion(bf16[256,1024]{1,0:T(8,128)(2,1)S(1)} %copy-done.1, bf16[256,1280]{1,0:T(8,128)(2,1)} %collective-permute-done.2), kind=kOutput, calls=%fused_computation.32 | convolution fusion | flops 134283264 | bytes 1310720 | tf_op jit(solution)/shard_map/dot_general | solution.py:65
  43.1 1.2 fusion.51
  44.3 0.8 copy.40
  45.2 1.4 %convolution_multiply_fusion.5 = f32[256,256]{1,0:T(8,128)S(1)} fusion(bf16[256,1024]{1,0:T(8,128)(2,1)S(1)} %copy-done.1, bf16[256,1280]{1,0:T(8,128)(2,1)} %collective-permute-done.3), kind=kOutput, calls=%fused_computation.31 | convolution fusion | flops 134283264 | bytes 1310720 | tf_op jit(solution)/shard_map/dot_general | solution.py:65
  46.5 1.2 fusion.50
  47.8 0.1 copy.43
  47.9 1.2 multiply_reduce_fusion.3
  49.1 1.1 multiply_reduce_fusion.8
  50.2 0.2 multiply_reduce_fusion.2
  50.4 0.1 multiply_reduce_fusion.7
  50.5 1.2 multiply_reduce_fusion.1
  51.7 1.0 multiply_reduce_fusion.6
  52.8 1.2 multiply_reduce_fusion
  54.0 1.0 multiply_reduce_fusion.5
  55.5 2.3 %collective-permute-done.4 = f32[5,2,72,256]{3,2,1,0:T(8,128)} collective-permute-done((f32[5,2,72,256]{3,2,1,0:T(8,128)S(1)}, f32[5,2,72,256]{3,2,1,0:T(8,128)}, u32[]{:S(2)}, u32[]{:S(2)}) %collective-permute-start.4) | collective-permute-done | bytes 737312 | tf_op jit(solution)/shard_map/ppermute | solution.py:17
  57.8 1.2 bitcast_add_fusion
  59.1 1.8 %collective-permute-start.5 = (f32[5,72,256]{2,1,0:T(8,128)S(1)}, f32[5,72,256]{2,1,0:T(8,128)S(1)}, u32[]{:S(2)}, u32[]{:S(2)}) collective-permute-start(f32[5,72,256]{2,1,0:T(8,128)S(1)} %dynamic-slice_bitcast_fusion.1), channel_id=1, source_target_pairs={{0,2},{1,3},{2,0},{3,1},{4,6},{5,7},{6,4},{7,5},{8,10},{9,11},{10,... | collective-permute-start | bytes 1105928 | tf_op jit(solution)/shard_map/ppermute | solution.py:17
  61.0 8.9 %collective-permute-done.5 = f32[5,72,256]{2,1,0:T(8,128)S(1)} collective-permute-done((f32[5,72,256]{2,1,0:T(8,128)S(1)}, f32[5,72,256]{2,1,0:T(8,128)S(1)}, u32[]{:S(2)}, u32[]{:S(2)}) %collective-permute-start.5) | collective-permute-done | bytes 368672 | tf_op jit(solution)/shard_map/ppermute | solution.py:17
  69.9 0.1 slice_reduce_fusion.1
  70.0 0.6 broadcast_multiply_fusion
  70.7 0.1 convert_dynamic-update-slice_fusion
  70.9 0.7 bitcast_subtract_fusion
  71.5 0.1 maximum_maximum_fusion
  71.6 15.4 %collective-permute-start.6 = (f32[72,256]{1,0:T(8,128)S(1)}, f32[72,256]{1,0:T(8,128)S(1)}, u32[]{:S(2)}, u32[]{:S(2)}) collective-permute-start(f32[72,256]{1,0:T(8,128)S(1)} %get-tuple-element.45), channel_id=1, source_target_pairs={{0,4},{4,8},{8,12},{12,16},{16,20},{20,24},{24,28},{1,5},{5,9},{9,... | collective-permute-start | bytes 221192 | tf_op jit(solution)/shard_map/ppermute | solution.py:12
  87.0 1.3 %collective-permute-start.7 = (f32[72,256]{1,0:T(8,128)S(1)}, f32[72,256]{1,0:T(8,128)S(1)}, u32[]{:S(2)}, u32[]{:S(2)}) collective-permute-start(f32[72,256]{1,0:T(8,128)S(1)} %get-tuple-element.46), channel_id=1, source_target_pairs={{8,0},{12,4},{16,8},{20,12},{24,16},{28,20},{9,1},{13,5},{17,9},{2... | collective-permute-start | bytes 221192 | tf_op jit(solution)/shard_map/ppermute | solution.py:12
  88.3 4.0 %collective-permute-start.8 = (f32[72,256]{1,0:T(8,128)S(1)}, f32[72,256]{1,0:T(8,128)S(1)}, u32[]{:S(2)}, u32[]{:S(2)}) collective-permute-start(f32[72,256]{1,0:T(8,128)S(1)} %get-tuple-element.47), channel_id=1, source_target_pairs={{0,12},{4,16},{8,20},{12,24},{16,28},{1,13},{5,17},{9,21},{13,25},... | collective-permute-start | bytes 221192 | tf_op jit(solution)/shard_map/ppermute | solution.py:12
  92.3 1.3 %collective-permute-start.9 = (f32[72,256]{1,0:T(8,128)S(1)}, f32[72,256]{1,0:T(8,128)S(1)}, u32[]{:S(2)}, u32[]{:S(2)}) collective-permute-start(f32[72,256]{1,0:T(8,128)S(1)} %get-tuple-element.48), channel_id=1, source_target_pairs={{16,0},{20,4},{24,8},{28,12},{17,1},{21,5},{25,9},{29,13},{18,2},{... | collective-permute-start | bytes 221192 | tf_op jit(solution)/shard_map/ppermute | solution.py:12
  93.6 0.6 collective-permute-done.8
  94.3 5.6 %collective-permute-done.9 = f32[72,256]{1,0:T(8,128)S(1)} collective-permute-done((f32[72,256]{1,0:T(8,128)S(1)}, f32[72,256]{1,0:T(8,128)S(1)}, u32[]{:S(2)}, u32[]{:S(2)}) %collective-permute-start.9) | collective-permute-done | bytes 73760 | tf_op jit(solution)/shard_map/ppermute | solution.py:12
  99.9 1.5 %collective-permute-start.10 = (bf16[9,64,256]{2,1,0:T(8,128)(2,1)S(1)}, bf16[9,64,256]{2,1,0:T(8,128)(2,1)S(1)}, u32[]{:S(2)}, u32[]{:S(2)}) collective-permute-start(bf16[9,64,256]{2,1,0:T(8,128)(2,1)S(1)} %fusion.46), channel_id=1, source_target_pairs={{0,2},{1,3},{2,0},{3,1},{4,6},{5,7},{6,4},{7,5},{8,10},{9,11},{10,... | collective-permute-start | bytes 884744 | tf_op jit(solution)/shard_map/ppermute | solution.py:17
  101.4 5.2 %collective-permute-done.10 = bf16[9,64,256]{2,1,0:T(8,128)(2,1)S(1)} collective-permute-done((bf16[9,64,256]{2,1,0:T(8,128)(2,1)S(1)}, bf16[9,64,256]{2,1,0:T(8,128)(2,1)S(1)}, u32[]{:S(2)}, u32[]{:S(2)}) %collective-permute-start.10) | collective-permute-done | bytes 294944 | tf_op jit(solution)/shard_map/ppermute | solution.py:17
  106.8 1.3 %collective-permute-start.12 = (bf16[256,256]{1,0:T(8,128)(2,1)S(1)}, bf16[256,256]{1,0:T(8,128)(2,1)S(1)}, u32[]{:S(2)}, u32[]{:S(2)}) collective-permute-start(bf16[256,256]{1,0:T(8,128)(2,1)S(1)} %copy-done), channel_id=1, source_target_pairs={{0,4},{4,8},{8,12},{12,16},{16,20},{20,24},{24,28},{1,5},{5,9},{9,... | collective-permute-start | bytes 393224 | tf_op jit(solution)/shard_map/ppermute | solution.py:12
  108.1 1.3 %collective-permute-start.13 = (bf16[256,256]{1,0:T(8,128)(2,1)S(1)}, bf16[256,256]{1,0:T(8,128)(2,1)S(1)}, u32[]{:S(2)}, u32[]{:S(2)}) collective-permute-start(bf16[256,256]{1,0:T(8,128)(2,1)S(1)} %copy-done), channel_id=1, source_target_pairs={{8,0},{12,4},{16,8},{20,12},{24,16},{28,20},{9,1},{13,5},{17,9},{2... | collective-permute-start | bytes 393224 | tf_op jit(solution)/shard_map/ppermute | solution.py:12
  109.4 5.9 %collective-permute-start.14 = (bf16[256,256]{1,0:T(8,128)(2,1)S(1)}, bf16[256,256]{1,0:T(8,128)(2,1)S(1)}, u32[]{:S(2)}, u32[]{:S(2)}) collective-permute-start(bf16[256,256]{1,0:T(8,128)(2,1)S(1)} %copy-done), channel_id=1, source_target_pairs={{0,12},{4,16},{8,20},{12,24},{16,28},{1,13},{5,17},{9,21},{13,25},... | collective-permute-start | bytes 393224 | tf_op jit(solution)/shard_map/ppermute | solution.py:12
  115.3 1.3 %collective-permute-start.15 = (bf16[256,256]{1,0:T(8,128)(2,1)S(1)}, bf16[256,256]{1,0:T(8,128)(2,1)S(1)}, u32[]{:S(2)}, u32[]{:S(2)}) collective-permute-start(bf16[256,256]{1,0:T(8,128)(2,1)S(1)} %copy-done), channel_id=1, source_target_pairs={{16,0},{20,4},{24,8},{28,12},{17,1},{21,5},{25,9},{29,13},{18,2},{... | collective-permute-start | bytes 393224 | tf_op jit(solution)/shard_map/ppermute | solution.py:12
  116.6 0.1 fusion.48
  116.9 0.1 fusion.22
  117.0 0.2 fusion.57
  117.3 1.1 fusion.27
  118.4 1.1 convolution_add_fusion.1
  119.5 1.1 fusion.30
  120.6 0.2 fusion.58
  120.9 0.2 fusion.59
  121.1 0.2 fusion.60
  121.3 4.5 %collective-permute-done.15 = bf16[256,256]{1,0:T(8,128)(2,1)S(1)} collective-permute-done((bf16[256,256]{1,0:T(8,128)(2,1)S(1)}, bf16[256,256]{1,0:T(8,128)(2,1)S(1)}, u32[]{:S(2)}, u32[]{:S(2)}) %collective-permute-start.15) | collective-permute-done | bytes 131104 | tf_op jit(solution)/shard_map/ppermute | solution.py:12
  125.8 0.2 fusion.61
  126.0 1.0 fusion.18
  (74 shorter events, 1.2 us)
Async XLA Ops:
  0.0 19.5 %copy-start.1 = (bf16[256,1024]{1,0:T(8,128)(2,1)S(1)}, bf16[256,1024]{1,0:T(8,128)(2,1)}, u32[]{:S(2)}) copy-start(bf16[256,1024]{1,0:T(8,128)(2,1)} %param.3) | copy-start | bytes 1572868
  0.0 20.0 %copy-start = (bf16[256,256]{1,0:T(8,128)(2,1)S(1)}, bf16[256,256]{1,0:T(8,128)(2,1)}, u32[]{:S(2)}) copy-start(bf16[256,256]{1,0:T(8,128)(2,1)} %param.4) | copy-start | bytes 393220
  3.5 34.0 %collective-permute-start = (bf16[256,1280]{1,0:T(8,128)(2,1)}, bf16[256,1280]{1,0:T(8,128)(2,1)}, u32[]{:S(2)}, u32[]{:S(2)}) collective-permute-start(bf16[256,1280]{1,0:T(8,128)(2,1)} %constant_dynamic-update-slice_fusion), channel_id=1, source_target_pairs={{4,0},{8,4},{12,8},{16,12},{20,16},{24,20},{28,24},{5,1},{9,5},{13... | collective-permute-start | bytes 1966088 | tf_op jit(solution)/shard_map/ppermute | solution.py:12
  4.8 35.4 %collective-permute-start.1 = (bf16[256,1280]{1,0:T(8,128)(2,1)}, bf16[256,1280]{1,0:T(8,128)(2,1)S(1)}, u32[]{:S(2)}, u32[]{:S(2)}) collective-permute-start(bf16[256,1280]{1,0:T(8,128)(2,1)} %constant_dynamic-update-slice_fusion), channel_id=1, source_target_pairs={{0,8},{4,12},{8,16},{12,20},{16,24},{20,28},{1,9},{5,13},{9,17},{1... | collective-permute-start | bytes 1966088 | tf_op jit(solution)/shard_map/ppermute | solution.py:12
  11.8 29.9 %collective-permute-start.2 = (bf16[256,1280]{1,0:T(8,128)(2,1)}, bf16[256,1280]{1,0:T(8,128)(2,1)}, u32[]{:S(2)}, u32[]{:S(2)}) collective-permute-start(bf16[256,1280]{1,0:T(8,128)(2,1)} %constant_dynamic-update-slice_fusion), channel_id=1, source_target_pairs={{12,0},{16,4},{20,8},{24,12},{28,16},{13,1},{17,5},{21,9},{25,13},... | collective-permute-start | bytes 1966088 | tf_op jit(solution)/shard_map/ppermute | solution.py:12
  13.1 32.0 %collective-permute-start.3 = (bf16[256,1280]{1,0:T(8,128)(2,1)}, bf16[256,1280]{1,0:T(8,128)(2,1)}, u32[]{:S(2)}, u32[]{:S(2)}) collective-permute-start(bf16[256,1280]{1,0:T(8,128)(2,1)} %constant_dynamic-update-slice_fusion), channel_id=1, source_target_pairs={{0,16},{4,20},{8,24},{12,28},{1,17},{5,21},{9,25},{13,29},{2,18},{... | collective-permute-start | bytes 1966088 | tf_op jit(solution)/shard_map/ppermute | solution.py:12
  49.1 6.0 %copy-start.2 = (f32[256,256]{1,0:T(8,128)S(1)}, f32[256,256]{1,0:T(8,128)}, u32[]{:S(2)}) copy-start(f32[256,256]{1,0:T(8,128)} %copy.37) | copy-start | bytes 786436
  50.4 4.8 %copy-start.3 = (f32[256,256]{1,0:T(8,128)S(1)}, f32[256,256]{1,0:T(8,128)}, u32[]{:S(2)}) copy-start(f32[256,256]{1,0:T(8,128)} %copy.40) | copy-start | bytes 786436
  55.4 2.4 %collective-permute-start.4 = (f32[5,2,72,256]{3,2,1,0:T(8,128)S(1)}, f32[5,2,72,256]{3,2,1,0:T(8,128)}, u32[]{:S(2)}, u32[]{:S(2)}) collective-permute-start(f32[5,2,72,256]{3,2,1,0:T(8,128)S(1)} %dynamic-slice_bitcast_fusion), channel_id=1, source_target_pairs={{0,1},{1,0},{2,3},{3,2},{4,5},{5,4},{6,7},{7,6},{8,9},{9,8},{10,11... | collective-permute-start | bytes 2211848 | tf_op jit(solution)/shard_map/ppermute | solution.py:17
  55.5 5.4 %copy-start.4 = (s32[5]{0:T(128)S(1)}, s32[5]{0:T(128)}, u32[]{:S(2)}) copy-start(s32[5]{0:T(128)} %constant.95.clone) | copy-start | bytes 64
  59.1 10.7 %collective-permute-start.5 = (f32[5,72,256]{2,1,0:T(8,128)S(1)}, f32[5,72,256]{2,1,0:T(8,128)S(1)}, u32[]{:S(2)}, u32[]{:S(2)}) collective-permute-start(f32[5,72,256]{2,1,0:T(8,128)S(1)} %dynamic-slice_bitcast_fusion.1), channel_id=1, source_target_pairs={{0,2},{1,3},{2,0},{3,1},{4,6},{5,7},{6,4},{7,5},{8,10},{9,11},{10,... | collective-permute-start | bytes 1105928 | tf_op jit(solution)/shard_map/ppermute | solution.py:17
  71.6 22.0 %collective-permute-start.6 = (f32[72,256]{1,0:T(8,128)S(1)}, f32[72,256]{1,0:T(8,128)S(1)}, u32[]{:S(2)}, u32[]{:S(2)}) collective-permute-start(f32[72,256]{1,0:T(8,128)S(1)} %get-tuple-element.45), channel_id=1, source_target_pairs={{0,4},{4,8},{8,12},{12,16},{16,20},{20,24},{24,28},{1,5},{5,9},{9,... | collective-permute-start | bytes 221192 | tf_op jit(solution)/shard_map/ppermute | solution.py:12
  87.0 6.6 %collective-permute-start.7 = (f32[72,256]{1,0:T(8,128)S(1)}, f32[72,256]{1,0:T(8,128)S(1)}, u32[]{:S(2)}, u32[]{:S(2)}) collective-permute-start(f32[72,256]{1,0:T(8,128)S(1)} %get-tuple-element.46), channel_id=1, source_target_pairs={{8,0},{12,4},{16,8},{20,12},{24,16},{28,20},{9,1},{13,5},{17,9},{2... | collective-permute-start | bytes 221192 | tf_op jit(solution)/shard_map/ppermute | solution.py:12
  88.3 6.0 %collective-permute-start.8 = (f32[72,256]{1,0:T(8,128)S(1)}, f32[72,256]{1,0:T(8,128)S(1)}, u32[]{:S(2)}, u32[]{:S(2)}) collective-permute-start(f32[72,256]{1,0:T(8,128)S(1)} %get-tuple-element.47), channel_id=1, source_target_pairs={{0,12},{4,16},{8,20},{12,24},{16,28},{1,13},{5,17},{9,21},{13,25},... | collective-permute-start | bytes 221192 | tf_op jit(solution)/shard_map/ppermute | solution.py:12
  92.3 7.6 %collective-permute-start.9 = (f32[72,256]{1,0:T(8,128)S(1)}, f32[72,256]{1,0:T(8,128)S(1)}, u32[]{:S(2)}, u32[]{:S(2)}) collective-permute-start(f32[72,256]{1,0:T(8,128)S(1)} %get-tuple-element.48), channel_id=1, source_target_pairs={{16,0},{20,4},{24,8},{28,12},{17,1},{21,5},{25,9},{29,13},{18,2},{... | collective-permute-start | bytes 221192 | tf_op jit(solution)/shard_map/ppermute | solution.py:12
  99.9 6.7 %collective-permute-start.10 = (bf16[9,64,256]{2,1,0:T(8,128)(2,1)S(1)}, bf16[9,64,256]{2,1,0:T(8,128)(2,1)S(1)}, u32[]{:S(2)}, u32[]{:S(2)}) collective-permute-start(bf16[9,64,256]{2,1,0:T(8,128)(2,1)S(1)} %fusion.46), channel_id=1, source_target_pairs={{0,2},{1,3},{2,0},{3,1},{4,6},{5,7},{6,4},{7,5},{8,10},{9,11},{10,... | collective-permute-start | bytes 884744 | tf_op jit(solution)/shard_map/ppermute | solution.py:17
  106.7 10.0 %collective-permute-start.11 = (bf16[9,2,64,256]{3,2,0,1:T(8,128)(2,1)S(1)}, bf16[9,2,64,256]{3,2,0,1:T(8,128)(2,1)S(1)}, u32[]{:S(2)}, u32[]{:S(2)}) collective-permute-start(bf16[9,2,64,256]{3,2,0,1:T(8,128)(2,1)S(1)} %pad_maximum_fusion), channel_id=1, source_target_pairs={{0,1},{1,0},{2,3},{3,2},{4,5},{5,4},{6,7},{7,6},{8,9},{9,8},{10,11... | collective-permute-start | bytes 1769480 | tf_op jit(solution)/shard_map/ppermute | solution.py:17
  106.8 13.8 %collective-permute-start.12 = (bf16[256,256]{1,0:T(8,128)(2,1)S(1)}, bf16[256,256]{1,0:T(8,128)(2,1)S(1)}, u32[]{:S(2)}, u32[]{:S(2)}) collective-permute-start(bf16[256,256]{1,0:T(8,128)(2,1)S(1)} %copy-done), channel_id=1, source_target_pairs={{0,4},{4,8},{8,12},{12,16},{16,20},{20,24},{24,28},{1,5},{5,9},{9,... | collective-permute-start | bytes 393224 | tf_op jit(solution)/shard_map/ppermute | solution.py:12
  108.1 12.7 %collective-permute-start.13 = (bf16[256,256]{1,0:T(8,128)(2,1)S(1)}, bf16[256,256]{1,0:T(8,128)(2,1)S(1)}, u32[]{:S(2)}, u32[]{:S(2)}) collective-permute-start(bf16[256,256]{1,0:T(8,128)(2,1)S(1)} %copy-done), channel_id=1, source_target_pairs={{8,0},{12,4},{16,8},{20,12},{24,16},{28,20},{9,1},{13,5},{17,9},{2... | collective-permute-start | bytes 393224 | tf_op jit(solution)/shard_map/ppermute | solution.py:12
  109.4 11.7 %collective-permute-start.14 = (bf16[256,256]{1,0:T(8,128)(2,1)S(1)}, bf16[256,256]{1,0:T(8,128)(2,1)S(1)}, u32[]{:S(2)}, u32[]{:S(2)}) collective-permute-start(bf16[256,256]{1,0:T(8,128)(2,1)S(1)} %copy-done), channel_id=1, source_target_pairs={{0,12},{4,16},{8,20},{12,24},{16,28},{1,13},{5,17},{9,21},{13,25},... | collective-permute-start | bytes 393224 | tf_op jit(solution)/shard_map/ppermute | solution.py:12
  115.3 10.5 %collective-permute-start.15 = (bf16[256,256]{1,0:T(8,128)(2,1)S(1)}, bf16[256,256]{1,0:T(8,128)(2,1)S(1)}, u32[]{:S(2)}, u32[]{:S(2)}) collective-permute-start(bf16[256,256]{1,0:T(8,128)(2,1)S(1)} %copy-done), channel_id=1, source_target_pairs={{16,0},{20,4},{24,8},{28,12},{17,1},{21,5},{25,9},{29,13},{18,2},{... | collective-permute-start | bytes 393224 | tf_op jit(solution)/shard_map/ppermute | solution.py:12

commit v6 on v5

--- a/solution.py
+++ b/solution.py
@@ -30,6 +30,23 @@
     return jnp.stack([first, second], axis=axis)
 
 
+def split3(x):
+    hi = lax.reduce_precision(x, exponent_bits=8, mantissa_bits=7)
+    r1 = x - hi
+    mid = lax.reduce_precision(r1, exponent_bits=8, mantissa_bits=7)
+    lo = r1 - mid
+    return jnp.stack([hi, mid, lo]).astype(jnp.bfloat16)
+
+
+def join3(rows):
+    rows = rows.astype(jnp.float32)
+    return (rows[0] + rows[1]) + rows[2]
+
+
+def pad_cols(x, cols):
+    return jnp.concatenate([x, jnp.zeros((x.shape[0], cols - x.shape[1]), x.dtype)], axis=1)
+
+
 def body(teacher, student):
     group = lax.axis_size("batch")
     owner = lax.axis_index("batch")
@@ -46,27 +63,27 @@
     reach = min(REACH, group - 1)
     near_count = (2 * REACH + 1) * n
 
-    offsets = [d if d % 2 else -d for d in range(1, reach + 1)]
-    both = jnp.concatenate([teacher, student], axis=1)
-    blocks = [shifted(both, "batch", e) for e in offsets]
-    givers = [shifted(student, "batch", -e) for e in offsets]
-    t_band = [teacher] + [b[:, :ft] for b in blocks]
-    s_band = [student] + [b[:, ft:] for b in blocks]
-    tiles = len(t_band)
-
     def sq(x):
         xf = x.astype(jnp.float32)
         return jnp.sum(xf * xf, axis=1)
 
     own_q = sq(student) / ds - sq(teacher) / dt
     zero = jnp.zeros((n,), jnp.float32)
+    offsets = [d if d % 2 else -d for d in range(1, reach + 1)]
+    both = jnp.concatenate([teacher, student], axis=1)
+    fwd = jnp.concatenate([both, pad_cols(jnp.concatenate([split3(own_q), jnp.zeros((5, n), jnp.bfloat16)]),
+                                          ft + fs)], axis=0)
+    blocks = [shifted(fwd, "batch", e) for e in offsets]
+    scaled = jnp.concatenate([teacher * jnp.bfloat16(-2.0 / dt), student * jnp.bfloat16(2.0 / ds)], axis=1)
+    rhs = [both] + [b[:n] for b in blocks]
+    q_band = [own_q] + [join3(b[n:n + 3, :n]) for b in blocks]
+    s_band = [student] + [b[:n, ft:] for b in blocks]
+    tiles = len(rhs)
+
     parts = []
     for k in range(tiles):
-        tg = lax.dot_general(teacher, t_band[k], (((1,), (1,)), ((), ())), preferred_element_type=jnp.float32)
-        sg = lax.dot_general(student, s_band[k], (((1,), (1,)), ((), ())), preferred_element_type=jnp.float32)
-        g = sg * (2.0 / ds) - tg * (2.0 / dt)
-        q_p = own_q if k == 0 else sq(s_band[k]) / ds - sq(t_band[k]) / dt
-        extra = jnp.stack([q_p, own_q if k == 0 else zero, jnp.sum(g, axis=0), jnp.sum(g, axis=1)]
+        g = lax.dot_general(scaled, rhs[k], (((1,), (1,)), ((), ())), preferred_element_type=jnp.float32)
+        extra = jnp.stack([q_band[k], own_q if k == 0 else zero, jnp.sum(g, axis=0), jnp.sum(g, axis=1)]
                           + [zero] * 4)
         chunks = jnp.concatenate([g.reshape(4, m, n), jnp.broadcast_to(extra, (4, 8, n))], axis=1)
         parts.append(chunks.reshape(2, 2, m + 8, n))
@@ -86,14 +103,18 @@
     col_sums = jnp.sum(own_q) + n * q_p - g_col
     row_total = jnp.sum(jnp.where(valid[:, None], row_sums, jnp.zeros_like(row_sums)), axis=0)
 
+    low_own = resid.astype(jnp.bfloat16)
     received = []
+    givers = []
     for k, e in enumerate(offsets):
-        pack = jnp.concatenate([resid[k + 1], col_sums[k + 1][None, :], jnp.zeros((7, n), jnp.float32)], axis=0)
+        pack = jnp.concatenate([low_own[k + 1], student, split3(col_sums[k + 1]), jnp.zeros((5, n), jnp.bfloat16)],
+                               axis=0)
         got = shifted(pack, "batch", -e)
         received.append(got[:m])
-        row_total = row_total + got[m]
+        givers.append(got[m:m + n])
+        row_total = row_total + join3(got[m + n:m + n + 3])
 
-    low = jnp.concatenate([resid, jnp.stack(received)], axis=0).astype(jnp.bfloat16)
+    low = jnp.concatenate([low_own, jnp.stack(received)], axis=0)
     low = gathered(low, 1, 2, chip_bit)
     low = gathered(low, 2, 1, core_bit)
     low = low.reshape(low.shape[0], n, n)

time: 128 us -> 114 us (0.89)
  starting transfers between devices: 51 us -> 42.5 us
  local copies, waits for them, and re-layouts: 6.01 us -> 0.63 us
  waiting for transfers between devices: 44.1 us -> 47.3 us
  other arithmetic: 10.8 us -> 8.73 us
    ppermute x12 -> x8, starting transfers between devices: 47.6 us -> 39.3 us  [shifted(): return lax.ppermute(block, axis, route)]
    reduce_sum x10 -> x2, other arithmetic: 7.36 us -> 1.37 us  [sq(): return jnp.sum(xf * xf, axis=1)]
    ppermute x4, waiting for transfers between devices: 16.4 us -> 20.7 us  [swapped(): return lax.ppermute(block, axis, [(i, i ^ mask) for i in range(size)])]
    convert_element_type x0 -> x8, other arithmetic: none -> 2.72 us  [join3(): rows = rows.astype(jnp.float32)]
    unnamed x15 -> x12, local copies, waits for them, and re-layouts: 1.97 us -> 0.03 us
    sub x4 -> x0, local copies, waits for them, and re-layouts: 1.92 us -> none  [body(): g = sg * (2.0 / ds) - tg * (2.0 / dt)]
    dot_general x10 -> x5, matrix products: 9.05 us -> 7.32 us  [body(): lax.dot_general(scaled, rhs[k], (((1,), (1,)), ((), ())), preferred_eleme...]
    concatenate x3 -> x5, local copies, waits for them, and re-layouts: 1.64 us -> 0.16 us  [the longest x4 0.15 us: body(): jnp.concatenate([low_own[k + 1], student, split3(col_sums[k + 1]), jnp.ze...]
  transfers between devices with their start and end apart: 16 -> 12, of which waited for: 7 -> 8; matrix products, arithmetic and copies ran while one was open for 10% -> 4% of each run, Pallas kernels for 0% -> 0%
where the time goes in v6:
time: 114 us; the launch traced here: 113 us
  waiting for transfers between devices  47.3 us (41%)
  starting transfers between devices  42.5 us (37%)
  matrix products  13.5 us (12%)
  other arithmetic  8.73 us (8%)
    ppermute x8, starting transfers between devices, shifted(): return lax.ppermute(block, axis, route)  39.3 us
    ppermute x8, waiting for transfers between devices, shifted(): return lax.ppermute(block, axis, route)  26.7 us
    ppermute x4, waiting for transfers between devices, swapped(): return lax.ppermute(block, axis, [(i, i ^ mask) for i in range(size)])  20.7 us
    dot_general x5, matrix products, body(): lax.dot_general(scaled, rhs[k], (((1,), (1,)), ((), ())), preferred_eleme...  7.32 us
    dot_general x5, matrix products, body(): jnp.dot(low[k], s_band[k], preferred_element_type=jnp.float32)  5.32 us
    ppermute x4, starting transfers between devices, swapped(): return lax.ppermute(block, axis, [(i, i ^ mask) for i in range(size)])  3.23 us
    convert_element_type x8, other arithmetic, join3(): rows = rows.astype(jnp.float32)  2.72 us
  transfers between devices with their start and end apart: 12, of which 8 were waited for; matrix products, arithmetic and copies ran while one was open for 4% of the time, Pallas kernels for 0%

profile of v6, /device:TPU:0, one launch (start us, length us, event | category | flops | bytes accessed | tf_op | source)
XLA Modules:
  0.0 113.3 jit_solution(2382069177093328845)
XLA Ops:
  0.0 1.3 %multiply_reduce_fusion = f32[256]{0:T(256)S(1)} fusion(bf16[256,1024]{1,0:T(8,128)(2,1)} %param.3), kind=kLoop, calls=%fused_computation.28 | loop fusion | flops 786176 | bytes 525312 | tf_op jit(solution)/shard_map/reduce_sum | solution.py:68
  1.3 1.3 %broadcast_multiply_fusion = (bf16[256,1024]{1,0:T(8,128)(2,1)S(1)}, bf16[256,1280]{1,0:T(8,128)(2,1)S(1)}) fusion(bf16[256,1024]{1,0:T(8,128)(2,1)} %param.3), kind=kLoop, calls=%fused_computation.59 | loop fusion | flops 1048575 | bytes 1572864 | tf_op jit(solution)/shard_map/mul | solution.py:77
  2.6 0.0 copy-done
  2.6 0.1 fusion.20
  2.8 0.0 copy-start.1
  2.9 1.3 %collective-permute-start = (bf16[264,1280]{1,0:T(8,128)(2,1)S(1)}, bf16[264,1280]{1,0:T(8,128)(2,1)}, u32[]{:S(2)}, u32[]{:S(2)}) collective-permute-start(bf16[264,1280]{1,0:T(8,128)(2,1)S(1)} %fusion.9), channel_id=1, source_target_pairs={{4,0},{8,4},{12,8},{16,12},{20,16},{24,20},{28,24},{5,1},{9,5},{13... | collective-permute-start | bytes 2027528 | tf_op jit(solution)/shard_map/ppermute | solution.py:12
  4.2 7.8 %collective-permute-start.1 = (bf16[264,1280]{1,0:T(8,128)(2,1)S(1)}, bf16[264,1280]{1,0:T(8,128)(2,1)}, u32[]{:S(2)}, u32[]{:S(2)}) collective-permute-start(bf16[264,1280]{1,0:T(8,128)(2,1)S(1)} %fusion.9), channel_id=1, source_target_pairs={{0,8},{4,12},{8,16},{12,20},{16,24},{20,28},{1,9},{5,13},{9,17},{1... | collective-permute-start | bytes 2027528 | tf_op jit(solution)/shard_map/ppermute | solution.py:12
  12.0 1.3 %collective-permute-start.2 = (bf16[264,1280]{1,0:T(8,128)(2,1)S(1)}, bf16[264,1280]{1,0:T(8,128)(2,1)}, u32[]{:S(2)}, u32[]{:S(2)}) collective-permute-start(bf16[264,1280]{1,0:T(8,128)(2,1)S(1)} %fusion.9), channel_id=1, source_target_pairs={{12,0},{16,4},{20,8},{24,12},{28,16},{13,1},{17,5},{21,9},{25,13},... | collective-permute-start | bytes 2027528 | tf_op jit(solution)/shard_map/ppermute | solution.py:12
  13.3 6.4 %collective-permute-start.3 = (bf16[264,1280]{1,0:T(8,128)(2,1)S(1)}, bf16[264,1280]{1,0:T(8,128)(2,1)}, u32[]{:S(2)}, u32[]{:S(2)}) collective-permute-start(bf16[264,1280]{1,0:T(8,128)(2,1)S(1)} %fusion.9), channel_id=1, source_target_pairs={{0,16},{4,20},{8,24},{12,28},{1,17},{5,21},{9,25},{13,29},{2,18},{... | collective-permute-start | bytes 2027528 | tf_op jit(solution)/shard_map/ppermute | solution.py:12
  19.7 1.1 fusion.65
  20.8 0.0 copy-done.1
  20.8 1.0 maximum_dynamic-update-slice_fusion.4
  21.8 15.7 %collective-permute-done = bf16[264,1280]{1,0:T(8,128)(2,1)} collective-permute-done((bf16[264,1280]{1,0:T(8,128)(2,1)S(1)}, bf16[264,1280]{1,0:T(8,128)(2,1)}, u32[]{:S(2)}, u32[]{:S(2)}) %collective-permute-start) | collective-permute-done | bytes 675872 | tf_op jit(solution)/shard_map/ppermute | solution.py:12
  37.5 0.7 slice_convert_fusion.7
  38.2 0.0 collective-permute-done.1
  38.2 0.7 slice_convert_fusion.6
  38.9 0.0 collective-permute-done.2
  38.9 0.7 slice_convert_fusion.5
  39.6 0.2 collective-permute-done.3
  39.8 0.7 slice_convert_fusion.4
  40.5 1.6 %fusion.64 = (f32[256]{0:T(256)S(1)}, f32[256]{0:T(256)S(1)}, f32[256,256]{1,0:T(8,128)S(1)}) fusion(bf16[264,1280]{1,0:T(8,128)(2,1)} %collective-permute-done, bf16[256,256]{1,0:T(8,128)(2,1)} %copy-done.1, bf16[256,1024]{1,0:T(8,128)(2,1)S(1)} %get-tuple-element.30), kind=kOutput, calls=%fused_computation.171 | convolution fusion | flops 169213440 | bytes 1574912 | tf_op jit(solution)/shard_map/dot_general | solution.py:85
  42.2 0.0 copy-done.2
  42.2 1.5 %fusion.63 = (f32[256]{0:T(256)S(1)}, f32[256]{0:T(256)S(1)}, f32[256,256]{1,0:T(8,128)S(1)}) fusion(bf16[264,1280]{1,0:T(8,128)(2,1)} %collective-permute-done.1, bf16[256,256]{1,0:T(8,128)(2,1)S(1)} %copy-done.2, bf16[256,1024]{1,0:T(8,128)(2,1)S(1)} %get-tuple-element.30), kind=kOutput, calls=%fused_computation.170 | convolution fusion | flops 169213440 | bytes 1574912 | tf_op jit(solution)/shard_map/dot_general | solution.py:85
  43.8 1.5 %fusion.62 = (f32[256]{0:T(256)S(1)}, f32[256]{0:T(256)S(1)}, f32[256,256]{1,0:T(8,128)S(1)}) fusion(bf16[264,1280]{1,0:T(8,128)(2,1)} %collective-permute-done.2, bf16[256,256]{1,0:T(8,128)(2,1)S(1)} %copy-done.2, bf16[256,1024]{1,0:T(8,128)(2,1)S(1)} %get-tuple-element.30), kind=kOutput, calls=%fused_computation.169 | convolution fusion | flops 169213440 | bytes 1574912 | tf_op jit(solution)/shard_map/dot_general | solution.py:85
  45.4 1.5 %fusion.61 = (f32[256]{0:T(256)S(1)}, f32[256]{0:T(256)S(1)}, f32[256,256]{1,0:T(8,128)S(1)}) fusion(bf16[264,1280]{1,0:T(8,128)(2,1)} %collective-permute-done.3, bf16[256,256]{1,0:T(8,128)(2,1)S(1)} %copy-done.2, bf16[256,1024]{1,0:T(8,128)(2,1)S(1)} %get-tuple-element.30), kind=kOutput, calls=%fused_computation.168 | convolution fusion | flops 169213440 | bytes 1574912 | tf_op jit(solution)/shard_map/dot_general | solution.py:85
  47.1 0.1 dynamic-slice_bitcast_fusion
  47.1 0.1 collective-permute-start.4
  47.2 0.0 copy-start.3
  47.3 2.1 %collective-permute-done.4 = f32[5,2,72,256]{3,2,1,0:T(8,128)S(1)} collective-permute-done((f32[5,2,72,256]{3,2,1,0:T(8,128)S(1)}, f32[5,2,72,256]{3,2,1,0:T(8,128)S(1)}, u32[]{:S(2)}, u32[]{:S(2)}) %collective-permute-start.4) | collective-permute-done | bytes 737312 | tf_op jit(solution)/shard_map/ppermute | solution.py:17
  49.4 0.1 bitcast_add_fusion
  49.5 1.6 %collective-permute-start.5 = (f32[5,72,256]{2,1,0:T(8,128)S(1)}, f32[5,72,256]{2,1,0:T(8,128)S(1)}, u32[]{:S(2)}, u32[]{:S(2)}) collective-permute-start(f32[5,72,256]{2,1,0:T(8,128)S(1)} %dynamic-slice_bitcast_fusion.1), channel_id=1, source_target_pairs={{0,2},{1,3},{2,0},{3,1},{4,6},{5,7},{6,4},{7,5},{8,10},{9,11},{10,... | collective-permute-start | bytes 1105928 | tf_op jit(solution)/shard_map/ppermute | solution.py:17
  51.1 9.1 %collective-permute-done.5 = f32[5,72,256]{2,1,0:T(8,128)S(1)} collective-permute-done((f32[5,72,256]{2,1,0:T(8,128)S(1)}, f32[5,72,256]{2,1,0:T(8,128)S(1)}, u32[]{:S(2)}, u32[]{:S(2)}) %collective-permute-start.5) | collective-permute-done | bytes 368672 | tf_op jit(solution)/shard_map/ppermute | solution.py:17
  60.2 0.1 bitcast_add_fusion.1
  60.3 0.1 slice_reduce_fusion.1
  60.4 0.6 broadcast_multiply_fusion.2
  61.0 0.6 bitcast_subtract_fusion
  61.7 0.1 fusion.59
  61.8 0.1 constant_dynamic-update-slice_fusion.2
  62.0 18.4 %collective-permute-start.6 = (bf16[328,256]{1,0:T(8,128)(2,1)S(1)}, bf16[328,256]{1,0:T(8,128)(2,1)S(1)}, u32[]{:S(2)}, u32[]{:S(2)}) collective-permute-start(bf16[328,256]{1,0:T(8,128)(2,1)S(1)} %concatenate.79), channel_id=1, source_target_pairs={{0,4},{4,8},{8,12},{12,16},{16,20},{20,24},{24,28},{1,5},{5,9},{9,... | collective-permute-start | bytes 503816 | tf_op jit(solution)/shard_map/ppermute | solution.py:12
  80.5 1.3 %collective-permute-start.9 = (bf16[328,256]{1,0:T(8,128)(2,1)S(1)}, bf16[328,256]{1,0:T(8,128)(2,1)S(1)}, u32[]{:S(2)}, u32[]{:S(2)}) collective-permute-start(bf16[328,256]{1,0:T(8,128)(2,1)S(1)} %concatenate.82), channel_id=1, source_target_pairs={{16,0},{20,4},{24,8},{28,12},{17,1},{21,5},{25,9},{29,13},{18,2},{... | collective-permute-start | bytes 503816 | tf_op jit(solution)/shard_map/ppermute | solution.py:12
  81.8 1.5 %collective-permute-start.8 = (bf16[328,256]{1,0:T(8,128)(2,1)S(1)}, bf16[328,256]{1,0:T(8,128)(2,1)S(1)}, u32[]{:S(2)}, u32[]{:S(2)}) collective-permute-start(bf16[328,256]{1,0:T(8,128)(2,1)S(1)} %concatenate.81), channel_id=1, source_target_pairs={{0,12},{4,16},{8,20},{12,24},{16,28},{1,13},{5,17},{9,21},{13,25},... | collective-permute-start | bytes 503816 | tf_op jit(solution)/shard_map/ppermute | solution.py:12
  83.3 1.3 %collective-permute-start.7 = (bf16[328,256]{1,0:T(8,128)(2,1)S(1)}, bf16[328,256]{1,0:T(8,128)(2,1)S(1)}, u32[]{:S(2)}, u32[]{:S(2)}) collective-permute-start(bf16[328,256]{1,0:T(8,128)(2,1)S(1)} %concatenate.80), channel_id=1, source_target_pairs={{8,0},{12,4},{16,8},{20,12},{24,16},{28,20},{9,1},{13,5},{17,9},{2... | collective-permute-start | bytes 503816 | tf_op jit(solution)/shard_map/ppermute | solution.py:12
  84.6 0.1 fusion.51
  84.7 0.0 collective-permute-done.6
  84.7 7.2 %collective-permute-done.9 = bf16[328,256]{1,0:T(8,128)(2,1)S(1)} collective-permute-done((bf16[328,256]{1,0:T(8,128)(2,1)S(1)}, bf16[328,256]{1,0:T(8,128)(2,1)S(1)}, u32[]{:S(2)}, u32[]{:S(2)}) %collective-permute-start.9) | collective-permute-done | bytes 167968 | tf_op jit(solution)/shard_map/ppermute | solution.py:12
  92.0 3.5 %collective-permute-done.7 = bf16[328,256]{1,0:T(8,128)(2,1)S(1)} collective-permute-done((bf16[328,256]{1,0:T(8,128)(2,1)S(1)}, bf16[328,256]{1,0:T(8,128)(2,1)S(1)}, u32[]{:S(2)}, u32[]{:S(2)}) %collective-permute-start.7) | collective-permute-done | bytes 167968 | tf_op jit(solution)/shard_map/ppermute | solution.py:12
  95.4 0.0 collective-permute-done.8
  95.5 1.5 %collective-permute-start.10 = (bf16[9,64,256]{2,1,0:T(8,128)(2,1)S(1)}, bf16[9,64,256]{2,1,0:T(8,128)(2,1)S(1)}, u32[]{:S(2)}, u32[]{:S(2)}) collective-permute-start(bf16[9,64,256]{2,1,0:T(8,128)(2,1)S(1)} %fusion.43), channel_id=1, source_target_pairs={{0,2},{1,3},{2,0},{3,1},{4,6},{5,7},{6,4},{7,5},{8,10},{9,11},{10,... | collective-permute-start | bytes 884744 | tf_op jit(solution)/shard_map/ppermute | solution.py:17
  97.0 7.4 %collective-permute-done.10 = bf16[9,64,256]{2,1,0:T(8,128)(2,1)S(1)} collective-permute-done((bf16[9,64,256]{2,1,0:T(8,128)(2,1)S(1)}, bf16[9,64,256]{2,1,0:T(8,128)(2,1)S(1)}, u32[]{:S(2)}, u32[]{:S(2)}) %collective-permute-start.10) | collective-permute-done | bytes 294944 | tf_op jit(solution)/shard_map/ppermute | solution.py:17
  104.5 0.1 select_bitcast_fusion.3
  104.5 0.1 pad_maximum_fusion.1
  104.6 0.1 collective-permute-start.11
  104.7 2.0 %collective-permute-done.11 = bf16[9,2,64,256]{3,2,0,1:T(8,128)(2,1)S(1)} collective-permute-done((bf16[9,2,64,256]{3,2,0,1:T(8,128)(2,1)S(1)}, bf16[9,2,64,256]{3,2,0,1:T(8,128)(2,1)S(1)}, u32[]{:S(2)}, u32[]{:S(2)}) %collective-permute-start.11) | collective-permute-done | bytes 589856 | tf_op jit(solution)/shard_map/ppermute | solution.py:17
  106.7 0.1 select_bitcast_fusion.1
  106.8 0.1 fusion.24
  106.9 0.2 fusion.67
  107.2 1.1 fusion.39
  108.3 1.1 fusion.37
  109.4 0.2 fusion.35
  109.7 0.2 fusion.33
  109.9 0.2 fusion.31
  110.1 0.2 fusion.29
  110.4 1.1 convolution_add_fusion.1
  111.5 1.9 %fusion.8 = f32[256,256]{1,0:T(8,128)} fusion(f32[256,256]{1,0:T(8,128)S(1)} %fusion.29, f32[256,256]{1,0:T(8,128)S(1)} %fusion.31, f32[256,256]{1,0:T(8,128)S(1)} %fusion.33, f32[256,256]{1,0:T(8,128)S(1)} %fusion.35, f32[256,256]{1,0:T(8,128)S(1)} %fusion.37, f32[256,256]{1,0:T(8,128)S(1)} %fusion.39, f32[256,256]{1,0:T(8,128)S(1)} %convolution_add_fusion.1, ...), kind=kOutput, calls=%fused_computation.27 | convolution fusion | flops 34275328 | bytes 2491392 | tf_op jit(solution)/shard_map/dot_general | solution.py:124
  (60 shorter events, 0.8 us)
Async XLA Ops:
  0.0 2.6 %copy-start = (bf16[256,256]{1,0:T(8,128)(2,1)S(1)}, bf16[256,256]{1,0:T(8,128)(2,1)}, u32[]{:S(2)}) copy-start(bf16[256,256]{1,0:T(8,128)(2,1)} %param.4) | copy-start | bytes 393220
  2.8 18.0 %copy-start.1 = (bf16[256,256]{1,0:T(8,128)(2,1)}, bf16[256,256]{1,0:T(8,128)(2,1)S(1)}, u32[]{:S(2)}) copy-start(bf16[256,256]{1,0:T(8,128)(2,1)S(1)} %get-tuple-element.43) | copy-start | bytes 393220
  2.9 34.7 %collective-permute-start = (bf16[264,1280]{1,0:T(8,128)(2,1)S(1)}, bf16[264,1280]{1,0:T(8,128)(2,1)}, u32[]{:S(2)}, u32[]{:S(2)}) collective-permute-start(bf16[264,1280]{1,0:T(8,128)(2,1)S(1)} %fusion.9), channel_id=1, source_target_pairs={{4,0},{8,4},{12,8},{16,12},{20,16},{24,20},{28,24},{5,1},{9,5},{13... | collective-permute-start | bytes 2027528 | tf_op jit(solution)/shard_map/ppermute | solution.py:12
  4.2 34.0 %collective-permute-start.1 = (bf16[264,1280]{1,0:T(8,128)(2,1)S(1)}, bf16[264,1280]{1,0:T(8,128)(2,1)}, u32[]{:S(2)}, u32[]{:S(2)}) collective-permute-start(bf16[264,1280]{1,0:T(8,128)(2,1)S(1)} %fusion.9), channel_id=1, source_target_pairs={{0,8},{4,12},{8,16},{12,20},{16,24},{20,28},{1,9},{5,13},{9,17},{1... | collective-permute-start | bytes 2027528 | tf_op jit(solution)/shard_map/ppermute | solution.py:12
  12.0 26.9 %collective-permute-start.2 = (bf16[264,1280]{1,0:T(8,128)(2,1)S(1)}, bf16[264,1280]{1,0:T(8,128)(2,1)}, u32[]{:S(2)}, u32[]{:S(2)}) collective-permute-start(bf16[264,1280]{1,0:T(8,128)(2,1)S(1)} %fusion.9), channel_id=1, source_target_pairs={{12,0},{16,4},{20,8},{24,12},{28,16},{13,1},{17,5},{21,9},{25,13},... | collective-permute-start | bytes 2027528 | tf_op jit(solution)/shard_map/ppermute | solution.py:12
  13.3 26.5 %collective-permute-start.3 = (bf16[264,1280]{1,0:T(8,128)(2,1)S(1)}, bf16[264,1280]{1,0:T(8,128)(2,1)}, u32[]{:S(2)}, u32[]{:S(2)}) collective-permute-start(bf16[264,1280]{1,0:T(8,128)(2,1)S(1)} %fusion.9), channel_id=1, source_target_pairs={{0,16},{4,20},{8,24},{12,28},{1,17},{5,21},{9,25},{13,29},{2,18},{... | collective-permute-start | bytes 2027528 | tf_op jit(solution)/shard_map/ppermute | solution.py:12
  40.5 1.7 %copy-start.2 = (bf16[256,256]{1,0:T(8,128)(2,1)S(1)}, bf16[256,256]{1,0:T(8,128)(2,1)}, u32[]{:S(2)}) copy-start(bf16[256,256]{1,0:T(8,128)(2,1)} %copy-done.1) | copy-start | bytes 393220
  47.1 2.3 %collective-permute-start.4 = (f32[5,2,72,256]{3,2,1,0:T(8,128)S(1)}, f32[5,2,72,256]{3,2,1,0:T(8,128)S(1)}, u32[]{:S(2)}, u32[]{:S(2)}) collective-permute-start(f32[5,2,72,256]{3,2,1,0:T(8,128)S(1)} %dynamic-slice_bitcast_fusion), channel_id=1, source_target_pairs={{0,1},{1,0},{2,3},{3,2},{4,5},{5,4},{6,7},{7,6},{8,9},{9,8},{10,11... | collective-permute-start | bytes 2211848 | tf_op jit(solution)/shard_map/ppermute | solution.py:17
  47.2 3.9 %copy-start.3 = (s32[5]{0:T(128)S(1)}, s32[5]{0:T(128)}, u32[]{:S(2)}) copy-start(s32[5]{0:T(128)} %constant.89.clone) | copy-start | bytes 64
  49.5 10.7 %collective-permute-start.5 = (f32[5,72,256]{2,1,0:T(8,128)S(1)}, f32[5,72,256]{2,1,0:T(8,128)S(1)}, u32[]{:S(2)}, u32[]{:S(2)}) collective-permute-start(f32[5,72,256]{2,1,0:T(8,128)S(1)} %dynamic-slice_bitcast_fusion.1), channel_id=1, source_target_pairs={{0,2},{1,3},{2,0},{3,1},{4,6},{5,7},{6,4},{7,5},{8,10},{9,11},{10,... | collective-permute-start | bytes 1105928 | tf_op jit(solution)/shard_map/ppermute | solution.py:17
  62.0 22.7 %collective-permute-start.6 = (bf16[328,256]{1,0:T(8,128)(2,1)S(1)}, bf16[328,256]{1,0:T(8,128)(2,1)S(1)}, u32[]{:S(2)}, u32[]{:S(2)}) collective-permute-start(bf16[328,256]{1,0:T(8,128)(2,1)S(1)} %concatenate.79), channel_id=1, source_target_pairs={{0,4},{4,8},{8,12},{12,16},{16,20},{20,24},{24,28},{1,5},{5,9},{9,... | collective-permute-start | bytes 503816 | tf_op jit(solution)/shard_map/ppermute | solution.py:12
  80.5 11.5 %collective-permute-start.9 = (bf16[328,256]{1,0:T(8,128)(2,1)S(1)}, bf16[328,256]{1,0:T(8,128)(2,1)S(1)}, u32[]{:S(2)}, u32[]{:S(2)}) collective-permute-start(bf16[328,256]{1,0:T(8,128)(2,1)S(1)} %concatenate.82), channel_id=1, source_target_pairs={{16,0},{20,4},{24,8},{28,12},{17,1},{21,5},{25,9},{29,13},{18,2},{... | collective-permute-start | bytes 503816 | tf_op jit(solution)/shard_map/ppermute | solution.py:12
  81.8 13.6 %collective-permute-start.8 = (bf16[328,256]{1,0:T(8,128)(2,1)S(1)}, bf16[328,256]{1,0:T(8,128)(2,1)S(1)}, u32[]{:S(2)}, u32[]{:S(2)}) collective-permute-start(bf16[328,256]{1,0:T(8,128)(2,1)S(1)} %concatenate.81), channel_id=1, source_target_pairs={{0,12},{4,16},{8,20},{12,24},{16,28},{1,13},{5,17},{9,21},{13,25},... | collective-permute-start | bytes 503816 | tf_op jit(solution)/shard_map/ppermute | solution.py:12
  83.3 12.1 %collective-permute-start.7 = (bf16[328,256]{1,0:T(8,128)(2,1)S(1)}, bf16[328,256]{1,0:T(8,128)(2,1)S(1)}, u32[]{:S(2)}, u32[]{:S(2)}) collective-permute-start(bf16[328,256]{1,0:T(8,128)(2,1)S(1)} %concatenate.80), channel_id=1, source_target_pairs={{8,0},{12,4},{16,8},{20,12},{24,16},{28,20},{9,1},{13,5},{17,9},{2... | collective-permute-start | bytes 503816 | tf_op jit(solution)/shard_map/ppermute | solution.py:12
  95.5 9.0 %collective-permute-start.10 = (bf16[9,64,256]{2,1,0:T(8,128)(2,1)S(1)}, bf16[9,64,256]{2,1,0:T(8,128)(2,1)S(1)}, u32[]{:S(2)}, u32[]{:S(2)}) collective-permute-start(bf16[9,64,256]{2,1,0:T(8,128)(2,1)S(1)} %fusion.43), channel_id=1, source_target_pairs={{0,2},{1,3},{2,0},{3,1},{4,6},{5,7},{6,4},{7,5},{8,10},{9,11},{10,... | collective-permute-start | bytes 884744 | tf_op jit(solution)/shard_map/ppermute | solution.py:17
  104.6 2.1 %collective-permute-start.11 = (bf16[9,2,64,256]{3,2,0,1:T(8,128)(2,1)S(1)}, bf16[9,2,64,256]{3,2,0,1:T(8,128)(2,1)S(1)}, u32[]{:S(2)}, u32[]{:S(2)}) collective-permute-start(bf16[9,2,64,256]{3,2,0,1:T(8,128)(2,1)S(1)} %pad_maximum_fusion.1), channel_id=1, source_target_pairs={{0,1},{1,0},{2,3},{3,2},{4,5},{5,4},{6,7},{7,6},{8,9},{9,8},{10,11... | collective-permute-start | bytes 1769480 | tf_op jit(solution)/shard_map/ppermute | solution.py:17

commit v7 on v4

--- a/solution.py
+++ b/solution.py
@@ -2,6 +2,7 @@
 import jax.numpy as jnp
 from jax import lax
 from jax.sharding import PartitionSpec as P
+
 
 REACH = 4
 
@@ -43,7 +44,7 @@
     return joined(part, swapped(part, "width", 1), 2, core)
 
 
-def body(teacher, student):
+def layer(teacher, student):
     group = lax.axis_size("batch")
     owner = lax.axis_index("batch")
     width = lax.axis_size("width")
@@ -68,9 +69,7 @@
         xf = x.astype(jnp.float32)
         return jnp.sum(xf * xf, axis=1)
 
-    pad = (-(rows_dev + 1)) % 8
-
-    def tile_part(t_d, s_d):
+    def tile_part(t_d, s_d, pad):
         tg = lax.dot_general(teacher, t_d, (((1,), (1,)), ((), ())), preferred_element_type=jnp.float32)
         sg = lax.dot_general(student, s_d, (((1,), (1,)), ((), ())), preferred_element_type=jnp.float32)
         q_d = sq(s_d) / ds - sq(t_d) / dt
@@ -85,7 +84,8 @@
     for group_idx in ([list(range(split)), list(range(split, len(offsets)))]):
         if not group_idx:
             continue
-        total = width_sum(jnp.stack([tile_part(teacher_band[d], student_band[d]) for d in group_idx]))
+        pad = (-(rows_dev + 1)) % 8 + (8 if group_idx[0] else 0)
+        total = width_sum(jnp.stack([tile_part(teacher_band[d], student_band[d], pad) for d in group_idx]))
         if own_q is None:
             own_q = total[0, rows_dev, :]
         for k, d in enumerate(group_idx):
@@ -115,4 +115,4 @@
 def solution(mesh):
     in_specs = (P("batch", "width"), P("batch", "width"))
     out_specs = P("batch", "width")
-    return jax.shard_map(body, mesh=mesh, in_specs=in_specs, out_specs=out_specs, check_vma=False)
+    return jax.shard_map(layer, mesh=mesh, in_specs=in_specs, out_specs=out_specs, check_vma=False)

time: 104 us -> 108 us (1.038)
  starting transfers between devices: 26.2 us -> 38.2 us
  waiting for transfers between devices: 56.4 us -> 47 us
  other arithmetic: 7.12 us -> 9.86 us
  local copies, waits for them, and re-layouts: 5.32 us -> 3.79 us
    ppermute x8, starting transfers between devices: 19.8 us -> 32.5 us  [shifted(): return lax.ppermute(block, axis, route)]
    ppermute x8, waiting for transfers between devices: 44.2 us -> 35.6 us  [shifted(): return lax.ppermute(block, axis, route)]
    reduce_sum x10, other arithmetic: 1.48 us -> 3.43 us  [sq(): return jnp.sum(xf * xf, axis=1)]
    unnamed x9 -> x5, local copies, waits for them, and re-layouts: 2.65 us -> 1.99 us
  transfers between devices with their start and end apart: 16 -> 16, of which waited for: 12 -> 9; matrix products, arithmetic and copies ran while one was open for 12% -> 16% of each run, Pallas kernels for 0% -> 0%
where the time goes in v7:
time: 108 us
  waiting for transfers between devices  47 us (44%)
  starting transfers between devices  38.2 us (35%)
  other arithmetic  9.86 us (9%)
  matrix products  8.32 us (8%)
  local copies, waits for them, and re-layouts  3.79 us (4%)
    ppermute x8, waiting for transfers between devices, shifted(): return lax.ppermute(block, axis, route)  35.6 us
    ppermute x8, starting transfers between devices, shifted(): return lax.ppermute(block, axis, route)  32.5 us
    ppermute x8, waiting for transfers between devices, swapped(): return lax.ppermute(block, axis, [(i, i ^ mask) for i in range(size)])  11.4 us
    ppermute x8, starting transfers between devices, swapped(): return lax.ppermute(block, axis, [(i, i ^ mask) for i in range(size)])  5.72 us
    reduce_sum x10, other arithmetic, sq(): return jnp.sum(xf * xf, axis=1)  3.43 us
    dot_general x5, matrix products, tile_part(): lax.dot_general(teacher, t_d, (((1,), (1,)), ((), ())), preferred_element...  2.73 us
    dot_general x5, matrix products, layer(): jnp.dot(low, student_band[d], preferred_element_type=jnp.float32)  2.69 us
  transfers between devices with their start and end apart: 16, of which 9 were waited for; matrix products, arithmetic and copies ran while one was open for 16% of the time, Pallas kernels for 0%

profile of v7, /device:TPU:24, one launch (start us, length us, event | category | flops | bytes accessed | tf_op | source)
XLA Modules:
  0.0 107.6 jit_solution(17856474981921014622)
XLA Ops:
  0.0 2.0 %constant_dynamic-update-slice_fusion.1 = bf16[256,1280]{1,0:T(8,128)(2,1)} fusion(bf16[256,1024]{1,0:T(8,128)(2,1)} %param.2), kind=kLoop, calls=%fused_computation.132 | loop fusion | bytes 1048576
  2.0 0.7 constant_dynamic-update-slice_fusion
  2.7 1.3 %collective-permute-start.9 = (bf16[256,1280]{1,0:T(8,128)(2,1)}, bf16[256,1280]{1,0:T(8,128)(2,1)S(1)}, u32[]{:S(2)}, u32[]{:S(2)}) collective-permute-start(bf16[256,1280]{1,0:T(8,128)(2,1)} %constant_dynamic-update-slice_fusion), channel_id=1, source_target_pairs={{0,16},{4,20},{8,24},{12,28},{1,17},{5,21},{9,25},{13,29},{2,18},{... | collective-permute-start | bytes 1966088 | tf_op jit(solution)/shard_map/ppermute | solution.py:13
  3.9 6.5 %collective-permute-start.8 = (bf16[256,1280]{1,0:T(8,128)(2,1)}, bf16[256,1280]{1,0:T(8,128)(2,1)S(1)}, u32[]{:S(2)}, u32[]{:S(2)}) collective-permute-start(bf16[256,1280]{1,0:T(8,128)(2,1)} %constant_dynamic-update-slice_fusion), channel_id=1, source_target_pairs={{12,0},{16,4},{20,8},{24,12},{28,16},{13,1},{17,5},{21,9},{25,13},... | collective-permute-start | bytes 1966088 | tf_op jit(solution)/shard_map/ppermute | solution.py:13
  10.4 2.4 %collective-permute-start = (bf16[256,1280]{1,0:T(8,128)(2,1)}, bf16[256,1280]{1,0:T(8,128)(2,1)S(1)}, u32[]{:S(2)}, u32[]{:S(2)}) collective-permute-start(bf16[256,1280]{1,0:T(8,128)(2,1)} %constant_dynamic-update-slice_fusion), channel_id=1, source_target_pairs={{4,0},{8,4},{12,8},{16,12},{20,16},{24,20},{28,24},{5,1},{9,5},{13... | collective-permute-start | bytes 1966088 | tf_op jit(solution)/shard_map/ppermute | solution.py:13
  12.9 1.3 %collective-permute-start.1 = (bf16[256,1280]{1,0:T(8,128)(2,1)}, bf16[256,1280]{1,0:T(8,128)(2,1)}, u32[]{:S(2)}, u32[]{:S(2)}) collective-permute-start(bf16[256,1280]{1,0:T(8,128)(2,1)} %constant_dynamic-update-slice_fusion), channel_id=1, source_target_pairs={{0,8},{4,12},{8,16},{12,20},{16,24},{20,28},{1,9},{5,13},{9,17},{1... | collective-permute-start | bytes 1966088 | tf_op jit(solution)/shard_map/ppermute | solution.py:13
  14.2 0.3 convolution_multiply_fusion.9
  14.5 0.1 fusion.23
  14.6 0.1 copy.5
  14.9 0.2 multiply_reduce_fusion.4
  15.1 0.2 fusion.10
  15.4 20.8 %collective-permute-done.9 = bf16[256,1280]{1,0:T(8,128)(2,1)S(1)} collective-permute-done((bf16[256,1280]{1,0:T(8,128)(2,1)}, bf16[256,1280]{1,0:T(8,128)(2,1)S(1)}, u32[]{:S(2)}, u32[]{:S(2)}) %collective-permute-start.9) | collective-permute-done | bytes 655392 | tf_op jit(solution)/shard_map/ppermute | solution.py:13
  36.2 0.1 multiply_reduce_fusion.5
  36.3 0.2 multiply_reduce_fusion
  36.5 0.3 convolution_multiply_fusion.5
  36.9 0.2 multiply_reduce_fusion.1
  37.0 0.1 multiply_reduce_fusion.6
  37.2 0.3 convolution_multiply_fusion.6
  37.5 0.2 fusion.3
  37.8 0.2 fusion.5
  38.0 0.1 maximum_bitcast_fusion.1
  38.1 0.7 fusion.20
  38.8 0.1 multiply_reduce_fusion.8
  39.0 0.2 multiply_reduce_fusion.3
  39.1 5.5 %collective-permute-done.1 = bf16[256,1280]{1,0:T(8,128)(2,1)} collective-permute-done((bf16[256,1280]{1,0:T(8,128)(2,1)}, bf16[256,1280]{1,0:T(8,128)(2,1)}, u32[]{:S(2)}, u32[]{:S(2)}) %collective-permute-start.1) | collective-permute-done | bytes 655392 | tf_op jit(solution)/shard_map/ppermute | solution.py:13
  44.6 1.2 %multiply_reduce_fusion.2 = f32[256]{0:T(256)S(1)} fusion(bf16[256,1280]{1,0:T(8,128)(2,1)} %collective-permute-done.1), kind=kLoop, calls=%fused_computation.37 | loop fusion | flops 786176 | bytes 525312 | tf_op jit(solution)/shard_map/reduce_sum | solution.py:70
  45.9 1.0 multiply_reduce_fusion.7
  46.9 0.3 convolution_multiply_fusion.8
  47.2 1.4 %convolution_multiply_fusion.7 = f32[256,256]{0,1:T(8,128)S(1)} fusion(bf16[256,1024]{1,0:T(8,128)(2,1)S(1)} %copy-done.1, bf16[256,1280]{1,0:T(8,128)(2,1)} %collective-permute-done.1), kind=kOutput, calls=%fused_computation.28 | convolution fusion | flops 134283264 | bytes 1310720 | tf_op jit(solution)/shard_map/dot_general | solution.py:73
  48.6 0.2 fusion.9
  48.9 1.1 %fusion.7 = f32[256,256]{1,0:T(8,128)S(1)} fusion(f32[256,256]{0,1:T(8,128)S(1)} %convolution_multiply_fusion.7, bf16[256,256]{1,0:T(8,128)(2,1)S(1)} %copy-done, bf16[256,1280]{1,0:T(8,128)(2,1)} %collective-permute-done.1), kind=kOutput, calls=%fused_computation.19 | convolution fusion | flops 33685504 | bytes 786432 | tf_op jit(solution)/shard_map/dot_general | solution.py:74
  50.0 0.1 maximum_bitcast_fusion.2
  50.2 0.8 constant_dynamic-slice_fusion.2
  51.0 1.0 fusion.22
  52.0 1.6 %collective-permute-start.11 = (f32[2,136,128]{2,1,0:T(8,128)S(1)}, f32[2,136,128]{2,1,0:T(8,128)S(1)}, u32[]{:S(2)}, u32[]{:S(2)}) collective-permute-start(f32[2,136,128]{2,1,0:T(8,128)S(1)} %constant_dynamic-slice_fusion), channel_id=1, source_target_pairs={{0,2},{1,3},{2,0},{3,1},{4,6},{5,7},{6,4},{7,5},{8,10},{9,11},{10,... | collective-permute-start | bytes 417800 | tf_op jit(solution)/shard_map/ppermute | solution.py:18
  53.6 1.0 dynamic-slice_add_fusion
  54.7 1.0 collective-permute-start.3
  55.7 2.9 %collective-permute-done.11 = f32[2,136,128]{2,1,0:T(8,128)S(1)} collective-permute-done((f32[2,136,128]{2,1,0:T(8,128)S(1)}, f32[2,136,128]{2,1,0:T(8,128)S(1)}, u32[]{:S(2)}, u32[]{:S(2)}) %collective-permute-start.11) | collective-permute-done | bytes 139296 | tf_op jit(solution)/shard_map/ppermute | solution.py:18
  58.6 1.6 %collective-permute-start.12 = (f32[2,136,128]{2,1,0:T(8,128)S(1)}, f32[2,136,128]{2,1,0:T(8,128)S(1)}, u32[]{:S(2)}, u32[]{:S(2)}) collective-permute-start(f32[2,136,128]{2,1,0:T(8,128)S(1)} %dynamic-slice_add_fusion.2), channel_id=1, source_target_pairs={{0,2},{1,3},{2,0},{3,1},{4,6},{5,7},{6,4},{7,5},{8,10},{9,11},{10,... | collective-permute-start | bytes 417800 | tf_op jit(solution)/shard_map/ppermute | solution.py:18
  60.2 2.9 %collective-permute-done.3 = f32[3,132,128]{2,1,0:T(8,128)S(1)} collective-permute-done((f32[3,132,128]{2,1,0:T(8,128)S(1)}, f32[3,132,128]{2,1,0:T(8,128)S(1)}, u32[]{:S(2)}, u32[]{:S(2)}) %collective-permute-start.3) | collective-permute-done | bytes 202784 | tf_op jit(solution)/shard_map/ppermute | solution.py:18
  63.1 1.6 %collective-permute-start.4 = (f32[3,132,128]{2,1,0:T(8,128)S(1)}, f32[3,132,128]{2,1,0:T(8,128)S(1)}, u32[]{:S(2)}, u32[]{:S(2)}) collective-permute-start(f32[3,132,128]{2,1,0:T(8,128)S(1)} %dynamic-slice_add_fusion.1), channel_id=1, source_target_pairs={{0,2},{1,3},{2,0},{3,1},{4,6},{5,7},{6,4},{7,5},{8,10},{9,11},{10,... | collective-permute-start | bytes 608264 | tf_op jit(solution)/shard_map/ppermute | solution.py:18
  64.7 1.4 %collective-permute-done.12 = f32[2,136,128]{2,1,0:T(8,128)S(1)} collective-permute-done((f32[2,136,128]{2,1,0:T(8,128)S(1)}, f32[2,136,128]{2,1,0:T(8,128)S(1)}, u32[]{:S(2)}, u32[]{:S(2)}) %collective-permute-start.12) | collective-permute-done | bytes 139296 | tf_op jit(solution)/shard_map/ppermute | solution.py:18
  66.1 0.7 pad_maximum_fusion.2
  66.9 3.2 %collective-permute-done.4 = f32[3,132,128]{2,1,0:T(8,128)S(1)} collective-permute-done((f32[3,132,128]{2,1,0:T(8,128)S(1)}, f32[3,132,128]{2,1,0:T(8,128)S(1)}, u32[]{:S(2)}, u32[]{:S(2)}) %collective-permute-start.4) | collective-permute-done | bytes 202784 | tf_op jit(solution)/shard_map/ppermute | solution.py:18
  70.1 0.8 pad_maximum_fusion.1
  70.9 1.0 broadcast_select_fusion.3
  71.9 0.9 collective-permute-done.5
  73.0 0.3 fusion.75
  73.2 0.2 fusion.57
  73.5 7.1 %collective-permute-start.15 = (f32[257,256]{1,0:T(8,128)S(1)}, f32[257,256]{1,0:T(8,128)S(1)}, u32[]{:S(2)}, u32[]{:S(2)}) collective-permute-start(f32[257,256]{1,0:T(8,128)S(1)} %pad_maximum_fusion.6), channel_id=1, source_target_pairs={{16,0},{20,4},{24,8},{28,12},{17,1},{21,5},{25,9},{29,13},{18,2},{... | collective-permute-start | bytes 789512 | tf_op jit(solution)/shard_map/ppermute | solution.py:13
  80.6 0.2 fusion.60
  80.8 1.3 %collective-permute-start.14 = (f32[257,256]{1,0:T(8,128)S(1)}, f32[257,256]{1,0:T(8,128)S(1)}, u32[]{:S(2)}, u32[]{:S(2)}) collective-permute-start(f32[257,256]{1,0:T(8,128)S(1)} %pad_maximum_fusion.5), channel_id=1, source_target_pairs={{0,12},{4,16},{8,20},{12,24},{16,28},{1,13},{5,17},{9,21},{13,25},... | collective-permute-start | bytes 789512 | tf_op jit(solution)/shard_map/ppermute | solution.py:13
  82.1 0.3 fusion.73
  82.4 0.2 fusion.63
  82.7 10.7 %collective-permute-start.7 = (f32[257,256]{1,0:T(8,128)S(1)}, f32[257,256]{1,0:T(8,128)S(1)}, u32[]{:S(2)}, u32[]{:S(2)}) collective-permute-start(f32[257,256]{1,0:T(8,128)S(1)} %pad_maximum_fusion.4), channel_id=1, source_target_pairs={{8,0},{12,4},{16,8},{20,12},{24,16},{28,20},{9,1},{13,5},{17,9},{2... | collective-permute-start | bytes 789512 | tf_op jit(solution)/shard_map/ppermute | solution.py:13
  93.4 0.2 fusion.66
  93.7 1.9 %collective-permute-start.6 = (f32[257,256]{1,0:T(8,128)S(1)}, f32[257,256]{1,0:T(8,128)S(1)}, u32[]{:S(2)}, u32[]{:S(2)}) collective-permute-start(f32[257,256]{1,0:T(8,128)S(1)} %pad_maximum_fusion.3), channel_id=1, source_target_pairs={{0,4},{4,8},{8,12},{12,16},{16,20},{20,24},{24,28},{1,5},{5,9},{9,... | collective-permute-start | bytes 789512 | tf_op jit(solution)/shard_map/ppermute | solution.py:13
  95.6 0.2 fusion.45
  95.8 0.2 fusion.48
  96.0 0.2 fusion.43
  96.2 1.1 %fusion.51 = f32[256,256]{1,0:T(8,128)S(1)} fusion(bf16[256,1280]{1,0:T(8,128)(2,1)} %collective-permute-done.1, bf16[256,256]{1,0:T(8,128)(2,1)S(1)} %get-tuple-element.20), kind=kOutput, calls=%fused_computation.112 | convolution fusion | flops 33554432 | bytes 524288 | tf_op jit(solution)/shard_map/dot_general | solution.py:99
  97.3 3.9 %collective-permute-done.14 = f32[257,256]{1,0:T(8,128)S(1)} collective-permute-done((f32[257,256]{1,0:T(8,128)S(1)}, f32[257,256]{1,0:T(8,128)S(1)}, u32[]{:S(2)}, u32[]{:S(2)}) %collective-permute-start.14) | collective-permute-done | bytes 263200 | tf_op jit(solution)/shard_map/ppermute | solution.py:13
  101.3 5.4 %collective-permute-done.6 = f32[257,256]{1,0:T(8,128)S(1)} collective-permute-done((f32[257,256]{1,0:T(8,128)S(1)}, f32[257,256]{1,0:T(8,128)S(1)}, u32[]{:S(2)}, u32[]{:S(2)}) %collective-permute-start.6) | collective-permute-done | bytes 263200 | tf_op jit(solution)/shard_map/ppermute | solution.py:13
  106.6 1.0 fusion.25
  (43 shorter events, 0.6 us)
Async XLA Ops:
  0.0 14.2 %copy-start.1 = (bf16[256,1024]{1,0:T(8,128)(2,1)S(1)}, bf16[256,1024]{1,0:T(8,128)(2,1)}, u32[]{:S(2)}) copy-start(bf16[256,1024]{1,0:T(8,128)(2,1)} %param.2) | copy-start | bytes 1572868
  0.0 2.0 %copy-start = (bf16[256,256]{1,0:T(8,128)(2,1)S(1)}, bf16[256,256]{1,0:T(8,128)(2,1)}, u32[]{:S(2)}) copy-start(bf16[256,256]{1,0:T(8,128)(2,1)} %param.3) | copy-start | bytes 393220
  2.7 33.5 %collective-permute-start.9 = (bf16[256,1280]{1,0:T(8,128)(2,1)}, bf16[256,1280]{1,0:T(8,128)(2,1)S(1)}, u32[]{:S(2)}, u32[]{:S(2)}) collective-permute-start(bf16[256,1280]{1,0:T(8,128)(2,1)} %constant_dynamic-update-slice_fusion), channel_id=1, source_target_pairs={{0,16},{4,20},{8,24},{12,28},{1,17},{5,21},{9,25},{13,29},{2,18},{... | collective-permute-start | bytes 1966088 | tf_op jit(solution)/shard_map/ppermute | solution.py:13
  3.9 32.9 %collective-permute-start.8 = (bf16[256,1280]{1,0:T(8,128)(2,1)}, bf16[256,1280]{1,0:T(8,128)(2,1)S(1)}, u32[]{:S(2)}, u32[]{:S(2)}) collective-permute-start(bf16[256,1280]{1,0:T(8,128)(2,1)} %constant_dynamic-update-slice_fusion), channel_id=1, source_target_pairs={{12,0},{16,4},{20,8},{24,12},{28,16},{13,1},{17,5},{21,9},{25,13},... | collective-permute-start | bytes 1966088 | tf_op jit(solution)/shard_map/ppermute | solution.py:13
  10.4 28.4 %collective-permute-start = (bf16[256,1280]{1,0:T(8,128)(2,1)}, bf16[256,1280]{1,0:T(8,128)(2,1)S(1)}, u32[]{:S(2)}, u32[]{:S(2)}) collective-permute-start(bf16[256,1280]{1,0:T(8,128)(2,1)} %constant_dynamic-update-slice_fusion), channel_id=1, source_target_pairs={{4,0},{8,4},{12,8},{16,12},{20,16},{24,20},{28,24},{5,1},{9,5},{13... | collective-permute-start | bytes 1966088 | tf_op jit(solution)/shard_map/ppermute | solution.py:13
  12.9 31.8 %collective-permute-start.1 = (bf16[256,1280]{1,0:T(8,128)(2,1)}, bf16[256,1280]{1,0:T(8,128)(2,1)}, u32[]{:S(2)}, u32[]{:S(2)}) collective-permute-start(bf16[256,1280]{1,0:T(8,128)(2,1)} %constant_dynamic-update-slice_fusion), channel_id=1, source_target_pairs={{0,8},{4,12},{8,16},{12,20},{16,24},{20,28},{1,9},{5,13},{9,17},{1... | collective-permute-start | bytes 1966088 | tf_op jit(solution)/shard_map/ppermute | solution.py:13
  38.8 12.2 %collective-permute-start.10 = (f32[2,272,128]{2,1,0:T(8,128)}, f32[2,272,128]{2,1,0:T(8,128)}, u32[]{:S(2)}, u32[]{:S(2)}) collective-permute-start(f32[2,272,128]{2,1,0:T(8,128)} %fusion.20), channel_id=1, source_target_pairs={{0,1},{1,0},{2,3},{3,2},{4,5},{5,4},{6,7},{7,6},{8,9},{9,8},{10,11... | collective-permute-start | bytes 835592 | tf_op jit(solution)/shard_map/ppermute | solution.py:18
  51.0 2.6 %collective-permute-start.2 = (f32[3,264,128]{2,1,0:T(8,128)}, f32[3,264,128]{2,1,0:T(8,128)}, u32[]{:S(2)}, u32[]{:S(2)}) collective-permute-start(f32[3,264,128]{2,1,0:T(8,128)} %constant_dynamic-slice_fusion.2), channel_id=1, source_target_pairs={{0,1},{1,0},{2,3},{3,2},{4,5},{5,4},{6,7},{7,6},{8,9},{9,8},{10,11... | collective-permute-start | bytes 1216520 | tf_op jit(solution)/shard_map/ppermute | solution.py:18
  52.0 6.6 %collective-permute-start.11 = (f32[2,136,128]{2,1,0:T(8,128)S(1)}, f32[2,136,128]{2,1,0:T(8,128)S(1)}, u32[]{:S(2)}, u32[]{:S(2)}) collective-permute-start(f32[2,136,128]{2,1,0:T(8,128)S(1)} %constant_dynamic-slice_fusion), channel_id=1, source_target_pairs={{0,2},{1,3},{2,0},{3,1},{4,6},{5,7},{6,4},{7,5},{8,10},{9,11},{10,... | collective-permute-start | bytes 417800 | tf_op jit(solution)/shard_map/ppermute | solution.py:18
  54.7 8.4 %collective-permute-start.3 = (f32[3,132,128]{2,1,0:T(8,128)S(1)}, f32[3,132,128]{2,1,0:T(8,128)S(1)}, u32[]{:S(2)}, u32[]{:S(2)}) collective-permute-start(f32[3,132,128]{2,1,0:T(8,128)S(1)} %constant_dynamic-slice_fusion.1), channel_id=1, source_target_pairs={{0,2},{1,3},{2,0},{3,1},{4,6},{5,7},{6,4},{7,5},{8,10},{9,11},{10,... | collective-permute-start | bytes 608264 | tf_op jit(solution)/shard_map/ppermute | solution.py:18
  58.6 7.4 %collective-permute-start.12 = (f32[2,136,128]{2,1,0:T(8,128)S(1)}, f32[2,136,128]{2,1,0:T(8,128)S(1)}, u32[]{:S(2)}, u32[]{:S(2)}) collective-permute-start(f32[2,136,128]{2,1,0:T(8,128)S(1)} %dynamic-slice_add_fusion.2), channel_id=1, source_target_pairs={{0,2},{1,3},{2,0},{3,1},{4,6},{5,7},{6,4},{7,5},{8,10},{9,11},{10,... | collective-permute-start | bytes 417800 | tf_op jit(solution)/shard_map/ppermute | solution.py:18
  63.1 7.0 %collective-permute-start.4 = (f32[3,132,128]{2,1,0:T(8,128)S(1)}, f32[3,132,128]{2,1,0:T(8,128)S(1)}, u32[]{:S(2)}, u32[]{:S(2)}) collective-permute-start(f32[3,132,128]{2,1,0:T(8,128)S(1)} %dynamic-slice_add_fusion.1), channel_id=1, source_target_pairs={{0,2},{1,3},{2,0},{3,1},{4,6},{5,7},{6,4},{7,5},{8,10},{9,11},{10,... | collective-permute-start | bytes 608264 | tf_op jit(solution)/shard_map/ppermute | solution.py:18
  66.9 4.1 %collective-permute-start.13 = (f32[2,272,128]{2,1,0:T(8,128)}, f32[2,272,128]{2,1,0:T(8,128)}, u32[]{:S(2)}, u32[]{:S(2)}) collective-permute-start(f32[2,272,128]{2,1,0:T(8,128)} %pad_maximum_fusion.2), channel_id=1, source_target_pairs={{0,1},{1,0},{2,3},{3,2},{4,5},{5,4},{6,7},{7,6},{8,9},{9,8},{10,11... | collective-permute-start | bytes 835592 | tf_op jit(solution)/shard_map/ppermute | solution.py:18
  70.9 2.0 %collective-permute-start.5 = (f32[3,264,128]{2,1,0:T(8,128)}, f32[3,264,128]{2,1,0:T(8,128)S(1)}, u32[]{:S(2)}, u32[]{:S(2)}) collective-permute-start(f32[3,264,128]{2,1,0:T(8,128)} %pad_maximum_fusion.1), channel_id=1, source_target_pairs={{0,1},{1,0},{2,3},{3,2},{4,5},{5,4},{6,7},{7,6},{8,9},{9,8},{10,11... | collective-permute-start | bytes 1216520 | tf_op jit(solution)/shard_map/ppermute | solution.py:18
  73.5 23.8 %collective-permute-start.15 = (f32[257,256]{1,0:T(8,128)S(1)}, f32[257,256]{1,0:T(8,128)S(1)}, u32[]{:S(2)}, u32[]{:S(2)}) collective-permute-start(f32[257,256]{1,0:T(8,128)S(1)} %pad_maximum_fusion.6), channel_id=1, source_target_pairs={{16,0},{20,4},{24,8},{28,12},{17,1},{21,5},{25,9},{29,13},{18,2},{... | collective-permute-start | bytes 789512 | tf_op jit(solution)/shard_map/ppermute | solution.py:13
  80.8 20.4 %collective-permute-start.14 = (f32[257,256]{1,0:T(8,128)S(1)}, f32[257,256]{1,0:T(8,128)S(1)}, u32[]{:S(2)}, u32[]{:S(2)}) collective-permute-start(f32[257,256]{1,0:T(8,128)S(1)} %pad_maximum_fusion.5), channel_id=1, source_target_pairs={{0,12},{4,16},{8,20},{12,24},{16,28},{1,13},{5,17},{9,21},{13,25},... | collective-permute-start | bytes 789512 | tf_op jit(solution)/shard_map/ppermute | solution.py:13
  82.7 18.6 %collective-permute-start.7 = (f32[257,256]{1,0:T(8,128)S(1)}, f32[257,256]{1,0:T(8,128)S(1)}, u32[]{:S(2)}, u32[]{:S(2)}) collective-permute-start(f32[257,256]{1,0:T(8,128)S(1)} %pad_maximum_fusion.4), channel_id=1, source_target_pairs={{8,0},{12,4},{16,8},{20,12},{24,16},{28,20},{9,1},{13,5},{17,9},{2... | collective-permute-start | bytes 789512 | tf_op jit(solution)/shard_map/ppermute | solution.py:13
  93.7 13.0 %collective-permute-start.6 = (f32[257,256]{1,0:T(8,128)S(1)}, f32[257,256]{1,0:T(8,128)S(1)}, u32[]{:S(2)}, u32[]{:S(2)}) collective-permute-start(f32[257,256]{1,0:T(8,128)S(1)} %pad_maximum_fusion.3), channel_id=1, source_target_pairs={{0,4},{4,8},{8,12},{12,16},{16,20},{20,24},{24,28},{1,5},{5,9},{9,... | collective-permute-start | bytes 789512 | tf_op jit(solution)/shard_map/ppermute | solution.py:13

commit v8 on v4

--- a/solution.py
+++ b/solution.py
@@ -43,6 +43,19 @@
     return joined(part, swapped(part, "width", 1), 2, core)
 
 
+def split3(x):
+    hi = lax.reduce_precision(x, exponent_bits=8, mantissa_bits=7)
+    r1 = x - hi
+    mid = lax.reduce_precision(r1, exponent_bits=8, mantissa_bits=7)
+    lo = r1 - mid
+    return jnp.stack([hi, mid, lo]).astype(jnp.bfloat16)
+
+
+def join3(rows):
+    rows = rows.astype(jnp.float32)
+    return (rows[0] + rows[1]) + rows[2]
+
+
 def body(teacher, student):
     group = lax.axis_size("batch")
     owner = lax.axis_index("batch")
@@ -55,27 +68,31 @@
     reach = min(REACH, group - 1)
     near_count = (2 * REACH + 1) * rows_dev
 
-    offsets = [0] + [d if d % 2 else -d for d in range(1, reach + 1)]
-    both = jnp.concatenate([teacher, student], axis=1)
-    teacher_band = [teacher]
-    student_band = [student]
-    for e in offsets[1:]:
-        got = shifted(both, "batch", e)
-        teacher_band.append(got[:, :ft])
-        student_band.append(got[:, ft:])
-
     def sq(x):
         xf = x.astype(jnp.float32)
         return jnp.sum(xf * xf, axis=1)
 
+    own_q = sq(student) / ds - sq(teacher) / dt
+    offsets = [0] + [d if d % 2 else -d for d in range(1, reach + 1)]
+    both = jnp.concatenate([teacher, student], axis=1)
+    q_rows = jnp.concatenate([split3(own_q), jnp.zeros((5, rows_dev), jnp.bfloat16)])
+    q_rows = jnp.concatenate([q_rows, jnp.zeros((8, ft + fs - rows_dev), jnp.bfloat16)], axis=1)
+    fwd = jnp.concatenate([both, q_rows], axis=0)
+    scaled = jnp.concatenate([teacher * jnp.bfloat16(-2.0 / dt), student * jnp.bfloat16(2.0 / ds)], axis=1)
+    rhs_band = [both]
+    q_band = [own_q]
+    student_band = [student]
+    for e in offsets[1:]:
+        got = shifted(fwd, "batch", e)
+        rhs_band.append(got[:rows_dev])
+        q_band.append(join3(got[rows_dev:rows_dev + 3, :rows_dev]))
+        student_band.append(got[:rows_dev, ft:])
+
     pad = (-(rows_dev + 1)) % 8
 
-    def tile_part(t_d, s_d):
-        tg = lax.dot_general(teacher, t_d, (((1,), (1,)), ((), ())), preferred_element_type=jnp.float32)
-        sg = lax.dot_general(student, s_d, (((1,), (1,)), ((), ())), preferred_element_type=jnp.float32)
-        q_d = sq(s_d) / ds - sq(t_d) / dt
-        return jnp.concatenate(
-            [sg * (2.0 / ds) - tg * (2.0 / dt), q_d[None, :], jnp.zeros((pad, rows_dev), jnp.float32)], axis=0)
+    def tile_part(d):
+        g = lax.dot_general(scaled, rhs_band[d], (((1,), (1,)), ((), ())), preferred_element_type=jnp.float32)
+        return jnp.concatenate([g, q_band[d][None, :], jnp.zeros((pad, rows_dev), jnp.float32)], axis=0)
 
     student_f = student.astype(jnp.float32)
     row_total = jnp.zeros((rows_dev,), jnp.float32)
@@ -85,7 +102,7 @@
     for group_idx in ([list(range(split)), list(range(split, len(offsets)))]):
         if not group_idx:
             continue
-        total = width_sum(jnp.stack([tile_part(teacher_band[d], student_band[d]) for d in group_idx]))
+        total = width_sum(jnp.stack([tile_part(d) for d in group_idx]))
         if own_q is None:
             own_q = total[0, rows_dev, :]
         for k, d in enumerate(group_idx):

time: 104 us -> 104 us (level)
  waiting for transfers between devices: 56.4 us -> 61.2 us
  local copies, waits for them, and re-layouts: 5.32 us -> 0.94 us
  other arithmetic: 7.12 us -> 4.29 us
  matrix products: 7.8 us -> 9.42 us
    ppermute x8, waiting for transfers between devices: 12.1 us -> 14.7 us  [swapped(): return lax.ppermute(block, axis, [(i, i ^ mask) for i in range(size)])]
    ppermute x8, waiting for transfers between devices: 44.2 us -> 46.6 us  [shifted(): return lax.ppermute(block, axis, route)]
    add x2, other arithmetic: 2.03 us -> 0.1 us  [width_sum(): part = keep + swapped(send, 'width', 1)]
    unnamed x9 -> x6, local copies, waits for them, and re-layouts: 2.65 us -> 0.77 us
    dot_general x5, matrix products: 2.7 us -> 4.5 us  [body(): jnp.dot(low, student_band[d], preferred_element_type=jnp.float32)]
    convert_element_type x0 -> x4, other arithmetic: none -> 1.35 us  [join3(): rows = rows.astype(jnp.float32)]
    mul x1 -> x0, local copies, waits for them, and re-layouts: 1.08 us -> none  [tile_part(): tg * (2.0 / dt)]
    dot_general x10 -> x5, matrix products: 4.2 us -> 4.02 us  [tile_part(): lax.dot_general(scaled, rhs_band[d], (((1,), (1,)), ((), ())), preferred_...]
  transfers between devices with their start and end apart: 16 -> 16, of which waited for: 12 -> 12; matrix products, arithmetic and copies ran while one was open for 12% -> 6% of each run, Pallas kernels for 0% -> 0%
where the time goes in v8:
time: 104 us; the launch traced here: 103 us
  waiting for transfers between devices  61.2 us (59%)
  starting transfers between devices  26.4 us (25%)
  matrix products  9.42 us (9%)
  other arithmetic  4.29 us (4%)
    ppermute x8, waiting for transfers between devices, shifted(): return lax.ppermute(block, axis, route)  46.6 us
    ppermute x8, starting transfers between devices, shifted(): return lax.ppermute(block, axis, route)  20.4 us
    ppermute x8, waiting for transfers between devices, swapped(): return lax.ppermute(block, axis, [(i, i ^ mask) for i in range(size)])  14.7 us
    ppermute x8, starting transfers between devices, swapped(): return lax.ppermute(block, axis, [(i, i ^ mask) for i in range(size)])  6.01 us
    dot_general x5, matrix products, body(): jnp.dot(low, student_band[d], preferred_element_type=jnp.float32)  4.5 us
    dot_general x5, matrix products, tile_part(): lax.dot_general(scaled, rhs_band[d], (((1,), (1,)), ((), ())), preferred_...  4.02 us
  transfers between devices with their start and end apart: 16, of which 12 were waited for; matrix products, arithmetic and copies ran while one was open for 6% of the time, Pallas kernels for 0%

profile of v8, /device:TPU:24, one launch (start us, length us, event | category | flops | bytes accessed | tf_op | source)
XLA Modules:
  0.0 102.8 jit_solution(657621911858047209)
XLA Ops:
  0.0 0.0 copy-start.1
  0.0 1.3 %multiply_reduce_fusion = f32[256]{0:T(256)S(1)} fusion(bf16[256,1024]{1,0:T(8,128)(2,1)} %param.2), kind=kLoop, calls=%fused_computation.18 | loop fusion | flops 786176 | bytes 525312 | tf_op jit(solution)/shard_map/reduce_sum | solution.py:73
  1.3 0.0 copy-done.1
  1.3 0.0 copy-start
  1.3 0.1 broadcast_multiply_fusion
  1.5 0.8 copy-done
  2.2 0.1 fusion.20
  2.5 3.3 %collective-permute-start = (bf16[264,1280]{1,0:T(8,128)(2,1)S(1)}, bf16[264,1280]{1,0:T(8,128)(2,1)S(1)}, u32[]{:S(2)}, u32[]{:S(2)}) collective-permute-start(bf16[264,1280]{1,0:T(8,128)(2,1)S(1)} %fusion.8), channel_id=1, source_target_pairs={{4,0},{8,4},{12,8},{16,12},{20,16},{24,20},{28,24},{5,1},{9,5},{13... | collective-permute-start | bytes 2027528 | tf_op jit(solution)/shard_map/ppermute | solution.py:12
  5.8 1.3 %collective-permute-start.1 = (bf16[264,1280]{1,0:T(8,128)(2,1)S(1)}, bf16[264,1280]{1,0:T(8,128)(2,1)S(1)}, u32[]{:S(2)}, u32[]{:S(2)}) collective-permute-start(bf16[264,1280]{1,0:T(8,128)(2,1)S(1)} %fusion.8), channel_id=1, source_target_pairs={{0,8},{4,12},{8,16},{12,20},{16,24},{20,28},{1,9},{5,13},{9,17},{1... | collective-permute-start | bytes 2027528 | tf_op jit(solution)/shard_map/ppermute | solution.py:12
  7.1 5.4 %collective-permute-start.8 = (bf16[264,1280]{1,0:T(8,128)(2,1)S(1)}, bf16[264,1280]{1,0:T(8,128)(2,1)}, u32[]{:S(2)}, u32[]{:S(2)}) collective-permute-start(bf16[264,1280]{1,0:T(8,128)(2,1)S(1)} %fusion.8), channel_id=1, source_target_pairs={{12,0},{16,4},{20,8},{24,12},{28,16},{13,1},{17,5},{21,9},{25,13},... | collective-permute-start | bytes 2027528 | tf_op jit(solution)/shard_map/ppermute | solution.py:12
  12.4 1.3 %collective-permute-start.9 = (bf16[264,1280]{1,0:T(8,128)(2,1)S(1)}, bf16[264,1280]{1,0:T(8,128)(2,1)}, u32[]{:S(2)}, u32[]{:S(2)}) collective-permute-start(bf16[264,1280]{1,0:T(8,128)(2,1)S(1)} %fusion.8), channel_id=1, source_target_pairs={{0,16},{4,20},{8,24},{12,28},{1,17},{5,21},{9,25},{13,29},{2,18},{... | collective-permute-start | bytes 2027528 | tf_op jit(solution)/shard_map/ppermute | solution.py:12
  13.8 0.1 pad.42.clone
  13.8 0.4 fusion.72
  14.2 7.1 %collective-permute-done = bf16[264,1280]{1,0:T(8,128)(2,1)S(1)} collective-permute-done((bf16[264,1280]{1,0:T(8,128)(2,1)S(1)}, bf16[264,1280]{1,0:T(8,128)(2,1)S(1)}, u32[]{:S(2)}, u32[]{:S(2)}) %collective-permute-start) | collective-permute-done | bytes 675872 | tf_op jit(solution)/shard_map/ppermute | solution.py:12
  21.3 3.5 %collective-permute-done.1 = bf16[264,1280]{1,0:T(8,128)(2,1)S(1)} collective-permute-done((bf16[264,1280]{1,0:T(8,128)(2,1)S(1)}, bf16[264,1280]{1,0:T(8,128)(2,1)S(1)}, u32[]{:S(2)}, u32[]{:S(2)}) %collective-permute-start.1) | collective-permute-done | bytes 675872 | tf_op jit(solution)/shard_map/ppermute | solution.py:12
  24.8 0.0 copy-start.2
  24.8 9.9 %collective-permute-done.8 = bf16[264,1280]{1,0:T(8,128)(2,1)} collective-permute-done((bf16[264,1280]{1,0:T(8,128)(2,1)S(1)}, bf16[264,1280]{1,0:T(8,128)(2,1)}, u32[]{:S(2)}, u32[]{:S(2)}) %collective-permute-start.8) | collective-permute-done | bytes 675872 | tf_op jit(solution)/shard_map/ppermute | solution.py:12
  34.7 0.7 slice_convert_fusion.1
  35.4 17.9 %collective-permute-done.9 = bf16[264,1280]{1,0:T(8,128)(2,1)} collective-permute-done((bf16[264,1280]{1,0:T(8,128)(2,1)S(1)}, bf16[264,1280]{1,0:T(8,128)(2,1)}, u32[]{:S(2)}, u32[]{:S(2)}) %collective-permute-start.9) | collective-permute-done | bytes 675872 | tf_op jit(solution)/shard_map/ppermute | solution.py:12
  53.3 0.7 slice_convert_fusion
  54.0 0.4 fusion.15
  54.3 0.0 copy-done.2
  54.3 0.4 fusion.13
  54.7 1.5 %fusion.11 = f32[256,256]{1,0:T(8,128)S(1)} fusion(bf16[264,1280]{1,0:T(8,128)(2,1)} %collective-permute-done.8, bf16[256,256]{1,0:T(8,128)(2,1)S(1)} %get-tuple-element.39, bf16[256,1024]{1,0:T(8,128)(2,1)S(1)} %get-tuple-element.33), kind=kOutput, calls=%fused_computation.23 | convolution fusion | flops 169082880 | bytes 1572864 | tf_op jit(solution)/shard_map/dot_general | solution.py:94
  56.2 1.5 %fusion.9 = f32[256,256]{1,0:T(8,128)S(1)} fusion(bf16[264,1280]{1,0:T(8,128)(2,1)} %collective-permute-done.9, bf16[256,256]{1,0:T(8,128)(2,1)S(1)} %get-tuple-element.39, bf16[256,1024]{1,0:T(8,128)(2,1)S(1)} %get-tuple-element.33), kind=kOutput, calls=%fused_computation.21 | convolution fusion | flops 169082880 | bytes 1572864 | tf_op jit(solution)/shard_map/dot_general | solution.py:94
  57.6 0.2 maximum_bitcast_fusion
  57.8 0.1 collective-permute-start.10
  57.9 0.1 pad_maximum_fusion
  58.0 0.6 collective-permute-start.2
  58.6 0.9 collective-permute-done.10
  59.5 1.5 %collective-permute-start.11 = (f32[2,132,128]{2,1,0:T(8,128)S(1)}, f32[2,132,128]{2,1,0:T(8,128)S(1)}, u32[]{:S(2)}, u32[]{:S(2)}) collective-permute-start(f32[2,132,128]{2,1,0:T(8,128)S(1)} %constant_dynamic-slice_fusion), channel_id=1, source_target_pairs={{0,2},{1,3},{2,0},{3,1},{4,6},{5,7},{6,4},{7,5},{8,10},{9,11},{10,... | collective-permute-start | bytes 405512 | tf_op jit(solution)/shard_map/ppermute | solution.py:17
  61.1 0.0 collective-permute-done.2
  61.1 0.1 dynamic-slice_add_fusion
  61.2 0.6 collective-permute-start.3
  61.8 4.4 %collective-permute-done.11 = f32[2,132,128]{2,1,0:T(8,128)S(1)} collective-permute-done((f32[2,132,128]{2,1,0:T(8,128)S(1)}, f32[2,132,128]{2,1,0:T(8,128)S(1)}, u32[]{:S(2)}, u32[]{:S(2)}) %collective-permute-start.11) | collective-permute-done | bytes 135200 | tf_op jit(solution)/shard_map/ppermute | solution.py:17
  66.2 1.5 %collective-permute-start.12 = (f32[2,132,128]{2,1,0:T(8,128)S(1)}, f32[2,132,128]{2,1,0:T(8,128)S(1)}, u32[]{:S(2)}, u32[]{:S(2)}) collective-permute-start(f32[2,132,128]{2,1,0:T(8,128)S(1)} %dynamic-slice_add_fusion.2), channel_id=1, source_target_pairs={{0,2},{1,3},{2,0},{3,1},{4,6},{5,7},{6,4},{7,5},{8,10},{9,11},{10,... | collective-permute-start | bytes 405512 | tf_op jit(solution)/shard_map/ppermute | solution.py:17
  67.7 2.9 %collective-permute-done.3 = f32[3,132,128]{2,1,0:T(8,128)S(1)} collective-permute-done((f32[3,132,128]{2,1,0:T(8,128)S(1)}, f32[3,132,128]{2,1,0:T(8,128)S(1)}, u32[]{:S(2)}, u32[]{:S(2)}) %collective-permute-start.3) | collective-permute-done | bytes 202784 | tf_op jit(solution)/shard_map/ppermute | solution.py:17
  70.7 1.5 %collective-permute-start.4 = (f32[3,132,128]{2,1,0:T(8,128)S(1)}, f32[3,132,128]{2,1,0:T(8,128)S(1)}, u32[]{:S(2)}, u32[]{:S(2)}) collective-permute-start(f32[3,132,128]{2,1,0:T(8,128)S(1)} %dynamic-slice_add_fusion.1), channel_id=1, source_target_pairs={{0,2},{1,3},{2,0},{3,1},{4,6},{5,7},{6,4},{7,5},{8,10},{9,11},{10,... | collective-permute-start | bytes 608264 | tf_op jit(solution)/shard_map/ppermute | solution.py:17
  72.2 1.4 %collective-permute-done.12 = f32[2,132,128]{2,1,0:T(8,128)S(1)} collective-permute-done((f32[2,132,128]{2,1,0:T(8,128)S(1)}, f32[2,132,128]{2,1,0:T(8,128)S(1)}, u32[]{:S(2)}, u32[]{:S(2)}) %collective-permute-start.12) | collective-permute-done | bytes 135200 | tf_op jit(solution)/shard_map/ppermute | solution.py:17
  73.7 0.1 collective-permute-start.13
  73.7 3.5 %collective-permute-done.4 = f32[3,132,128]{2,1,0:T(8,128)S(1)} collective-permute-done((f32[3,132,128]{2,1,0:T(8,128)S(1)}, f32[3,132,128]{2,1,0:T(8,128)S(1)}, u32[]{:S(2)}, u32[]{:S(2)}) %collective-permute-start.4) | collective-permute-done | bytes 202784 | tf_op jit(solution)/shard_map/ppermute | solution.py:17
  77.3 0.1 collective-permute-start.5
  77.4 0.0 collective-permute-done.13
  77.5 1.6 %collective-permute-done.5 = f32[3,264,128]{2,1,0:T(8,128)S(1)} collective-permute-done((f32[3,264,128]{2,1,0:T(8,128)S(1)}, f32[3,264,128]{2,1,0:T(8,128)S(1)}, u32[]{:S(2)}, u32[]{:S(2)}) %collective-permute-start.5) | collective-permute-done | bytes 405536 | tf_op jit(solution)/shard_map/ppermute | solution.py:17
  79.1 0.1 broadcast_select_fusion.1
  79.2 0.3 fusion.75
  79.5 0.2 fusion.50
  79.7 1.4 %collective-permute-start.15 = (f32[257,256]{1,0:T(8,128)S(1)}, f32[257,256]{1,0:T(8,128)S(1)}, u32[]{:S(2)}, u32[]{:S(2)}) collective-permute-start(f32[257,256]{1,0:T(8,128)S(1)} %pad_maximum_fusion.7), channel_id=1, source_target_pairs={{16,0},{20,4},{24,8},{28,12},{17,1},{21,5},{25,9},{29,13},{18,2},{... | collective-permute-start | bytes 789512 | tf_op jit(solution)/shard_map/ppermute | solution.py:12
  81.1 0.2 fusion.53
  81.4 1.3 %collective-permute-start.14 = (f32[257,256]{1,0:T(8,128)S(1)}, f32[257,256]{1,0:T(8,128)S(1)}, u32[]{:S(2)}, u32[]{:S(2)}) collective-permute-start(f32[257,256]{1,0:T(8,128)S(1)} %pad_maximum_fusion.6), channel_id=1, source_target_pairs={{0,12},{4,16},{8,20},{12,24},{16,28},{1,13},{5,17},{9,21},{13,25},... | collective-permute-start | bytes 789512 | tf_op jit(solution)/shard_map/ppermute | solution.py:12
  82.7 0.3 fusion.73
  82.9 0.2 fusion.56
  83.2 4.6 %collective-permute-start.7 = (f32[257,256]{1,0:T(8,128)S(1)}, f32[257,256]{1,0:T(8,128)S(1)}, u32[]{:S(2)}, u32[]{:S(2)}) collective-permute-start(f32[257,256]{1,0:T(8,128)S(1)} %pad_maximum_fusion.4), channel_id=1, source_target_pairs={{8,0},{12,4},{16,8},{20,12},{24,16},{28,20},{9,1},{13,5},{17,9},{2... | collective-permute-start | bytes 789512 | tf_op jit(solution)/shard_map/ppermute | solution.py:12
  87.8 0.2 fusion.59
  88.1 1.9 %collective-permute-start.6 = (f32[257,256]{1,0:T(8,128)S(1)}, f32[257,256]{1,0:T(8,128)S(1)}, u32[]{:S(2)}, u32[]{:S(2)}) collective-permute-start(f32[257,256]{1,0:T(8,128)S(1)} %pad_maximum_fusion.3), channel_id=1, source_target_pairs={{0,4},{4,8},{8,12},{12,16},{16,20},{20,24},{24,28},{1,5},{5,9},{9,... | collective-permute-start | bytes 789512 | tf_op jit(solution)/shard_map/ppermute | solution.py:12
  90.0 1.1 %fusion.40 = f32[256,256]{1,0:T(8,128)S(1)} fusion(bf16[264,1280]{1,0:T(8,128)(2,1)} %collective-permute-done.9, bf16[256,256]{1,0:T(8,128)(2,1)S(1)} %get-tuple-element.28), kind=kOutput, calls=%fused_computation.84 | convolution fusion | flops 33554432 | bytes 524288 | tf_op jit(solution)/shard_map/dot_general | solution.py:116
  91.1 1.1 %fusion.42 = f32[256,256]{1,0:T(8,128)S(1)} fusion(bf16[264,1280]{1,0:T(8,128)(2,1)} %collective-permute-done.8, bf16[256,256]{1,0:T(8,128)(2,1)S(1)} %get-tuple-element.15), kind=kOutput, calls=%fused_computation.86 | convolution fusion | flops 33554432 | bytes 524288 | tf_op jit(solution)/shard_map/dot_general | solution.py:116
  92.2 0.2 fusion.47
  92.4 1.1 %fusion.44 = f32[256,256]{1,0:T(8,128)S(1)} fusion(bf16[264,1280]{1,0:T(8,128)(2,1)} %copy-done.2, bf16[256,256]{1,0:T(8,128)(2,1)S(1)} %get-tuple-element.20), kind=kOutput, calls=%fused_computation.88 | convolution fusion | flops 33554432 | bytes 524288 | tf_op jit(solution)/shard_map/dot_general | solution.py:116
  93.5 0.0 collective-permute-done.15
  93.6 2.5 %collective-permute-done.14 = f32[257,256]{1,0:T(8,128)S(1)} collective-permute-done((f32[257,256]{1,0:T(8,128)S(1)}, f32[257,256]{1,0:T(8,128)S(1)}, u32[]{:S(2)}, u32[]{:S(2)}) %collective-permute-start.14) | collective-permute-done | bytes 263200 | tf_op jit(solution)/shard_map/ppermute | solution.py:12
  96.1 0.0 collective-permute-done.7
  96.1 5.7 %collective-permute-done.6 = f32[257,256]{1,0:T(8,128)S(1)} collective-permute-done((f32[257,256]{1,0:T(8,128)S(1)}, f32[257,256]{1,0:T(8,128)S(1)}, u32[]{:S(2)}, u32[]{:S(2)}) %collective-permute-start.6) | collective-permute-done | bytes 263200 | tf_op jit(solution)/shard_map/ppermute | solution.py:12
  101.8 1.0 fusion.22
  (35 shorter events, 0.6 us)
Async XLA Ops:
  0.0 1.3 %copy-start.1 = (bf16[256,1024]{1,0:T(8,128)(2,1)S(1)}, bf16[256,1024]{1,0:T(8,128)(2,1)}, u32[]{:S(2)}) copy-start(bf16[256,1024]{1,0:T(8,128)(2,1)} %param.2) | copy-start | bytes 1572868
  1.3 0.9 copy-start
  2.5 18.9 %collective-permute-start = (bf16[264,1280]{1,0:T(8,128)(2,1)S(1)}, bf16[264,1280]{1,0:T(8,128)(2,1)S(1)}, u32[]{:S(2)}, u32[]{:S(2)}) collective-permute-start(bf16[264,1280]{1,0:T(8,128)(2,1)S(1)} %fusion.8), channel_id=1, source_target_pairs={{4,0},{8,4},{12,8},{16,12},{20,16},{24,20},{28,24},{5,1},{9,5},{13... | collective-permute-start | bytes 2027528 | tf_op jit(solution)/shard_map/ppermute | solution.py:12
  5.8 19.0 %collective-permute-start.1 = (bf16[264,1280]{1,0:T(8,128)(2,1)S(1)}, bf16[264,1280]{1,0:T(8,128)(2,1)S(1)}, u32[]{:S(2)}, u32[]{:S(2)}) collective-permute-start(bf16[264,1280]{1,0:T(8,128)(2,1)S(1)} %fusion.8), channel_id=1, source_target_pairs={{0,8},{4,12},{8,16},{12,20},{16,24},{20,28},{1,9},{5,13},{9,17},{1... | collective-permute-start | bytes 2027528 | tf_op jit(solution)/shard_map/ppermute | solution.py:12
  7.1 27.6 %collective-permute-start.8 = (bf16[264,1280]{1,0:T(8,128)(2,1)S(1)}, bf16[264,1280]{1,0:T(8,128)(2,1)}, u32[]{:S(2)}, u32[]{:S(2)}) collective-permute-start(bf16[264,1280]{1,0:T(8,128)(2,1)S(1)} %fusion.8), channel_id=1, source_target_pairs={{12,0},{16,4},{20,8},{24,12},{28,16},{13,1},{17,5},{21,9},{25,13},... | collective-permute-start | bytes 2027528 | tf_op jit(solution)/shard_map/ppermute | solution.py:12
  12.4 40.8 %collective-permute-start.9 = (bf16[264,1280]{1,0:T(8,128)(2,1)S(1)}, bf16[264,1280]{1,0:T(8,128)(2,1)}, u32[]{:S(2)}, u32[]{:S(2)}) collective-permute-start(bf16[264,1280]{1,0:T(8,128)(2,1)S(1)} %fusion.8), channel_id=1, source_target_pairs={{0,16},{4,20},{8,24},{12,28},{1,17},{5,21},{9,25},{13,29},{2,18},{... | collective-permute-start | bytes 2027528 | tf_op jit(solution)/shard_map/ppermute | solution.py:12
  24.8 29.6 %copy-start.2 = (bf16[264,1280]{1,0:T(8,128)(2,1)}, bf16[264,1280]{1,0:T(8,128)(2,1)S(1)}, u32[]{:S(2)}) copy-start(bf16[264,1280]{1,0:T(8,128)(2,1)S(1)} %collective-permute-done.1) | copy-start | bytes 2027524
  57.8 1.6 %collective-permute-start.10 = (f32[2,264,128]{2,1,0:T(8,128)S(1)}, f32[2,264,128]{2,1,0:T(8,128)S(1)}, u32[]{:S(2)}, u32[]{:S(2)}) collective-permute-start(f32[2,264,128]{2,1,0:T(8,128)S(1)} %fusion.17), channel_id=1, source_target_pairs={{0,1},{1,0},{2,3},{3,2},{4,5},{5,4},{6,7},{7,6},{8,9},{9,8},{10,11... | collective-permute-start | bytes 811016 | tf_op jit(solution)/shard_map/ppermute | solution.py:17
  58.0 3.0 %collective-permute-start.2 = (f32[3,264,128]{2,1,0:T(8,128)S(1)}, f32[3,264,128]{2,1,0:T(8,128)S(1)}, u32[]{:S(2)}, u32[]{:S(2)}) collective-permute-start(f32[3,264,128]{2,1,0:T(8,128)S(1)} %constant_dynamic-slice_fusion.2), channel_id=1, source_target_pairs={{0,1},{1,0},{2,3},{3,2},{4,5},{5,4},{6,7},{7,6},{8,9},{9,8},{10,11... | collective-permute-start | bytes 1216520 | tf_op jit(solution)/shard_map/ppermute | solution.py:17
  59.5 6.6 %collective-permute-start.11 = (f32[2,132,128]{2,1,0:T(8,128)S(1)}, f32[2,132,128]{2,1,0:T(8,128)S(1)}, u32[]{:S(2)}, u32[]{:S(2)}) collective-permute-start(f32[2,132,128]{2,1,0:T(8,128)S(1)} %constant_dynamic-slice_fusion), channel_id=1, source_target_pairs={{0,2},{1,3},{2,0},{3,1},{4,6},{5,7},{6,4},{7,5},{8,10},{9,11},{10,... | collective-permute-start | bytes 405512 | tf_op jit(solution)/shard_map/ppermute | solution.py:17
  61.2 9.4 %collective-permute-start.3 = (f32[3,132,128]{2,1,0:T(8,128)S(1)}, f32[3,132,128]{2,1,0:T(8,128)S(1)}, u32[]{:S(2)}, u32[]{:S(2)}) collective-permute-start(f32[3,132,128]{2,1,0:T(8,128)S(1)} %constant_dynamic-slice_fusion.1), channel_id=1, source_target_pairs={{0,2},{1,3},{2,0},{3,1},{4,6},{5,7},{6,4},{7,5},{8,10},{9,11},{10,... | collective-permute-start | bytes 608264 | tf_op jit(solution)/shard_map/ppermute | solution.py:17
  66.2 7.4 %collective-permute-start.12 = (f32[2,132,128]{2,1,0:T(8,128)S(1)}, f32[2,132,128]{2,1,0:T(8,128)S(1)}, u32[]{:S(2)}, u32[]{:S(2)}) collective-permute-start(f32[2,132,128]{2,1,0:T(8,128)S(1)} %dynamic-slice_add_fusion.2), channel_id=1, source_target_pairs={{0,2},{1,3},{2,0},{3,1},{4,6},{5,7},{6,4},{7,5},{8,10},{9,11},{10,... | collective-permute-start | bytes 405512 | tf_op jit(solution)/shard_map/ppermute | solution.py:17
  70.7 6.6 %collective-permute-start.4 = (f32[3,132,128]{2,1,0:T(8,128)S(1)}, f32[3,132,128]{2,1,0:T(8,128)S(1)}, u32[]{:S(2)}, u32[]{:S(2)}) collective-permute-start(f32[3,132,128]{2,1,0:T(8,128)S(1)} %dynamic-slice_add_fusion.1), channel_id=1, source_target_pairs={{0,2},{1,3},{2,0},{3,1},{4,6},{5,7},{6,4},{7,5},{8,10},{9,11},{10,... | collective-permute-start | bytes 608264 | tf_op jit(solution)/shard_map/ppermute | solution.py:17
  73.7 3.8 %collective-permute-start.13 = (f32[2,264,128]{2,1,0:T(8,128)S(1)}, f32[2,264,128]{2,1,0:T(8,128)S(1)}, u32[]{:S(2)}, u32[]{:S(2)}) collective-permute-start(f32[2,264,128]{2,1,0:T(8,128)S(1)} %pad_maximum_fusion.5), channel_id=1, source_target_pairs={{0,1},{1,0},{2,3},{3,2},{4,5},{5,4},{6,7},{7,6},{8,9},{9,8},{10,11... | collective-permute-start | bytes 811016 | tf_op jit(solution)/shard_map/ppermute | solution.py:17
  77.3 1.8 %collective-permute-start.5 = (f32[3,264,128]{2,1,0:T(8,128)S(1)}, f32[3,264,128]{2,1,0:T(8,128)S(1)}, u32[]{:S(2)}, u32[]{:S(2)}) collective-permute-start(f32[3,264,128]{2,1,0:T(8,128)S(1)} %pad_maximum_fusion.2), channel_id=1, source_target_pairs={{0,1},{1,0},{2,3},{3,2},{4,5},{5,4},{6,7},{7,6},{8,9},{9,8},{10,11... | collective-permute-start | bytes 1216520 | tf_op jit(solution)/shard_map/ppermute | solution.py:17
  79.7 13.8 %collective-permute-start.15 = (f32[257,256]{1,0:T(8,128)S(1)}, f32[257,256]{1,0:T(8,128)S(1)}, u32[]{:S(2)}, u32[]{:S(2)}) collective-permute-start(f32[257,256]{1,0:T(8,128)S(1)} %pad_maximum_fusion.7), channel_id=1, source_target_pairs={{16,0},{20,4},{24,8},{28,12},{17,1},{21,5},{25,9},{29,13},{18,2},{... | collective-permute-start | bytes 789512 | tf_op jit(solution)/shard_map/ppermute | solution.py:12
  81.4 14.7 %collective-permute-start.14 = (f32[257,256]{1,0:T(8,128)S(1)}, f32[257,256]{1,0:T(8,128)S(1)}, u32[]{:S(2)}, u32[]{:S(2)}) collective-permute-start(f32[257,256]{1,0:T(8,128)S(1)} %pad_maximum_fusion.6), channel_id=1, source_target_pairs={{0,12},{4,16},{8,20},{12,24},{16,28},{1,13},{5,17},{9,21},{13,25},... | collective-permute-start | bytes 789512 | tf_op jit(solution)/shard_map/ppermute | solution.py:12
  83.2 12.9 %collective-permute-start.7 = (f32[257,256]{1,0:T(8,128)S(1)}, f32[257,256]{1,0:T(8,128)S(1)}, u32[]{:S(2)}, u32[]{:S(2)}) collective-permute-start(f32[257,256]{1,0:T(8,128)S(1)} %pad_maximum_fusion.4), channel_id=1, source_target_pairs={{8,0},{12,4},{16,8},{20,12},{24,16},{28,20},{9,1},{13,5},{17,9},{2... | collective-permute-start | bytes 789512 | tf_op jit(solution)/shard_map/ppermute | solution.py:12
  88.1 13.7 %collective-permute-start.6 = (f32[257,256]{1,0:T(8,128)S(1)}, f32[257,256]{1,0:T(8,128)S(1)}, u32[]{:S(2)}, u32[]{:S(2)}) collective-permute-start(f32[257,256]{1,0:T(8,128)S(1)} %pad_maximum_fusion.3), channel_id=1, source_target_pairs={{0,4},{4,8},{8,12},{12,16},{16,20},{20,24},{24,28},{1,5},{5,9},{9,... | collective-permute-start | bytes 789512 | tf_op jit(solution)/shard_map/ppermute | solution.py:12

commit v9 on v8

--- a/solution.py
+++ b/solution.py
@@ -98,8 +98,12 @@
     row_total = jnp.zeros((rows_dev,), jnp.float32)
     pulled = jnp.zeros(student.shape, jnp.float32)
     own_q = None
-    split = min(3, len(offsets))
-    for group_idx in ([list(range(split)), list(range(split, len(offsets)))]):
+    sizes = [2, 2, 1]
+    groups = []
+    for size in sizes:
+        used = sum(len(g) for g in groups)
+        groups.append(list(range(used, min(used + size, len(offsets)))))
+    for group_idx in groups:
         if not group_idx:
             continue
         total = width_sum(jnp.stack([tile_part(d) for d in group_idx]))

time: 104 us -> 110 us (1.058)
  starting transfers between devices: 26.4 us -> 45.1 us
  waiting for transfers between devices: 61.2 us -> 49.9 us
    ppermute x8, starting transfers between devices: 20.4 us -> 36.3 us  [shifted(): return lax.ppermute(block, axis, route)]
    ppermute x8, waiting for transfers between devices: 46.6 us -> 33.7 us  [shifted(): return lax.ppermute(block, axis, route)]
    ppermute x8 -> x12, starting transfers between devices: 6.01 us -> 8.81 us  [swapped(): return lax.ppermute(block, axis, [(i, i ^ mask) for i in range(size)])]
    ppermute x8 -> x12, waiting for transfers between devices: 14.7 us -> 16.2 us  [swapped(): return lax.ppermute(block, axis, [(i, i ^ mask) for i in range(size)])]
  transfers between devices with their start and end apart: 16 -> 20, of which waited for: 12 -> 10; matrix products, arithmetic and copies ran while one was open for 6% -> 6% of each run, Pallas kernels for 0% -> 0%
where the time goes in v9:
time: 110 us
  waiting for transfers between devices  49.9 us (45%)
  starting transfers between devices  45.1 us (41%)
  matrix products  8.65 us (8%)
  other arithmetic  4.29 us (4%)
    ppermute x8, starting transfers between devices, shifted(): return lax.ppermute(block, axis, route)  36.3 us
    ppermute x8, waiting for transfers between devices, shifted(): return lax.ppermute(block, axis, route)  33.7 us
    ppermute x12, waiting for transfers between devices, swapped(): return lax.ppermute(block, axis, [(i, i ^ mask) for i in range(size)])  16.2 us
    ppermute x12, starting transfers between devices, swapped(): return lax.ppermute(block, axis, [(i, i ^ mask) for i in range(size)])  8.81 us
    dot_general x5, matrix products, tile_part(): lax.dot_general(scaled, rhs_band[d], (((1,), (1,)), ((), ())), preferred_...  4.01 us
    dot_general x5, matrix products, body(): jnp.dot(low, student_band[d], preferred_element_type=jnp.float32)  3.65 us
  transfers between devices with their start and end apart: 20, of which 10 were waited for; matrix products, arithmetic and copies ran while one was open for 6% of the time, Pallas kernels for 0%

profile of v9, /device:TPU:24, one launch (start us, length us, event | category | flops | bytes accessed | tf_op | source)
XLA Modules:
  0.0 109.5 jit_solution(7010140884641440342)
XLA Ops:
  0.0 1.3 %multiply_reduce_fusion = f32[256]{0:T(256)S(1)} fusion(bf16[256,1024]{1,0:T(8,128)(2,1)} %param.2), kind=kLoop, calls=%fused_computation.10 | loop fusion | flops 786176 | bytes 525312 | tf_op jit(solution)/shard_map/reduce_sum | solution.py:73
  1.3 0.0 copy-start
  1.3 0.1 broadcast_multiply_fusion
  1.5 0.8 copy-done
  2.2 0.1 fusion.23
  2.5 1.3 %collective-permute-start.14 = (bf16[264,1280]{1,0:T(8,128)(2,1)S(1)}, bf16[264,1280]{1,0:T(8,128)(2,1)}, u32[]{:S(2)}, u32[]{:S(2)}) collective-permute-start(bf16[264,1280]{1,0:T(8,128)(2,1)S(1)} %fusion.8), channel_id=1, source_target_pairs={{0,16},{4,20},{8,24},{12,28},{1,17},{5,21},{9,25},{13,29},{2,18},{... | collective-permute-start | bytes 2027528 | tf_op jit(solution)/shard_map/ppermute | solution.py:12
  3.8 8.1 %collective-permute-start.7 = (bf16[264,1280]{1,0:T(8,128)(2,1)S(1)}, bf16[264,1280]{1,0:T(8,128)(2,1)}, u32[]{:S(2)}, u32[]{:S(2)}) collective-permute-start(bf16[264,1280]{1,0:T(8,128)(2,1)S(1)} %fusion.8), channel_id=1, source_target_pairs={{12,0},{16,4},{20,8},{24,12},{28,16},{13,1},{17,5},{21,9},{25,13},... | collective-permute-start | bytes 2027528 | tf_op jit(solution)/shard_map/ppermute | solution.py:12
  11.9 1.3 %collective-permute-start.6 = (bf16[264,1280]{1,0:T(8,128)(2,1)S(1)}, bf16[264,1280]{1,0:T(8,128)(2,1)S(1)}, u32[]{:S(2)}, u32[]{:S(2)}) collective-permute-start(bf16[264,1280]{1,0:T(8,128)(2,1)S(1)} %fusion.8), channel_id=1, source_target_pairs={{0,8},{4,12},{8,16},{12,20},{16,24},{20,28},{1,9},{5,13},{9,17},{1... | collective-permute-start | bytes 2027528 | tf_op jit(solution)/shard_map/ppermute | solution.py:12
  13.1 3.0 %collective-permute-start = (bf16[264,1280]{1,0:T(8,128)(2,1)S(1)}, bf16[264,1280]{1,0:T(8,128)(2,1)S(1)}, u32[]{:S(2)}, u32[]{:S(2)}) collective-permute-start(bf16[264,1280]{1,0:T(8,128)(2,1)S(1)} %fusion.8), channel_id=1, source_target_pairs={{4,0},{8,4},{12,8},{16,12},{20,16},{24,20},{28,24},{5,1},{9,5},{13... | collective-permute-start | bytes 2027528 | tf_op jit(solution)/shard_map/ppermute | solution.py:12
  16.2 0.1 pad.45.clone
  16.3 0.4 fusion.77
  16.7 20.1 %collective-permute-done.14 = bf16[264,1280]{1,0:T(8,128)(2,1)} collective-permute-done((bf16[264,1280]{1,0:T(8,128)(2,1)S(1)}, bf16[264,1280]{1,0:T(8,128)(2,1)}, u32[]{:S(2)}, u32[]{:S(2)}) %collective-permute-start.14) | collective-permute-done | bytes 675872 | tf_op jit(solution)/shard_map/ppermute | solution.py:12
  36.8 0.7 slice_convert_fusion
  37.5 0.0 collective-permute-done.7
  37.5 0.7 slice_convert_fusion.1
  38.2 6.3 %collective-permute-done.6 = bf16[264,1280]{1,0:T(8,128)(2,1)S(1)} collective-permute-done((bf16[264,1280]{1,0:T(8,128)(2,1)S(1)}, bf16[264,1280]{1,0:T(8,128)(2,1)S(1)}, u32[]{:S(2)}, u32[]{:S(2)}) %collective-permute-start.6) | collective-permute-done | bytes 675872 | tf_op jit(solution)/shard_map/ppermute | solution.py:12
  44.5 0.0 collective-permute-done
  44.5 1.5 %fusion.9 = f32[256,256]{1,0:T(8,128)S(1)} fusion(bf16[264,1280]{1,0:T(8,128)(2,1)} %collective-permute-done.14, bf16[256,256]{1,0:T(8,128)(2,1)S(1)} %get-tuple-element.41, bf16[256,1024]{1,0:T(8,128)(2,1)S(1)} %get-tuple-element.31), kind=kOutput, calls=%fused_computation.12 | convolution fusion | flops 169082880 | bytes 1572864 | tf_op jit(solution)/shard_map/dot_general | solution.py:94
  46.0 1.5 %fusion.11 = f32[256,256]{1,0:T(8,128)S(1)} fusion(bf16[264,1280]{1,0:T(8,128)(2,1)} %collective-permute-done.7, bf16[256,256]{1,0:T(8,128)(2,1)S(1)} %get-tuple-element.41, bf16[256,1024]{1,0:T(8,128)(2,1)S(1)} %get-tuple-element.31), kind=kOutput, calls=%fused_computation.14 | convolution fusion | flops 169082880 | bytes 1572864 | tf_op jit(solution)/shard_map/dot_general | solution.py:94
  47.4 0.4 fusion.13
  47.8 0.4 fusion.15
  48.2 0.2 maximum_bitcast_fusion.3
  48.4 0.1 collective-permute-start.15
  48.5 1.3 %collective-permute-done.15 = f32[1,264,128]{2,1,0:T(8,128)S(1)} collective-permute-done((f32[1,264,128]{2,1,0:T(8,128)S(1)}, f32[1,264,128]{2,1,0:T(8,128)S(1)}, u32[]{:S(2)}, u32[]{:S(2)}) %collective-permute-start.15) | collective-permute-done | bytes 135200 | tf_op jit(solution)/shard_map/ppermute | solution.py:17
  49.9 1.6 %collective-permute-start.16 = (f32[1,132,128]{2,1,0:T(8,128)S(1)}, f32[1,132,128]{2,1,0:T(8,128)S(1)}, u32[]{:S(2)}, u32[]{:S(2)}) collective-permute-start(f32[1,132,128]{2,1,0:T(8,128)S(1)} %constant_dynamic-slice_fusion), channel_id=1, source_target_pairs={{0,2},{1,3},{2,0},{3,1},{4,6},{5,7},{6,4},{7,5},{8,10},{9,11},{10,... | collective-permute-start | bytes 202760 | tf_op jit(solution)/shard_map/ppermute | solution.py:17
  51.4 0.1 collective-permute-start.1
  51.5 2.7 %collective-permute-done.16 = f32[1,132,128]{2,1,0:T(8,128)S(1)} collective-permute-done((f32[1,132,128]{2,1,0:T(8,128)S(1)}, f32[1,132,128]{2,1,0:T(8,128)S(1)}, u32[]{:S(2)}, u32[]{:S(2)}) %collective-permute-start.16) | collective-permute-done | bytes 67616 | tf_op jit(solution)/shard_map/ppermute | solution.py:17
  54.2 1.6 %collective-permute-start.17 = (f32[1,132,128]{2,1,0:T(8,128)S(1)}, f32[1,132,128]{2,1,0:T(8,128)S(1)}, u32[]{:S(2)}, u32[]{:S(2)}) collective-permute-start(f32[1,132,128]{2,1,0:T(8,128)S(1)} %dynamic-slice_add_fusion.2), channel_id=1, source_target_pairs={{0,2},{1,3},{2,0},{3,1},{4,6},{5,7},{6,4},{7,5},{8,10},{9,11},{10,... | collective-permute-start | bytes 202760 | tf_op jit(solution)/shard_map/ppermute | solution.py:17
  55.8 0.1 collective-permute-start.8
  55.9 2.7 %collective-permute-done.17 = f32[1,132,128]{2,1,0:T(8,128)S(1)} collective-permute-done((f32[1,132,128]{2,1,0:T(8,128)S(1)}, f32[1,132,128]{2,1,0:T(8,128)S(1)}, u32[]{:S(2)}, u32[]{:S(2)}) %collective-permute-start.17) | collective-permute-done | bytes 67616 | tf_op jit(solution)/shard_map/ppermute | solution.py:17
  58.7 0.1 collective-permute-start.18
  58.7 0.0 collective-permute-done.1
  58.8 1.6 %collective-permute-start.2 = (f32[2,132,128]{2,1,0:T(8,128)S(1)}, f32[2,132,128]{2,1,0:T(8,128)S(1)}, u32[]{:S(2)}, u32[]{:S(2)}) collective-permute-start(f32[2,132,128]{2,1,0:T(8,128)S(1)} %constant_dynamic-slice_fusion.2), channel_id=1, source_target_pairs={{0,2},{1,3},{2,0},{3,1},{4,6},{5,7},{6,4},{7,5},{8,10},{9,11},{10,... | collective-permute-start | bytes 405512 | tf_op jit(solution)/shard_map/ppermute | solution.py:17
  60.4 0.0 collective-permute-done.8
  60.5 0.6 collective-permute-start.9
  61.1 4.4 %collective-permute-done.2 = f32[2,132,128]{2,1,0:T(8,128)S(1)} collective-permute-done((f32[2,132,128]{2,1,0:T(8,128)S(1)}, f32[2,132,128]{2,1,0:T(8,128)S(1)}, u32[]{:S(2)}, u32[]{:S(2)}) %collective-permute-start.2) | collective-permute-done | bytes 135200 | tf_op jit(solution)/shard_map/ppermute | solution.py:17
  65.5 1.6 %collective-permute-start.3 = (f32[2,132,128]{2,1,0:T(8,128)S(1)}, f32[2,132,128]{2,1,0:T(8,128)S(1)}, u32[]{:S(2)}, u32[]{:S(2)}) collective-permute-start(f32[2,132,128]{2,1,0:T(8,128)S(1)} %dynamic-slice_add_fusion.1), channel_id=1, source_target_pairs={{0,2},{1,3},{2,0},{3,1},{4,6},{5,7},{6,4},{7,5},{8,10},{9,11},{10,... | collective-permute-start | bytes 405512 | tf_op jit(solution)/shard_map/ppermute | solution.py:17
  67.0 1.4 %collective-permute-done.9 = f32[2,132,128]{2,1,0:T(8,128)S(1)} collective-permute-done((f32[2,132,128]{2,1,0:T(8,128)S(1)}, f32[2,132,128]{2,1,0:T(8,128)S(1)}, u32[]{:S(2)}, u32[]{:S(2)}) %collective-permute-start.9) | collective-permute-done | bytes 135200 | tf_op jit(solution)/shard_map/ppermute | solution.py:17
  68.4 1.6 %collective-permute-start.10 = (f32[2,132,128]{2,1,0:T(8,128)S(1)}, f32[2,132,128]{2,1,0:T(8,128)S(1)}, u32[]{:S(2)}, u32[]{:S(2)}) collective-permute-start(f32[2,132,128]{2,1,0:T(8,128)S(1)} %dynamic-slice_add_fusion), channel_id=1, source_target_pairs={{0,2},{1,3},{2,0},{3,1},{4,6},{5,7},{6,4},{7,5},{8,10},{9,11},{10,... | collective-permute-start | bytes 405512 | tf_op jit(solution)/shard_map/ppermute | solution.py:17
  70.0 0.0 collective-permute-done.18
  70.0 1.5 %collective-permute-done.3 = f32[2,132,128]{2,1,0:T(8,128)S(1)} collective-permute-done((f32[2,132,128]{2,1,0:T(8,128)S(1)}, f32[2,132,128]{2,1,0:T(8,128)S(1)}, u32[]{:S(2)}, u32[]{:S(2)}) %collective-permute-start.3) | collective-permute-done | bytes 135200 | tf_op jit(solution)/shard_map/ppermute | solution.py:17
  71.6 0.1 collective-permute-start.4
  71.7 2.2 %collective-permute-done.10 = f32[2,132,128]{2,1,0:T(8,128)S(1)} collective-permute-done((f32[2,132,128]{2,1,0:T(8,128)S(1)}, f32[2,132,128]{2,1,0:T(8,128)S(1)}, u32[]{:S(2)}, u32[]{:S(2)}) %collective-permute-start.10) | collective-permute-done | bytes 135200 | tf_op jit(solution)/shard_map/ppermute | solution.py:17
  74.0 0.1 collective-permute-start.11
  74.0 0.0 collective-permute-done.4
  74.1 0.3 fusion.52
  74.4 0.3 fusion.78
  74.7 0.2 fusion.61
  75.0 1.9 %collective-permute-start.5 = (f32[257,256]{1,0:T(8,128)S(1)}, f32[257,256]{1,0:T(8,128)S(1)}, u32[]{:S(2)}, u32[]{:S(2)}) collective-permute-start(f32[257,256]{1,0:T(8,128)S(1)} %pad_maximum_fusion.2), channel_id=1, source_target_pairs={{0,4},{4,8},{8,12},{12,16},{16,20},{20,24},{24,28},{1,5},{5,9},{9,... | collective-permute-start | bytes 789512 | tf_op jit(solution)/shard_map/ppermute | solution.py:12
  76.9 15.4 %collective-permute-start.19 = (f32[257,256]{1,0:T(8,128)S(1)}, f32[257,256]{1,0:T(8,128)S(1)}, u32[]{:S(2)}, u32[]{:S(2)}) collective-permute-start(f32[257,256]{1,0:T(8,128)S(1)} %pad_maximum_fusion.6), channel_id=1, source_target_pairs={{16,0},{20,4},{24,8},{28,12},{17,1},{21,5},{25,9},{29,13},{18,2},{... | collective-permute-start | bytes 789512 | tf_op jit(solution)/shard_map/ppermute | solution.py:12
  92.3 0.2 fusion.49
  92.6 0.0 collective-permute-done.11
  92.6 0.3 fusion.79
  92.9 0.2 fusion.58
  93.1 0.2 fusion.55
  93.4 1.3 %collective-permute-start.13 = (f32[257,256]{1,0:T(8,128)S(1)}, f32[257,256]{1,0:T(8,128)S(1)}, u32[]{:S(2)}, u32[]{:S(2)}) collective-permute-start(f32[257,256]{1,0:T(8,128)S(1)} %pad_maximum_fusion.5), channel_id=1, source_target_pairs={{0,12},{4,16},{8,20},{12,24},{16,28},{1,13},{5,17},{9,21},{13,25},... | collective-permute-start | bytes 789512 | tf_op jit(solution)/shard_map/ppermute | solution.py:12
  94.7 4.0 %collective-permute-start.12 = (f32[257,256]{1,0:T(8,128)S(1)}, f32[257,256]{1,0:T(8,128)S(1)}, u32[]{:S(2)}, u32[]{:S(2)}) collective-permute-start(f32[257,256]{1,0:T(8,128)S(1)} %pad_maximum_fusion.4), channel_id=1, source_target_pairs={{8,0},{12,4},{16,8},{20,12},{24,16},{28,20},{9,1},{13,5},{17,9},{2... | collective-permute-start | bytes 789512 | tf_op jit(solution)/shard_map/ppermute | solution.py:12
  98.7 1.1 fusion.44
  99.8 1.1 %fusion.42 = f32[256,256]{1,0:T(8,128)S(1)} fusion(bf16[264,1280]{1,0:T(8,128)(2,1)} %collective-permute-done.14, f32[1,264,128]{2,1,0:T(8,128)S(1)} %get-tuple-element.38, f32[1,264,128]{2,1,0:T(8,128)S(1)} %get-tuple-element.37, f32[256]{0:T(256)S(1)} %bitcast.101, f32[256]{0:T(256)S(1)} %bitcast.88, pred[]{:T(512)S(6)} %and.44), kind=kOutput, calls=%fused_computation.88 | convolution fusion | flops 33882112 | bytes 665601 | tf_op jit(solution)/shard_map/dot_general | solution.py:120
  101.0 0.2 fusion.46
  101.2 0.0 collective-permute-done.5
  101.2 7.3 %collective-permute-done.13 = f32[257,256]{1,0:T(8,128)S(1)} collective-permute-done((f32[257,256]{1,0:T(8,128)S(1)}, f32[257,256]{1,0:T(8,128)S(1)}, u32[]{:S(2)}, u32[]{:S(2)}) %collective-permute-start.13) | collective-permute-done | bytes 263200 | tf_op jit(solution)/shard_map/ppermute | solution.py:12
  108.5 0.0 collective-permute-done.12
  108.5 1.0 fusion.25
  (48 shorter events, 0.8 us)
Async XLA Ops:
  0.0 1.3 %copy-start.1 = (bf16[256,1024]{1,0:T(8,128)(2,1)S(1)}, bf16[256,1024]{1,0:T(8,128)(2,1)}, u32[]{:S(2)}) copy-start(bf16[256,1024]{1,0:T(8,128)(2,1)} %param.2) | copy-start | bytes 1572868
  1.3 0.9 copy-start
  2.5 34.3 %collective-permute-start.14 = (bf16[264,1280]{1,0:T(8,128)(2,1)S(1)}, bf16[264,1280]{1,0:T(8,128)(2,1)}, u32[]{:S(2)}, u32[]{:S(2)}) collective-permute-start(bf16[264,1280]{1,0:T(8,128)(2,1)S(1)} %fusion.8), channel_id=1, source_target_pairs={{0,16},{4,20},{8,24},{12,28},{1,17},{5,21},{9,25},{13,29},{2,18},{... | collective-permute-start | bytes 2027528 | tf_op jit(solution)/shard_map/ppermute | solution.py:12
  3.8 33.7 %collective-permute-start.7 = (bf16[264,1280]{1,0:T(8,128)(2,1)S(1)}, bf16[264,1280]{1,0:T(8,128)(2,1)}, u32[]{:S(2)}, u32[]{:S(2)}) collective-permute-start(bf16[264,1280]{1,0:T(8,128)(2,1)S(1)} %fusion.8), channel_id=1, source_target_pairs={{12,0},{16,4},{20,8},{24,12},{28,16},{13,1},{17,5},{21,9},{25,13},... | collective-permute-start | bytes 2027528 | tf_op jit(solution)/shard_map/ppermute | solution.py:12
  11.9 32.6 %collective-permute-start.6 = (bf16[264,1280]{1,0:T(8,128)(2,1)S(1)}, bf16[264,1280]{1,0:T(8,128)(2,1)S(1)}, u32[]{:S(2)}, u32[]{:S(2)}) collective-permute-start(bf16[264,1280]{1,0:T(8,128)(2,1)S(1)} %fusion.8), channel_id=1, source_target_pairs={{0,8},{4,12},{8,16},{12,20},{16,24},{20,28},{1,9},{5,13},{9,17},{1... | collective-permute-start | bytes 2027528 | tf_op jit(solution)/shard_map/ppermute | solution.py:12
  13.1 31.3 %collective-permute-start = (bf16[264,1280]{1,0:T(8,128)(2,1)S(1)}, bf16[264,1280]{1,0:T(8,128)(2,1)S(1)}, u32[]{:S(2)}, u32[]{:S(2)}) collective-permute-start(bf16[264,1280]{1,0:T(8,128)(2,1)S(1)} %fusion.8), channel_id=1, source_target_pairs={{4,0},{8,4},{12,8},{16,12},{20,16},{24,20},{28,24},{5,1},{9,5},{13... | collective-permute-start | bytes 2027528 | tf_op jit(solution)/shard_map/ppermute | solution.py:12
  48.4 1.4 %collective-permute-start.15 = (f32[1,264,128]{2,1,0:T(8,128)S(1)}, f32[1,264,128]{2,1,0:T(8,128)S(1)}, u32[]{:S(2)}, u32[]{:S(2)}) collective-permute-start(f32[1,264,128]{2,1,0:T(8,128)S(1)} %dynamic-slice_bitcast_fusion), channel_id=1, source_target_pairs={{0,1},{1,0},{2,3},{3,2},{4,5},{5,4},{6,7},{7,6},{8,9},{9,8},{10,11... | collective-permute-start | bytes 405512 | tf_op jit(solution)/shard_map/ppermute | solution.py:17
  49.9 4.4 %collective-permute-start.16 = (f32[1,132,128]{2,1,0:T(8,128)S(1)}, f32[1,132,128]{2,1,0:T(8,128)S(1)}, u32[]{:S(2)}, u32[]{:S(2)}) collective-permute-start(f32[1,132,128]{2,1,0:T(8,128)S(1)} %constant_dynamic-slice_fusion), channel_id=1, source_target_pairs={{0,2},{1,3},{2,0},{3,1},{4,6},{5,7},{6,4},{7,5},{8,10},{9,11},{10,... | collective-permute-start | bytes 202760 | tf_op jit(solution)/shard_map/ppermute | solution.py:17
  51.4 7.3 %collective-permute-start.1 = (f32[2,264,128]{2,1,0:T(8,128)S(1)}, f32[2,264,128]{2,1,0:T(8,128)S(1)}, u32[]{:S(2)}, u32[]{:S(2)}) collective-permute-start(f32[2,264,128]{2,1,0:T(8,128)S(1)} %fusion.20), channel_id=1, source_target_pairs={{0,1},{1,0},{2,3},{3,2},{4,5},{5,4},{6,7},{7,6},{8,9},{9,8},{10,11... | collective-permute-start | bytes 811016 | tf_op jit(solution)/shard_map/ppermute | solution.py:17
  54.2 4.4 %collective-permute-start.17 = (f32[1,132,128]{2,1,0:T(8,128)S(1)}, f32[1,132,128]{2,1,0:T(8,128)S(1)}, u32[]{:S(2)}, u32[]{:S(2)}) collective-permute-start(f32[1,132,128]{2,1,0:T(8,128)S(1)} %dynamic-slice_add_fusion.2), channel_id=1, source_target_pairs={{0,2},{1,3},{2,0},{3,1},{4,6},{5,7},{6,4},{7,5},{8,10},{9,11},{10,... | collective-permute-start | bytes 202760 | tf_op jit(solution)/shard_map/ppermute | solution.py:17
  55.8 4.6 %collective-permute-start.8 = (f32[2,264,128]{2,1,0:T(8,128)S(1)}, f32[2,264,128]{2,1,0:T(8,128)S(1)}, u32[]{:S(2)}, u32[]{:S(2)}) collective-permute-start(f32[2,264,128]{2,1,0:T(8,128)S(1)} %fusion.17), channel_id=1, source_target_pairs={{0,1},{1,0},{2,3},{3,2},{4,5},{5,4},{6,7},{7,6},{8,9},{9,8},{10,11... | collective-permute-start | bytes 811016 | tf_op jit(solution)/shard_map/ppermute | solution.py:17
  58.7 11.3 %collective-permute-start.18 = (f32[1,264,128]{2,1,0:T(8,128)S(1)}, f32[1,264,128]{2,1,0:T(8,128)S(1)}, u32[]{:S(2)}, u32[]{:S(2)}) collective-permute-start(f32[1,264,128]{2,1,0:T(8,128)S(1)} %pad_maximum_fusion.10), channel_id=1, source_target_pairs={{0,1},{1,0},{2,3},{3,2},{4,5},{5,4},{6,7},{7,6},{8,9},{9,8},{10,11... | collective-permute-start | bytes 405512 | tf_op jit(solution)/shard_map/ppermute | solution.py:17
  58.8 6.6 %collective-permute-start.2 = (f32[2,132,128]{2,1,0:T(8,128)S(1)}, f32[2,132,128]{2,1,0:T(8,128)S(1)}, u32[]{:S(2)}, u32[]{:S(2)}) collective-permute-start(f32[2,132,128]{2,1,0:T(8,128)S(1)} %constant_dynamic-slice_fusion.2), channel_id=1, source_target_pairs={{0,2},{1,3},{2,0},{3,1},{4,6},{5,7},{6,4},{7,5},{8,10},{9,11},{10,... | collective-permute-start | bytes 405512 | tf_op jit(solution)/shard_map/ppermute | solution.py:17
  60.5 8.0 %collective-permute-start.9 = (f32[2,132,128]{2,1,0:T(8,128)S(1)}, f32[2,132,128]{2,1,0:T(8,128)S(1)}, u32[]{:S(2)}, u32[]{:S(2)}) collective-permute-start(f32[2,132,128]{2,1,0:T(8,128)S(1)} %constant_dynamic-slice_fusion.1), channel_id=1, source_target_pairs={{0,2},{1,3},{2,0},{3,1},{4,6},{5,7},{6,4},{7,5},{8,10},{9,11},{10,... | collective-permute-start | bytes 405512 | tf_op jit(solution)/shard_map/ppermute | solution.py:17
  65.5 6.1 %collective-permute-start.3 = (f32[2,132,128]{2,1,0:T(8,128)S(1)}, f32[2,132,128]{2,1,0:T(8,128)S(1)}, u32[]{:S(2)}, u32[]{:S(2)}) collective-permute-start(f32[2,132,128]{2,1,0:T(8,128)S(1)} %dynamic-slice_add_fusion.1), channel_id=1, source_target_pairs={{0,2},{1,3},{2,0},{3,1},{4,6},{5,7},{6,4},{7,5},{8,10},{9,11},{10,... | collective-permute-start | bytes 405512 | tf_op jit(solution)/shard_map/ppermute | solution.py:17
  68.4 5.5 %collective-permute-start.10 = (f32[2,132,128]{2,1,0:T(8,128)S(1)}, f32[2,132,128]{2,1,0:T(8,128)S(1)}, u32[]{:S(2)}, u32[]{:S(2)}) collective-permute-start(f32[2,132,128]{2,1,0:T(8,128)S(1)} %dynamic-slice_add_fusion), channel_id=1, source_target_pairs={{0,2},{1,3},{2,0},{3,1},{4,6},{5,7},{6,4},{7,5},{8,10},{9,11},{10,... | collective-permute-start | bytes 405512 | tf_op jit(solution)/shard_map/ppermute | solution.py:17
  71.6 2.4 %collective-permute-start.4 = (f32[2,264,128]{2,1,0:T(8,128)S(1)}, f32[2,264,128]{2,1,0:T(8,128)S(1)}, u32[]{:S(2)}, u32[]{:S(2)}) collective-permute-start(f32[2,264,128]{2,1,0:T(8,128)S(1)} %pad_maximum_fusion.1), channel_id=1, source_target_pairs={{0,1},{1,0},{2,3},{3,2},{4,5},{5,4},{6,7},{7,6},{8,9},{9,8},{10,11... | collective-permute-start | bytes 811016 | tf_op jit(solution)/shard_map/ppermute | solution.py:17
  74.0 18.6 %collective-permute-start.11 = (f32[2,264,128]{2,1,0:T(8,128)S(1)}, f32[2,264,128]{2,1,0:T(8,128)S(1)}, u32[]{:S(2)}, u32[]{:S(2)}) collective-permute-start(f32[2,264,128]{2,1,0:T(8,128)S(1)} %pad_maximum_fusion.3), channel_id=1, source_target_pairs={{0,1},{1,0},{2,3},{3,2},{4,5},{5,4},{6,7},{7,6},{8,9},{9,8},{10,11... | collective-permute-start | bytes 811016 | tf_op jit(solution)/shard_map/ppermute | solution.py:17
  75.0 26.2 %collective-permute-start.5 = (f32[257,256]{1,0:T(8,128)S(1)}, f32[257,256]{1,0:T(8,128)S(1)}, u32[]{:S(2)}, u32[]{:S(2)}) collective-permute-start(f32[257,256]{1,0:T(8,128)S(1)} %pad_maximum_fusion.2), channel_id=1, source_target_pairs={{0,4},{4,8},{8,12},{12,16},{16,20},{20,24},{24,28},{1,5},{5,9},{9,... | collective-permute-start | bytes 789512 | tf_op jit(solution)/shard_map/ppermute | solution.py:12
  76.9 24.3 %collective-permute-start.19 = (f32[257,256]{1,0:T(8,128)S(1)}, f32[257,256]{1,0:T(8,128)S(1)}, u32[]{:S(2)}, u32[]{:S(2)}) collective-permute-start(f32[257,256]{1,0:T(8,128)S(1)} %pad_maximum_fusion.6), channel_id=1, source_target_pairs={{16,0},{20,4},{24,8},{28,12},{17,1},{21,5},{25,9},{29,13},{18,2},{... | collective-permute-start | bytes 789512 | tf_op jit(solution)/shard_map/ppermute | solution.py:12
  93.4 15.1 %collective-permute-start.13 = (f32[257,256]{1,0:T(8,128)S(1)}, f32[257,256]{1,0:T(8,128)S(1)}, u32[]{:S(2)}, u32[]{:S(2)}) collective-permute-start(f32[257,256]{1,0:T(8,128)S(1)} %pad_maximum_fusion.5), channel_id=1, source_target_pairs={{0,12},{4,16},{8,20},{12,24},{16,28},{1,13},{5,17},{9,21},{13,25},... | collective-permute-start | bytes 789512 | tf_op jit(solution)/shard_map/ppermute | solution.py:12
  94.7 13.8 %collective-permute-start.12 = (f32[257,256]{1,0:T(8,128)S(1)}, f32[257,256]{1,0:T(8,128)S(1)}, u32[]{:S(2)}, u32[]{:S(2)}) collective-permute-start(f32[257,256]{1,0:T(8,128)S(1)} %pad_maximum_fusion.4), channel_id=1, source_target_pairs={{8,0},{12,4},{16,8},{20,12},{24,16},{28,20},{9,1},{13,5},{17,9},{2... | collective-permute-start | bytes 789512 | tf_op jit(solution)/shard_map/ppermute | solution.py:12

commit v10 on v8

--- a/solution.py
+++ b/solution.py
@@ -97,6 +97,8 @@
     student_f = student.astype(jnp.float32)
     row_total = jnp.zeros((rows_dev,), jnp.float32)
     pulled = jnp.zeros(student.shape, jnp.float32)
+    pulled_t = jnp.zeros((fs, rows_dev), jnp.float32)
+    student_t = student.T
     own_q = None
     split = min(3, len(offsets))
     for group_idx in ([list(range(split)), list(range(split, len(offsets)))]):
@@ -115,16 +117,19 @@
             row_total = row_total + jnp.sum(resid, axis=1)
             pulled = pulled + jnp.dot(low, student_band[d], preferred_element_type=jnp.float32)
             if d > 0:
-                back = lax.dot_general(low, student, (((0,), (0,)), ((), ())), preferred_element_type=jnp.float32)
                 col = jnp.sum(resid, axis=0)
                 if fs == rows_dev:
-                    got = shifted(jnp.concatenate([back, col[None, :]], axis=0), "batch", -e)
-                    pulled = pulled + got[:rows_dev]
-                    row_total = row_total + got[rows_dev]
+                    back_t = jnp.dot(student_t, low, preferred_element_type=jnp.float32)
+                    got = shifted(jnp.concatenate([back_t, col[None, :]], axis=0), "batch", -e)
+                    pulled_t = pulled_t + got[:fs]
+                    row_total = row_total + got[fs]
                 else:
+                    back = lax.dot_general(low, student, (((0,), (0,)), ((), ())), preferred_element_type=jnp.float32)
                     back_r, col_r = shifted((back, col), "batch", -e)
                     pulled = pulled + back_r
                     row_total = row_total + col_r
+    if fs == rows_dev:
+        pulled = pulled + pulled_t.T
     grad = (student_f * row_total[:, None] - pulled) / near_count
     return grad
 

time: 104 us -> 106 us (1.019)
  matrix products: 9.42 us -> 10.9 us
    dot_general x5, matrix products: 4.02 us -> 5.11 us  [tile_part(): lax.dot_general(scaled, rhs_band[d], (((1,), (1,)), ((), ())), preferred_...]
  transfers between devices with their start and end apart: 16 -> 16, of which waited for: 12 -> 12; matrix products, arithmetic and copies ran while one was open for 6% -> 7% of each run, Pallas kernels for 0% -> 0%
where the time goes in v10:
time: 106 us; the launch traced here: 105 us
  waiting for transfers between devices  60.3 us (57%)
  starting transfers between devices  26.5 us (25%)
  matrix products  10.9 us (10%)
  other arithmetic  4.9 us (5%)
  local copies, waits for them, and re-layouts  1.88 us (2%)
    ppermute x8, waiting for transfers between devices, shifted(): return lax.ppermute(block, axis, route)  45.7 us
    ppermute x8, starting transfers between devices, shifted(): return lax.ppermute(block, axis, route)  20.4 us
    ppermute x8, waiting for transfers between devices, swapped(): return lax.ppermute(block, axis, [(i, i ^ mask) for i in range(size)])  14.6 us
    ppermute x8, starting transfers between devices, swapped(): return lax.ppermute(block, axis, [(i, i ^ mask) for i in range(size)])  6.05 us
    dot_general x5, matrix products, tile_part(): lax.dot_general(scaled, rhs_band[d], (((1,), (1,)), ((), ())), preferred_...  5.11 us
    dot_general x5, matrix products, body(): jnp.dot(low, student_band[d], preferred_element_type=jnp.float32)  4.85 us
  transfers between devices with their start and end apart: 16, of which 12 were waited for; matrix products, arithmetic and copies ran while one was open for 7% of the time, Pallas kernels for 0%

profile of v10, /device:TPU:24, one launch (start us, length us, event | category | flops | bytes accessed | tf_op | source)
XLA Modules:
  0.0 105.0 jit_solution(9671511799401476800)
XLA Ops:
  0.0 1.3 %multiply_reduce_fusion = f32[256]{0:T(256)S(1)} fusion(bf16[256,1024]{1,0:T(8,128)(2,1)} %param.2), kind=kLoop, calls=%fused_computation.19 | loop fusion | flops 786176 | bytes 525312 | tf_op jit(solution)/shard_map/reduce_sum | solution.py:73
  1.3 0.0 copy-start
  1.3 0.1 broadcast_multiply_fusion
  1.4 0.8 copy-done
  2.2 0.1 copy.3
  2.3 0.1 fusion.16
  2.5 3.3 %collective-permute-start = (bf16[264,1280]{1,0:T(8,128)(2,1)S(1)}, bf16[264,1280]{1,0:T(8,128)(2,1)}, u32[]{:S(2)}, u32[]{:S(2)}) collective-permute-start(bf16[264,1280]{1,0:T(8,128)(2,1)S(1)} %fusion.4), channel_id=1, source_target_pairs={{4,0},{8,4},{12,8},{16,12},{20,16},{24,20},{28,24},{5,1},{9,5},{13... | collective-permute-start | bytes 2027528 | tf_op jit(solution)/shard_map/ppermute | solution.py:12
  5.8 1.3 %collective-permute-start.1 = (bf16[264,1280]{1,0:T(8,128)(2,1)S(1)}, bf16[264,1280]{1,0:T(8,128)(2,1)S(1)}, u32[]{:S(2)}, u32[]{:S(2)}) collective-permute-start(bf16[264,1280]{1,0:T(8,128)(2,1)S(1)} %fusion.4), channel_id=1, source_target_pairs={{0,8},{4,12},{8,16},{12,20},{16,24},{20,28},{1,9},{5,13},{9,17},{1... | collective-permute-start | bytes 2027528 | tf_op jit(solution)/shard_map/ppermute | solution.py:12
  7.1 5.4 %collective-permute-start.8 = (bf16[264,1280]{1,0:T(8,128)(2,1)S(1)}, bf16[264,1280]{1,0:T(8,128)(2,1)}, u32[]{:S(2)}, u32[]{:S(2)}) collective-permute-start(bf16[264,1280]{1,0:T(8,128)(2,1)S(1)} %fusion.4), channel_id=1, source_target_pairs={{12,0},{16,4},{20,8},{24,12},{28,16},{13,1},{17,5},{21,9},{25,13},... | collective-permute-start | bytes 2027528 | tf_op jit(solution)/shard_map/ppermute | solution.py:12
  12.5 1.3 %collective-permute-start.9 = (bf16[264,1280]{1,0:T(8,128)(2,1)S(1)}, bf16[264,1280]{1,0:T(8,128)(2,1)}, u32[]{:S(2)}, u32[]{:S(2)}) collective-permute-start(bf16[264,1280]{1,0:T(8,128)(2,1)S(1)} %fusion.4), channel_id=1, source_target_pairs={{0,16},{4,20},{8,24},{12,28},{1,17},{5,21},{9,25},{13,29},{2,18},{... | collective-permute-start | bytes 2027528 | tf_op jit(solution)/shard_map/ppermute | solution.py:12
  13.8 0.1 pad.42.clone
  13.9 0.4 fusion.64
  14.3 7.2 %collective-permute-done = bf16[264,1280]{1,0:T(8,128)(2,1)} collective-permute-done((bf16[264,1280]{1,0:T(8,128)(2,1)S(1)}, bf16[264,1280]{1,0:T(8,128)(2,1)}, u32[]{:S(2)}, u32[]{:S(2)}) %collective-permute-start) | collective-permute-done | bytes 675872 | tf_op jit(solution)/shard_map/ppermute | solution.py:12
  21.4 0.7 slice_convert_fusion.3
  22.1 2.7 %collective-permute-done.1 = bf16[264,1280]{1,0:T(8,128)(2,1)S(1)} collective-permute-done((bf16[264,1280]{1,0:T(8,128)(2,1)S(1)}, bf16[264,1280]{1,0:T(8,128)(2,1)S(1)}, u32[]{:S(2)}, u32[]{:S(2)}) %collective-permute-start.1) | collective-permute-done | bytes 675872 | tf_op jit(solution)/shard_map/ppermute | solution.py:12
  24.9 9.9 %collective-permute-done.8 = bf16[264,1280]{1,0:T(8,128)(2,1)} collective-permute-done((bf16[264,1280]{1,0:T(8,128)(2,1)S(1)}, bf16[264,1280]{1,0:T(8,128)(2,1)}, u32[]{:S(2)}, u32[]{:S(2)}) %collective-permute-start.8) | collective-permute-done | bytes 675872 | tf_op jit(solution)/shard_map/ppermute | solution.py:12
  34.8 0.7 slice_convert_fusion.1
  35.5 17.9 %collective-permute-done.9 = bf16[264,1280]{1,0:T(8,128)(2,1)} collective-permute-done((bf16[264,1280]{1,0:T(8,128)(2,1)S(1)}, bf16[264,1280]{1,0:T(8,128)(2,1)}, u32[]{:S(2)}, u32[]{:S(2)}) %collective-permute-start.9) | collective-permute-done | bytes 675872 | tf_op jit(solution)/shard_map/ppermute | solution.py:12
  53.3 0.7 slice_convert_fusion
  54.0 1.5 %fusion.11 = f32[256,256]{1,0:T(8,128)S(1)} fusion(bf16[264,1280]{1,0:T(8,128)(2,1)} %collective-permute-done, bf16[256,256]{1,0:T(8,128)(2,1)S(1)} %get-tuple-element.40, bf16[256,1024]{1,0:T(8,128)(2,1)S(1)} %get-tuple-element.34), kind=kOutput, calls=%fused_computation.28 | convolution fusion | flops 169082880 | bytes 1572864 | tf_op jit(solution)/shard_map/dot_general | solution.py:94
  55.5 0.4 fusion.9
  55.9 1.5 %fusion.7 = f32[256,256]{1,0:T(8,128)S(1)} fusion(bf16[264,1280]{1,0:T(8,128)(2,1)} %collective-permute-done.8, bf16[256,256]{1,0:T(8,128)(2,1)S(1)} %get-tuple-element.40, bf16[256,1024]{1,0:T(8,128)(2,1)S(1)} %get-tuple-element.34), kind=kOutput, calls=%fused_computation.24 | convolution fusion | flops 169082880 | bytes 1572864 | tf_op jit(solution)/shard_map/dot_general | solution.py:94
  57.3 1.5 %fusion.5 = f32[256,256]{1,0:T(8,128)S(1)} fusion(bf16[264,1280]{1,0:T(8,128)(2,1)} %collective-permute-done.9, bf16[256,256]{1,0:T(8,128)(2,1)S(1)} %get-tuple-element.40, bf16[256,1024]{1,0:T(8,128)(2,1)S(1)} %get-tuple-element.34), kind=kOutput, calls=%fused_computation.22 | convolution fusion | flops 169082880 | bytes 1572864 | tf_op jit(solution)/shard_map/dot_general | solution.py:94
  58.8 0.2 maximum_bitcast_fusion
  59.0 0.1 collective-permute-start.10
  59.1 0.1 pad_maximum_fusion
  59.2 0.6 collective-permute-start.2
  59.7 0.9 collective-permute-done.10
  60.7 1.6 %collective-permute-start.11 = (f32[2,132,128]{2,1,0:T(8,128)S(1)}, f32[2,132,128]{2,1,0:T(8,128)S(1)}, u32[]{:S(2)}, u32[]{:S(2)}) collective-permute-start(f32[2,132,128]{2,1,0:T(8,128)S(1)} %constant_dynamic-slice_fusion), channel_id=1, source_target_pairs={{0,2},{1,3},{2,0},{3,1},{4,6},{5,7},{6,4},{7,5},{8,10},{9,11},{10,... | collective-permute-start | bytes 405512 | tf_op jit(solution)/shard_map/ppermute | solution.py:17
  62.2 0.0 collective-permute-done.2
  62.2 0.1 dynamic-slice_add_fusion
  62.3 0.6 collective-permute-start.3
  62.9 4.4 %collective-permute-done.11 = f32[2,132,128]{2,1,0:T(8,128)S(1)} collective-permute-done((f32[2,132,128]{2,1,0:T(8,128)S(1)}, f32[2,132,128]{2,1,0:T(8,128)S(1)}, u32[]{:S(2)}, u32[]{:S(2)}) %collective-permute-start.11) | collective-permute-done | bytes 135200 | tf_op jit(solution)/shard_map/ppermute | solution.py:17
  67.3 1.6 %collective-permute-start.12 = (f32[2,132,128]{2,1,0:T(8,128)S(1)}, f32[2,132,128]{2,1,0:T(8,128)S(1)}, u32[]{:S(2)}, u32[]{:S(2)}) collective-permute-start(f32[2,132,128]{2,1,0:T(8,128)S(1)} %dynamic-slice_add_fusion.2), channel_id=1, source_target_pairs={{0,2},{1,3},{2,0},{3,1},{4,6},{5,7},{6,4},{7,5},{8,10},{9,11},{10,... | collective-permute-start | bytes 405512 | tf_op jit(solution)/shard_map/ppermute | solution.py:17
  68.9 2.9 %collective-permute-done.3 = f32[3,132,128]{2,1,0:T(8,128)S(1)} collective-permute-done((f32[3,132,128]{2,1,0:T(8,128)S(1)}, f32[3,132,128]{2,1,0:T(8,128)S(1)}, u32[]{:S(2)}, u32[]{:S(2)}) %collective-permute-start.3) | collective-permute-done | bytes 202784 | tf_op jit(solution)/shard_map/ppermute | solution.py:17
  71.8 1.6 %collective-permute-start.4 = (f32[3,132,128]{2,1,0:T(8,128)S(1)}, f32[3,132,128]{2,1,0:T(8,128)S(1)}, u32[]{:S(2)}, u32[]{:S(2)}) collective-permute-start(f32[3,132,128]{2,1,0:T(8,128)S(1)} %dynamic-slice_add_fusion.1), channel_id=1, source_target_pairs={{0,2},{1,3},{2,0},{3,1},{4,6},{5,7},{6,4},{7,5},{8,10},{9,11},{10,... | collective-permute-start | bytes 608264 | tf_op jit(solution)/shard_map/ppermute | solution.py:17
  73.4 1.4 %collective-permute-done.12 = f32[2,132,128]{2,1,0:T(8,128)S(1)} collective-permute-done((f32[2,132,128]{2,1,0:T(8,128)S(1)}, f32[2,132,128]{2,1,0:T(8,128)S(1)}, u32[]{:S(2)}, u32[]{:S(2)}) %collective-permute-start.12) | collective-permute-done | bytes 135200 | tf_op jit(solution)/shard_map/ppermute | solution.py:17
  74.8 0.1 collective-permute-start.13
  74.9 3.5 %collective-permute-done.4 = f32[3,132,128]{2,1,0:T(8,128)S(1)} collective-permute-done((f32[3,132,128]{2,1,0:T(8,128)S(1)}, f32[3,132,128]{2,1,0:T(8,128)S(1)}, u32[]{:S(2)}, u32[]{:S(2)}) %collective-permute-start.4) | collective-permute-done | bytes 202784 | tf_op jit(solution)/shard_map/ppermute | solution.py:17
  78.5 0.1 collective-permute-start.5
  78.6 0.0 collective-permute-done.13
  78.6 0.1 broadcast_select_fusion.3
  78.6 1.6 %collective-permute-done.5 = f32[3,264,128]{2,1,0:T(8,128)S(1)} collective-permute-done((f32[3,264,128]{2,1,0:T(8,128)S(1)}, f32[3,264,128]{2,1,0:T(8,128)S(1)}, u32[]{:S(2)}, u32[]{:S(2)}) %collective-permute-start.5) | collective-permute-done | bytes 405536 | tf_op jit(solution)/shard_map/ppermute | solution.py:17
  80.3 0.1 broadcast_select_fusion.1
  80.3 0.3 fusion.67
  80.6 0.2 convolution_bitcast_fusion
  80.9 1.4 %collective-permute-start.15 = (f32[257,256]{1,0:T(8,128)S(1)}, f32[257,256]{1,0:T(8,128)S(1)}, u32[]{:S(2)}, u32[]{:S(2)}) collective-permute-start(f32[257,256]{1,0:T(8,128)S(1)} %pad_maximum_fusion.7), channel_id=1, source_target_pairs={{16,0},{20,4},{24,8},{28,12},{17,1},{21,5},{25,9},{29,13},{18,2},{... | collective-permute-start | bytes 789512 | tf_op jit(solution)/shard_map/ppermute | solution.py:12
  82.2 0.2 convolution_bitcast_fusion.1
  82.5 1.3 %collective-permute-start.14 = (f32[257,256]{1,0:T(8,128)S(1)}, f32[257,256]{1,0:T(8,128)S(1)}, u32[]{:S(2)}, u32[]{:S(2)}) collective-permute-start(f32[257,256]{1,0:T(8,128)S(1)} %pad_maximum_fusion.6), channel_id=1, source_target_pairs={{0,12},{4,16},{8,20},{12,24},{16,28},{1,13},{5,17},{9,21},{13,25},... | collective-permute-start | bytes 789512 | tf_op jit(solution)/shard_map/ppermute | solution.py:12
  83.8 0.3 fusion.66
  84.1 0.2 convolution_bitcast_fusion.2
  84.3 4.6 %collective-permute-start.7 = (f32[257,256]{1,0:T(8,128)S(1)}, f32[257,256]{1,0:T(8,128)S(1)}, u32[]{:S(2)}, u32[]{:S(2)}) collective-permute-start(f32[257,256]{1,0:T(8,128)S(1)} %pad_maximum_fusion.4), channel_id=1, source_target_pairs={{8,0},{12,4},{16,8},{20,12},{24,16},{28,20},{9,1},{13,5},{17,9},{2... | collective-permute-start | bytes 789512 | tf_op jit(solution)/shard_map/ppermute | solution.py:12
  89.0 0.2 convolution_bitcast_fusion.3
  89.2 1.9 %collective-permute-start.6 = (f32[257,256]{1,0:T(8,128)S(1)}, f32[257,256]{1,0:T(8,128)S(1)}, u32[]{:S(2)}, u32[]{:S(2)}) collective-permute-start(f32[257,256]{1,0:T(8,128)S(1)} %pad_maximum_fusion.3), channel_id=1, source_target_pairs={{0,4},{4,8},{8,12},{12,16},{16,20},{20,24},{24,28},{1,5},{5,9},{9,... | collective-permute-start | bytes 789512 | tf_op jit(solution)/shard_map/ppermute | solution.py:12
  91.2 1.1 %fusion.37 = f32[256,256]{0,1:T(8,128)S(1)} fusion(bf16[264,1280]{1,0:T(8,128)(2,1)} %collective-permute-done.9, bf16[256,256]{1,0:T(8,128)(2,1)S(1)} %get-tuple-element.29), kind=kOutput, calls=%fused_computation.89 | convolution fusion | flops 33554432 | bytes 524288 | tf_op jit(solution)/shard_map/dot_general | solution.py:118
  92.3 1.1 %fusion.39 = f32[256,256]{0,1:T(8,128)S(1)} fusion(bf16[264,1280]{1,0:T(8,128)(2,1)} %collective-permute-done.8, bf16[256,256]{1,0:T(8,128)(2,1)S(1)} %get-tuple-element.15), kind=kOutput, calls=%fused_computation.91 | convolution fusion | flops 33554432 | bytes 524288 | tf_op jit(solution)/shard_map/dot_general | solution.py:118
  93.4 0.3 fusion.43
  93.7 1.1 %convolution_add_fusion.1 = f32[256,256]{0,1:T(8,128)S(1)} fusion(f32[256,256]{0,1:T(8,128)S(1)} %fusion.43, bf16[264,1280]{1,0:T(8,128)(2,1)} %collective-permute-done, bf16[256,256]{1,0:T(8,128)(2,1)S(1)} %get-tuple-element.21), kind=kOutput, calls=%fused_computation.13 | convolution fusion | flops 33619968 | bytes 786432 | tf_op jit(solution)/shard_map/dot_general | solution.py:118
  94.9 0.0 collective-permute-done.15
  94.9 2.4 %collective-permute-done.14 = f32[257,256]{1,0:T(8,128)S(1)} collective-permute-done((f32[257,256]{1,0:T(8,128)S(1)}, f32[257,256]{1,0:T(8,128)S(1)}, u32[]{:S(2)}, u32[]{:S(2)}) %collective-permute-start.14) | collective-permute-done | bytes 263200 | tf_op jit(solution)/shard_map/ppermute | solution.py:12
  97.3 0.0 collective-permute-done.7
  97.3 5.7 %collective-permute-done.6 = f32[257,256]{1,0:T(8,128)S(1)} collective-permute-done((f32[257,256]{1,0:T(8,128)S(1)}, f32[257,256]{1,0:T(8,128)S(1)}, u32[]{:S(2)}, u32[]{:S(2)}) %collective-permute-start.6) | collective-permute-done | bytes 263200 | tf_op jit(solution)/shard_map/ppermute | solution.py:12
  102.9 1.2 %fusion.18 = f32[256,256]{0,1:T(8,128)S(1)} fusion(bf16[256,256]{0,1:T(8,128)(2,1)S(1)} %copy.3, f32[257,256]{1,0:T(8,128)S(1)} %collective-permute-done.15, f32[256,256]{0,1:T(8,128)S(1)} %fusion.37, f32[256,256]{0,1:T(8,128)S(1)} %fusion.39, f32[256,256]{0,1:T(8,128)S(1)} %convolution_add_fusion.1, f32[257,256]{1,0:T(8,128)S(1)} %collective-permute-done.14, ...), kind=kOutput, calls=%fused_computation.58 | convolution fusion | flops 34275328 | bytes 2491392 | tf_op jit(solution)/shard_map/dot_general | solution.py:118
  104.1 0.8 copy.9
  (37 shorter events, 0.6 us)
Async XLA Ops:
  0.0 1.3 %copy-start.1 = (bf16[256,1024]{1,0:T(8,128)(2,1)S(1)}, bf16[256,1024]{1,0:T(8,128)(2,1)}, u32[]{:S(2)}) copy-start(bf16[256,1024]{1,0:T(8,128)(2,1)} %param.2) | copy-start | bytes 1572868
  1.3 0.9 copy-start
  2.5 18.9 %collective-permute-start = (bf16[264,1280]{1,0:T(8,128)(2,1)S(1)}, bf16[264,1280]{1,0:T(8,128)(2,1)}, u32[]{:S(2)}, u32[]{:S(2)}) collective-permute-start(bf16[264,1280]{1,0:T(8,128)(2,1)S(1)} %fusion.4), channel_id=1, source_target_pairs={{4,0},{8,4},{12,8},{16,12},{20,16},{24,20},{28,24},{5,1},{9,5},{13... | collective-permute-start | bytes 2027528 | tf_op jit(solution)/shard_map/ppermute | solution.py:12
  5.8 19.0 %collective-permute-start.1 = (bf16[264,1280]{1,0:T(8,128)(2,1)S(1)}, bf16[264,1280]{1,0:T(8,128)(2,1)S(1)}, u32[]{:S(2)}, u32[]{:S(2)}) collective-permute-start(bf16[264,1280]{1,0:T(8,128)(2,1)S(1)} %fusion.4), channel_id=1, source_target_pairs={{0,8},{4,12},{8,16},{12,20},{16,24},{20,28},{1,9},{5,13},{9,17},{1... | collective-permute-start | bytes 2027528 | tf_op jit(solution)/shard_map/ppermute | solution.py:12
  7.1 27.6 %collective-permute-start.8 = (bf16[264,1280]{1,0:T(8,128)(2,1)S(1)}, bf16[264,1280]{1,0:T(8,128)(2,1)}, u32[]{:S(2)}, u32[]{:S(2)}) collective-permute-start(bf16[264,1280]{1,0:T(8,128)(2,1)S(1)} %fusion.4), channel_id=1, source_target_pairs={{12,0},{16,4},{20,8},{24,12},{28,16},{13,1},{17,5},{21,9},{25,13},... | collective-permute-start | bytes 2027528 | tf_op jit(solution)/shard_map/ppermute | solution.py:12
  12.5 40.8 %collective-permute-start.9 = (bf16[264,1280]{1,0:T(8,128)(2,1)S(1)}, bf16[264,1280]{1,0:T(8,128)(2,1)}, u32[]{:S(2)}, u32[]{:S(2)}) collective-permute-start(bf16[264,1280]{1,0:T(8,128)(2,1)S(1)} %fusion.4), channel_id=1, source_target_pairs={{0,16},{4,20},{8,24},{12,28},{1,17},{5,21},{9,25},{13,29},{2,18},{... | collective-permute-start | bytes 2027528 | tf_op jit(solution)/shard_map/ppermute | solution.py:12
  24.8 30.7 %copy-start.2 = (bf16[264,1280]{1,0:T(8,128)(2,1)}, bf16[264,1280]{1,0:T(8,128)(2,1)S(1)}, u32[]{:S(2)}) copy-start(bf16[264,1280]{1,0:T(8,128)(2,1)S(1)} %collective-permute-done.1) | copy-start | bytes 2027524
  59.0 1.6 %collective-permute-start.10 = (f32[2,264,128]{2,1,0:T(8,128)S(1)}, f32[2,264,128]{2,1,0:T(8,128)S(1)}, u32[]{:S(2)}, u32[]{:S(2)}) collective-permute-start(f32[2,264,128]{2,1,0:T(8,128)S(1)} %fusion.13), channel_id=1, source_target_pairs={{0,1},{1,0},{2,3},{3,2},{4,5},{5,4},{6,7},{7,6},{8,9},{9,8},{10,11... | collective-permute-start | bytes 811016 | tf_op jit(solution)/shard_map/ppermute | solution.py:17
  59.2 3.1 %collective-permute-start.2 = (f32[3,264,128]{2,1,0:T(8,128)S(1)}, f32[3,264,128]{2,1,0:T(8,128)S(1)}, u32[]{:S(2)}, u32[]{:S(2)}) collective-permute-start(f32[3,264,128]{2,1,0:T(8,128)S(1)} %constant_dynamic-slice_fusion.2), channel_id=1, source_target_pairs={{0,1},{1,0},{2,3},{3,2},{4,5},{5,4},{6,7},{7,6},{8,9},{9,8},{10,11... | collective-permute-start | bytes 1216520 | tf_op jit(solution)/shard_map/ppermute | solution.py:17
  60.7 6.6 %collective-permute-start.11 = (f32[2,132,128]{2,1,0:T(8,128)S(1)}, f32[2,132,128]{2,1,0:T(8,128)S(1)}, u32[]{:S(2)}, u32[]{:S(2)}) collective-permute-start(f32[2,132,128]{2,1,0:T(8,128)S(1)} %constant_dynamic-slice_fusion), channel_id=1, source_target_pairs={{0,2},{1,3},{2,0},{3,1},{4,6},{5,7},{6,4},{7,5},{8,10},{9,11},{10,... | collective-permute-start | bytes 405512 | tf_op jit(solution)/shard_map/ppermute | solution.py:17
  62.3 9.4 %collective-permute-start.3 = (f32[3,132,128]{2,1,0:T(8,128)S(1)}, f32[3,132,128]{2,1,0:T(8,128)S(1)}, u32[]{:S(2)}, u32[]{:S(2)}) collective-permute-start(f32[3,132,128]{2,1,0:T(8,128)S(1)} %constant_dynamic-slice_fusion.1), channel_id=1, source_target_pairs={{0,2},{1,3},{2,0},{3,1},{4,6},{5,7},{6,4},{7,5},{8,10},{9,11},{10,... | collective-permute-start | bytes 608264 | tf_op jit(solution)/shard_map/ppermute | solution.py:17
  67.3 7.4 %collective-permute-start.12 = (f32[2,132,128]{2,1,0:T(8,128)S(1)}, f32[2,132,128]{2,1,0:T(8,128)S(1)}, u32[]{:S(2)}, u32[]{:S(2)}) collective-permute-start(f32[2,132,128]{2,1,0:T(8,128)S(1)} %dynamic-slice_add_fusion.2), channel_id=1, source_target_pairs={{0,2},{1,3},{2,0},{3,1},{4,6},{5,7},{6,4},{7,5},{8,10},{9,11},{10,... | collective-permute-start | bytes 405512 | tf_op jit(solution)/shard_map/ppermute | solution.py:17
  71.8 6.6 %collective-permute-start.4 = (f32[3,132,128]{2,1,0:T(8,128)S(1)}, f32[3,132,128]{2,1,0:T(8,128)S(1)}, u32[]{:S(2)}, u32[]{:S(2)}) collective-permute-start(f32[3,132,128]{2,1,0:T(8,128)S(1)} %dynamic-slice_add_fusion.1), channel_id=1, source_target_pairs={{0,2},{1,3},{2,0},{3,1},{4,6},{5,7},{6,4},{7,5},{8,10},{9,11},{10,... | collective-permute-start | bytes 608264 | tf_op jit(solution)/shard_map/ppermute | solution.py:17
  74.8 3.8 %collective-permute-start.13 = (f32[2,264,128]{2,1,0:T(8,128)S(1)}, f32[2,264,128]{2,1,0:T(8,128)S(1)}, u32[]{:S(2)}, u32[]{:S(2)}) collective-permute-start(f32[2,264,128]{2,1,0:T(8,128)S(1)} %pad_maximum_fusion.5), channel_id=1, source_target_pairs={{0,1},{1,0},{2,3},{3,2},{4,5},{5,4},{6,7},{7,6},{8,9},{9,8},{10,11... | collective-permute-start | bytes 811016 | tf_op jit(solution)/shard_map/ppermute | solution.py:17
  78.5 1.8 %collective-permute-start.5 = (f32[3,264,128]{2,1,0:T(8,128)S(1)}, f32[3,264,128]{2,1,0:T(8,128)S(1)}, u32[]{:S(2)}, u32[]{:S(2)}) collective-permute-start(f32[3,264,128]{2,1,0:T(8,128)S(1)} %pad_maximum_fusion.2), channel_id=1, source_target_pairs={{0,1},{1,0},{2,3},{3,2},{4,5},{5,4},{6,7},{7,6},{8,9},{9,8},{10,11... | collective-permute-start | bytes 1216520 | tf_op jit(solution)/shard_map/ppermute | solution.py:17
  80.9 14.0 %collective-permute-start.15 = (f32[257,256]{1,0:T(8,128)S(1)}, f32[257,256]{1,0:T(8,128)S(1)}, u32[]{:S(2)}, u32[]{:S(2)}) collective-permute-start(f32[257,256]{1,0:T(8,128)S(1)} %pad_maximum_fusion.7), channel_id=1, source_target_pairs={{16,0},{20,4},{24,8},{28,12},{17,1},{21,5},{25,9},{29,13},{18,2},{... | collective-permute-start | bytes 789512 | tf_op jit(solution)/shard_map/ppermute | solution.py:12
  82.5 14.8 %collective-permute-start.14 = (f32[257,256]{1,0:T(8,128)S(1)}, f32[257,256]{1,0:T(8,128)S(1)}, u32[]{:S(2)}, u32[]{:S(2)}) collective-permute-start(f32[257,256]{1,0:T(8,128)S(1)} %pad_maximum_fusion.6), channel_id=1, source_target_pairs={{0,12},{4,16},{8,20},{12,24},{16,28},{1,13},{5,17},{9,21},{13,25},... | collective-permute-start | bytes 789512 | tf_op jit(solution)/shard_map/ppermute | solution.py:12
  84.3 12.9 %collective-permute-start.7 = (f32[257,256]{1,0:T(8,128)S(1)}, f32[257,256]{1,0:T(8,128)S(1)}, u32[]{:S(2)}, u32[]{:S(2)}) collective-permute-start(f32[257,256]{1,0:T(8,128)S(1)} %pad_maximum_fusion.4), channel_id=1, source_target_pairs={{8,0},{12,4},{16,8},{20,12},{24,16},{28,20},{9,1},{13,5},{17,9},{2... | collective-permute-start | bytes 789512 | tf_op jit(solution)/shard_map/ppermute | solution.py:12
  89.2 13.7 %collective-permute-start.6 = (f32[257,256]{1,0:T(8,128)S(1)}, f32[257,256]{1,0:T(8,128)S(1)}, u32[]{:S(2)}, u32[]{:S(2)}) collective-permute-start(f32[257,256]{1,0:T(8,128)S(1)} %pad_maximum_fusion.3), channel_id=1, source_target_pairs={{0,4},{4,8},{8,12},{12,16},{16,20},{20,24},{24,28},{1,5},{5,9},{9,... | collective-permute-start | bytes 789512 | tf_op jit(solution)/shard_map/ppermute | solution.py:12

commit v11 on v8

--- a/solution.py
+++ b/solution.py
@@ -2,6 +2,7 @@
 import jax.numpy as jnp
 from jax import lax
 from jax.sharding import PartitionSpec as P
+
 
 REACH = 4
 
@@ -56,7 +57,7 @@
     return (rows[0] + rows[1]) + rows[2]
 
 
-def body(teacher, student):
+def layer(teacher, student):
     group = lax.axis_size("batch")
     owner = lax.axis_index("batch")
     width = lax.axis_size("width")
@@ -90,9 +91,10 @@
 
     pad = (-(rows_dev + 1)) % 8
 
-    def tile_part(d):
+    def tile_part(d, near):
         g = lax.dot_general(scaled, rhs_band[d], (((1,), (1,)), ((), ())), preferred_element_type=jnp.float32)
-        return jnp.concatenate([g, q_band[d][None, :], jnp.zeros((pad, rows_dev), jnp.float32)], axis=0)
+        rows = jnp.zeros((pad + (0 if near else 8), rows_dev), jnp.float32)
+        return jnp.concatenate([g, q_band[d][None, :], rows], axis=0)
 
     student_f = student.astype(jnp.float32)
     row_total = jnp.zeros((rows_dev,), jnp.float32)
@@ -102,7 +104,8 @@
     for group_idx in ([list(range(split)), list(range(split, len(offsets)))]):
         if not group_idx:
             continue
-        total = width_sum(jnp.stack([tile_part(d) for d in group_idx]))
+        near = group_idx[0] == 0
+        total = width_sum(jnp.stack([tile_part(d, near) for d in group_idx]))
         if own_q is None:
             own_q = total[0, rows_dev, :]
         for k, d in enumerate(group_idx):
@@ -132,4 +135,4 @@
 def solution(mesh):
     in_specs = (P("batch", "width"), P("batch", "width"))
     out_specs = P("batch", "width")
-    return jax.shard_map(body, mesh=mesh, in_specs=in_specs, out_specs=out_specs, check_vma=False)
+    return jax.shard_map(layer, mesh=mesh, in_specs=in_specs, out_specs=out_specs, check_vma=False)

time: 104 us -> 107 us (1.029)
  waiting for transfers between devices: 61.2 us -> 47.3 us
  starting transfers between devices: 26.4 us -> 39.9 us
  matrix products: 9.42 us -> 11.4 us
    ppermute x8, starting transfers between devices: 20.4 us -> 33.4 us  [shifted(): return lax.ppermute(block, axis, route)]
    ppermute x8, waiting for transfers between devices: 46.6 us -> 34.2 us  [shifted(): return lax.ppermute(block, axis, route)]
    ppermute x8, waiting for transfers between devices: 14.7 us -> 13.2 us  [swapped(): return lax.ppermute(block, axis, [(i, i ^ mask) for i in range(size)])]
    dot_general x5, matrix products: 4.02 us -> 5.1 us  [tile_part(): lax.dot_general(scaled, rhs_band[d], (((1,), (1,)), ((), ())), preferred_...]
  transfers between devices with their start and end apart: 16 -> 16, of which waited for: 12 -> 9; matrix products, arithmetic and copies ran while one was open for 6% -> 12% of each run, Pallas kernels for 0% -> 0%
where the time goes in v11:
time: 107 us; the launch traced here: 106 us
  waiting for transfers between devices  47.3 us (44%)
  starting transfers between devices  39.9 us (37%)
  matrix products  11.4 us (11%)
  other arithmetic  5.01 us (5%)
  local copies, waits for them, and re-layouts  1.48 us (1%)
    ppermute x8, waiting for transfers between devices, shifted(): return lax.ppermute(block, axis, route)  34.2 us
    ppermute x8, starting transfers between devices, shifted(): return lax.ppermute(block, axis, route)  33.4 us
    ppermute x8, waiting for transfers between devices, swapped(): return lax.ppermute(block, axis, [(i, i ^ mask) for i in range(size)])  13.2 us
    ppermute x8, starting transfers between devices, swapped(): return lax.ppermute(block, axis, [(i, i ^ mask) for i in range(size)])  6.48 us
    dot_general x5, matrix products, layer(): jnp.dot(low, student_band[d], preferred_element_type=jnp.float32)  5.4 us
    dot_general x5, matrix products, tile_part(): lax.dot_general(scaled, rhs_band[d], (((1,), (1,)), ((), ())), preferred_...  5.1 us
  transfers between devices with their start and end apart: 16, of which 9 were waited for; matrix products, arithmetic and copies ran while one was open for 12% of the time, Pallas kernels for 0%

profile of v11, /device:TPU:24, one launch (start us, length us, event | category | flops | bytes accessed | tf_op | source)
XLA Modules:
  0.0 105.7 jit_solution(2022013712173368736)
XLA Ops:
  0.0 1.3 %multiply_reduce_fusion = f32[256]{0:T(256)S(1)} fusion(bf16[256,1024]{1,0:T(8,128)(2,1)} %param.2), kind=kLoop, calls=%fused_computation.18 | loop fusion | flops 786176 | bytes 525312 | tf_op jit(solution)/shard_map/reduce_sum | solution.py:74
  1.3 0.0 copy-start
  1.3 0.1 broadcast_multiply_fusion
  1.4 0.8 copy-done
  2.2 0.1 fusion.20
  2.5 1.3 %collective-permute-start.9 = (bf16[264,1280]{1,0:T(8,128)(2,1)S(1)}, bf16[264,1280]{1,0:T(8,128)(2,1)S(1)}, u32[]{:S(2)}, u32[]{:S(2)}) collective-permute-start(bf16[264,1280]{1,0:T(8,128)(2,1)S(1)} %fusion.8), channel_id=1, source_target_pairs={{0,16},{4,20},{8,24},{12,28},{1,17},{5,21},{9,25},{13,29},{2,18},{... | collective-permute-start | bytes 2027528 | tf_op jit(solution)/shard_map/ppermute | solution.py:13
  3.8 7.3 %collective-permute-start.8 = (bf16[264,1280]{1,0:T(8,128)(2,1)S(1)}, bf16[264,1280]{1,0:T(8,128)(2,1)}, u32[]{:S(2)}, u32[]{:S(2)}) collective-permute-start(bf16[264,1280]{1,0:T(8,128)(2,1)S(1)} %fusion.8), channel_id=1, source_target_pairs={{12,0},{16,4},{20,8},{24,12},{28,16},{13,1},{17,5},{21,9},{25,13},... | collective-permute-start | bytes 2027528 | tf_op jit(solution)/shard_map/ppermute | solution.py:13
  11.1 2.4 %collective-permute-start = (bf16[264,1280]{1,0:T(8,128)(2,1)S(1)}, bf16[264,1280]{1,0:T(8,128)(2,1)}, u32[]{:S(2)}, u32[]{:S(2)}) collective-permute-start(bf16[264,1280]{1,0:T(8,128)(2,1)S(1)} %fusion.8), channel_id=1, source_target_pairs={{4,0},{8,4},{12,8},{16,12},{20,16},{24,20},{28,24},{5,1},{9,5},{13... | collective-permute-start | bytes 2027528 | tf_op jit(solution)/shard_map/ppermute | solution.py:13
  13.5 1.3 %collective-permute-start.1 = (bf16[264,1280]{1,0:T(8,128)(2,1)S(1)}, bf16[264,1280]{1,0:T(8,128)(2,1)}, u32[]{:S(2)}, u32[]{:S(2)}) collective-permute-start(bf16[264,1280]{1,0:T(8,128)(2,1)S(1)} %fusion.8), channel_id=1, source_target_pairs={{0,8},{4,12},{8,16},{12,20},{16,24},{20,28},{1,9},{5,13},{9,17},{1... | collective-permute-start | bytes 2027528 | tf_op jit(solution)/shard_map/ppermute | solution.py:13
  14.8 0.1 pad.17.clone
  14.9 0.1 pad.42.clone
  15.0 0.4 fusion.72
  15.3 21.3 %collective-permute-done.9 = bf16[264,1280]{1,0:T(8,128)(2,1)S(1)} collective-permute-done((bf16[264,1280]{1,0:T(8,128)(2,1)S(1)}, bf16[264,1280]{1,0:T(8,128)(2,1)S(1)}, u32[]{:S(2)}, u32[]{:S(2)}) %collective-permute-start.9) | collective-permute-done | bytes 675872 | tf_op jit(solution)/shard_map/ppermute | solution.py:13
  36.7 0.4 fusion.9
  37.1 0.5 copy-done.2
  37.5 0.0 collective-permute-done.8
  37.5 0.7 slice_convert_fusion.1
  38.2 1.5 %fusion.11 = f32[256,256]{1,0:T(8,128)S(1)} fusion(bf16[264,1280]{1,0:T(8,128)(2,1)} %collective-permute-done.8, bf16[256,256]{1,0:T(8,128)(2,1)S(1)} %get-tuple-element.39, bf16[256,1024]{1,0:T(8,128)(2,1)S(1)} %get-tuple-element.33), kind=kOutput, calls=%fused_computation.31 | convolution fusion | flops 169082880 | bytes 1572864 | tf_op jit(solution)/shard_map/dot_general | solution.py:95
  39.7 0.1 maximum_bitcast_fusion.1
  39.8 0.1 collective-permute-start.10
  39.9 0.0 collective-permute-done
  39.9 0.7 slice_convert_fusion.3
  40.6 5.3 %collective-permute-done.1 = bf16[264,1280]{1,0:T(8,128)(2,1)} collective-permute-done((bf16[264,1280]{1,0:T(8,128)(2,1)S(1)}, bf16[264,1280]{1,0:T(8,128)(2,1)}, u32[]{:S(2)}, u32[]{:S(2)}) %collective-permute-start.1) | collective-permute-done | bytes 675872 | tf_op jit(solution)/shard_map/ppermute | solution.py:13
  45.9 0.7 slice_convert_fusion.2
  46.6 1.5 %fusion.15 = f32[256,256]{1,0:T(8,128)S(1)} fusion(bf16[264,1280]{1,0:T(8,128)(2,1)} %collective-permute-done, bf16[256,256]{1,0:T(8,128)(2,1)S(1)} %get-tuple-element.39, bf16[256,1024]{1,0:T(8,128)(2,1)S(1)} %get-tuple-element.33), kind=kOutput, calls=%fused_computation.35 | convolution fusion | flops 169082880 | bytes 1572864 | tf_op jit(solution)/shard_map/dot_general | solution.py:95
  48.1 1.5 %fusion.13 = f32[256,256]{1,0:T(8,128)S(1)} fusion(bf16[264,1280]{1,0:T(8,128)(2,1)} %collective-permute-done.1, bf16[256,256]{1,0:T(8,128)(2,1)S(1)} %get-tuple-element.39, bf16[256,1024]{1,0:T(8,128)(2,1)S(1)} %get-tuple-element.33), kind=kOutput, calls=%fused_computation.33 | convolution fusion | flops 169082880 | bytes 1572864 | tf_op jit(solution)/shard_map/dot_general | solution.py:95
  49.5 0.1 maximum_bitcast_fusion.2
  49.7 0.1 pad_maximum_fusion
  49.8 0.1 collective-permute-start.2
  49.9 0.0 collective-permute-done.10
  50.0 1.5 %collective-permute-start.11 = (f32[2,136,128]{2,1,0:T(8,128)S(1)}, f32[2,136,128]{2,1,0:T(8,128)S(1)}, u32[]{:S(2)}, u32[]{:S(2)}) collective-permute-start(f32[2,136,128]{2,1,0:T(8,128)S(1)} %constant_dynamic-slice_fusion), channel_id=1, source_target_pairs={{0,2},{1,3},{2,0},{3,1},{4,6},{5,7},{6,4},{7,5},{8,10},{9,11},{10,... | collective-permute-start | bytes 417800 | tf_op jit(solution)/shard_map/ppermute | solution.py:18
  51.6 0.0 collective-permute-done.2
  51.6 0.1 dynamic-slice_add_fusion
  51.7 1.5 %collective-permute-start.3 = (f32[3,132,128]{2,1,0:T(8,128)S(1)}, f32[3,132,128]{2,1,0:T(8,128)S(1)}, u32[]{:S(2)}, u32[]{:S(2)}) collective-permute-start(f32[3,132,128]{2,1,0:T(8,128)S(1)} %constant_dynamic-slice_fusion.1), channel_id=1, source_target_pairs={{0,2},{1,3},{2,0},{3,1},{4,6},{5,7},{6,4},{7,5},{8,10},{9,11},{10,... | collective-permute-start | bytes 608264 | tf_op jit(solution)/shard_map/ppermute | solution.py:18
  53.2 3.4 %collective-permute-done.11 = f32[2,136,128]{2,1,0:T(8,128)S(1)} collective-permute-done((f32[2,136,128]{2,1,0:T(8,128)S(1)}, f32[2,136,128]{2,1,0:T(8,128)S(1)}, u32[]{:S(2)}, u32[]{:S(2)}) %collective-permute-start.11) | collective-permute-done | bytes 139296 | tf_op jit(solution)/shard_map/ppermute | solution.py:18
  56.6 1.5 %collective-permute-start.12 = (f32[2,136,128]{2,1,0:T(8,128)S(1)}, f32[2,136,128]{2,1,0:T(8,128)S(1)}, u32[]{:S(2)}, u32[]{:S(2)}) collective-permute-start(f32[2,136,128]{2,1,0:T(8,128)S(1)} %dynamic-slice_add_fusion.2), channel_id=1, source_target_pairs={{0,2},{1,3},{2,0},{3,1},{4,6},{5,7},{6,4},{7,5},{8,10},{9,11},{10,... | collective-permute-start | bytes 417800 | tf_op jit(solution)/shard_map/ppermute | solution.py:18
  58.2 2.9 %collective-permute-done.3 = f32[3,132,128]{2,1,0:T(8,128)S(1)} collective-permute-done((f32[3,132,128]{2,1,0:T(8,128)S(1)}, f32[3,132,128]{2,1,0:T(8,128)S(1)}, u32[]{:S(2)}, u32[]{:S(2)}) %collective-permute-start.3) | collective-permute-done | bytes 202784 | tf_op jit(solution)/shard_map/ppermute | solution.py:18
  61.1 1.5 %collective-permute-start.4 = (f32[3,132,128]{2,1,0:T(8,128)S(1)}, f32[3,132,128]{2,1,0:T(8,128)S(1)}, u32[]{:S(2)}, u32[]{:S(2)}) collective-permute-start(f32[3,132,128]{2,1,0:T(8,128)S(1)} %dynamic-slice_add_fusion.1), channel_id=1, source_target_pairs={{0,2},{1,3},{2,0},{3,1},{4,6},{5,7},{6,4},{7,5},{8,10},{9,11},{10,... | collective-permute-start | bytes 608264 | tf_op jit(solution)/shard_map/ppermute | solution.py:18
  62.7 1.4 %collective-permute-done.12 = f32[2,136,128]{2,1,0:T(8,128)S(1)} collective-permute-done((f32[2,136,128]{2,1,0:T(8,128)S(1)}, f32[2,136,128]{2,1,0:T(8,128)S(1)}, u32[]{:S(2)}, u32[]{:S(2)}) %collective-permute-start.12) | collective-permute-done | bytes 139296 | tf_op jit(solution)/shard_map/ppermute | solution.py:18
  64.1 0.1 collective-permute-start.13
  64.2 3.8 %collective-permute-done.4 = f32[3,132,128]{2,1,0:T(8,128)S(1)} collective-permute-done((f32[3,132,128]{2,1,0:T(8,128)S(1)}, f32[3,132,128]{2,1,0:T(8,128)S(1)}, u32[]{:S(2)}, u32[]{:S(2)}) %collective-permute-start.4) | collective-permute-done | bytes 202784 | tf_op jit(solution)/shard_map/ppermute | solution.py:18
  68.1 0.1 collective-permute-start.5
  68.2 0.0 collective-permute-done.13
  68.3 1.6 %collective-permute-done.5 = f32[3,264,128]{2,1,0:T(8,128)S(1)} collective-permute-done((f32[3,264,128]{2,1,0:T(8,128)S(1)}, f32[3,264,128]{2,1,0:T(8,128)S(1)}, u32[]{:S(2)}, u32[]{:S(2)}) %collective-permute-start.5) | collective-permute-done | bytes 405536 | tf_op jit(solution)/shard_map/ppermute | solution.py:18
  69.9 0.1 broadcast_select_fusion.1
  70.0 0.3 fusion.75
  70.2 0.2 fusion.50
  70.5 6.6 %collective-permute-start.15 = (f32[257,256]{1,0:T(8,128)S(1)}, f32[257,256]{1,0:T(8,128)S(1)}, u32[]{:S(2)}, u32[]{:S(2)}) collective-permute-start(f32[257,256]{1,0:T(8,128)S(1)} %pad_maximum_fusion.7), channel_id=1, source_target_pairs={{16,0},{20,4},{24,8},{28,12},{17,1},{21,5},{25,9},{29,13},{18,2},{... | collective-permute-start | bytes 789512 | tf_op jit(solution)/shard_map/ppermute | solution.py:13
  77.1 0.2 fusion.53
  77.4 1.3 %collective-permute-start.14 = (f32[257,256]{1,0:T(8,128)S(1)}, f32[257,256]{1,0:T(8,128)S(1)}, u32[]{:S(2)}, u32[]{:S(2)}) collective-permute-start(f32[257,256]{1,0:T(8,128)S(1)} %pad_maximum_fusion.6), channel_id=1, source_target_pairs={{0,12},{4,16},{8,20},{12,24},{16,28},{1,13},{5,17},{9,21},{13,25},... | collective-permute-start | bytes 789512 | tf_op jit(solution)/shard_map/ppermute | solution.py:13
  78.7 0.3 fusion.73
  78.9 0.2 fusion.56
  79.2 11.3 %collective-permute-start.7 = (f32[257,256]{1,0:T(8,128)S(1)}, f32[257,256]{1,0:T(8,128)S(1)}, u32[]{:S(2)}, u32[]{:S(2)}) collective-permute-start(f32[257,256]{1,0:T(8,128)S(1)} %pad_maximum_fusion.5), channel_id=1, source_target_pairs={{8,0},{12,4},{16,8},{20,12},{24,16},{28,20},{9,1},{13,5},{17,9},{2... | collective-permute-start | bytes 789512 | tf_op jit(solution)/shard_map/ppermute | solution.py:13
  90.5 0.2 fusion.59
  90.8 1.9 %collective-permute-start.6 = (f32[257,256]{1,0:T(8,128)S(1)}, f32[257,256]{1,0:T(8,128)S(1)}, u32[]{:S(2)}, u32[]{:S(2)}) collective-permute-start(f32[257,256]{1,0:T(8,128)S(1)} %pad_maximum_fusion.4), channel_id=1, source_target_pairs={{0,4},{4,8},{8,12},{12,16},{16,20},{20,24},{24,28},{1,5},{5,9},{9,... | collective-permute-start | bytes 789512 | tf_op jit(solution)/shard_map/ppermute | solution.py:13
  92.7 1.1 %fusion.40 = f32[256,256]{1,0:T(8,128)S(1)} fusion(bf16[264,1280]{1,0:T(8,128)(2,1)} %copy-done.2, bf16[256,256]{1,0:T(8,128)(2,1)S(1)} %get-tuple-element.28), kind=kOutput, calls=%fused_computation.84 | convolution fusion | flops 33554432 | bytes 524288 | tf_op jit(solution)/shard_map/dot_general | solution.py:119
  93.8 1.1 %fusion.42 = f32[256,256]{1,0:T(8,128)S(1)} fusion(bf16[264,1280]{1,0:T(8,128)(2,1)} %collective-permute-done.8, bf16[256,256]{1,0:T(8,128)(2,1)S(1)} %get-tuple-element.15), kind=kOutput, calls=%fused_computation.86 | convolution fusion | flops 33554432 | bytes 524288 | tf_op jit(solution)/shard_map/dot_general | solution.py:119
  94.9 0.2 fusion.47
  95.1 1.1 %fusion.44 = f32[256,256]{1,0:T(8,128)S(1)} fusion(bf16[264,1280]{1,0:T(8,128)(2,1)} %collective-permute-done.1, bf16[256,256]{1,0:T(8,128)(2,1)S(1)} %get-tuple-element.20), kind=kOutput, calls=%fused_computation.88 | convolution fusion | flops 33554432 | bytes 524288 | tf_op jit(solution)/shard_map/dot_general | solution.py:119
  96.2 0.0 collective-permute-done.15
  96.3 1.9 %collective-permute-done.14 = f32[257,256]{1,0:T(8,128)S(1)} collective-permute-done((f32[257,256]{1,0:T(8,128)S(1)}, f32[257,256]{1,0:T(8,128)S(1)}, u32[]{:S(2)}, u32[]{:S(2)}) %collective-permute-start.14) | collective-permute-done | bytes 263200 | tf_op jit(solution)/shard_map/ppermute | solution.py:13
  98.2 0.0 collective-permute-done.7
  98.2 5.6 %collective-permute-done.6 = f32[257,256]{1,0:T(8,128)S(1)} collective-permute-done((f32[257,256]{1,0:T(8,128)S(1)}, f32[257,256]{1,0:T(8,128)S(1)}, u32[]{:S(2)}, u32[]{:S(2)}) %collective-permute-start.6) | collective-permute-done | bytes 263200 | tf_op jit(solution)/shard_map/ppermute | solution.py:13
  103.8 1.9 %fusion.22 = f32[256,256]{1,0:T(8,128)} fusion(bf16[256,256]{1,0:T(8,128)(2,1)S(1)} %copy-done, f32[257,256]{1,0:T(8,128)S(1)} %collective-permute-done.15, f32[256,256]{1,0:T(8,128)S(1)} %fusion.40, f32[256,256]{1,0:T(8,128)S(1)} %fusion.42, f32[256,256]{1,0:T(8,128)S(1)} %fusion.44, f32[256,256]{1,0:T(8,128)S(1)} %fusion.47, ...), kind=kOutput, calls=%fused_computation.57 | convolution fusion | flops 34340864 | bytes 2753536 | tf_op jit(solution)/shard_map/dot_general | solution.py:119
  (38 shorter events, 0.6 us)
Async XLA Ops:
  0.0 1.3 %copy-start.1 = (bf16[256,1024]{1,0:T(8,128)(2,1)S(1)}, bf16[256,1024]{1,0:T(8,128)(2,1)}, u32[]{:S(2)}) copy-start(bf16[256,1024]{1,0:T(8,128)(2,1)} %param.2) | copy-start | bytes 1572868
  1.3 0.9 copy-start
  2.5 34.2 %collective-permute-start.9 = (bf16[264,1280]{1,0:T(8,128)(2,1)S(1)}, bf16[264,1280]{1,0:T(8,128)(2,1)S(1)}, u32[]{:S(2)}, u32[]{:S(2)}) collective-permute-start(bf16[264,1280]{1,0:T(8,128)(2,1)S(1)} %fusion.8), channel_id=1, source_target_pairs={{0,16},{4,20},{8,24},{12,28},{1,17},{5,21},{9,25},{13,29},{2,18},{... | collective-permute-start | bytes 2027528 | tf_op jit(solution)/shard_map/ppermute | solution.py:13
  3.8 33.8 %collective-permute-start.8 = (bf16[264,1280]{1,0:T(8,128)(2,1)S(1)}, bf16[264,1280]{1,0:T(8,128)(2,1)}, u32[]{:S(2)}, u32[]{:S(2)}) collective-permute-start(bf16[264,1280]{1,0:T(8,128)(2,1)S(1)} %fusion.8), channel_id=1, source_target_pairs={{12,0},{16,4},{20,8},{24,12},{28,16},{13,1},{17,5},{21,9},{25,13},... | collective-permute-start | bytes 2027528 | tf_op jit(solution)/shard_map/ppermute | solution.py:13
  11.1 28.8 %collective-permute-start = (bf16[264,1280]{1,0:T(8,128)(2,1)S(1)}, bf16[264,1280]{1,0:T(8,128)(2,1)}, u32[]{:S(2)}, u32[]{:S(2)}) collective-permute-start(bf16[264,1280]{1,0:T(8,128)(2,1)S(1)} %fusion.8), channel_id=1, source_target_pairs={{4,0},{8,4},{12,8},{16,12},{20,16},{24,20},{28,24},{5,1},{9,5},{13... | collective-permute-start | bytes 2027528 | tf_op jit(solution)/shard_map/ppermute | solution.py:13
  13.5 32.5 %collective-permute-start.1 = (bf16[264,1280]{1,0:T(8,128)(2,1)S(1)}, bf16[264,1280]{1,0:T(8,128)(2,1)}, u32[]{:S(2)}, u32[]{:S(2)}) collective-permute-start(bf16[264,1280]{1,0:T(8,128)(2,1)S(1)} %fusion.8), channel_id=1, source_target_pairs={{0,8},{4,12},{8,16},{12,20},{16,24},{20,28},{1,9},{5,13},{9,17},{1... | collective-permute-start | bytes 2027528 | tf_op jit(solution)/shard_map/ppermute | solution.py:13
  36.7 0.8 copy-start.2
  39.8 10.1 %collective-permute-start.10 = (f32[2,272,128]{2,1,0:T(8,128)S(1)}, f32[2,272,128]{2,1,0:T(8,128)S(1)}, u32[]{:S(2)}, u32[]{:S(2)}) collective-permute-start(f32[2,272,128]{2,1,0:T(8,128)S(1)} %fusion.17), channel_id=1, source_target_pairs={{0,1},{1,0},{2,3},{3,2},{4,5},{5,4},{6,7},{7,6},{8,9},{9,8},{10,11... | collective-permute-start | bytes 835592 | tf_op jit(solution)/shard_map/ppermute | solution.py:18
  49.8 1.8 %collective-permute-start.2 = (f32[3,264,128]{2,1,0:T(8,128)S(1)}, f32[3,264,128]{2,1,0:T(8,128)S(1)}, u32[]{:S(2)}, u32[]{:S(2)}) collective-permute-start(f32[3,264,128]{2,1,0:T(8,128)S(1)} %constant_dynamic-slice_fusion.2), channel_id=1, source_target_pairs={{0,1},{1,0},{2,3},{3,2},{4,5},{5,4},{6,7},{7,6},{8,9},{9,8},{10,11... | collective-permute-start | bytes 1216520 | tf_op jit(solution)/shard_map/ppermute | solution.py:18
  50.0 6.6 %collective-permute-start.11 = (f32[2,136,128]{2,1,0:T(8,128)S(1)}, f32[2,136,128]{2,1,0:T(8,128)S(1)}, u32[]{:S(2)}, u32[]{:S(2)}) collective-permute-start(f32[2,136,128]{2,1,0:T(8,128)S(1)} %constant_dynamic-slice_fusion), channel_id=1, source_target_pairs={{0,2},{1,3},{2,0},{3,1},{4,6},{5,7},{6,4},{7,5},{8,10},{9,11},{10,... | collective-permute-start | bytes 417800 | tf_op jit(solution)/shard_map/ppermute | solution.py:18
  51.7 9.4 %collective-permute-start.3 = (f32[3,132,128]{2,1,0:T(8,128)S(1)}, f32[3,132,128]{2,1,0:T(8,128)S(1)}, u32[]{:S(2)}, u32[]{:S(2)}) collective-permute-start(f32[3,132,128]{2,1,0:T(8,128)S(1)} %constant_dynamic-slice_fusion.1), channel_id=1, source_target_pairs={{0,2},{1,3},{2,0},{3,1},{4,6},{5,7},{6,4},{7,5},{8,10},{9,11},{10,... | collective-permute-start | bytes 608264 | tf_op jit(solution)/shard_map/ppermute | solution.py:18
  56.6 7.4 %collective-permute-start.12 = (f32[2,136,128]{2,1,0:T(8,128)S(1)}, f32[2,136,128]{2,1,0:T(8,128)S(1)}, u32[]{:S(2)}, u32[]{:S(2)}) collective-permute-start(f32[2,136,128]{2,1,0:T(8,128)S(1)} %dynamic-slice_add_fusion.2), channel_id=1, source_target_pairs={{0,2},{1,3},{2,0},{3,1},{4,6},{5,7},{6,4},{7,5},{8,10},{9,11},{10,... | collective-permute-start | bytes 417800 | tf_op jit(solution)/shard_map/ppermute | solution.py:18
  61.1 6.9 %collective-permute-start.4 = (f32[3,132,128]{2,1,0:T(8,128)S(1)}, f32[3,132,128]{2,1,0:T(8,128)S(1)}, u32[]{:S(2)}, u32[]{:S(2)}) collective-permute-start(f32[3,132,128]{2,1,0:T(8,128)S(1)} %dynamic-slice_add_fusion.1), channel_id=1, source_target_pairs={{0,2},{1,3},{2,0},{3,1},{4,6},{5,7},{6,4},{7,5},{8,10},{9,11},{10,... | collective-permute-start | bytes 608264 | tf_op jit(solution)/shard_map/ppermute | solution.py:18
  64.1 4.1 %collective-permute-start.13 = (f32[2,272,128]{2,1,0:T(8,128)S(1)}, f32[2,272,128]{2,1,0:T(8,128)S(1)}, u32[]{:S(2)}, u32[]{:S(2)}) collective-permute-start(f32[2,272,128]{2,1,0:T(8,128)S(1)} %pad_maximum_fusion.3), channel_id=1, source_target_pairs={{0,1},{1,0},{2,3},{3,2},{4,5},{5,4},{6,7},{7,6},{8,9},{9,8},{10,11... | collective-permute-start | bytes 835592 | tf_op jit(solution)/shard_map/ppermute | solution.py:18
  68.1 1.8 %collective-permute-start.5 = (f32[3,264,128]{2,1,0:T(8,128)S(1)}, f32[3,264,128]{2,1,0:T(8,128)S(1)}, u32[]{:S(2)}, u32[]{:S(2)}) collective-permute-start(f32[3,264,128]{2,1,0:T(8,128)S(1)} %pad_maximum_fusion.2), channel_id=1, source_target_pairs={{0,1},{1,0},{2,3},{3,2},{4,5},{5,4},{6,7},{7,6},{8,9},{9,8},{10,11... | collective-permute-start | bytes 1216520 | tf_op jit(solution)/shard_map/ppermute | solution.py:18
  70.5 25.7 %collective-permute-start.15 = (f32[257,256]{1,0:T(8,128)S(1)}, f32[257,256]{1,0:T(8,128)S(1)}, u32[]{:S(2)}, u32[]{:S(2)}) collective-permute-start(f32[257,256]{1,0:T(8,128)S(1)} %pad_maximum_fusion.7), channel_id=1, source_target_pairs={{16,0},{20,4},{24,8},{28,12},{17,1},{21,5},{25,9},{29,13},{18,2},{... | collective-permute-start | bytes 789512 | tf_op jit(solution)/shard_map/ppermute | solution.py:13
  77.4 20.8 %collective-permute-start.14 = (f32[257,256]{1,0:T(8,128)S(1)}, f32[257,256]{1,0:T(8,128)S(1)}, u32[]{:S(2)}, u32[]{:S(2)}) collective-permute-start(f32[257,256]{1,0:T(8,128)S(1)} %pad_maximum_fusion.6), channel_id=1, source_target_pairs={{0,12},{4,16},{8,20},{12,24},{16,28},{1,13},{5,17},{9,21},{13,25},... | collective-permute-start | bytes 789512 | tf_op jit(solution)/shard_map/ppermute | solution.py:13
  79.2 19.0 %collective-permute-start.7 = (f32[257,256]{1,0:T(8,128)S(1)}, f32[257,256]{1,0:T(8,128)S(1)}, u32[]{:S(2)}, u32[]{:S(2)}) collective-permute-start(f32[257,256]{1,0:T(8,128)S(1)} %pad_maximum_fusion.5), channel_id=1, source_target_pairs={{8,0},{12,4},{16,8},{20,12},{24,16},{28,20},{9,1},{13,5},{17,9},{2... | collective-permute-start | bytes 789512 | tf_op jit(solution)/shard_map/ppermute | solution.py:13
  90.8 13.0 %collective-permute-start.6 = (f32[257,256]{1,0:T(8,128)S(1)}, f32[257,256]{1,0:T(8,128)S(1)}, u32[]{:S(2)}, u32[]{:S(2)}) collective-permute-start(f32[257,256]{1,0:T(8,128)S(1)} %pad_maximum_fusion.4), channel_id=1, source_target_pairs={{0,4},{4,8},{8,12},{12,16},{16,20},{20,24},{24,28},{1,5},{5,9},{9,... | collective-permute-start | bytes 789512 | tf_op jit(solution)/shard_map/ppermute | solution.py:13

commit v12 on v11

--- a/solution.py
+++ b/solution.py
@@ -91,9 +91,9 @@
 
     pad = (-(rows_dev + 1)) % 8
 
-    def tile_part(d, near):
+    def tile_part(d):
         g = lax.dot_general(scaled, rhs_band[d], (((1,), (1,)), ((), ())), preferred_element_type=jnp.float32)
-        rows = jnp.zeros((pad + (0 if near else 8), rows_dev), jnp.float32)
+        rows = jnp.zeros((pad + (8 if d == 0 else 16 if d >= 3 else 0), rows_dev), jnp.float32)
         return jnp.concatenate([g, q_band[d][None, :], rows], axis=0)
 
     student_f = student.astype(jnp.float32)
@@ -101,11 +101,10 @@
     pulled = jnp.zeros(student.shape, jnp.float32)
     own_q = None
     split = min(3, len(offsets))
-    for group_idx in ([list(range(split)), list(range(split, len(offsets)))]):
+    for group_idx in ([[0], list(range(1, split)), list(range(split, len(offsets)))]):
         if not group_idx:
             continue
-        near = group_idx[0] == 0
-        total = width_sum(jnp.stack([tile_part(d, near) for d in group_idx]))
+        total = width_sum(jnp.stack([tile_part(d) for d in group_idx]))
         if own_q is None:
             own_q = total[0, rows_dev, :]
         for k, d in enumerate(group_idx):

time: 107 us -> 118 us (1.10)
  waiting for transfers between devices: 47.3 us -> 56.7 us
  starting transfers between devices: 39.9 us -> 43.3 us
    ppermute x8, waiting for transfers between devices: 34.2 us -> 40.8 us  [shifted(): return lax.ppermute(block, axis, route)]
    ppermute x8 -> x12, starting transfers between devices: 6.48 us -> 9.84 us  [swapped(): return lax.ppermute(block, axis, [(i, i ^ mask) for i in range(size)])]
    ppermute x8 -> x12, waiting for transfers between devices: 13.2 us -> 15.9 us  [swapped(): return lax.ppermute(block, axis, [(i, i ^ mask) for i in range(size)])]
  transfers between devices with their start and end apart: 16 -> 20, of which waited for: 9 -> 11; matrix products, arithmetic and copies ran while one was open for 12% -> 9% of each run, Pallas kernels for 0% -> 0%
where the time goes in v12:
time: 118 us; the launch traced here: 117 us
  waiting for transfers between devices  56.7 us (48%)
  starting transfers between devices  43.3 us (37%)
  matrix products  10.5 us (9%)
  other arithmetic  5.12 us (4%)
    ppermute x8, waiting for transfers between devices, shifted(): return lax.ppermute(block, axis, route)  40.8 us
    ppermute x8, starting transfers between devices, shifted(): return lax.ppermute(block, axis, route)  33.5 us
    ppermute x12, waiting for transfers between devices, swapped(): return lax.ppermute(block, axis, [(i, i ^ mask) for i in range(size)])  15.9 us
    ppermute x12, starting transfers between devices, swapped(): return lax.ppermute(block, axis, [(i, i ^ mask) for i in range(size)])  9.84 us
    dot_general x5, matrix products, tile_part(): lax.dot_general(scaled, rhs_band[d], (((1,), (1,)), ((), ())), preferred_...  5.1 us
    dot_general x5, matrix products, layer(): jnp.dot(low, student_band[d], preferred_element_type=jnp.float32)  4.51 us
  transfers between devices with their start and end apart: 20, of which 11 were waited for; matrix products, arithmetic and copies ran while one was open for 9% of the time, Pallas kernels for 0%

profile of v12, /device:TPU:24, one launch (start us, length us, event | category | flops | bytes accessed | tf_op | source)
XLA Modules:
  0.0 117.3 jit_solution(1451150647431120372)
XLA Ops:
  0.0 1.3 %multiply_reduce_fusion = f32[256]{0:T(256)S(1)} fusion(bf16[256,1024]{1,0:T(8,128)(2,1)} %param.2), kind=kLoop, calls=%fused_computation.10 | loop fusion | flops 786176 | bytes 525312 | tf_op jit(solution)/shard_map/reduce_sum | solution.py:74
  1.3 0.0 copy-start
  1.3 0.1 broadcast_multiply_fusion
  1.5 0.8 copy-done
  2.2 0.1 fusion.23
  2.4 0.1 pad.45.clone
  2.5 0.4 fusion.76
  2.8 0.1 maximum_maximum_fusion
  3.0 0.1 collective-permute-start
  3.1 1.3 %collective-permute-done = f32[1,272,128]{2,1,0:T(8,128)S(1)} collective-permute-done((f32[1,272,128]{2,1,0:T(8,128)S(1)}, f32[1,272,128]{2,1,0:T(8,128)S(1)}, u32[]{:S(2)}, u32[]{:S(2)}) %collective-permute-start) | collective-permute-done | bytes 139296 | tf_op jit(solution)/shard_map/ppermute | solution.py:18
  4.4 1.6 %collective-permute-start.1 = (f32[1,136,128]{2,1,0:T(8,128)S(1)}, f32[1,136,128]{2,1,0:T(8,128)S(1)}, u32[]{:S(2)}, u32[]{:S(2)}) collective-permute-start(f32[1,136,128]{2,1,0:T(8,128)S(1)} %constant_dynamic-slice_fusion.2), channel_id=1, source_target_pairs={{0,2},{1,3},{2,0},{3,1},{4,6},{5,7},{6,4},{7,5},{8,10},{9,11},{10,... | collective-permute-start | bytes 208904 | tf_op jit(solution)/shard_map/ppermute | solution.py:18
  6.0 2.8 %collective-permute-done.1 = f32[1,136,128]{2,1,0:T(8,128)S(1)} collective-permute-done((f32[1,136,128]{2,1,0:T(8,128)S(1)}, f32[1,136,128]{2,1,0:T(8,128)S(1)}, u32[]{:S(2)}, u32[]{:S(2)}) %collective-permute-start.1) | collective-permute-done | bytes 69664 | tf_op jit(solution)/shard_map/ppermute | solution.py:18
  8.8 1.6 %collective-permute-start.2 = (f32[1,136,128]{2,1,0:T(8,128)S(1)}, f32[1,136,128]{2,1,0:T(8,128)S(1)}, u32[]{:S(2)}, u32[]{:S(2)}) collective-permute-start(f32[1,136,128]{2,1,0:T(8,128)S(1)} %dynamic-slice_add_fusion.2), channel_id=1, source_target_pairs={{0,2},{1,3},{2,0},{3,1},{4,6},{5,7},{6,4},{7,5},{8,10},{9,11},{10,... | collective-permute-start | bytes 208904 | tf_op jit(solution)/shard_map/ppermute | solution.py:18
  10.4 2.8 %collective-permute-done.2 = f32[1,136,128]{2,1,0:T(8,128)S(1)} collective-permute-done((f32[1,136,128]{2,1,0:T(8,128)S(1)}, f32[1,136,128]{2,1,0:T(8,128)S(1)}, u32[]{:S(2)}, u32[]{:S(2)}) %collective-permute-start.2) | collective-permute-done | bytes 69664 | tf_op jit(solution)/shard_map/ppermute | solution.py:18
  13.2 0.1 collective-permute-start.3
  13.4 1.3 %collective-permute-start.13 = (bf16[264,1280]{1,0:T(8,128)(2,1)S(1)}, bf16[264,1280]{1,0:T(8,128)(2,1)}, u32[]{:S(2)}, u32[]{:S(2)}) collective-permute-start(bf16[264,1280]{1,0:T(8,128)(2,1)S(1)} %fusion.8), channel_id=1, source_target_pairs={{0,16},{4,20},{8,24},{12,28},{1,17},{5,21},{9,25},{13,29},{2,18},{... | collective-permute-start | bytes 2027528 | tf_op jit(solution)/shard_map/ppermute | solution.py:13
  14.7 8.1 %collective-permute-start.12 = (bf16[264,1280]{1,0:T(8,128)(2,1)S(1)}, bf16[264,1280]{1,0:T(8,128)(2,1)}, u32[]{:S(2)}, u32[]{:S(2)}) collective-permute-start(bf16[264,1280]{1,0:T(8,128)(2,1)S(1)} %fusion.8), channel_id=1, source_target_pairs={{12,0},{16,4},{20,8},{24,12},{28,16},{13,1},{17,5},{21,9},{25,13},... | collective-permute-start | bytes 2027528 | tf_op jit(solution)/shard_map/ppermute | solution.py:13
  22.8 1.3 %collective-permute-start.5 = (bf16[264,1280]{1,0:T(8,128)(2,1)S(1)}, bf16[264,1280]{1,0:T(8,128)(2,1)}, u32[]{:S(2)}, u32[]{:S(2)}) collective-permute-start(bf16[264,1280]{1,0:T(8,128)(2,1)S(1)} %fusion.8), channel_id=1, source_target_pairs={{0,8},{4,12},{8,16},{12,20},{16,24},{20,28},{1,9},{5,13},{9,17},{1... | collective-permute-start | bytes 2027528 | tf_op jit(solution)/shard_map/ppermute | solution.py:13
  24.0 3.0 %collective-permute-start.4 = (bf16[264,1280]{1,0:T(8,128)(2,1)S(1)}, bf16[264,1280]{1,0:T(8,128)(2,1)S(1)}, u32[]{:S(2)}, u32[]{:S(2)}) collective-permute-start(bf16[264,1280]{1,0:T(8,128)(2,1)S(1)} %fusion.8), channel_id=1, source_target_pairs={{4,0},{8,4},{12,8},{16,12},{20,16},{24,20},{28,24},{5,1},{9,5},{13... | collective-permute-start | bytes 2027528 | tf_op jit(solution)/shard_map/ppermute | solution.py:13
  27.2 0.1 pad.33.clone
  27.2 0.1 pad.17.clone
  27.3 0.0 collective-permute-done.3
  27.4 0.2 fusion.44
  27.6 20.7 %collective-permute-done.13 = bf16[264,1280]{1,0:T(8,128)(2,1)} collective-permute-done((bf16[264,1280]{1,0:T(8,128)(2,1)S(1)}, bf16[264,1280]{1,0:T(8,128)(2,1)}, u32[]{:S(2)}, u32[]{:S(2)}) %collective-permute-start.13) | collective-permute-done | bytes 675872 | tf_op jit(solution)/shard_map/ppermute | solution.py:13
  48.3 0.7 slice_convert_fusion
  49.0 0.0 collective-permute-done.12
  49.0 0.7 slice_convert_fusion.1
  49.7 6.4 %collective-permute-done.5 = bf16[264,1280]{1,0:T(8,128)(2,1)} collective-permute-done((bf16[264,1280]{1,0:T(8,128)(2,1)S(1)}, bf16[264,1280]{1,0:T(8,128)(2,1)}, u32[]{:S(2)}, u32[]{:S(2)}) %collective-permute-start.5) | collective-permute-done | bytes 675872 | tf_op jit(solution)/shard_map/ppermute | solution.py:13
  56.1 0.7 slice_convert_fusion.2
  56.9 1.5 %fusion.13 = f32[256,256]{1,0:T(8,128)S(1)} fusion(bf16[264,1280]{1,0:T(8,128)(2,1)} %collective-permute-done.5, bf16[256,256]{1,0:T(8,128)(2,1)S(1)} %get-tuple-element.41, bf16[256,1024]{1,0:T(8,128)(2,1)S(1)} %get-tuple-element.31), kind=kOutput, calls=%fused_computation.24 | convolution fusion | flops 169082880 | bytes 1572864 | tf_op jit(solution)/shard_map/dot_general | solution.py:95
  58.3 0.4 fusion.15
  58.7 0.1 maximum_bitcast_fusion.3
  58.8 0.1 collective-permute-start.6
  58.9 1.5 %fusion.9 = f32[256,256]{1,0:T(8,128)S(1)} fusion(bf16[264,1280]{1,0:T(8,128)(2,1)} %collective-permute-done.13, bf16[256,256]{1,0:T(8,128)(2,1)S(1)} %get-tuple-element.41, bf16[256,1024]{1,0:T(8,128)(2,1)S(1)} %get-tuple-element.31), kind=kOutput, calls=%fused_computation.20 | convolution fusion | flops 169082880 | bytes 1572864 | tf_op jit(solution)/shard_map/dot_general | solution.py:95
  60.4 1.5 %fusion.11 = f32[256,256]{1,0:T(8,128)S(1)} fusion(bf16[264,1280]{1,0:T(8,128)(2,1)} %collective-permute-done.12, bf16[256,256]{1,0:T(8,128)(2,1)S(1)} %get-tuple-element.41, bf16[256,1024]{1,0:T(8,128)(2,1)S(1)} %get-tuple-element.31), kind=kOutput, calls=%fused_computation.22 | convolution fusion | flops 169082880 | bytes 1572864 | tf_op jit(solution)/shard_map/dot_general | solution.py:95
  61.8 0.1 maximum_bitcast_fusion.1
  62.0 0.6 collective-permute-start.14
  62.6 1.6 %collective-permute-start.7 = (f32[2,132,128]{2,1,0:T(8,128)S(1)}, f32[2,132,128]{2,1,0:T(8,128)S(1)}, u32[]{:S(2)}, u32[]{:S(2)}) collective-permute-start(f32[2,132,128]{2,1,0:T(8,128)S(1)} %constant_dynamic-slice_fusion.1), channel_id=1, source_target_pairs={{0,2},{1,3},{2,0},{3,1},{4,6},{5,7},{6,4},{7,5},{8,10},{9,11},{10,... | collective-permute-start | bytes 405512 | tf_op jit(solution)/shard_map/ppermute | solution.py:18
  64.3 1.1 collective-permute-start.15
  65.4 3.8 %collective-permute-done.7 = f32[2,132,128]{2,1,0:T(8,128)S(1)} collective-permute-done((f32[2,132,128]{2,1,0:T(8,128)S(1)}, f32[2,132,128]{2,1,0:T(8,128)S(1)}, u32[]{:S(2)}, u32[]{:S(2)}) %collective-permute-start.7) | collective-permute-done | bytes 135200 | tf_op jit(solution)/shard_map/ppermute | solution.py:18
  69.3 1.6 %collective-permute-start.8 = (f32[2,132,128]{2,1,0:T(8,128)S(1)}, f32[2,132,128]{2,1,0:T(8,128)S(1)}, u32[]{:S(2)}, u32[]{:S(2)}) collective-permute-start(f32[2,132,128]{2,1,0:T(8,128)S(1)} %dynamic-slice_add_fusion.1), channel_id=1, source_target_pairs={{0,2},{1,3},{2,0},{3,1},{4,6},{5,7},{6,4},{7,5},{8,10},{9,11},{10,... | collective-permute-start | bytes 405512 | tf_op jit(solution)/shard_map/ppermute | solution.py:18
  70.8 1.6 %collective-permute-done.15 = f32[2,140,128]{2,1,0:T(8,128)S(1)} collective-permute-done((f32[2,140,128]{2,1,0:T(8,128)S(1)}, f32[2,140,128]{2,1,0:T(8,128)S(1)}, u32[]{:S(2)}, u32[]{:S(2)}) %collective-permute-start.15) | collective-permute-done | bytes 143392 | tf_op jit(solution)/shard_map/ppermute | solution.py:18
  72.4 1.6 %collective-permute-start.16 = (f32[2,140,128]{2,1,0:T(8,128)S(1)}, f32[2,140,128]{2,1,0:T(8,128)S(1)}, u32[]{:S(2)}, u32[]{:S(2)}) collective-permute-start(f32[2,140,128]{2,1,0:T(8,128)S(1)} %dynamic-slice_add_fusion), channel_id=1, source_target_pairs={{0,2},{1,3},{2,0},{3,1},{4,6},{5,7},{6,4},{7,5},{8,10},{9,11},{10,... | collective-permute-start | bytes 430088 | tf_op jit(solution)/shard_map/ppermute | solution.py:18
  74.0 1.6 %collective-permute-done.8 = f32[2,132,128]{2,1,0:T(8,128)S(1)} collective-permute-done((f32[2,132,128]{2,1,0:T(8,128)S(1)}, f32[2,132,128]{2,1,0:T(8,128)S(1)}, u32[]{:S(2)}, u32[]{:S(2)}) %collective-permute-start.8) | collective-permute-done | bytes 135200 | tf_op jit(solution)/shard_map/ppermute | solution.py:18
  75.6 0.1 collective-permute-start.9
  75.7 1.9 %collective-permute-done.16 = f32[2,140,128]{2,1,0:T(8,128)S(1)} collective-permute-done((f32[2,140,128]{2,1,0:T(8,128)S(1)}, f32[2,140,128]{2,1,0:T(8,128)S(1)}, u32[]{:S(2)}, u32[]{:S(2)}) %collective-permute-start.16) | collective-permute-done | bytes 143392 | tf_op jit(solution)/shard_map/ppermute | solution.py:18
  77.7 0.1 collective-permute-start.17
  77.8 0.1 broadcast_select_fusion.3
  77.9 0.3 fusion.77
  78.1 0.2 fusion.65
  78.4 0.2 fusion.62
  78.6 11.3 %collective-permute-start.11 = (f32[257,256]{1,0:T(8,128)S(1)}, f32[257,256]{1,0:T(8,128)S(1)}, u32[]{:S(2)}, u32[]{:S(2)}) collective-permute-start(f32[257,256]{1,0:T(8,128)S(1)} %pad_maximum_fusion.4), channel_id=1, source_target_pairs={{8,0},{12,4},{16,8},{20,12},{24,16},{28,20},{9,1},{13,5},{17,9},{2... | collective-permute-start | bytes 789512 | tf_op jit(solution)/shard_map/ppermute | solution.py:13
  89.9 1.9 %collective-permute-start.10 = (f32[257,256]{1,0:T(8,128)S(1)}, f32[257,256]{1,0:T(8,128)S(1)}, u32[]{:S(2)}, u32[]{:S(2)}) collective-permute-start(f32[257,256]{1,0:T(8,128)S(1)} %pad_maximum_fusion.3), channel_id=1, source_target_pairs={{0,4},{4,8},{8,12},{12,16},{16,20},{20,24},{24,28},{1,5},{5,9},{9,... | collective-permute-start | bytes 789512 | tf_op jit(solution)/shard_map/ppermute | solution.py:13
  91.8 1.1 fusion.50
  93.0 0.3 fusion.79
  93.3 0.2 fusion.59
  93.5 0.2 fusion.56
  93.8 5.3 %collective-permute-start.19 = (f32[257,256]{1,0:T(8,128)S(1)}, f32[257,256]{1,0:T(8,128)S(1)}, u32[]{:S(2)}, u32[]{:S(2)}) collective-permute-start(f32[257,256]{1,0:T(8,128)S(1)} %pad_maximum_fusion.6), channel_id=1, source_target_pairs={{16,0},{20,4},{24,8},{28,12},{17,1},{21,5},{25,9},{29,13},{18,2},{... | collective-permute-start | bytes 789512 | tf_op jit(solution)/shard_map/ppermute | solution.py:13
  99.1 1.3 %collective-permute-start.18 = (f32[257,256]{1,0:T(8,128)S(1)}, f32[257,256]{1,0:T(8,128)S(1)}, u32[]{:S(2)}, u32[]{:S(2)}) collective-permute-start(f32[257,256]{1,0:T(8,128)S(1)} %pad_maximum_fusion.5), channel_id=1, source_target_pairs={{0,12},{4,16},{8,20},{12,24},{16,28},{1,13},{5,17},{9,21},{13,25},... | collective-permute-start | bytes 789512 | tf_op jit(solution)/shard_map/ppermute | solution.py:13
  100.4 1.1 fusion.46
  101.5 1.1 fusion.48
  102.6 2.6 %collective-permute-done.19 = f32[257,256]{1,0:T(8,128)S(1)} collective-permute-done((f32[257,256]{1,0:T(8,128)S(1)}, f32[257,256]{1,0:T(8,128)S(1)}, u32[]{:S(2)}, u32[]{:S(2)}) %collective-permute-start.19) | collective-permute-done | bytes 263200 | tf_op jit(solution)/shard_map/ppermute | solution.py:13
  105.2 11.1 %collective-permute-done.18 = f32[257,256]{1,0:T(8,128)S(1)} collective-permute-done((f32[257,256]{1,0:T(8,128)S(1)}, f32[257,256]{1,0:T(8,128)S(1)}, u32[]{:S(2)}, u32[]{:S(2)}) %collective-permute-start.18) | collective-permute-done | bytes 263200 | tf_op jit(solution)/shard_map/ppermute | solution.py:13
  116.3 1.0 fusion.25
  (54 shorter events, 0.8 us)
Async XLA Ops:
  0.0 1.3 %copy-start.1 = (bf16[256,1024]{1,0:T(8,128)(2,1)S(1)}, bf16[256,1024]{1,0:T(8,128)(2,1)}, u32[]{:S(2)}) copy-start(bf16[256,1024]{1,0:T(8,128)(2,1)} %param.2) | copy-start | bytes 1572868
  1.3 0.9 copy-start
  3.0 1.4 %collective-permute-start = (f32[1,272,128]{2,1,0:T(8,128)S(1)}, f32[1,272,128]{2,1,0:T(8,128)S(1)}, u32[]{:S(2)}, u32[]{:S(2)}) collective-permute-start(f32[1,272,128]{2,1,0:T(8,128)S(1)} %dynamic-slice_bitcast_fusion), channel_id=1, source_target_pairs={{0,1},{1,0},{2,3},{3,2},{4,5},{5,4},{6,7},{7,6},{8,9},{9,8},{10,11... | collective-permute-start | bytes 417800 | tf_op jit(solution)/shard_map/ppermute | solution.py:18
  4.4 4.4 %collective-permute-start.1 = (f32[1,136,128]{2,1,0:T(8,128)S(1)}, f32[1,136,128]{2,1,0:T(8,128)S(1)}, u32[]{:S(2)}, u32[]{:S(2)}) collective-permute-start(f32[1,136,128]{2,1,0:T(8,128)S(1)} %constant_dynamic-slice_fusion.2), channel_id=1, source_target_pairs={{0,2},{1,3},{2,0},{3,1},{4,6},{5,7},{6,4},{7,5},{8,10},{9,11},{10,... | collective-permute-start | bytes 208904 | tf_op jit(solution)/shard_map/ppermute | solution.py:18
  8.8 4.4 %collective-permute-start.2 = (f32[1,136,128]{2,1,0:T(8,128)S(1)}, f32[1,136,128]{2,1,0:T(8,128)S(1)}, u32[]{:S(2)}, u32[]{:S(2)}) collective-permute-start(f32[1,136,128]{2,1,0:T(8,128)S(1)} %dynamic-slice_add_fusion.2), channel_id=1, source_target_pairs={{0,2},{1,3},{2,0},{3,1},{4,6},{5,7},{6,4},{7,5},{8,10},{9,11},{10,... | collective-permute-start | bytes 208904 | tf_op jit(solution)/shard_map/ppermute | solution.py:18
  13.2 14.1 %collective-permute-start.3 = (f32[1,272,128]{2,1,0:T(8,128)S(1)}, f32[1,272,128]{2,1,0:T(8,128)S(1)}, u32[]{:S(2)}, u32[]{:S(2)}) collective-permute-start(f32[1,272,128]{2,1,0:T(8,128)S(1)} %pad_maximum_fusion.10), channel_id=1, source_target_pairs={{0,1},{1,0},{2,3},{3,2},{4,5},{5,4},{6,7},{7,6},{8,9},{9,8},{10,11... | collective-permute-start | bytes 417800 | tf_op jit(solution)/shard_map/ppermute | solution.py:18
  13.4 34.9 %collective-permute-start.13 = (bf16[264,1280]{1,0:T(8,128)(2,1)S(1)}, bf16[264,1280]{1,0:T(8,128)(2,1)}, u32[]{:S(2)}, u32[]{:S(2)}) collective-permute-start(bf16[264,1280]{1,0:T(8,128)(2,1)S(1)} %fusion.8), channel_id=1, source_target_pairs={{0,16},{4,20},{8,24},{12,28},{1,17},{5,21},{9,25},{13,29},{2,18},{... | collective-permute-start | bytes 2027528 | tf_op jit(solution)/shard_map/ppermute | solution.py:13
  14.7 34.3 %collective-permute-start.12 = (bf16[264,1280]{1,0:T(8,128)(2,1)S(1)}, bf16[264,1280]{1,0:T(8,128)(2,1)}, u32[]{:S(2)}, u32[]{:S(2)}) collective-permute-start(bf16[264,1280]{1,0:T(8,128)(2,1)S(1)} %fusion.8), channel_id=1, source_target_pairs={{12,0},{16,4},{20,8},{24,12},{28,16},{13,1},{17,5},{21,9},{25,13},... | collective-permute-start | bytes 2027528 | tf_op jit(solution)/shard_map/ppermute | solution.py:13
  22.8 33.4 %collective-permute-start.5 = (bf16[264,1280]{1,0:T(8,128)(2,1)S(1)}, bf16[264,1280]{1,0:T(8,128)(2,1)}, u32[]{:S(2)}, u32[]{:S(2)}) collective-permute-start(bf16[264,1280]{1,0:T(8,128)(2,1)S(1)} %fusion.8), channel_id=1, source_target_pairs={{0,8},{4,12},{8,16},{12,20},{16,24},{20,28},{1,9},{5,13},{9,17},{1... | collective-permute-start | bytes 2027528 | tf_op jit(solution)/shard_map/ppermute | solution.py:13
  24.0 32.8 %collective-permute-start.4 = (bf16[264,1280]{1,0:T(8,128)(2,1)S(1)}, bf16[264,1280]{1,0:T(8,128)(2,1)S(1)}, u32[]{:S(2)}, u32[]{:S(2)}) collective-permute-start(bf16[264,1280]{1,0:T(8,128)(2,1)S(1)} %fusion.8), channel_id=1, source_target_pairs={{4,0},{8,4},{12,8},{16,12},{20,16},{24,20},{28,24},{5,1},{9,5},{13... | collective-permute-start | bytes 2027528 | tf_op jit(solution)/shard_map/ppermute | solution.py:13
  58.8 3.7 %collective-permute-start.6 = (f32[2,264,128]{2,1,0:T(8,128)S(1)}, f32[2,264,128]{2,1,0:T(8,128)S(1)}, u32[]{:S(2)}, u32[]{:S(2)}) collective-permute-start(f32[2,264,128]{2,1,0:T(8,128)S(1)} %fusion.20), channel_id=1, source_target_pairs={{0,1},{1,0},{2,3},{3,2},{4,5},{5,4},{6,7},{7,6},{8,9},{9,8},{10,11... | collective-permute-start | bytes 811016 | tf_op jit(solution)/shard_map/ppermute | solution.py:18
  62.0 2.2 %collective-permute-start.14 = (f32[2,280,128]{2,1,0:T(8,128)S(1)}, f32[2,280,128]{2,1,0:T(8,128)S(1)}, u32[]{:S(2)}, u32[]{:S(2)}) collective-permute-start(f32[2,280,128]{2,1,0:T(8,128)S(1)} %fusion.17), channel_id=1, source_target_pairs={{0,1},{1,0},{2,3},{3,2},{4,5},{5,4},{6,7},{7,6},{8,9},{9,8},{10,11... | collective-permute-start | bytes 860168 | tf_op jit(solution)/shard_map/ppermute | solution.py:18
  62.6 6.6 %collective-permute-start.7 = (f32[2,132,128]{2,1,0:T(8,128)S(1)}, f32[2,132,128]{2,1,0:T(8,128)S(1)}, u32[]{:S(2)}, u32[]{:S(2)}) collective-permute-start(f32[2,132,128]{2,1,0:T(8,128)S(1)} %constant_dynamic-slice_fusion.1), channel_id=1, source_target_pairs={{0,2},{1,3},{2,0},{3,1},{4,6},{5,7},{6,4},{7,5},{8,10},{9,11},{10,... | collective-permute-start | bytes 405512 | tf_op jit(solution)/shard_map/ppermute | solution.py:18
  64.3 8.1 %collective-permute-start.15 = (f32[2,140,128]{2,1,0:T(8,128)S(1)}, f32[2,140,128]{2,1,0:T(8,128)S(1)}, u32[]{:S(2)}, u32[]{:S(2)}) collective-permute-start(f32[2,140,128]{2,1,0:T(8,128)S(1)} %constant_dynamic-slice_fusion), channel_id=1, source_target_pairs={{0,2},{1,3},{2,0},{3,1},{4,6},{5,7},{6,4},{7,5},{8,10},{9,11},{10,... | collective-permute-start | bytes 430088 | tf_op jit(solution)/shard_map/ppermute | solution.py:18
  69.3 6.3 %collective-permute-start.8 = (f32[2,132,128]{2,1,0:T(8,128)S(1)}, f32[2,132,128]{2,1,0:T(8,128)S(1)}, u32[]{:S(2)}, u32[]{:S(2)}) collective-permute-start(f32[2,132,128]{2,1,0:T(8,128)S(1)} %dynamic-slice_add_fusion.1), channel_id=1, source_target_pairs={{0,2},{1,3},{2,0},{3,1},{4,6},{5,7},{6,4},{7,5},{8,10},{9,11},{10,... | collective-permute-start | bytes 405512 | tf_op jit(solution)/shard_map/ppermute | solution.py:18
  72.4 5.2 %collective-permute-start.16 = (f32[2,140,128]{2,1,0:T(8,128)S(1)}, f32[2,140,128]{2,1,0:T(8,128)S(1)}, u32[]{:S(2)}, u32[]{:S(2)}) collective-permute-start(f32[2,140,128]{2,1,0:T(8,128)S(1)} %dynamic-slice_add_fusion), channel_id=1, source_target_pairs={{0,2},{1,3},{2,0},{3,1},{4,6},{5,7},{6,4},{7,5},{8,10},{9,11},{10,... | collective-permute-start | bytes 430088 | tf_op jit(solution)/shard_map/ppermute | solution.py:18
  75.6 2.2 %collective-permute-start.9 = (f32[2,264,128]{2,1,0:T(8,128)S(1)}, f32[2,264,128]{2,1,0:T(8,128)S(1)}, u32[]{:S(2)}, u32[]{:S(2)}) collective-permute-start(f32[2,264,128]{2,1,0:T(8,128)S(1)} %pad_maximum_fusion.2), channel_id=1, source_target_pairs={{0,1},{1,0},{2,3},{3,2},{4,5},{5,4},{6,7},{7,6},{8,9},{9,8},{10,11... | collective-permute-start | bytes 811016 | tf_op jit(solution)/shard_map/ppermute | solution.py:18
  77.7 15.2 %collective-permute-start.17 = (f32[2,280,128]{2,1,0:T(8,128)S(1)}, f32[2,280,128]{2,1,0:T(8,128)S(1)}, u32[]{:S(2)}, u32[]{:S(2)}) collective-permute-start(f32[2,280,128]{2,1,0:T(8,128)S(1)} %pad_maximum_fusion.1), channel_id=1, source_target_pairs={{0,1},{1,0},{2,3},{3,2},{4,5},{5,4},{6,7},{7,6},{8,9},{9,8},{10,11... | collective-permute-start | bytes 860168 | tf_op jit(solution)/shard_map/ppermute | solution.py:18
  78.6 24.0 %collective-permute-start.11 = (f32[257,256]{1,0:T(8,128)S(1)}, f32[257,256]{1,0:T(8,128)S(1)}, u32[]{:S(2)}, u32[]{:S(2)}) collective-permute-start(f32[257,256]{1,0:T(8,128)S(1)} %pad_maximum_fusion.4), channel_id=1, source_target_pairs={{8,0},{12,4},{16,8},{20,12},{24,16},{28,20},{9,1},{13,5},{17,9},{2... | collective-permute-start | bytes 789512 | tf_op jit(solution)/shard_map/ppermute | solution.py:13
  89.9 12.7 %collective-permute-start.10 = (f32[257,256]{1,0:T(8,128)S(1)}, f32[257,256]{1,0:T(8,128)S(1)}, u32[]{:S(2)}, u32[]{:S(2)}) collective-permute-start(f32[257,256]{1,0:T(8,128)S(1)} %pad_maximum_fusion.3), channel_id=1, source_target_pairs={{0,4},{4,8},{8,12},{12,16},{16,20},{20,24},{24,28},{1,5},{5,9},{9,... | collective-permute-start | bytes 789512 | tf_op jit(solution)/shard_map/ppermute | solution.py:13
  93.8 11.4 %collective-permute-start.19 = (f32[257,256]{1,0:T(8,128)S(1)}, f32[257,256]{1,0:T(8,128)S(1)}, u32[]{:S(2)}, u32[]{:S(2)}) collective-permute-start(f32[257,256]{1,0:T(8,128)S(1)} %pad_maximum_fusion.6), channel_id=1, source_target_pairs={{16,0},{20,4},{24,8},{28,12},{17,1},{21,5},{25,9},{29,13},{18,2},{... | collective-permute-start | bytes 789512 | tf_op jit(solution)/shard_map/ppermute | solution.py:13
  99.1 17.2 %collective-permute-start.18 = (f32[257,256]{1,0:T(8,128)S(1)}, f32[257,256]{1,0:T(8,128)S(1)}, u32[]{:S(2)}, u32[]{:S(2)}) collective-permute-start(f32[257,256]{1,0:T(8,128)S(1)} %pad_maximum_fusion.5), channel_id=1, source_target_pairs={{0,12},{4,16},{8,20},{12,24},{16,28},{1,13},{5,17},{9,21},{13,25},... | collective-permute-start | bytes 789512 | tf_op jit(solution)/shard_map/ppermute | solution.py:13

commit v13 on v12

--- a/solution.py
+++ b/solution.py
@@ -44,19 +44,6 @@
     return joined(part, swapped(part, "width", 1), 2, core)
 
 
-def split3(x):
-    hi = lax.reduce_precision(x, exponent_bits=8, mantissa_bits=7)
-    r1 = x - hi
-    mid = lax.reduce_precision(r1, exponent_bits=8, mantissa_bits=7)
-    lo = r1 - mid
-    return jnp.stack([hi, mid, lo]).astype(jnp.bfloat16)
-
-
-def join3(rows):
-    rows = rows.astype(jnp.float32)
-    return (rows[0] + rows[1]) + rows[2]
-
-
 def layer(teacher, student):
     group = lax.axis_size("batch")
     owner = lax.axis_index("batch")
@@ -73,27 +60,20 @@
         xf = x.astype(jnp.float32)
         return jnp.sum(xf * xf, axis=1)
 
-    own_q = sq(student) / ds - sq(teacher) / dt
     offsets = [0] + [d if d % 2 else -d for d in range(1, reach + 1)]
     both = jnp.concatenate([teacher, student], axis=1)
-    q_rows = jnp.concatenate([split3(own_q), jnp.zeros((5, rows_dev), jnp.bfloat16)])
-    q_rows = jnp.concatenate([q_rows, jnp.zeros((8, ft + fs - rows_dev), jnp.bfloat16)], axis=1)
-    fwd = jnp.concatenate([both, q_rows], axis=0)
+    rhs_band = [both]
+    for e in offsets[1:]:
+        rhs_band.append(shifted(both, "batch", e))
     scaled = jnp.concatenate([teacher * jnp.bfloat16(-2.0 / dt), student * jnp.bfloat16(2.0 / ds)], axis=1)
-    rhs_band = [both]
-    q_band = [own_q]
-    student_band = [student]
-    for e in offsets[1:]:
-        got = shifted(fwd, "batch", e)
-        rhs_band.append(got[:rows_dev])
-        q_band.append(join3(got[rows_dev:rows_dev + 3, :rows_dev]))
-        student_band.append(got[:rows_dev, ft:])
+    q_band = [sq(b[:, ft:]) / ds - sq(b[:, :ft]) / dt for b in rhs_band]
+    student_band = [b[:, ft:] for b in rhs_band]
 
     pad = (-(rows_dev + 1)) % 8
 
     def tile_part(d):
         g = lax.dot_general(scaled, rhs_band[d], (((1,), (1,)), ((), ())), preferred_element_type=jnp.float32)
-        rows = jnp.zeros((pad + (8 if d == 0 else 16 if d >= 3 else 0), rows_dev), jnp.float32)
+        rows = jnp.zeros((pad + (8 if d == 0 else 0), rows_dev), jnp.float32)
         return jnp.concatenate([g, q_band[d][None, :], rows], axis=0)
 
     student_f = student.astype(jnp.float32)

time: 118 us -> 107 us (0.907)
  matrix products: 10.5 us -> 5.61 us
  starting transfers between devices: 43.3 us -> 39 us
  waiting for transfers between devices: 56.7 us -> 54.2 us
    dot_general x5, matrix products: 4.51 us -> 1.78 us  [layer(): jnp.dot(low, student_band[d], preferred_element_type=jnp.float32)]
    ppermute x8, waiting for transfers between devices: 40.8 us -> 38.2 us  [shifted(): return lax.ppermute(block, axis, route)]
    ppermute x12, starting transfers between devices: 9.84 us -> 7.34 us  [swapped(): return lax.ppermute(block, axis, [(i, i ^ mask) for i in range(size)])]
    dot_general x5, matrix products: 5.1 us -> 2.94 us  [tile_part(): lax.dot_general(scaled, rhs_band[d], (((1,), (1,)), ((), ())), preferred_...]
    convert_element_type x4 -> x0, other arithmetic: 2.04 us -> none  [join3(): rows = rows.astype(jnp.float32)]
    ppermute x8, starting transfers between devices: 33.5 us -> 31.7 us  [shifted(): return lax.ppermute(block, axis, route)]
    reduce_sum x2 -> x10, other arithmetic: 1.41 us -> 2.59 us  [sq(): return jnp.sum(xf * xf, axis=1)]
  transfers between devices with their start and end apart: 20 -> 20, of which waited for: 11 -> 11; matrix products, arithmetic and copies ran while one was open for 9% -> 5% of each run, Pallas kernels for 0% -> 0%
where the time goes in v13:
time: 107 us
  waiting for transfers between devices  54.2 us (51%)
  starting transfers between devices  39 us (36%)
  other arithmetic  6.19 us (6%)
  matrix products  5.61 us (5%)
  local copies, waits for them, and re-layouts  1.13 us (1%)
    ppermute x8, waiting for transfers between devices, shifted(): return lax.ppermute(block, axis, route)  38.2 us
    ppermute x8, starting transfers between devices, shifted(): return lax.ppermute(block, axis, route)  31.7 us
    ppermute x12, waiting for transfers between devices, swapped(): return lax.ppermute(block, axis, [(i, i ^ mask) for i in range(size)])  15.9 us
    ppermute x12, starting transfers between devices, swapped(): return lax.ppermute(block, axis, [(i, i ^ mask) for i in range(size)])  7.34 us
    dot_general x5, matrix products, tile_part(): lax.dot_general(scaled, rhs_band[d], (((1,), (1,)), ((), ())), preferred_...  2.94 us
    reduce_sum x10, other arithmetic, sq(): return jnp.sum(xf * xf, axis=1)  2.59 us
  transfers between devices with their start and end apart: 20, of which 11 were waited for; matrix products, arithmetic and copies ran while one was open for 5% of the time, Pallas kernels for 0%

profile of v13, /device:TPU:24, one launch (start us, length us, event | category | flops | bytes accessed | tf_op | source)
XLA Modules:
  0.0 106.7 jit_solution(17317066714672585351)
XLA Ops:
  0.0 1.3 %multiply_reduce_fusion.4 = f32[256]{0:T(256)S(1)} fusion(bf16[256,1024]{1,0:T(8,128)(2,1)} %param.2), kind=kLoop, calls=%fused_computation.12 | loop fusion | flops 786176 | bytes 525312 | tf_op jit(solution)/shard_map/reduce_sum | solution.py:61
  1.3 0.9 broadcast_multiply_fusion
  2.2 0.1 fusion.13
  2.3 0.7 broadcast_multiply_fusion.1
  3.0 0.1 pad.38.clone
  3.1 1.5 %fusion.64 = f32[256,256]{1,0:T(8,128)S(1)} fusion(bf16[256,1280]{1,0:T(8,128)(2,1)} %get-tuple-element.42, bf16[256,256]{1,0:T(8,128)(2,1)S(1)} %get-tuple-element.41, bf16[256,1024]{1,0:T(8,128)(2,1)S(1)} %get-tuple-element.31), kind=kOutput, calls=%fused_computation.140 | convolution fusion | flops 169082880 | bytes 1572864 | tf_op jit(solution)/shard_map/dot_general | solution.py:75
  4.6 0.1 maximum_maximum_fusion
  4.7 0.1 collective-permute-start
  4.8 1.3 %collective-permute-done = f32[1,272,128]{2,1,0:T(8,128)S(1)} collective-permute-done((f32[1,272,128]{2,1,0:T(8,128)S(1)}, f32[1,272,128]{2,1,0:T(8,128)S(1)}, u32[]{:S(2)}, u32[]{:S(2)}) %collective-permute-start) | collective-permute-done | bytes 139296 | tf_op jit(solution)/shard_map/ppermute | solution.py:18
  6.2 1.6 %collective-permute-start.1 = (f32[1,136,128]{2,1,0:T(8,128)S(1)}, f32[1,136,128]{2,1,0:T(8,128)S(1)}, u32[]{:S(2)}, u32[]{:S(2)}) collective-permute-start(f32[1,136,128]{2,1,0:T(8,128)S(1)} %constant_dynamic-slice_fusion.2), channel_id=1, source_target_pairs={{0,2},{1,3},{2,0},{3,1},{4,6},{5,7},{6,4},{7,5},{8,10},{9,11},{10,... | collective-permute-start | bytes 208904 | tf_op jit(solution)/shard_map/ppermute | solution.py:18
  7.7 2.8 %collective-permute-done.1 = f32[1,136,128]{2,1,0:T(8,128)S(1)} collective-permute-done((f32[1,136,128]{2,1,0:T(8,128)S(1)}, f32[1,136,128]{2,1,0:T(8,128)S(1)}, u32[]{:S(2)}, u32[]{:S(2)}) %collective-permute-start.1) | collective-permute-done | bytes 69664 | tf_op jit(solution)/shard_map/ppermute | solution.py:18
  10.6 1.6 %collective-permute-start.2 = (f32[1,136,128]{2,1,0:T(8,128)S(1)}, f32[1,136,128]{2,1,0:T(8,128)S(1)}, u32[]{:S(2)}, u32[]{:S(2)}) collective-permute-start(f32[1,136,128]{2,1,0:T(8,128)S(1)} %dynamic-slice_add_fusion.2), channel_id=1, source_target_pairs={{0,2},{1,3},{2,0},{3,1},{4,6},{5,7},{6,4},{7,5},{8,10},{9,11},{10,... | collective-permute-start | bytes 208904 | tf_op jit(solution)/shard_map/ppermute | solution.py:18
  12.1 1.3 %collective-permute-start.13 = (bf16[256,1280]{1,0:T(8,128)(2,1)}, bf16[256,1280]{1,0:T(8,128)(2,1)S(1)}, u32[]{:S(2)}, u32[]{:S(2)}) collective-permute-start(bf16[256,1280]{1,0:T(8,128)(2,1)} %get-tuple-element.42), channel_id=1, source_target_pairs={{0,16},{4,20},{8,24},{12,28},{1,17},{5,21},{9,25},{13,29},{2,18},{... | collective-permute-start | bytes 1966088 | tf_op jit(solution)/shard_map/ppermute | solution.py:13
  13.4 6.5 %collective-permute-start.12 = (bf16[256,1280]{1,0:T(8,128)(2,1)}, bf16[256,1280]{1,0:T(8,128)(2,1)S(1)}, u32[]{:S(2)}, u32[]{:S(2)}) collective-permute-start(bf16[256,1280]{1,0:T(8,128)(2,1)} %get-tuple-element.42), channel_id=1, source_target_pairs={{12,0},{16,4},{20,8},{24,12},{28,16},{13,1},{17,5},{21,9},{25,13},... | collective-permute-start | bytes 1966088 | tf_op jit(solution)/shard_map/ppermute | solution.py:13
  19.9 0.7 pad_maximum_fusion.10
  20.6 1.3 %collective-permute-start.5 = (bf16[256,1280]{1,0:T(8,128)(2,1)}, bf16[256,1280]{1,0:T(8,128)(2,1)S(1)}, u32[]{:S(2)}, u32[]{:S(2)}) collective-permute-start(bf16[256,1280]{1,0:T(8,128)(2,1)} %get-tuple-element.42), channel_id=1, source_target_pairs={{0,8},{4,12},{8,16},{12,20},{16,24},{20,28},{1,9},{5,13},{9,17},{1... | collective-permute-start | bytes 1966088 | tf_op jit(solution)/shard_map/ppermute | solution.py:13
  21.9 3.0 %collective-permute-start.4 = (bf16[256,1280]{1,0:T(8,128)(2,1)}, bf16[256,1280]{1,0:T(8,128)(2,1)S(1)}, u32[]{:S(2)}, u32[]{:S(2)}) collective-permute-start(bf16[256,1280]{1,0:T(8,128)(2,1)} %get-tuple-element.42), channel_id=1, source_target_pairs={{4,0},{8,4},{12,8},{16,12},{20,16},{24,20},{28,24},{5,1},{9,5},{13... | collective-permute-start | bytes 1966088 | tf_op jit(solution)/shard_map/ppermute | solution.py:13
  25.0 0.7 pad.31.clone
  25.7 18.8 %collective-permute-done.13 = bf16[256,1280]{1,0:T(8,128)(2,1)S(1)} collective-permute-done((bf16[256,1280]{1,0:T(8,128)(2,1)}, bf16[256,1280]{1,0:T(8,128)(2,1)S(1)}, u32[]{:S(2)}, u32[]{:S(2)}) %collective-permute-start.13) | collective-permute-done | bytes 655392 | tf_op jit(solution)/shard_map/ppermute | solution.py:13
  44.5 0.1 multiply_reduce_fusion.5
  44.7 0.1 multiply_reduce_fusion.6
  44.8 0.2 multiply_reduce_fusion
  45.0 0.2 multiply_reduce_fusion.1
  45.2 8.6 %collective-permute-done.5 = bf16[256,1280]{1,0:T(8,128)(2,1)S(1)} collective-permute-done((bf16[256,1280]{1,0:T(8,128)(2,1)}, bf16[256,1280]{1,0:T(8,128)(2,1)S(1)}, u32[]{:S(2)}, u32[]{:S(2)}) %collective-permute-start.5) | collective-permute-done | bytes 655392 | tf_op jit(solution)/shard_map/ppermute | solution.py:13
  53.8 0.2 multiply_reduce_fusion.2
  54.0 0.1 multiply_reduce_fusion.7
  54.1 0.2 multiply_reduce_fusion.3
  54.3 0.1 multiply_reduce_fusion.8
  54.5 0.4 fusion.60
  54.8 0.4 fusion.61
  55.2 0.4 fusion.62
  55.6 0.4 fusion.63
  56.0 0.3 copy-done.4
  56.3 0.1 maximum_bitcast_fusion.1
  56.5 0.1 collective-permute-start.14
  56.5 0.2 fusion.34
  56.8 0.6 collective-permute-start.6
  57.4 0.7 collective-permute-done.14
  58.1 0.6 collective-permute-start.15
  58.8 1.5 %collective-permute-start.7 = (f32[2,132,128]{2,1,0:T(8,128)S(1)}, f32[2,132,128]{2,1,0:T(8,128)S(1)}, u32[]{:S(2)}, u32[]{:S(2)}) collective-permute-start(f32[2,132,128]{2,1,0:T(8,128)S(1)} %constant_dynamic-slice_fusion.1), channel_id=1, source_target_pairs={{0,2},{1,3},{2,0},{3,1},{4,6},{5,7},{6,4},{7,5},{8,10},{9,11},{10,... | collective-permute-start | bytes 405512 | tf_op jit(solution)/shard_map/ppermute | solution.py:18
  60.4 4.4 %collective-permute-done.15 = f32[2,132,128]{2,1,0:T(8,128)S(1)} collective-permute-done((f32[2,132,128]{2,1,0:T(8,128)S(1)}, f32[2,132,128]{2,1,0:T(8,128)S(1)}, u32[]{:S(2)}, u32[]{:S(2)}) %collective-permute-start.15) | collective-permute-done | bytes 135200 | tf_op jit(solution)/shard_map/ppermute | solution.py:18
  64.8 0.6 collective-permute-start.16
  65.4 2.3 %collective-permute-done.7 = f32[2,132,128]{2,1,0:T(8,128)S(1)} collective-permute-done((f32[2,132,128]{2,1,0:T(8,128)S(1)}, f32[2,132,128]{2,1,0:T(8,128)S(1)}, u32[]{:S(2)}, u32[]{:S(2)}) %collective-permute-start.7) | collective-permute-done | bytes 135200 | tf_op jit(solution)/shard_map/ppermute | solution.py:18
  67.8 0.6 collective-permute-start.8
  68.4 2.6 %collective-permute-done.16 = f32[2,132,128]{2,1,0:T(8,128)S(1)} collective-permute-done((f32[2,132,128]{2,1,0:T(8,128)S(1)}, f32[2,132,128]{2,1,0:T(8,128)S(1)}, u32[]{:S(2)}, u32[]{:S(2)}) %collective-permute-start.16) | collective-permute-done | bytes 135200 | tf_op jit(solution)/shard_map/ppermute | solution.py:18
  71.0 0.1 collective-permute-start.17
  71.1 1.8 %collective-permute-done.8 = f32[2,132,128]{2,1,0:T(8,128)S(1)} collective-permute-done((f32[2,132,128]{2,1,0:T(8,128)S(1)}, f32[2,132,128]{2,1,0:T(8,128)S(1)}, u32[]{:S(2)}, u32[]{:S(2)}) %collective-permute-start.8) | collective-permute-done | bytes 135200 | tf_op jit(solution)/shard_map/ppermute | solution.py:18
  72.9 0.1 collective-permute-start.9
  73.1 0.3 fusion.67
  73.4 0.2 fusion.46
  73.6 6.3 %collective-permute-start.19 = (f32[257,256]{1,0:T(8,128)S(1)}, f32[257,256]{1,0:T(8,128)S(1)}, u32[]{:S(2)}, u32[]{:S(2)}) collective-permute-start(f32[257,256]{1,0:T(8,128)S(1)} %pad_maximum_fusion.6), channel_id=1, source_target_pairs={{16,0},{20,4},{24,8},{28,12},{17,1},{21,5},{25,9},{29,13},{18,2},{... | collective-permute-start | bytes 789512 | tf_op jit(solution)/shard_map/ppermute | solution.py:13
  79.9 0.2 fusion.49
  80.2 1.3 %collective-permute-start.18 = (f32[257,256]{1,0:T(8,128)S(1)}, f32[257,256]{1,0:T(8,128)S(1)}, u32[]{:S(2)}, u32[]{:S(2)}) collective-permute-start(f32[257,256]{1,0:T(8,128)S(1)} %pad_maximum_fusion.5), channel_id=1, source_target_pairs={{0,12},{4,16},{8,20},{12,24},{16,28},{1,13},{5,17},{9,21},{13,25},... | collective-permute-start | bytes 789512 | tf_op jit(solution)/shard_map/ppermute | solution.py:13
  81.6 0.3 fusion.65
  81.8 0.2 fusion.55
  82.0 0.2 fusion.52
  82.3 10.1 %collective-permute-start.11 = (f32[257,256]{1,0:T(8,128)S(1)}, f32[257,256]{1,0:T(8,128)S(1)}, u32[]{:S(2)}, u32[]{:S(2)}) collective-permute-start(f32[257,256]{1,0:T(8,128)S(1)} %pad_maximum_fusion.3), channel_id=1, source_target_pairs={{8,0},{12,4},{16,8},{20,12},{24,16},{28,20},{9,1},{13,5},{17,9},{2... | collective-permute-start | bytes 789512 | tf_op jit(solution)/shard_map/ppermute | solution.py:13
  92.5 1.9 %collective-permute-start.10 = (f32[257,256]{1,0:T(8,128)S(1)}, f32[257,256]{1,0:T(8,128)S(1)}, u32[]{:S(2)}, u32[]{:S(2)}) collective-permute-start(f32[257,256]{1,0:T(8,128)S(1)} %pad_maximum_fusion.2), channel_id=1, source_target_pairs={{0,4},{4,8},{8,12},{12,16},{16,20},{20,24},{24,28},{1,5},{5,9},{9,... | collective-permute-start | bytes 789512 | tf_op jit(solution)/shard_map/ppermute | solution.py:13
  94.4 0.2 fusion.38
  94.6 0.2 fusion.40
  94.8 0.2 fusion.42
  95.0 5.2 %collective-permute-done.18 = f32[257,256]{1,0:T(8,128)S(1)} collective-permute-done((f32[257,256]{1,0:T(8,128)S(1)}, f32[257,256]{1,0:T(8,128)S(1)}, u32[]{:S(2)}, u32[]{:S(2)}) %collective-permute-start.18) | collective-permute-done | bytes 263200 | tf_op jit(solution)/shard_map/ppermute | solution.py:13
  100.2 5.5 %collective-permute-done.10 = f32[257,256]{1,0:T(8,128)S(1)} collective-permute-done((f32[257,256]{1,0:T(8,128)S(1)}, f32[257,256]{1,0:T(8,128)S(1)}, u32[]{:S(2)}, u32[]{:S(2)}) %collective-permute-start.10) | collective-permute-done | bytes 263200 | tf_op jit(solution)/shard_map/ppermute | solution.py:13
  105.7 1.0 fusion.15
  (58 shorter events, 0.7 us)
Async XLA Ops:
  0.0 1.3 %copy-start.1 = (bf16[256,1024]{1,0:T(8,128)(2,1)S(1)}, bf16[256,1024]{1,0:T(8,128)(2,1)}, u32[]{:S(2)}) copy-start(bf16[256,1024]{1,0:T(8,128)(2,1)} %param.2) | copy-start | bytes 1572868
  1.3 0.9 copy-start
  3.0 1.6 %copy-start.2 = (bf16[256,256]{1,0:T(8,128)(2,1)}, bf16[256,256]{1,0:T(8,128)(2,1)S(1)}, u32[]{:S(2)}) copy-start(bf16[256,256]{1,0:T(8,128)(2,1)S(1)} %get-tuple-element.41) | copy-start | bytes 393220
  4.7 1.4 %collective-permute-start = (f32[1,272,128]{2,1,0:T(8,128)S(1)}, f32[1,272,128]{2,1,0:T(8,128)S(1)}, u32[]{:S(2)}, u32[]{:S(2)}) collective-permute-start(f32[1,272,128]{2,1,0:T(8,128)S(1)} %dynamic-slice_bitcast_fusion), channel_id=1, source_target_pairs={{0,1},{1,0},{2,3},{3,2},{4,5},{5,4},{6,7},{7,6},{8,9},{9,8},{10,11... | collective-permute-start | bytes 417800 | tf_op jit(solution)/shard_map/ppermute | solution.py:18
  6.2 4.4 %collective-permute-start.1 = (f32[1,136,128]{2,1,0:T(8,128)S(1)}, f32[1,136,128]{2,1,0:T(8,128)S(1)}, u32[]{:S(2)}, u32[]{:S(2)}) collective-permute-start(f32[1,136,128]{2,1,0:T(8,128)S(1)} %constant_dynamic-slice_fusion.2), channel_id=1, source_target_pairs={{0,2},{1,3},{2,0},{3,1},{4,6},{5,7},{6,4},{7,5},{8,10},{9,11},{10,... | collective-permute-start | bytes 208904 | tf_op jit(solution)/shard_map/ppermute | solution.py:18
  10.6 9.3 %collective-permute-start.2 = (f32[1,136,128]{2,1,0:T(8,128)S(1)}, f32[1,136,128]{2,1,0:T(8,128)S(1)}, u32[]{:S(2)}, u32[]{:S(2)}) collective-permute-start(f32[1,136,128]{2,1,0:T(8,128)S(1)} %dynamic-slice_add_fusion.2), channel_id=1, source_target_pairs={{0,2},{1,3},{2,0},{3,1},{4,6},{5,7},{6,4},{7,5},{8,10},{9,11},{10,... | collective-permute-start | bytes 208904 | tf_op jit(solution)/shard_map/ppermute | solution.py:18
  12.1 32.4 %collective-permute-start.13 = (bf16[256,1280]{1,0:T(8,128)(2,1)}, bf16[256,1280]{1,0:T(8,128)(2,1)S(1)}, u32[]{:S(2)}, u32[]{:S(2)}) collective-permute-start(bf16[256,1280]{1,0:T(8,128)(2,1)} %get-tuple-element.42), channel_id=1, source_target_pairs={{0,16},{4,20},{8,24},{12,28},{1,17},{5,21},{9,25},{13,29},{2,18},{... | collective-permute-start | bytes 1966088 | tf_op jit(solution)/shard_map/ppermute | solution.py:13
  13.4 31.2 %collective-permute-start.12 = (bf16[256,1280]{1,0:T(8,128)(2,1)}, bf16[256,1280]{1,0:T(8,128)(2,1)S(1)}, u32[]{:S(2)}, u32[]{:S(2)}) collective-permute-start(bf16[256,1280]{1,0:T(8,128)(2,1)} %get-tuple-element.42), channel_id=1, source_target_pairs={{12,0},{16,4},{20,8},{24,12},{28,16},{13,1},{17,5},{21,9},{25,13},... | collective-permute-start | bytes 1966088 | tf_op jit(solution)/shard_map/ppermute | solution.py:13
  20.6 5.1 %collective-permute-start.3 = (f32[1,272,128]{2,1,0:T(8,128)}, f32[1,272,128]{2,1,0:T(8,128)S(1)}, u32[]{:S(2)}, u32[]{:S(2)}) collective-permute-start(f32[1,272,128]{2,1,0:T(8,128)} %pad_maximum_fusion.10), channel_id=1, source_target_pairs={{0,1},{1,0},{2,3},{3,2},{4,5},{5,4},{6,7},{7,6},{8,9},{9,8},{10,11... | collective-permute-start | bytes 417800 | tf_op jit(solution)/shard_map/ppermute | solution.py:18
  20.6 33.2 %collective-permute-start.5 = (bf16[256,1280]{1,0:T(8,128)(2,1)}, bf16[256,1280]{1,0:T(8,128)(2,1)S(1)}, u32[]{:S(2)}, u32[]{:S(2)}) collective-permute-start(bf16[256,1280]{1,0:T(8,128)(2,1)} %get-tuple-element.42), channel_id=1, source_target_pairs={{0,8},{4,12},{8,16},{12,20},{16,24},{20,28},{1,9},{5,13},{9,17},{1... | collective-permute-start | bytes 1966088 | tf_op jit(solution)/shard_map/ppermute | solution.py:13
  21.9 32.2 %collective-permute-start.4 = (bf16[256,1280]{1,0:T(8,128)(2,1)}, bf16[256,1280]{1,0:T(8,128)(2,1)S(1)}, u32[]{:S(2)}, u32[]{:S(2)}) collective-permute-start(bf16[256,1280]{1,0:T(8,128)(2,1)} %get-tuple-element.42), channel_id=1, source_target_pairs={{4,0},{8,4},{12,8},{16,12},{20,16},{24,20},{28,24},{5,1},{9,5},{13... | collective-permute-start | bytes 1966088 | tf_op jit(solution)/shard_map/ppermute | solution.py:13
  45.2 9.3 %copy-start.3 = (bf16[256,256]{1,0:T(8,128)(2,1)S(1)}, bf16[256,256]{1,0:T(8,128)(2,1)}, u32[]{:S(2)}) copy-start(bf16[256,256]{1,0:T(8,128)(2,1)} %copy-done.2) | copy-start | bytes 393220
  55.6 0.7 copy-start.4
  56.5 1.6 %collective-permute-start.14 = (f32[2,264,128]{2,1,0:T(8,128)S(1)}, f32[2,264,128]{2,1,0:T(8,128)S(1)}, u32[]{:S(2)}, u32[]{:S(2)}) collective-permute-start(f32[2,264,128]{2,1,0:T(8,128)S(1)} %fusion.7), channel_id=1, source_target_pairs={{0,1},{1,0},{2,3},{3,2},{4,5},{5,4},{6,7},{7,6},{8,9},{9,8},{10,11... | collective-permute-start | bytes 811016 | tf_op jit(solution)/shard_map/ppermute | solution.py:18
  56.8 1.9 %collective-permute-start.6 = (f32[2,264,128]{2,1,0:T(8,128)S(1)}, f32[2,264,128]{2,1,0:T(8,128)S(1)}, u32[]{:S(2)}, u32[]{:S(2)}) collective-permute-start(f32[2,264,128]{2,1,0:T(8,128)S(1)} %fusion.10), channel_id=1, source_target_pairs={{0,1},{1,0},{2,3},{3,2},{4,5},{5,4},{6,7},{7,6},{8,9},{9,8},{10,11... | collective-permute-start | bytes 811016 | tf_op jit(solution)/shard_map/ppermute | solution.py:18
  58.1 6.6 %collective-permute-start.15 = (f32[2,132,128]{2,1,0:T(8,128)S(1)}, f32[2,132,128]{2,1,0:T(8,128)S(1)}, u32[]{:S(2)}, u32[]{:S(2)}) collective-permute-start(f32[2,132,128]{2,1,0:T(8,128)S(1)} %constant_dynamic-slice_fusion), channel_id=1, source_target_pairs={{0,2},{1,3},{2,0},{3,1},{4,6},{5,7},{6,4},{7,5},{8,10},{9,11},{10,... | collective-permute-start | bytes 405512 | tf_op jit(solution)/shard_map/ppermute | solution.py:18
  58.8 8.9 %collective-permute-start.7 = (f32[2,132,128]{2,1,0:T(8,128)S(1)}, f32[2,132,128]{2,1,0:T(8,128)S(1)}, u32[]{:S(2)}, u32[]{:S(2)}) collective-permute-start(f32[2,132,128]{2,1,0:T(8,128)S(1)} %constant_dynamic-slice_fusion.1), channel_id=1, source_target_pairs={{0,2},{1,3},{2,0},{3,1},{4,6},{5,7},{6,4},{7,5},{8,10},{9,11},{10,... | collective-permute-start | bytes 405512 | tf_op jit(solution)/shard_map/ppermute | solution.py:18
  64.8 6.2 %collective-permute-start.16 = (f32[2,132,128]{2,1,0:T(8,128)S(1)}, f32[2,132,128]{2,1,0:T(8,128)S(1)}, u32[]{:S(2)}, u32[]{:S(2)}) collective-permute-start(f32[2,132,128]{2,1,0:T(8,128)S(1)} %dynamic-slice_add_fusion), channel_id=1, source_target_pairs={{0,2},{1,3},{2,0},{3,1},{4,6},{5,7},{6,4},{7,5},{8,10},{9,11},{10,... | collective-permute-start | bytes 405512 | tf_op jit(solution)/shard_map/ppermute | solution.py:18
  67.8 5.1 %collective-permute-start.8 = (f32[2,132,128]{2,1,0:T(8,128)S(1)}, f32[2,132,128]{2,1,0:T(8,128)S(1)}, u32[]{:S(2)}, u32[]{:S(2)}) collective-permute-start(f32[2,132,128]{2,1,0:T(8,128)S(1)} %dynamic-slice_add_fusion.1), channel_id=1, source_target_pairs={{0,2},{1,3},{2,0},{3,1},{4,6},{5,7},{6,4},{7,5},{8,10},{9,11},{10,... | collective-permute-start | bytes 405512 | tf_op jit(solution)/shard_map/ppermute | solution.py:18
  71.0 2.0 %collective-permute-start.17 = (f32[2,264,128]{2,1,0:T(8,128)S(1)}, f32[2,264,128]{2,1,0:T(8,128)S(1)}, u32[]{:S(2)}, u32[]{:S(2)}) collective-permute-start(f32[2,264,128]{2,1,0:T(8,128)S(1)} %pad_maximum_fusion.4), channel_id=1, source_target_pairs={{0,1},{1,0},{2,3},{3,2},{4,5},{5,4},{6,7},{7,6},{8,9},{9,8},{10,11... | collective-permute-start | bytes 811016 | tf_op jit(solution)/shard_map/ppermute | solution.py:18
  72.9 8.5 %collective-permute-start.9 = (f32[2,264,128]{2,1,0:T(8,128)S(1)}, f32[2,264,128]{2,1,0:T(8,128)S(1)}, u32[]{:S(2)}, u32[]{:S(2)}) collective-permute-start(f32[2,264,128]{2,1,0:T(8,128)S(1)} %pad_maximum_fusion.1), channel_id=1, source_target_pairs={{0,1},{1,0},{2,3},{3,2},{4,5},{5,4},{6,7},{7,6},{8,9},{9,8},{10,11... | collective-permute-start | bytes 811016 | tf_op jit(solution)/shard_map/ppermute | solution.py:18
  73.6 21.3 %collective-permute-start.19 = (f32[257,256]{1,0:T(8,128)S(1)}, f32[257,256]{1,0:T(8,128)S(1)}, u32[]{:S(2)}, u32[]{:S(2)}) collective-permute-start(f32[257,256]{1,0:T(8,128)S(1)} %pad_maximum_fusion.6), channel_id=1, source_target_pairs={{16,0},{20,4},{24,8},{28,12},{17,1},{21,5},{25,9},{29,13},{18,2},{... | collective-permute-start | bytes 789512 | tf_op jit(solution)/shard_map/ppermute | solution.py:13
  80.2 20.0 %collective-permute-start.18 = (f32[257,256]{1,0:T(8,128)S(1)}, f32[257,256]{1,0:T(8,128)S(1)}, u32[]{:S(2)}, u32[]{:S(2)}) collective-permute-start(f32[257,256]{1,0:T(8,128)S(1)} %pad_maximum_fusion.5), channel_id=1, source_target_pairs={{0,12},{4,16},{8,20},{12,24},{16,28},{1,13},{5,17},{9,21},{13,25},... | collective-permute-start | bytes 789512 | tf_op jit(solution)/shard_map/ppermute | solution.py:13
  82.3 17.9 %collective-permute-start.11 = (f32[257,256]{1,0:T(8,128)S(1)}, f32[257,256]{1,0:T(8,128)S(1)}, u32[]{:S(2)}, u32[]{:S(2)}) collective-permute-start(f32[257,256]{1,0:T(8,128)S(1)} %pad_maximum_fusion.3), channel_id=1, source_target_pairs={{8,0},{12,4},{16,8},{20,12},{24,16},{28,20},{9,1},{13,5},{17,9},{2... | collective-permute-start | bytes 789512 | tf_op jit(solution)/shard_map/ppermute | solution.py:13
  92.5 13.3 %collective-permute-start.10 = (f32[257,256]{1,0:T(8,128)S(1)}, f32[257,256]{1,0:T(8,128)S(1)}, u32[]{:S(2)}, u32[]{:S(2)}) collective-permute-start(f32[257,256]{1,0:T(8,128)S(1)} %pad_maximum_fusion.2), channel_id=1, source_target_pairs={{0,4},{4,8},{8,12},{12,16},{16,20},{20,24},{24,28},{1,5},{5,9},{9,... | collective-permute-start | bytes 789512 | tf_op jit(solution)/shard_map/ppermute | solution.py:13
